TPU v7x, 32 devices: a whole 2x2x4 slice. The times are simulated.
32 devices in a mesh: rep: 8 (over z, x), shard: 4 (over y, core).
Axes of the slice: x: 2, y: 2, z: 4, core: 2. Of those that a mesh axis runs over, the one named last changes fastest.
Arguments:
- tokens: bfloat16 [32, 384, 1024], P(('rep', 'shard')), may hold values from -6 to 6
- cont_segment: int32 [32, 2, 64], P(('rep', 'shard')), may hold values from 0 to 1, as said below
- cotangent: bfloat16 [32, 384, 1024], P(('rep', 'shard')), may hold values from -6 to 6
- ln1_gain: bfloat16 [1024], P('shard'), may hold values from 0.099609375 to 1.8984375
- ln1_bias: bfloat16 [1024], P('shard'), may hold values from -3 to 3
- w_qkv: bfloat16 [1024, 3072], P(None, 'shard'), may hold values from -0.1875 to 0.1875
- q_bias: bfloat16 [1024], P('shard'), may hold values from -3 to 3
- v_bias: bfloat16 [1024], P('shard'), may hold values from -3 to 3
- w_out: bfloat16 [1024, 1024], P('shard'), may hold values from -0.75 to 0.75
- b_out: bfloat16 [1024], P('shard'), may hold values from -3 to 3
- ln2_gain: bfloat16 [1024], P('shard'), may hold values from 0.099609375 to 1.8984375
- ln2_bias: bfloat16 [1024], P('shard'), may hold values from -3 to 3
- w_up: bfloat16 [1024, 4096], P(None, 'shard'), may hold values from -0.1875 to 0.1875
- b_up: bfloat16 [4096], P('shard'), may hold values from -3 to 3
- w_down: bfloat16 [4096, 1024], P('shard'), may hold values from -0.125 to 0.125
- b_down: bfloat16 [1024], P('shard'), may hold values from -3 to 3
Outputs:
- layer_out: bfloat16 [32, 384, 1024], P(('rep', 'shard'))
- grad_tokens: bfloat16 [32, 384, 1024], P(('rep', 'shard'))
- grad_ln1_gain: float32 [1024], P('shard')
- grad_ln1_bias: float32 [1024], P('shard')
- grad_w_qkv: float32 [1024, 3072], P(None, 'shard')
- grad_q_bias: float32 [1024], P('shard')
- grad_v_bias: float32 [1024], P('shard')
- grad_w_out: float32 [1024, 1024], P('shard')
- grad_b_out: float32 [1024], P('shard')
- grad_ln2_gain: float32 [1024], P('shard')
- grad_ln2_bias: float32 [1024], P('shard')
- grad_w_up: float32 [1024, 4096], P(None, 'shard')
- grad_b_up: float32 [4096], P('shard')
- grad_w_down: float32 [4096, 1024], P('shard')
- grad_b_down: float32 [1024], P('shard')
Inputs may be any that keep to these rules, and one draw needn't show every extreme that they name: `cont_segment`: each micro-batch holds 2 continuations, numbers never falling, each of 16 to 48 rows; in the first micro-batch of every prompt one continuation has exactly 48 rows.
All inputs are finite; a program needn't handle non-finite values.
Results may differ from a plain program's by a relative error of at most 0.015.
Values may be sent and summed in bfloat16 or wider, within the bound.
No kernel may reach another device: no remote copies, remote signals or barrier semaphores. Data moves between devices by JAX's collectives and lax.ppermute only.
A program may use at most 256 MiB of HBM per device.

v0:
```python
from functools import partial

import jax
import jax.numpy as jnp
from jax import lax
from jax.sharding import PartitionSpec as P

HEADS = 16
HDIM = 64
PROMPT = 256


def normalize(values, gain, shift):
    center = values - jnp.mean(values, -1, keepdims=True)
    spread = jnp.mean(center * center, -1, keepdims=True)
    return center * lax.rsqrt(spread + 1e-05) * gain + shift


def layout(segments):
    micros, row_count = segments.shape
    same_seg = segments[:, :, None] == segments[:, None, :]
    earlier = jnp.arange(row_count)[None, :] < jnp.arange(row_count)[:, None]
    offsets = jnp.sum(jnp.where(same_seg & earlier[None], 1, 0), -1).astype(jnp.int32)
    cont_pos = PROMPT + offsets
    owners = jnp.arange(micros, dtype=jnp.int32)[:, None] * row_count + segments
    positions = jnp.concatenate([jnp.arange(PROMPT, dtype=jnp.int32), cont_pos.reshape(-1)])
    groups = jnp.concatenate([jnp.full((PROMPT,), -1, jnp.int32), owners.reshape(-1)])
    places = jnp.arange(positions.shape[0], dtype=jnp.int32)
    allowed = (places[None, :] <= places[:, None]) & (
        (places[None, :] < PROMPT) | (groups[None, :] == groups[:, None])
    )
    distance = (positions[:, None] - positions[None, :]).astype(jnp.float32)
    return (distance, allowed)


def head_slice(matrix, block):
    block_width = 4 * HDIM
    part = lax.dynamic_slice_in_dim(matrix, block * block_width, block_width, 1)
    return part.reshape(matrix.shape[0], 4, HDIM)


def block_scores(q_part, k_part, block, distance, allowed):
    heads = (block * 4 + jnp.arange(4, dtype=jnp.int32)).astype(jnp.float32)
    slopes = jnp.exp2(-8.0 * (heads + 1.0) / HEADS)
    scores = jnp.einsum(
        "qhd,khd->hqk", q_part, k_part, preferred_element_type=jnp.float32
    ) * HDIM ** (-0.5)
    scores = scores - slopes[:, None, None] * distance[None]
    return jnp.where(allowed[None], scores, -jnp.inf)


def side_by_side(blocks):
    return jnp.transpose(blocks, (1, 0, 2)).reshape(
        blocks.shape[1], blocks.shape[0] * blocks.shape[2]
    )


def attend_forward(queries, key_rows, values, distance, allowed):
    length = queries.shape[0]

    def head_block(block):
        q_part = head_slice(queries, block)
        k_part = head_slice(key_rows, block)
        v_part = head_slice(values, block)
        scores = block_scores(q_part, k_part, block, distance, allowed)
        peak = jnp.max(scores, -1, keepdims=True)
        exps_rel = jnp.exp(scores - peak)
        row_totals = jnp.sum(exps_rel, -1, keepdims=True)
        attn_probs = (exps_rel / row_totals).astype(jnp.bfloat16)
        mixed = jnp.einsum("hqk,khd->qhd", attn_probs, v_part, preferred_element_type=jnp.float32)
        return (mixed.reshape(length, 4 * HDIM), (peak + jnp.log(row_totals))[:, :, 0])

    mixed, log_norms = lax.map(head_block, jnp.arange(HEADS // 4, dtype=jnp.int32))
    return (side_by_side(mixed).astype(jnp.bfloat16), log_norms)


def attend_backward(queries, key_rows, values, grad_mixed, log_norms, distance, allowed):
    length = queries.shape[0]
    scale = HDIM ** (-0.5)

    def head_block(block):
        q_part = head_slice(queries, block)
        k_part = head_slice(key_rows, block)
        v_part = head_slice(values, block)
        g_part = head_slice(grad_mixed, block)
        scores = block_scores(q_part, k_part, block, distance, allowed)
        attn_probs = jnp.exp(scores - log_norms[block][:, :, None])
        grad_probs = jnp.einsum("qhd,khd->hqk", g_part, v_part, preferred_element_type=jnp.float32)
        inner = jnp.sum(attn_probs * grad_probs, -1, keepdims=True)
        grad_scores = (attn_probs * (grad_probs - inner)).astype(jnp.bfloat16)
        grad_q = (
            jnp.einsum("hqk,khd->qhd", grad_scores, k_part, preferred_element_type=jnp.float32)
            * scale
        )
        grad_k = (
            jnp.einsum("hqk,qhd->khd", grad_scores, q_part, preferred_element_type=jnp.float32)
            * scale
        )
        grad_v = jnp.einsum(
            "hqk,qhd->khd",
            attn_probs.astype(jnp.bfloat16),
            g_part,
            preferred_element_type=jnp.float32,
        )
        block_width = 4 * HDIM
        return (
            grad_q.reshape(length, block_width),
            grad_k.reshape(length, block_width),
            grad_v.reshape(length, block_width),
        )

    grad_q, grad_k, grad_v = lax.map(head_block, jnp.arange(HEADS // 4, dtype=jnp.int32))
    return (
        side_by_side(grad_q).astype(jnp.bfloat16),
        side_by_side(grad_k).astype(jnp.bfloat16),
        side_by_side(grad_v).astype(jnp.bfloat16),
    )


def body(
    tokens,
    cont_segment,
    cotangent,
    ln1_gain,
    ln1_bias,
    w_qkv,
    q_bias,
    v_bias,
    w_out,
    b_out,
    ln2_gain,
    ln2_bias,
    w_up,
    b_up,
    w_down,
    b_down,
):
    (
        full_g1,
        full_s1,
        full_qkv,
        full_qb,
        full_vb,
        full_out,
        full_bo,
        full_g2,
        full_s2,
        full_up,
        full_bu,
        full_down,
        full_bd,
    ) = (
        lax.all_gather(ln1_gain, "shard", axis=0, tiled=True),
        lax.all_gather(ln1_bias, "shard", axis=0, tiled=True),
        lax.all_gather(w_qkv, "shard", axis=1, tiled=True),
        lax.all_gather(q_bias, "shard", axis=0, tiled=True),
        lax.all_gather(v_bias, "shard", axis=0, tiled=True),
        lax.all_gather(w_out, "shard", axis=0, tiled=True),
        lax.all_gather(b_out, "shard", axis=0, tiled=True),
        lax.all_gather(ln2_gain, "shard", axis=0, tiled=True),
        lax.all_gather(ln2_bias, "shard", axis=0, tiled=True),
        lax.all_gather(w_up, "shard", axis=1, tiled=True),
        lax.all_gather(b_up, "shard", axis=0, tiled=True),
        lax.all_gather(w_down, "shard", axis=0, tiled=True),
        lax.all_gather(b_down, "shard", axis=0, tiled=True),
    )
    inputs = tokens[0].astype(jnp.float32)
    length, model_width = inputs.shape
    distance, allowed = layout(cont_segment[0])
    normed = normalize(inputs, full_g1.astype(jnp.float32), full_s1.astype(jnp.float32)).astype(
        jnp.bfloat16
    )
    projected = jnp.dot(normed, full_qkv, preferred_element_type=jnp.float32)
    queries = (projected[:, :model_width] + full_qb.astype(jnp.float32)).astype(jnp.bfloat16)
    key_rows = projected[:, model_width : 2 * model_width].astype(jnp.bfloat16)
    values = (projected[:, 2 * model_width :] + full_vb.astype(jnp.float32)).astype(jnp.bfloat16)
    mixed, log_norms = attend_forward(queries, key_rows, values, distance, allowed)
    branch = jnp.dot(mixed, full_out, preferred_element_type=jnp.float32) + full_bo.astype(
        jnp.float32
    )
    middle = inputs + branch
    normed_two = normalize(middle, full_g2.astype(jnp.float32), full_s2.astype(jnp.float32)).astype(
        jnp.bfloat16
    )
    pre_act = jnp.dot(normed_two, full_up, preferred_element_type=jnp.float32) + full_bu.astype(
        jnp.float32
    )
    activated = jax.nn.gelu(pre_act, approximate=True).astype(jnp.bfloat16)
    outputs = middle + (
        jnp.dot(activated, full_down, preferred_element_type=jnp.float32)
        + full_bd.astype(jnp.float32)
    )
    back_g1, back_qkv, back_out, back_g2, back_up, back_down = (
        lax.all_gather(ln1_gain, "shard", axis=0, tiled=True),
        lax.all_gather(w_qkv, "shard", axis=1, tiled=True),
        lax.all_gather(w_out, "shard", axis=0, tiled=True),
        lax.all_gather(ln2_gain, "shard", axis=0, tiled=True),
        lax.all_gather(w_up, "shard", axis=1, tiled=True),
        lax.all_gather(w_down, "shard", axis=0, tiled=True),
    )
    cot_low = cotangent[0]
    cot_full = cot_low.astype(jnp.float32)
    zero_shift = jnp.zeros((model_width,), jnp.float32)
    grad_bd = jnp.sum(cot_full, 0)
    grad_act = jnp.einsum("to,fo->tf", cot_low, back_down, preferred_element_type=jnp.float32)
    gelu_value, gelu_pull = jax.vjp(partial(jax.nn.gelu, approximate=True), pre_act)
    grad_pre = gelu_pull(grad_act)[0].astype(jnp.bfloat16)
    grad_bu = jnp.sum(grad_pre.astype(jnp.float32), 0)
    grad_normed_two = jnp.einsum("tf,if->ti", grad_pre, back_up, preferred_element_type=jnp.float32)
    norm_value_two, norm_pull_two = jax.vjp(
        normalize, middle, back_g2.astype(jnp.float32), zero_shift
    )
    grad_mid_part, grad_g2, grad_s2 = norm_pull_two(grad_normed_two)
    grad_middle = cot_full + grad_mid_part
    grad_branch = grad_middle.astype(jnp.bfloat16)
    grad_bo = jnp.sum(grad_branch.astype(jnp.float32), 0)
    grad_mixed = jnp.einsum(
        "to,io->ti", grad_branch, back_out, preferred_element_type=jnp.float32
    ).astype(jnp.bfloat16)
    grad_q, grad_k, grad_v = attend_backward(
        queries, key_rows, values, grad_mixed, log_norms, distance, allowed
    )
    grad_proj = jnp.concatenate([grad_q, grad_k, grad_v], 1)
    grad_qb = jnp.sum(grad_q.astype(jnp.float32), 0)
    grad_vb = jnp.sum(grad_v.astype(jnp.float32), 0)
    grad_normed = jnp.einsum("tc,ic->ti", grad_proj, back_qkv, preferred_element_type=jnp.float32)
    norm_value_one, norm_pull_one = jax.vjp(
        normalize, inputs, back_g1.astype(jnp.float32), zero_shift
    )
    grad_in_part, grad_g1, grad_s1 = norm_pull_one(grad_normed)
    grad_inputs = grad_middle + grad_in_part
    grad_down = jnp.einsum("tf,to->fo", activated, cot_low, preferred_element_type=jnp.float32)
    grad_up = jnp.einsum("ti,tf->if", normed_two, grad_pre, preferred_element_type=jnp.float32)
    grad_out = jnp.einsum("ti,to->io", mixed, grad_branch, preferred_element_type=jnp.float32)
    grad_qkv = jnp.einsum("ti,tc->ic", normed, grad_proj, preferred_element_type=jnp.float32)
    owned = (
        lax.psum_scatter(
            grad_g1.astype(jnp.bfloat16), "shard", scatter_dimension=0, tiled=True
        ).astype(jnp.float32),
        lax.psum_scatter(
            grad_s1.astype(jnp.bfloat16), "shard", scatter_dimension=0, tiled=True
        ).astype(jnp.float32),
        lax.psum_scatter(
            grad_qkv.astype(jnp.bfloat16), "shard", scatter_dimension=1, tiled=True
        ).astype(jnp.float32),
        lax.psum_scatter(
            grad_qb.astype(jnp.bfloat16), "shard", scatter_dimension=0, tiled=True
        ).astype(jnp.float32),
        lax.psum_scatter(
            grad_vb.astype(jnp.bfloat16), "shard", scatter_dimension=0, tiled=True
        ).astype(jnp.float32),
        lax.psum_scatter(
            grad_out.astype(jnp.bfloat16), "shard", scatter_dimension=0, tiled=True
        ).astype(jnp.float32),
        lax.psum_scatter(
            grad_bo.astype(jnp.bfloat16), "shard", scatter_dimension=0, tiled=True
        ).astype(jnp.float32),
        lax.psum_scatter(
            grad_g2.astype(jnp.bfloat16), "shard", scatter_dimension=0, tiled=True
        ).astype(jnp.float32),
        lax.psum_scatter(
            grad_s2.astype(jnp.bfloat16), "shard", scatter_dimension=0, tiled=True
        ).astype(jnp.float32),
        lax.psum_scatter(
            grad_up.astype(jnp.bfloat16), "shard", scatter_dimension=1, tiled=True
        ).astype(jnp.float32),
        lax.psum_scatter(
            grad_bu.astype(jnp.bfloat16), "shard", scatter_dimension=0, tiled=True
        ).astype(jnp.float32),
        lax.psum_scatter(
            grad_down.astype(jnp.bfloat16), "shard", scatter_dimension=0, tiled=True
        ).astype(jnp.float32),
        lax.psum_scatter(
            grad_bd.astype(jnp.bfloat16), "shard", scatter_dimension=0, tiled=True
        ).astype(jnp.float32),
    )
    finals = lax.psum(
        (
            owned[0],
            owned[1],
            owned[2],
            owned[3],
            owned[4],
            owned[5],
            owned[6],
            owned[7],
            owned[8],
            owned[9],
            owned[10],
            owned[11],
            owned[12],
        ),
        "rep",
    )
    return (
        outputs.astype(jnp.bfloat16)[None],
        grad_inputs.astype(jnp.bfloat16)[None],
        finals[0],
        finals[1],
        finals[2],
        finals[3],
        finals[4],
        finals[5],
        finals[6],
        finals[7],
        finals[8],
        finals[9],
        finals[10],
        finals[11],
        finals[12],
    )


def solution(mesh):
    return jax.shard_map(
        body,
        mesh=mesh,
        in_specs=(
            P(("rep", "shard"), None, None),
            P(("rep", "shard"), None, None),
            P(("rep", "shard"), None, None),
            P("shard"),
            P("shard"),
            P(None, "shard"),
            P("shard"),
            P("shard"),
            P("shard", None),
            P("shard"),
            P("shard"),
            P("shard"),
            P(None, "shard"),
            P("shard"),
            P("shard", None),
            P("shard"),
        ),
        out_specs=(
            P(("rep", "shard"), None, None),
            P(("rep", "shard"), None, None),
            P("shard"),
            P("shard"),
            P(None, "shard"),
            P("shard"),
            P("shard"),
            P("shard", None),
            P("shard"),
            P("shard"),
            P("shard"),
            P(None, "shard"),
            P("shard"),
            P("shard", None),
            P("shard"),
        ),
        check_vma=False,
    )
```

profile of v0, /device:TPU:0, one launch (start us, length us, event | category | flops | bytes accessed | tf_op | source)
XLA Modules:
  0.0 994.4 jit_solution(5725867691567302922)
XLA Ops:
  10.2 6.0 all-gather.4
  16.2 5.4 all-gather.1
  21.7 5.2 all-gather
  26.9 5.2 all-gather.3
  32.1 5.2 all-gather.2
  37.9 5.4 all_gather.55
  43.2 5.2 all-gather.6
  48.5 5.2 all-gather.5
  54.3 4.5 all-gather.13.cloned.1.call-done
  58.8 4.9 fusion.50
  63.8 1.0 slice.23
  66.0 1.5 copy.59
  67.5 0.9 broadcast.216.clone
  68.5 21.3 %while.32 = (s32[]{:T(128)}, bf16[4,384,256]{1,2,0:T(8,128)(2,1)}, f32[4,4,384]{2,1,0:T(4,128)}, s32[4]{0:T(128)S(1)}, bf16[384,1024]{0,1:T(8,128)(2,1)S(1)}, /*...) while((s32[]{:T(128)}, bf16[4,384,256]{1,2,0:T(8,128)(2,1)}, ...), condition=%wide.region_6.7_spmd.clone, body=%wide.region_3.6_spmd.clone.sunk | while | flops 157776416 | bytes 10964623 | solution.py:73
  90.9 3.3 fusion.58
  94.6 48.3 %all-gather.17.cloned.1.call-done = bf16[1024,4096]{1,0:T(8,128)(2,1)} async-done(((bf16[1024,1024]{1,0:T(8,128)(2,1)}), bf16[1024,4096]{1,0:T(8,128)(2,1)}) %all-gather.17.cloned.1.call-update) | async-done | bytes 8388624 | tf_op jit(solution)/shard_map/all_gather | solution.py:162
  142.8 9.0 convolution_add_fusion
  151.9 50.7 %all-gather.19.cloned.1.call-done = bf16[4096,1024]{1,0:T(8,128)(2,1)} async-done(((bf16[1024,1024]{1,0:T(8,128)(2,1)}), bf16[4096,1024]{1,0:T(8,128)(2,1)}) %all-gather.19.cloned.1.call-update) | async-done | bytes 8388624 | tf_op jit(solution)/shard_map/all_gather | solution.py:164
  202.6 11.1 %fusion.59 = (bf16[4096]{0:T(1024)(128)(2,1)}, bf16[384,4096]{1,0:T(8,128)(2,1)S(1)}) fusion(f32[384,4096]{1,0:T(8,128)} %convolution_add_fusion, bf16[4096,1024]{1,0:T(8,128)(2,1)} %all-gather.19.cloned.1.call-done, bf16[1,384,1024]{2,1,0:T(8,128)(2,1)S(1)} %copy-done.9), kind=kOutput, calls=%fused_computation.124 | convolution fusion | flops 3254251520 | bytes 18620416 | tf_op jit(solution)/shard_map/to,fo->tf/dot_general | solution.py:205
  213.7 4.3 multiply_reduce_fusion.1
  218.7 1.1 copy-done.4
  219.8 0.9 fusion.54
  221.6 2.6 convolution_convert_fusion.3
  224.3 3.0 convolution_convert_fusion.4
  227.8 0.9 broadcast.216
  228.7 0.9 broadcast.216.clone.1
  229.7 0.9 broadcast.216.clone.2
  230.6 54.2 %while.33 = (s32[]{:T(128)}, bf16[4,384,256]{1,2,0:T(8,128)(2,1)}, bf16[4,384,256]{1,2,0:T(8,128)(2,1)}, bf16[4,384,256]{1,2,0:T(8,128)(2,1)}, s32[4]{0:T(128)},...) while((s32[]{:T(128)}, bf16[4,384,256]{1,2,0:T(8,128)(2,1)}, ...), condition=%wide.region_13.14_spmd.clone, body=%wide.region_11.13_spmd.clone.sunk | while | flops 385251872 | bytes 30607116 | solution.py:112
  230.8 1.3 dynamic_slice.96
  232.8 1.0 constant_dynamic-slice_fusion.15
  233.7 1.0 constant_dynamic-slice_fusion.16
  238.9 1.0 constant_dynamic-slice_fusion.18
  240.0 1.1 multiply_reduce_fusion.5
  244.4 1.2 dynamic_slice.96
  246.3 1.0 constant_dynamic-slice_fusion.15
  247.2 0.9 constant_dynamic-slice_fusion.16
  252.4 1.0 constant_dynamic-slice_fusion.18
  253.5 1.1 multiply_reduce_fusion.5
  257.9 1.2 dynamic_slice.96
  259.8 1.0 constant_dynamic-slice_fusion.15
  260.7 0.9 constant_dynamic-slice_fusion.16
  265.8 1.0 constant_dynamic-slice_fusion.18
  267.0 1.1 multiply_reduce_fusion.5
  271.4 1.2 dynamic_slice.96
  273.3 1.0 constant_dynamic-slice_fusion.15
  274.2 0.9 constant_dynamic-slice_fusion.16
  279.3 1.0 constant_dynamic-slice_fusion.18
  280.5 1.1 multiply_reduce_fusion.5
  284.9 8.3 convolution_convert_fusion.2
  293.2 1.3 copy-done.3
  294.6 9.7 convolution_convert_fusion.1
  304.3 1.1 copy-done.10
  305.4 10.9 %convolution_convert_fusion = bf16[4096,1024]{1,0:T(8,128)(2,1)} fusion(bf16[1,384,1024]{2,1,0:T(8,128)(2,1)S(1)} %copy-done.10, f32[384,4096]{1,0:T(8,128)} %convolution_add_fusion), kind=kOutput, calls=%fused_computation.39 | convolution fusion | flops 3239575552 | bytes 15466496 | tf_op jit(solution)/shard_map/tf,to->fo/dot_general | solution.py:232
  316.9 5.2 all-gather.7
  324.2 1.4 reduce_sum.264
  325.6 1.4 reduce_sum.266
  327.0 6.4 fusion.53
  333.5 1.1 copy-done.11
  335.3 12.8 %all-reduce.11 = (bf16[1024]{0:T(1024)(128)(2,1)S(1)}, bf16[1024]{0:T(1024)(128)(2,1)S(1)}, bf16[1024]{0:T(1024)(128)(2,1)S(1)}, bf16[1024]{0:T(1024)(128)(2,1)S...) all-reduce(bf16[1024]{0:T(1024)(128)(2,1)S(1)} %get-tuple-element.4, ...), channel_id=2, replica_groups=mesh['rep'=8,'shard'=4] {'shard'}, use_global_device_ids=true, to_apply=%region_17.18.clone | all-reduce | flops 12288 | bytes 49152
  348.4 3.5 fusion.39
  351.9 10.1 %fusion.36 = bf16[1,384,1024]{2,1,0:T(8,128)(2,1)} fusion(f32[384,1024]{1,0:T(8,128)S(1)} %copy-done.3, bf16[4096,1024]{1,0:T(8,128)(2,1)} %all-gather.19.cloned.1.call-done, f32[1024]{0:T(1024)S(1)} %bitcast.228, f32[384,4096]{1,0:T(8,128)} %convolution_add_fusion), kind=kOutput, calls=%fused_computation.83 | convolution fusion | flops 3236560896 | bytes 17043456 | tf_op jit(solution)/shard_map/dot_general | solution.py:190
  362.0 63.6 %reduce-scatter.9.cloned.1.call-done = bf16[1024,1024]{1,0:T(8,128)(2,1)} async-done(((bf16[1024,4096]{1,0:T(8,128)(2,1)}), bf16[1024,1024]{1,0:T(8,128)(2,1)}) %reduce-scatter.9.cloned.1.call-update) | async-done | bytes 2097168 | tf_op jit(solution)/shard_map/reduce_scatter | solution.py:264
  425.7 74.0 %reduce-scatter.11.cloned.1.call-done = bf16[1024,1024]{1,0:T(8,128)(2,1)} async-done(((bf16[4096,1024]{1,0:T(8,128)(2,1)}), bf16[1024,1024]{1,0:T(8,128)(2,1)}) %reduce-scatter.11.cloned.1.call-update) | async-done | bytes 2097168 | tf_op jit(solution)/shard_map/reduce_scatter | solution.py:270
  499.7 487.4 %all-reduce.13 = (f32[256]{0:T(256)}, f32[256]{0:T(256)}, f32[1024,768]{1,0:T(8,128)}, f32[256]{0:T(256)}, f32[256]{0:T(256)}, /*index=5*/f32[256,1024]{1,0:T(8,...) all-reduce(f32[256]{0:T(256)S(1)} %get-tuple-element.516, ...), channel_id=1, replica_groups=mesh['rep'=8,'shard'=4] {'rep'}, use_global_device_ids=true, to_apply=%region_18.19 | all-reduce | flops 3148800 | bytes 18898944 | tf_op jit(solution)/shard_map/psum | solution.py:277
  (279 shorter events, 46.9 us)
Async XLA Ops:
  7.2 51.6 %all-gather.13.cloned.1.call-start = ((), (), s32[]{:S(2)}) async-start(), calls=%async_computation.4 | async-start | bytes 7864320 | tf_op jit(solution)/shard_map/all_gather | solution.py:155
  7.9 2.2 copy-start.39
  7.9 8.3 copy-start.40
  7.9 13.7 %copy-start.41 = (bf16[256]{0:T(256)(128)(2,1)S(1)}, bf16[256]{0:T(256)(128)(2,1)}, u32[]{:S(2)}) copy-start(bf16[256]{0:T(256)(128)(2,1)} %param.23) | copy-start | bytes 1540
  7.9 18.9 %copy-start.42 = (bf16[256]{0:T(256)(128)(2,1)S(1)}, bf16[256]{0:T(256)(128)(2,1)}, u32[]{:S(2)}) copy-start(bf16[256]{0:T(256)(128)(2,1)} %param.26) | copy-start | bytes 1540
  8.0 24.2 %copy-start.43 = (bf16[256]{0:T(256)(128)(2,1)S(1)}, bf16[256]{0:T(256)(128)(2,1)}, u32[]{:S(2)}) copy-start(bf16[256]{0:T(256)(128)(2,1)} %param.27) | copy-start | bytes 1540
  8.0 29.5 %copy-start.34 = (s32[1,2,64]{2,1,0:T(2,128)S(1)}, s32[1,2,64]{2,1,0:T(2,128)}, u32[]{:S(2)}) copy-start(s32[1,2,64]{2,1,0:T(2,128)} %param.21) | copy-start | bytes 1540
  8.0 29.9 %copy-start.35 = (bf16[1024]{0:T(1024)(128)(2,1)S(1)}, bf16[1024]{0:T(1024)(128)(2,1)}, u32[]{:S(2)}) copy-start(bf16[1024]{0:T(1024)(128)(2,1)} %param.33) | copy-start | bytes 6148
  8.0 35.2 %copy-start.44 = (bf16[256]{0:T(256)(128)(2,1)S(1)}, bf16[256]{0:T(256)(128)(2,1)}, u32[]{:S(2)}) copy-start(bf16[256]{0:T(256)(128)(2,1)} %param.31) | copy-start | bytes 1540
  8.0 40.5 %copy-start.45 = (bf16[256]{0:T(256)(128)(2,1)S(1)}, bf16[256]{0:T(256)(128)(2,1)}, u32[]{:S(2)}) copy-start(bf16[256]{0:T(256)(128)(2,1)} %param.30) | copy-start | bytes 1540
  8.0 45.7 %copy-start = (bf16[1,384,1024]{2,1,0:T(8,128)(2,1)S(1)}, bf16[1,384,1024]{2,1,0:T(8,128)(2,1)}, u32[]{:S(2)}) copy-start(bf16[1,384,1024]{2,1,0:T(8,128)(2,1)} %param.20) | copy-start | bytes 2359300
  8.0 81.7 %all-gather.15.cloned.1.call-start = ((), (), s32[]{:S(2)}) async-start(), calls=%async_computation.5 | async-start | bytes 2621440 | tf_op jit(solution)/shard_map/all_gather | solution.py:158
  8.8 134.1 %all-gather.17.cloned.1.call-start = ((), (), s32[]{:S(2)}) async-start(), calls=%async_computation.6 | async-start | bytes 10485760 | tf_op jit(solution)/shard_map/all_gather | solution.py:162
  9.5 193.0 %all-gather.19.cloned.1.call-start = ((), (), s32[]{:S(2)}) async-start(), calls=%async_computation.7 | async-start | bytes 10485760 | tf_op jit(solution)/shard_map/all_gather | solution.py:164
  10.1 351.9 %reduce-scatter.7.cloned.1.call-start = ((), (), s32[]{:S(2)}) async-start(), calls=%async_computation.9 | async-start | bytes 2621440 | tf_op jit(solution)/shard_map/reduce_scatter | solution.py:252
  21.6 42.1 %copy-start.31 = (f32[4,1,256]{2,1,0:T(1,128)}, f32[4,1,256]{2,1,0:T(1,128)S(1)}, u32[]{:S(2)}) copy-start(f32[4,1,256]{2,1,0:T(1,128)S(1)} %convert_element_type.279) | copy-start | bytes 12292
  48.5 94.4 %copy-start.32 = (f32[4,1,256]{2,1,0:T(1,128)}, f32[4,1,256]{2,1,0:T(1,128)S(1)}, u32[]{:S(2)}) copy-start(f32[4,1,256]{2,1,0:T(1,128)S(1)} %convert_element_type.284) | copy-start | bytes 12292
  53.7 164.4 %copy-start.25 = (f32[4,1,256]{2,1,0:T(1,128)}, f32[4,1,256]{2,1,0:T(1,128)S(1)}, u32[]{:S(2)}) copy-start(f32[4,1,256]{2,1,0:T(1,128)S(1)} %convert_element_type.283) | copy-start | bytes 12292
  54.0 9.8 copy-start.15
  54.3 9.5 copy-start.21
  54.3 9.5 copy-start.23
  89.8 0.9 copy-start.7
  89.8 1.2 copy-start.8
  94.2 123.8 %copy-start.2 = (f32[384,1024]{1,0:T(8,128)}, f32[384,1024]{1,0:T(8,128)S(1)}, u32[]{:S(2)}) copy-start(f32[384,1024]{1,0:T(8,128)S(1)} %get-tuple-element.504) | copy-start | bytes 4718596
  94.2 123.8 %copy-start.19 = (f32[384]{0:T(512)}, f32[384]{0:T(512)S(1)}, u32[]{:S(2)}) copy-start(f32[384]{0:T(512)S(1)} %broadcast_multiply_fusion) | copy-start | bytes 4612
  94.6 123.5 %copy-start.28 = (f32[384]{0:T(512)}, f32[384]{0:T(512)S(1)}, u32[]{:S(2)}) copy-start(f32[384]{0:T(512)S(1)} %fusion.46) | copy-start | bytes 4612
  142.8 59.7 %copy-start.9 = (bf16[1,384,1024]{2,1,0:T(8,128)(2,1)S(1)}, bf16[1,384,1024]{2,1,0:T(8,128)(2,1)}, u32[]{:S(2)}) copy-start(bf16[1,384,1024]{2,1,0:T(8,128)(2,1)} %param.22) | copy-start | bytes 2359300
  202.6 11.1 %copy-start.38 = (bf16[1024,4096]{1,0:T(8,128)(2,1)S(1)}, bf16[1024,4096]{1,0:T(8,128)(2,1)}, u32[]{:S(2)}) copy-start(bf16[1024,4096]{1,0:T(8,128)(2,1)} %all-gather.17.cloned.1.call-done) | copy-start | bytes 25165828
  213.7 4.3 copy-start.48
  218.6 1.2 copy-start.4
  218.7 3.0 copy-start.12
  218.7 2.0 copy-start.17
  220.7 0.9 copy-start.14
  221.6 2.6 copy-start.13
  224.2 137.8 %reduce-scatter.5.cloned.1.call-start = ((), (), s32[]{:S(2)}) async-start(), calls=%async_computation.8 | async-start | bytes 7864320 | tf_op jit(solution)/shard_map/reduce_scatter | solution.py:243
  230.8 4.1 copy-start.5
  242.5 1.9 copy-start.6
  244.4 4.0 copy-start.5
  256.0 1.9 copy-start.6
  257.9 4.0 copy-start.5
  269.5 1.9 copy-start.6
  271.4 4.0 copy-start.5
  283.0 1.9 copy-start.6
  293.1 1.4 copy-start.3
  293.1 1.4 copy-start.20
  293.1 1.4 copy-start.26
  293.1 1.4 copy-start.29
  293.2 1.4 copy-start.33
  293.2 132.5 %reduce-scatter.9.cloned.1.call-start = ((), (), s32[]{:S(2)}) async-start(), calls=%async_computation.10 | async-start | bytes 10485760 | tf_op jit(solution)/shard_map/reduce_scatter | solution.py:264
  304.2 1.2 copy-start.10
  304.2 195.4 %reduce-scatter.11.cloned.1.call-start = ((), (), s32[]{:S(2)}) async-start(), calls=%async_computation.11 | async-start | bytes 10485760 | tf_op jit(solution)/shard_map/reduce_scatter | solution.py:270
  316.3 0.7 copy-start.46
  316.3 6.0 copy-start.47
  316.3 10.6 %copy-start.1 = (bf16[1,384,1024]{2,1,0:T(8,128)(2,1)S(1)}, bf16[1,384,1024]{2,1,0:T(8,128)(2,1)}, u32[]{:S(2)}) copy-start(bf16[1,384,1024]{2,1,0:T(8,128)(2,1)} %param.20) | copy-start | bytes 2359300
  316.3 10.6 %copy-start.16 = (f32[384]{0:T(512)S(1)}, f32[384]{0:T(512)}, u32[]{:S(2)}) copy-start(f32[384]{0:T(512)} %copy-done.15) | copy-start | bytes 4612
  327.0 6.5 copy-start.22
  327.0 7.6 copy-start.24
  333.4 1.1 copy-start.11
  333.4 1.9 copy-start.27
  333.4 1.9 copy-start.30
  333.4 1.9 copy-start.36
  333.5 1.9 copy-start.37
  333.5 15.0 %copy-start.18 = (f32[384]{0:T(512)S(1)}, f32[384]{0:T(512)}, u32[]{:S(2)}) copy-start(f32[384]{0:T(512)} %copy-done.17) | copy-start | bytes 4612
Sparse Core Ops, SparseCore 0:
  9.6 49.2 all-gather.12
  60.4 22.5 all-gather.14
  84.5 58.2 all-gather.16
  144.3 58.2 all-gather.18
  224.3 31.1 reduce-scatter.6
  293.3 58.4 reduce-scatter.4
  354.4 71.2 reduce-scatter.8
  428.2 71.3 reduce-scatter.10
where the time goes:
time: 1000 us; the launch traced here: 994 us
  blocking collectives  548 us (55%)
  waiting for transfers between devices  244 us (24%)
  matrix products  101 us (10%)
  local copies, waits for them, and re-layouts  47.3 us (5%)
  loops' own time  19 us (2%)
  other arithmetic  18 us (2%)
  between operations  16.5 us (2%)
    psum x1, blocking collectives, body(): lax.psum((owned[0], owned[1], owned[2], owned[3], owned[4], owned[5], own...  487 us
    reduce_scatter x1, waiting for transfers between devices, body(): lax.psum_scatter(grad_down.astype(jnp.bfloat16), 'shard', scatter_dimensi...  74 us
    reduce_scatter x1, waiting for transfers between devices, body(): lax.psum_scatter(grad_up.astype(jnp.bfloat16), 'shard', scatter_dimension...  63.6 us
    all_gather x1, waiting for transfers between devices, body(): lax.all_gather(w_down, 'shard', axis=0, tiled=True)  50.7 us
    all_gather x1, waiting for transfers between devices, body(): lax.all_gather(w_up, 'shard', axis=1, tiled=True)  48.3 us
  transfers between devices with their start and end apart: 8, of which 5 were waited for; matrix products, arithmetic and copies ran while one was open for 14% of the time, Pallas kernels for 0%

commit v1 on v0

--- a/solution.py
+++ b/solution.py
@@ -117,6 +117,20 @@
     )
 
 
+SMALL = ("ln1_gain", "ln1_bias", "q_bias", "v_bias", "b_out", "ln2_gain", "ln2_bias", "b_up", "b_down")
+
+
+def gather_small(pieces):
+    packed = jnp.concatenate(pieces)
+    shards = lax.all_gather(packed, "shard", axis=0, tiled=False)
+    fulls, offset = [], 0
+    for piece in pieces:
+        width = piece.shape[0]
+        fulls.append(shards[:, offset : offset + width].reshape(-1))
+        offset += width
+    return fulls
+
+
 def body(
     tokens,
     cont_segment,
@@ -135,35 +149,14 @@
     w_down,
     b_down,
 ):
-    (
-        full_g1,
-        full_s1,
-        full_qkv,
-        full_qb,
-        full_vb,
-        full_out,
-        full_bo,
-        full_g2,
-        full_s2,
-        full_up,
-        full_bu,
-        full_down,
-        full_bd,
-    ) = (
-        lax.all_gather(ln1_gain, "shard", axis=0, tiled=True),
-        lax.all_gather(ln1_bias, "shard", axis=0, tiled=True),
-        lax.all_gather(w_qkv, "shard", axis=1, tiled=True),
-        lax.all_gather(q_bias, "shard", axis=0, tiled=True),
-        lax.all_gather(v_bias, "shard", axis=0, tiled=True),
-        lax.all_gather(w_out, "shard", axis=0, tiled=True),
-        lax.all_gather(b_out, "shard", axis=0, tiled=True),
-        lax.all_gather(ln2_gain, "shard", axis=0, tiled=True),
-        lax.all_gather(ln2_bias, "shard", axis=0, tiled=True),
-        lax.all_gather(w_up, "shard", axis=1, tiled=True),
-        lax.all_gather(b_up, "shard", axis=0, tiled=True),
-        lax.all_gather(w_down, "shard", axis=0, tiled=True),
-        lax.all_gather(b_down, "shard", axis=0, tiled=True),
-    )
+    shard_count = lax.psum(1, "shard")
+    full_g1, full_s1, full_qb, full_vb, full_bo, full_g2, full_s2, full_bu, full_bd = gather_small(
+        [ln1_gain, ln1_bias, q_bias, v_bias, b_out, ln2_gain, ln2_bias, b_up, b_down]
+    )
+    full_qkv = lax.all_gather(w_qkv, "shard", axis=1, tiled=True)
+    full_out = lax.all_gather(w_out, "shard", axis=0, tiled=True)
+    full_up = lax.all_gather(w_up, "shard", axis=1, tiled=True)
+    full_down = lax.all_gather(w_down, "shard", axis=0, tiled=True)
     inputs = tokens[0].astype(jnp.float32)
     length, model_width = inputs.shape
     distance, allowed = layout(cont_segment[0])
@@ -191,12 +184,7 @@
         + full_bd.astype(jnp.float32)
     )
     back_g1, back_qkv, back_out, back_g2, back_up, back_down = (
-        lax.all_gather(ln1_gain, "shard", axis=0, tiled=True),
-        lax.all_gather(w_qkv, "shard", axis=1, tiled=True),
-        lax.all_gather(w_out, "shard", axis=0, tiled=True),
-        lax.all_gather(ln2_gain, "shard", axis=0, tiled=True),
-        lax.all_gather(w_up, "shard", axis=1, tiled=True),
-        lax.all_gather(w_down, "shard", axis=0, tiled=True),
+        full_g1, full_qkv, full_out, full_g2, full_up, full_down
     )
     cot_low = cotangent[0]
     cot_full = cot_low.astype(jnp.float32)
@@ -233,81 +221,50 @@
     grad_up = jnp.einsum("ti,tf->if", normed_two, grad_pre, preferred_element_type=jnp.float32)
     grad_out = jnp.einsum("ti,to->io", mixed, grad_branch, preferred_element_type=jnp.float32)
     grad_qkv = jnp.einsum("ti,tc->ic", normed, grad_proj, preferred_element_type=jnp.float32)
-    owned = (
-        lax.psum_scatter(
-            grad_g1.astype(jnp.bfloat16), "shard", scatter_dimension=0, tiled=True
-        ).astype(jnp.float32),
-        lax.psum_scatter(
-            grad_s1.astype(jnp.bfloat16), "shard", scatter_dimension=0, tiled=True
-        ).astype(jnp.float32),
-        lax.psum_scatter(
-            grad_qkv.astype(jnp.bfloat16), "shard", scatter_dimension=1, tiled=True
-        ).astype(jnp.float32),
-        lax.psum_scatter(
-            grad_qb.astype(jnp.bfloat16), "shard", scatter_dimension=0, tiled=True
-        ).astype(jnp.float32),
-        lax.psum_scatter(
-            grad_vb.astype(jnp.bfloat16), "shard", scatter_dimension=0, tiled=True
-        ).astype(jnp.float32),
-        lax.psum_scatter(
-            grad_out.astype(jnp.bfloat16), "shard", scatter_dimension=0, tiled=True
-        ).astype(jnp.float32),
-        lax.psum_scatter(
-            grad_bo.astype(jnp.bfloat16), "shard", scatter_dimension=0, tiled=True
-        ).astype(jnp.float32),
-        lax.psum_scatter(
-            grad_g2.astype(jnp.bfloat16), "shard", scatter_dimension=0, tiled=True
-        ).astype(jnp.float32),
-        lax.psum_scatter(
-            grad_s2.astype(jnp.bfloat16), "shard", scatter_dimension=0, tiled=True
-        ).astype(jnp.float32),
-        lax.psum_scatter(
-            grad_up.astype(jnp.bfloat16), "shard", scatter_dimension=1, tiled=True
-        ).astype(jnp.float32),
-        lax.psum_scatter(
-            grad_bu.astype(jnp.bfloat16), "shard", scatter_dimension=0, tiled=True
-        ).astype(jnp.float32),
-        lax.psum_scatter(
-            grad_down.astype(jnp.bfloat16), "shard", scatter_dimension=0, tiled=True
-        ).astype(jnp.float32),
-        lax.psum_scatter(
-            grad_bd.astype(jnp.bfloat16), "shard", scatter_dimension=0, tiled=True
-        ).astype(jnp.float32),
-    )
-    finals = lax.psum(
-        (
-            owned[0],
-            owned[1],
-            owned[2],
-            owned[3],
-            owned[4],
-            owned[5],
-            owned[6],
-            owned[7],
-            owned[8],
-            owned[9],
-            owned[10],
-            owned[11],
-            owned[12],
-        ),
-        "rep",
-    )
+    smalls = [grad_g1, grad_s1, grad_qb, grad_vb, grad_bo, grad_g2, grad_s2, grad_bu, grad_bd]
+    small_rows = jnp.concatenate([g.reshape(shard_count, -1) for g in smalls], 1)
+    small_rows = small_rows.reshape(shard_count, -1, model_width)
+    small_rows = jnp.pad(small_rows, ((0, 0), (0, 16 - small_rows.shape[1]), (0, 0)))
+    down_rows = grad_down.reshape(shard_count, -1, model_width)
+    down_width = down_rows.shape[1] * model_width
+    joined = jnp.concatenate([down_rows, small_rows], 1).reshape(-1, model_width)
+    joined_own = lax.psum_scatter(
+        joined.astype(jnp.bfloat16), "shard", scatter_dimension=0, tiled=True
+    ).reshape(-1)
+    qkv_own = lax.psum_scatter(grad_qkv.astype(jnp.bfloat16), "shard", scatter_dimension=1, tiled=True)
+    out_own = lax.psum_scatter(grad_out.astype(jnp.bfloat16), "shard", scatter_dimension=0, tiled=True)
+    up_own = lax.psum_scatter(grad_up.astype(jnp.bfloat16), "shard", scatter_dimension=1, tiled=True)
+    owned = [qkv_own, out_own, up_own, joined_own]
+    flat = jnp.concatenate([o.reshape(-1).astype(jnp.float32) for o in owned])
+    total = lax.psum(flat, "rep")
+    pieces, offset = [], 0
+    for o in owned:
+        pieces.append(total[offset : offset + o.size].reshape(o.shape))
+        offset += o.size
+    qkv_fin, out_fin, up_fin, joined_fin = pieces
+    down_fin = joined_fin[:down_width].reshape(grad_down.shape[0] // shard_count, -1)
+    small_fin, offset = [], down_width
+    for g in smalls:
+        width = g.shape[0] // shard_count
+        small_fin.append(joined_fin[offset : offset + width])
+        offset += width
+    g1_fin, s1_fin, qb_fin, vb_fin, bo_fin, g2_fin, s2_fin, bu_fin, bd_fin = small_fin
     return (
         outputs.astype(jnp.bfloat16)[None],
         grad_inputs.astype(jnp.bfloat16)[None],
-        finals[0],
-        finals[1],
-        finals[2],
-        finals[3],
-        finals[4],
-        finals[5],
-        finals[6],
-        finals[7],
-        finals[8],
-        finals[9],
-        finals[10],
-        finals[11],
-        finals[12],
+        g1_fin,
+        s1_fin,
+        qkv_fin,
+        qb_fin,
+        vb_fin,
+        out_fin,
+        bo_fin,
+        g2_fin,
+        s2_fin,
+        up_fin,
+        bu_fin,
+        down_fin,
+        bd_fin,
     )
 
 

time: 1000 us -> 973 us (0.973)
  blocking collectives: 548 us -> 6.26 us
  waiting for transfers between devices: 244 us -> 679 us
  other arithmetic: 18 us -> 67.6 us
  local copies, waits for them, and re-layouts: 47.3 us -> 81.8 us
    psum x1 -> x0, blocking collectives: 487 us -> none  [body(): lax.psum((owned[0], owned[1], owned[2], owned[3], owned[4], owned[5], own...]
    psum x0 -> x1, waiting for transfers between devices: none -> 381 us  [body(): total = lax.psum(flat, 'rep')]
    concatenate x0 -> x2, other arithmetic: none -> 52.1 us  [the longest x1 48.4 us: body(): flat = jnp.concatenate([o.reshape(-1).astype(jnp.float32) for o in owned])]
    all_gather x9 -> x1, blocking collectives: 48.1 us -> 6.26 us  [gather_small(): shards = lax.all_gather(packed, 'shard', axis=0, tiled=False)]
    all_gather x4, waiting for transfers between devices: 103 us -> 137 us  [the longest x1 50.2 us: body(): full_up = lax.all_gather(w_up, 'shard', axis=1, tiled=True)]
    slice x0 -> x10, local copies, waits for them, and re-layouts: none -> 24.1 us  [the longest x2 12.3 us: body(): joined_fin[:down_width].reshape(grad_down.shape[0] // shard_count, -1)]
    reduce_scatter x1, waiting for transfers between devices: 0.01 us -> 17 us  [body(): lax.psum_scatter(grad_qkv.astype(jnp.bfloat16), 'shard', scatter_dimensio...]
    unnamed x1 -> x0, blocking collectives: 12.8 us -> none
  transfers between devices with their start and end apart: 8 -> 9, of which waited for: 5 -> 7; matrix products, arithmetic and copies ran while one was open for 14% -> 15% of each run, Pallas kernels for 0% -> 0%
where the time goes in v1:
time: 973 us; the launch traced here: 968 us
  waiting for transfers between devices  679 us (70%)
  matrix products  99.1 us (10%)
  local copies, waits for them, and re-layouts  81.8 us (8%)
  other arithmetic  67.6 us (7%)
  loops' own time  19.1 us (2%)
  between operations  14.6 us (2%)
    psum x1, waiting for transfers between devices, body(): total = lax.psum(flat, 'rep')  381 us
    reduce_scatter x1, waiting for transfers between devices, body(): lax.psum_scatter(joined.astype(jnp.bfloat16), 'shard', scatter_dimension=...  71.4 us
    reduce_scatter x1, waiting for transfers between devices, body(): lax.psum_scatter(grad_up.astype(jnp.bfloat16), 'shard', scatter_dimension...  69.8 us
    all_gather x1, waiting for transfers between devices, body(): full_up = lax.all_gather(w_up, 'shard', axis=1, tiled=True)  50.2 us
    all_gather x1, waiting for transfers between devices, body(): full_down = lax.all_gather(w_down, 'shard', axis=0, tiled=True)  48.4 us
    concatenate x1, other arithmetic, body(): flat = jnp.concatenate([o.reshape(-1).astype(jnp.float32) for o in owned])  48.4 us
    all_gather x1, waiting for transfers between devices, body(): full_qkv = lax.all_gather(w_qkv, 'shard', axis=1, tiled=True)  38.4 us
  transfers between devices with their start and end apart: 9, of which 7 were waited for; matrix products, arithmetic and copies ran while one was open for 15% of the time, Pallas kernels for 0%

profile of v1, /device:TPU:0, one launch (start us, length us, event | category | flops | bytes accessed | tf_op | source)
XLA Modules:
  0.0 967.8 jit_solution(11583978581339955561)
XLA Ops:
  12.2 6.3 all-gather
  20.3 38.4 %all-gather.6.cloned.1.call-done = bf16[1024,3072]{1,0:T(8,128)(2,1)} async-done(((bf16[1024,768]{1,0:T(8,128)(2,1)}), bf16[1024,3072]{1,0:T(8,128)(2,1)}) %all-gather.6.cloned.1.call-update) | async-done | bytes 6291472 | tf_op jit(solution)/shard_map/all_gather | solution.py:156
  58.7 5.4 fusion.69
  64.1 1.0 slice.186
  66.3 1.5 copy.75
  67.8 0.9 broadcast.223.clone
  68.8 19.0 %while.32 = (s32[]{:T(128)}, bf16[4,384,256]{1,2,0:T(8,128)(2,1)}, f32[4,4,384]{2,1,0:T(4,128)S(1)}, s32[4]{0:T(128)S(1)}, bf16[384,1024]{0,1:T(8,128)(2,1)S(1)}...) while((s32[]{:T(128)}, bf16[4,384,256]{1,2,0:T(8,128)(2,1)}, ...), condition=%wide.region_6.7_spmd.clone, body=%wide.region_3.6_spmd.clone.sunk | while | flops 157776416 | bytes 10964623 | solution.py:73
  71.1 0.8 fusion.133
  87.8 0.8 copy-done.7
  89.0 3.2 fusion.79
  92.5 50.2 %all-gather.10.cloned.1.call-done = bf16[1024,4096]{1,0:T(8,128)(2,1)} async-done(((bf16[1024,1024]{1,0:T(8,128)(2,1)}), bf16[1024,4096]{1,0:T(8,128)(2,1)}) %all-gather.10.cloned.1.call-update) | async-done | bytes 8388624 | tf_op jit(solution)/shard_map/all_gather | solution.py:158
  142.7 11.3 %fusion.30 = (bf16[4096,384]{0,1:T(8,128)(2,1)}, f32[384,4096]{1,0:T(8,128)}) fusion(f32[4096]{0:T(1024)S(1)} %bitcast.254, bf16[1024,4096]{1,0:T(8,128)(2,1)} %all-gather.10.cloned.1.call-done, f32[384,1024]{1,0:T(8,128)S(1)} %get-tuple-element.523, f32[1024]{0:T(1024)S(1)} %bitcast.261, f32[1024]{0:T(1024)S(1)} %bitcast.255, f32[384]{0:T(512)S(1)} %fusion.61, ...), kind=kOutput, calls=%fused_computation.60 | convolution fusion | flops 3238920192 | bytes 19426304 | tf_op jit(solution)/shard_map/dot_general | solution.py:178
  154.0 48.4 %all-gather.12.cloned.1.call-done = bf16[4096,1024]{1,0:T(8,128)(2,1)} async-done(((bf16[1024,1024]{1,0:T(8,128)(2,1)}), bf16[4096,1024]{1,0:T(8,128)(2,1)}) %all-gather.12.cloned.1.call-update) | async-done | bytes 8388624 | tf_op jit(solution)/shard_map/all_gather | solution.py:159
  202.4 10.5 %fusion.80 = (bf16[4096]{0:T(1024)(128)(2,1)S(1)}, bf16[384,4096]{1,0:T(8,128)(2,1)S(1)}) fusion(f32[384,4096]{1,0:T(8,128)} %get-tuple-element.529, bf16[4096,1024]{1,0:T(8,128)(2,1)} %all-gather.12.cloned.1.call-done, bf16[1,384,1024]{2,1,0:T(8,128)(2,1)S(1)} %copy-done.10), kind=kOutput, calls=%fused_computation.158 | convolution fusion | flops 3254251520 | bytes 18620416 | tf_op jit(solution)/shard_map/to,fo->tf/dot_general | solution.py:193
  213.0 3.8 multiply_reduce_fusion.1
  217.4 1.1 copy-done.4
  219.1 2.6 convolution_convert_fusion.3
  221.7 2.6 convolution_convert_fusion.4
  224.3 0.9 broadcast.223
  225.3 0.9 broadcast.223.clone.1
  226.2 0.9 broadcast.223.clone.2
  227.2 45.8 %while.33 = (s32[]{:T(128)}, bf16[4,384,256]{1,2,0:T(8,128)(2,1)}, bf16[4,384,256]{1,2,0:T(8,128)(2,1)}, bf16[4,384,256]{1,2,0:T(8,128)(2,1)}, s32[4]{0:T(128)S(...) while((s32[]{:T(128)}, bf16[4,384,256]{1,2,0:T(8,128)(2,1)}, ...), condition=%wide.region_13.14_spmd.clone, body=%wide.region_11.13_spmd.clone.sunk | while | flops 385251872 | bytes 36898628 | solution.py:112
  228.7 1.0 constant_dynamic-slice_fusion.15
  233.3 1.0 constant_dynamic-slice_fusion.18
  234.4 1.1 multiply_reduce_fusion.5
  240.2 1.0 constant_dynamic-slice_fusion.15
  244.7 1.0 constant_dynamic-slice_fusion.18
  245.8 1.1 multiply_reduce_fusion.5
  251.5 1.0 constant_dynamic-slice_fusion.15
  256.0 1.0 constant_dynamic-slice_fusion.18
  257.2 1.1 multiply_reduce_fusion.5
  262.9 1.0 constant_dynamic-slice_fusion.15
  267.4 1.0 constant_dynamic-slice_fusion.18
  268.5 1.1 multiply_reduce_fusion.5
  273.0 8.2 convolution_convert_fusion.2
  281.2 1.3 copy-done.3
  282.5 9.7 convolution_convert_fusion
  293.7 6.5 fusion.72
  300.2 1.1 copy-done.13
  302.1 1.5 reduce.5
  303.6 1.4 reduce.6
  305.2 4.6 copy.86
  309.8 6.6 convolution_convert_fusion.1
  316.4 3.7 fusion.15
  320.3 1.9 copy.97
  322.2 17.0 %reduce-scatter.5.cloned.1.call-done = bf16[1024,768]{1,0:T(8,128)(2,1)} async-done(((bf16[1024,3072]{1,0:T(8,128)(2,1)}), bf16[1024,768]{1,0:T(8,128)(2,1)}) %reduce-scatter.5.cloned.1.call-update) | async-done | bytes 1572880 | tf_op jit(solution)/shard_map/reduce_scatter | solution.py:234
  339.2 4.0 convert_element_type.308
  343.2 69.8 %reduce-scatter.9.cloned.1.call-done = bf16[1024,1024]{1,0:T(8,128)(2,1)} async-done(((bf16[1024,4096]{1,0:T(8,128)(2,1)}), bf16[1024,1024]{1,0:T(8,128)(2,1)}) %reduce-scatter.9.cloned.1.call-update) | async-done | bytes 2097168 | tf_op jit(solution)/shard_map/reduce_scatter | solution.py:236
  413.1 3.5 copy.98
  416.6 71.4 %reduce-scatter.11.cloned.1.call-done = bf16[1040,1024]{1,0:T(8,128)(2,1)} async-done(((bf16[4160,1024]{1,0:T(8,128)(2,1)}), bf16[1040,1024]{1,0:T(8,128)(2,1)}) %reduce-scatter.11.cloned.1.call-update) | async-done | bytes 2129936 | tf_op jit(solution)/shard_map/reduce_scatter | solution.py:231
  488.0 2.4 copy.99
  490.8 48.4 %maximum_convert_fusion = f32[3162112]{0:T(1024)} fusion(bf16[1064960]{0:T(1024)(128)(2,1)S(1)} %bitcast.226, bf16[1048576]{0:T(1024)(128)(2,1)S(1)} %bitcast.227, bf16[262144]{0:T(1024)(128)(2,1)S(1)} %bitcast.240, bf16[786432]{0:T(1024)(128)(2,1)S(1)} %copy-done.12), kind=kLoop, calls=%fused_computation.45 | loop fusion | flops 25296896 | bytes 18972672 | tf_op jit(solution)/shard_map/concatenate | solution.py:238
  539.8 3.5 fusion.54
  543.3 11.1 %fusion.51 = bf16[1,384,1024]{2,1,0:T(8,128)(2,1)} fusion(f32[384,1024]{1,0:T(8,128)S(1)} %copy-done.3, bf16[4096,1024]{1,0:T(8,128)(2,1)} %all-gather.12.cloned.1.call-done, f32[384,4096]{1,0:T(8,128)} %get-tuple-element.529, f32[1024]{0:T(1024)S(1)} %bitcast.263), kind=kOutput, calls=%fused_computation.101 | convolution fusion | flops 3236560896 | bytes 17043456 | tf_op jit(solution)/shard_map/dot_general | solution.py:183
  554.4 380.6 %all-reduce.4.cloned.1.call-done = f32[3162112]{0:T(1024)} async-done(((f32[3162112]{0:T(1024)}), f32[3162112]{0:T(1024)}) %all-reduce.4.cloned.1.call-update) | async-done | bytes 12648464 | tf_op jit(solution)/shard_map/psum | solution.py:239
  935.0 1.9 slice-done
  936.9 2.0 reshape.407
  938.8 1.2 slice-done.1
  940.0 1.1 slice.135
  941.2 7.4 fusion.78
  948.6 4.9 slice.140
  953.5 4.9 slice.143
  958.3 1.4 fusion.77
  959.8 1.3 slice.167
  (280 shorter events, 45.8 us)
Async XLA Ops:
  7.2 51.5 %all-gather.6.cloned.1.call-start = ((), (), s32[]{:S(2)}) async-start(), calls=%async_computation.4 | async-start | bytes 7864320 | tf_op jit(solution)/shard_map/all_gather | solution.py:156
  7.9 2.3 copy-start.21
  7.9 2.5 copy-start.22
  7.9 2.7 copy-start.23
  7.9 2.9 copy-start.24
  8.0 3.1 copy-start.25
  8.0 3.4 copy-start.26
  8.0 3.6 copy-start.27
  8.0 3.8 copy-start.20
  8.0 4.0 copy-start.28
  8.0 79.8 %all-gather.8.cloned.1.call-start = ((), (), s32[]{:S(2)}) async-start(), calls=%async_computation.5 | async-start | bytes 2621440 | tf_op jit(solution)/shard_map/all_gather | solution.py:157
  8.8 10.5 %copy-start.19 = (s32[1,2,64]{2,1,0:T(2,128)S(1)}, s32[1,2,64]{2,1,0:T(2,128)}, u32[]{:S(2)}) copy-start(s32[1,2,64]{2,1,0:T(2,128)} %param.21) | copy-start | bytes 1540
  8.8 10.9 %copy-start = (bf16[1,384,1024]{2,1,0:T(8,128)(2,1)S(1)}, bf16[1,384,1024]{2,1,0:T(8,128)(2,1)}, u32[]{:S(2)}) copy-start(bf16[1,384,1024]{2,1,0:T(8,128)(2,1)} %param.20) | copy-start | bytes 2359300
  8.8 133.9 %all-gather.10.cloned.1.call-start = ((), (), s32[]{:S(2)}) async-start(), calls=%async_computation.6 | async-start | bytes 10485760 | tf_op jit(solution)/shard_map/all_gather | solution.py:158
  9.5 192.9 %all-gather.12.cloned.1.call-start = ((), (), s32[]{:S(2)}) async-start(), calls=%async_computation.7 | async-start | bytes 10485760 | tf_op jit(solution)/shard_map/all_gather | solution.py:159
  10.1 310.2 %reduce-scatter.7.cloned.1.call-start = ((), (), s32[]{:S(2)}) async-start(), calls=%async_computation.9 | async-start | bytes 2621440 | tf_op jit(solution)/shard_map/reduce_scatter | solution.py:235
  87.8 0.9 copy-start.7
  87.8 1.2 copy-start.8
  92.1 124.7 %copy-start.2 = (f32[384,1024]{1,0:T(8,128)}, f32[384,1024]{1,0:T(8,128)S(1)}, u32[]{:S(2)}) copy-start(f32[384,1024]{1,0:T(8,128)S(1)} %get-tuple-element.523) | copy-start | bytes 4718596
  142.7 59.7 %copy-start.10 = (bf16[1,384,1024]{2,1,0:T(8,128)(2,1)S(1)}, bf16[1,384,1024]{2,1,0:T(8,128)(2,1)}, u32[]{:S(2)}) copy-start(bf16[1,384,1024]{2,1,0:T(8,128)(2,1)} %param.22) | copy-start | bytes 2359300
  202.4 10.6 %copy-start.29 = (bf16[1024,4096]{1,0:T(8,128)(2,1)S(1)}, bf16[1024,4096]{1,0:T(8,128)(2,1)}, u32[]{:S(2)}) copy-start(bf16[1024,4096]{1,0:T(8,128)(2,1)} %all-gather.10.cloned.1.call-done) | copy-start | bytes 25165828
  212.9 3.8 copy-start.30
  217.4 1.2 copy-start.4
  217.4 1.7 copy-start.14
  221.7 117.6 %reduce-scatter.5.cloned.1.call-start = ((), (), s32[]{:S(2)}) async-start(), calls=%async_computation.8 | async-start | bytes 7864320 | tf_op jit(solution)/shard_map/reduce_scatter | solution.py:234
  227.4 2.6 copy-start.5
  227.4 2.6 copy-start.16
  236.9 1.9 copy-start.6
  236.9 1.9 copy-start.17
  238.8 2.5 copy-start.5
  238.8 2.6 copy-start.16
  248.3 1.9 copy-start.6
  248.3 1.9 copy-start.17
  250.2 2.5 copy-start.5
  250.2 2.6 copy-start.16
  259.7 1.9 copy-start.6
  259.7 1.9 copy-start.17
  261.6 2.5 copy-start.5
  261.6 2.6 copy-start.16
  271.1 1.9 copy-start.6
  271.1 1.9 copy-start.17
  281.1 1.4 copy-start.3
  281.2 131.9 %reduce-scatter.9.cloned.1.call-start = ((), (), s32[]{:S(2)}) async-start(), calls=%async_computation.10 | async-start | bytes 10485760 | tf_op jit(solution)/shard_map/reduce_scatter | solution.py:236
  292.2 1.2 copy-start.11
  292.2 1.5 copy-start.1
  292.2 195.8 %reduce-scatter.11.cloned.1.call-start = ((), (), s32[]{:S(2)}) async-start(), calls=%async_computation.11 | async-start | bytes 10649600 | tf_op jit(solution)/shard_map/reduce_scatter | solution.py:231
  300.2 1.2 copy-start.13
  320.2 614.8 %all-reduce.4.cloned.1.call-start = ((), (), s32[]{:S(2)}) async-start(), calls=%async_computation.12 | async-start | bytes 25296896 | tf_op jit(solution)/shard_map/psum | solution.py:239
  488.0 2.4 copy-start.9
  488.0 2.7 copy-start.12
  488.0 2.8 copy-start.15
  539.1 0.7 copy-start.18
  935.0 1.9 slice-start
  938.8 1.2 slice-start.1
Sparse Core Ops, SparseCore 0:
  9.6 49.0 all-gather.5
  60.2 22.5 all-gather.7
  84.4 58.2 all-gather.9
  144.1 58.2 all-gather.11
  221.8 31.1 reduce-scatter.6
  281.3 57.9 reduce-scatter.4
  341.8 71.2 reduce-scatter.8
  415.7 72.2 reduce-scatter.10
  539.3 395.6 all-reduce.3

commit v2 on v1

--- a/solution.py
+++ b/solution.py
@@ -220,33 +220,38 @@
     grad_down = jnp.einsum("tf,to->fo", activated, cot_low, preferred_element_type=jnp.float32)
     grad_up = jnp.einsum("ti,tf->if", normed_two, grad_pre, preferred_element_type=jnp.float32)
     grad_out = jnp.einsum("ti,to->io", mixed, grad_branch, preferred_element_type=jnp.float32)
-    grad_qkv = jnp.einsum("ti,tc->ic", normed, grad_proj, preferred_element_type=jnp.float32)
+    grad_qkv_t = jnp.einsum("tc,ti->ci", grad_proj, normed, preferred_element_type=jnp.float32)
     smalls = [grad_g1, grad_s1, grad_qb, grad_vb, grad_bo, grad_g2, grad_s2, grad_bu, grad_bd]
     small_rows = jnp.concatenate([g.reshape(shard_count, -1) for g in smalls], 1)
     small_rows = small_rows.reshape(shard_count, -1, model_width)
     small_rows = jnp.pad(small_rows, ((0, 0), (0, 16 - small_rows.shape[1]), (0, 0)))
     down_rows = grad_down.reshape(shard_count, -1, model_width)
-    down_width = down_rows.shape[1] * model_width
+    down_height = down_rows.shape[1]
     joined = jnp.concatenate([down_rows, small_rows], 1).reshape(-1, model_width)
     joined_own = lax.psum_scatter(
         joined.astype(jnp.bfloat16), "shard", scatter_dimension=0, tiled=True
-    ).reshape(-1)
-    qkv_own = lax.psum_scatter(grad_qkv.astype(jnp.bfloat16), "shard", scatter_dimension=1, tiled=True)
+    )
+    qkv_own = lax.psum_scatter(
+        grad_qkv_t.astype(jnp.bfloat16), "shard", scatter_dimension=0, tiled=True
+    )
     out_own = lax.psum_scatter(grad_out.astype(jnp.bfloat16), "shard", scatter_dimension=0, tiled=True)
     up_own = lax.psum_scatter(grad_up.astype(jnp.bfloat16), "shard", scatter_dimension=1, tiled=True)
     owned = [qkv_own, out_own, up_own, joined_own]
-    flat = jnp.concatenate([o.reshape(-1).astype(jnp.float32) for o in owned])
-    total = lax.psum(flat, "rep")
+    total = lax.psum(jnp.concatenate(owned, 0), "rep")
     pieces, offset = [], 0
     for o in owned:
-        pieces.append(total[offset : offset + o.size].reshape(o.shape))
-        offset += o.size
+        pieces.append(total[offset : offset + o.shape[0]])
+        offset += o.shape[0]
     qkv_fin, out_fin, up_fin, joined_fin = pieces
-    down_fin = joined_fin[:down_width].reshape(grad_down.shape[0] // shard_count, -1)
-    small_fin, offset = [], down_width
+    qkv_fin = qkv_fin.astype(jnp.float32).T
+    out_fin = out_fin.astype(jnp.float32)
+    up_fin = up_fin.astype(jnp.float32)
+    down_fin = joined_fin[:down_height].astype(jnp.float32)
+    small_flat = joined_fin[down_height:].reshape(-1).astype(jnp.float32)
+    small_fin, offset = [], 0
     for g in smalls:
         width = g.shape[0] // shard_count
-        small_fin.append(joined_fin[offset : offset + width])
+        small_fin.append(small_flat[offset : offset + width])
         offset += width
     g1_fin, s1_fin, qb_fin, vb_fin, bo_fin, g2_fin, s2_fin, bu_fin, bd_fin = small_fin
     return (

time: 973 us -> 735 us (0.76)
  waiting for transfers between devices: 679 us -> 502 us
  local copies, waits for them, and re-layouts: 81.8 us -> 49.9 us
  other arithmetic: 67.6 us -> 39.3 us
    psum x1, waiting for transfers between devices: 381 us -> 198 us  [body(): total = lax.psum(jnp.concatenate(owned, 0), 'rep')]
    concatenate x1, other arithmetic: 48.4 us -> 6 us  [body(): total = lax.psum(jnp.concatenate(owned, 0), 'rep')]
    slice x10 -> x2, local copies, waits for them, and re-layouts: 24.1 us -> 1.19 us  [body(): small_fin.append(small_flat[offset:offset + width])]
  transfers between devices with their start and end apart: 9 -> 9, of which waited for: 7 -> 7; matrix products, arithmetic and copies ran while one was open for 15% -> 19% of each run, Pallas kernels for 0% -> 0%
where the time goes in v2:
time: 735 us; the launch traced here: 731 us
  waiting for transfers between devices  502 us (68%)
  matrix products  98.6 us (13%)
  local copies, waits for them, and re-layouts  49.9 us (7%)
  other arithmetic  39.3 us (5%)
  loops' own time  19.1 us (3%)
  between operations  14.5 us (2%)
    psum x1, waiting for transfers between devices, body(): total = lax.psum(jnp.concatenate(owned, 0), 'rep')  198 us
    reduce_scatter x1, waiting for transfers between devices, body(): lax.psum_scatter(joined.astype(jnp.bfloat16), 'shard', scatter_dimension=...  74.9 us
    reduce_scatter x1, waiting for transfers between devices, body(): lax.psum_scatter(grad_up.astype(jnp.bfloat16), 'shard', scatter_dimension...  73.9 us
    all_gather x1, waiting for transfers between devices, body(): full_down = lax.all_gather(w_down, 'shard', axis=0, tiled=True)  48.5 us
    all_gather x1, waiting for transfers between devices, body(): full_up = lax.all_gather(w_up, 'shard', axis=1, tiled=True)  46.3 us
    all_gather x1, waiting for transfers between devices, body(): full_qkv = lax.all_gather(w_qkv, 'shard', axis=1, tiled=True)  38.4 us
    reduce_scatter x1, waiting for transfers between devices, body(): lax.psum_scatter(grad_qkv_t.astype(jnp.bfloat16), 'shard', scatter_dimens...  19.5 us
  transfers between devices with their start and end apart: 9, of which 7 were waited for; matrix products, arithmetic and copies ran while one was open for 19% of the time, Pallas kernels for 0%

profile of v2, /device:TPU:0, one launch (start us, length us, event | category | flops | bytes accessed | tf_op | source)
XLA Modules:
  0.0 730.6 jit_solution(3960130433894804833)
XLA Ops:
  12.2 6.3 all-gather
  20.3 38.4 %all-gather.6.cloned.1.call-done = bf16[1024,3072]{1,0:T(8,128)(2,1)} async-done(((bf16[1024,768]{1,0:T(8,128)(2,1)}), bf16[1024,3072]{1,0:T(8,128)(2,1)}) %all-gather.6.cloned.1.call-update) | async-done | bytes 6291472 | tf_op jit(solution)/shard_map/all_gather | solution.py:156
  58.7 5.1 fusion.69
  63.7 1.0 slice.155
  65.5 1.2 copy.77
  66.7 1.5 copy.78
  68.2 0.9 broadcast.223.clone
  69.2 22.7 %while.32 = (s32[]{:T(128)}, bf16[4,384,256]{1,2,0:T(8,128)(2,1)}, f32[4,4,384]{2,1,0:T(4,128)S(1)}, s32[4]{0:T(128)S(1)}, bf16[384,1024]{0,1:T(8,128)(2,1)S(1)}...) while((s32[]{:T(128)}, bf16[4,384,256]{1,2,0:T(8,128)(2,1)}, ...), condition=%wide.region_6.7_spmd.clone, body=%wide.region_3.6_spmd.clone.sunk | while | flops 157776416 | bytes 10964623 | solution.py:73
  71.3 1.0 constant_dynamic-slice_fusion.14
  72.4 0.8 fusion.132
  76.9 1.0 constant_dynamic-slice_fusion.14
  78.1 0.8 fusion.132
  82.6 1.0 constant_dynamic-slice_fusion.14
  83.8 0.8 fusion.132
  88.3 1.0 constant_dynamic-slice_fusion.14
  89.4 0.8 fusion.132
  91.9 0.8 copy-done.6
  92.8 3.3 fusion.78
  96.4 46.3 %all-gather.10.cloned.1.call-done = bf16[1024,4096]{1,0:T(8,128)(2,1)} async-done(((bf16[1024,1024]{1,0:T(8,128)(2,1)}), bf16[1024,4096]{1,0:T(8,128)(2,1)}) %all-gather.10.cloned.1.call-update) | async-done | bytes 8388624 | tf_op jit(solution)/shard_map/all_gather | solution.py:158
  142.7 11.3 %fusion.30 = (bf16[4096,384]{0,1:T(8,128)(2,1)}, f32[384,4096]{1,0:T(8,128)}) fusion(f32[4096]{0:T(1024)S(1)} %bitcast.249, bf16[1024,4096]{1,0:T(8,128)(2,1)} %all-gather.10.cloned.1.call-done, f32[384,1024]{1,0:T(8,128)S(1)} %get-tuple-element.583, f32[1024]{0:T(1024)S(1)} %bitcast.256, f32[1024]{0:T(1024)S(1)} %bitcast.250, f32[384]{0:T(512)S(1)} %fusion.61, ...), kind=kOutput, calls=%fused_computation.60 | convolution fusion | flops 3238920192 | bytes 19426304 | tf_op jit(solution)/shard_map/dot_general | solution.py:178
  153.9 48.5 %all-gather.12.cloned.1.call-done = bf16[4096,1024]{1,0:T(8,128)(2,1)} async-done(((bf16[1024,1024]{1,0:T(8,128)(2,1)}), bf16[4096,1024]{1,0:T(8,128)(2,1)}) %all-gather.12.cloned.1.call-update) | async-done | bytes 8388624 | tf_op jit(solution)/shard_map/all_gather | solution.py:159
  202.4 10.6 %fusion.79 = (bf16[4096]{0:T(1024)(128)(2,1)S(1)}, bf16[384,4096]{1,0:T(8,128)(2,1)S(1)}) fusion(f32[384,4096]{1,0:T(8,128)} %get-tuple-element.589, bf16[4096,1024]{1,0:T(8,128)(2,1)} %all-gather.12.cloned.1.call-done, bf16[1,384,1024]{2,1,0:T(8,128)(2,1)S(1)} %copy-done.7), kind=kOutput, calls=%fused_computation.162 | convolution fusion | flops 3254251520 | bytes 18620416 | tf_op jit(solution)/shard_map/to,fo->tf/dot_general | solution.py:193
  213.0 3.8 multiply_reduce_fusion.1
  216.9 1.7 fusion.75
  218.5 1.8 fusion.73
  220.3 2.6 convolution_convert_fusion.3
  223.0 2.6 convolution_convert_fusion.4
  225.6 0.9 broadcast.223
  226.6 0.9 broadcast.223.clone.1
  227.5 0.9 broadcast.223.clone.2
  228.5 45.8 %while.33 = (s32[]{:T(128)}, bf16[4,384,256]{1,2,0:T(8,128)(2,1)}, bf16[4,384,256]{1,2,0:T(8,128)(2,1)}, bf16[4,384,256]{1,2,0:T(8,128)(2,1)}, s32[4]{0:T(128)S(...) while((s32[]{:T(128)}, bf16[4,384,256]{1,2,0:T(8,128)(2,1)}, ...), condition=%wide.region_13.14_spmd.clone, body=%wide.region_11.13_spmd.clone.sunk | while | flops 385251872 | bytes 36898628 | solution.py:112
  230.1 1.0 constant_dynamic-slice_fusion.15
  234.6 1.0 constant_dynamic-slice_fusion.18
  235.7 1.1 multiply_reduce_fusion.5
  241.5 1.0 constant_dynamic-slice_fusion.15
  246.0 1.0 constant_dynamic-slice_fusion.18
  247.1 1.1 multiply_reduce_fusion.5
  252.9 1.0 constant_dynamic-slice_fusion.15
  257.4 1.0 constant_dynamic-slice_fusion.18
  258.5 1.1 multiply_reduce_fusion.5
  264.2 1.0 constant_dynamic-slice_fusion.15
  268.7 1.0 constant_dynamic-slice_fusion.18
  269.9 1.1 multiply_reduce_fusion.5
  274.3 8.1 %convolution_convert_fusion.2 = bf16[3072,1024]{1,0:T(8,128)(2,1)} fusion(bf16[384,1024]{0,1:T(8,128)(2,1)} %bitcast.232, bf16[384,1024]{0,1:T(8,128)(2,1)} %bitcast.236, bf16[384,1024]{0,1:T(8,128)(2,1)} %bitcast.230, bf16[1,384,1024]{2,1,0:T(8,128)(2,1)} %param.20, f32[1024]{0:T(1024)S(1)} %bitcast.255, f32[1024]{0:T(1024)S(1)} %bitcast.242, ...), kind=kOutput, calls=%fused_computation.62 | convolution fusion | flops 2428502016 | bytes 9448448 | tf_op jit(solution)/shard_map/tc,ti->ci/dot_general | solution.py:223
  282.4 1.3 copy-done.3
  283.7 9.7 %convolution_convert_fusion = bf16[1024,4096]{1,0:T(8,128)(2,1)} fusion(bf16[384,4096]{1,0:T(8,128)(2,1)} %copy-done.25, f32[384,1024]{1,0:T(8,128)S(1)} %copy-done.3, f32[1024]{0:T(1024)S(1)} %bitcast.257, f32[1024]{0:T(1024)S(1)} %bitcast.253, f32[384]{0:T(512)S(1)} %fusion.61, f32[384]{0:T(512)S(1)} %broadcast_multiply_fusion), kind=kOutput, calls=%fused_computation.43 | convolution fusion | flops 3227385856 | bytes 13118464 | tf_op jit(solution)/shard_map/ti,tf->if/dot_general | solution.py:221
  295.0 6.5 fusion.72
  301.5 1.1 copy-done.9
  303.4 1.6 reduce.5
  305.0 1.4 reduce.6
  306.6 4.6 copy.90
  311.3 6.6 convolution_convert_fusion.1
  317.9 3.8 fusion.15
  321.9 19.5 %reduce-scatter.5.cloned.1.call-done = bf16[768,1024]{1,0:T(8,128)(2,1)} async-done(((bf16[3072,1024]{1,0:T(8,128)(2,1)}), bf16[768,1024]{1,0:T(8,128)(2,1)}) %reduce-scatter.5.cloned.1.call-update) | async-done | bytes 1572880 | tf_op jit(solution)/shard_map/reduce_scatter | solution.py:234
  341.4 73.9 %reduce-scatter.9.cloned.1.call-done = bf16[1024,1024]{1,0:T(8,128)(2,1)} async-done(((bf16[1024,4096]{1,0:T(8,128)(2,1)}), bf16[1024,1024]{1,0:T(8,128)(2,1)}) %reduce-scatter.9.cloned.1.call-update) | async-done | bytes 2097168 | tf_op jit(solution)/shard_map/reduce_scatter | solution.py:238
  415.3 74.9 %reduce-scatter.11.cloned.1.call-done = bf16[1040,1024]{1,0:T(8,128)(2,1)} async-done(((bf16[4160,1024]{1,0:T(8,128)(2,1)}), bf16[1040,1024]{1,0:T(8,128)(2,1)}) %reduce-scatter.11.cloned.1.call-update) | async-done | bytes 2129936 | tf_op jit(solution)/shard_map/reduce_scatter | solution.py:231
  490.1 6.0 pad_maximum_fusion
  496.8 3.5 fusion.54
  500.3 10.8 %fusion.51 = bf16[1,384,1024]{2,1,0:T(8,128)(2,1)} fusion(f32[384,1024]{1,0:T(8,128)S(1)} %copy-done.3, bf16[4096,1024]{1,0:T(8,128)(2,1)} %all-gather.12.cloned.1.call-done, f32[384,4096]{1,0:T(8,128)} %get-tuple-element.589, f32[1024]{0:T(1024)S(1)} %bitcast.258), kind=kOutput, calls=%fused_computation.104 | convolution fusion | flops 3236560896 | bytes 17043456 | tf_op jit(solution)/shard_map/dot_general | solution.py:183
  511.1 197.9 %all-reduce.4.cloned.1.call-done = bf16[3088,1024]{1,0:T(8,128)(2,1)} async-done(((bf16[3088,1024]{1,0:T(8,128)(2,1)}), bf16[3088,1024]{1,0:T(8,128)(2,1)}) %all-reduce.4.cloned.1.call-update) | async-done | bytes 6324240 | tf_op jit(solution)/shard_map/psum | solution.py:240
  711.0 1.8 convert_bitcast_fusion
  712.8 2.4 copy.85
  715.1 2.1 slice_convert_fusion.3
  717.3 6.7 slice_convert_fusion
  (263 shorter events, 43.1 us)
Async XLA Ops:
  7.2 51.5 %all-gather.6.cloned.1.call-start = ((), (), s32[]{:S(2)}) async-start(), calls=%async_computation.4 | async-start | bytes 7864320 | tf_op jit(solution)/shard_map/all_gather | solution.py:156
  7.9 2.3 copy-start.16
  7.9 2.5 copy-start.17
  7.9 2.7 copy-start.18
  7.9 2.9 copy-start.19
  8.0 3.1 copy-start.20
  8.0 3.4 copy-start.21
  8.0 3.6 copy-start.22
  8.0 3.8 copy-start.15
  8.0 4.0 copy-start.23
  8.0 83.9 %all-gather.8.cloned.1.call-start = ((), (), s32[]{:S(2)}) async-start(), calls=%async_computation.5 | async-start | bytes 2621440 | tf_op jit(solution)/shard_map/all_gather | solution.py:157
  8.8 10.5 %copy-start.14 = (s32[1,2,64]{2,1,0:T(2,128)S(1)}, s32[1,2,64]{2,1,0:T(2,128)}, u32[]{:S(2)}) copy-start(s32[1,2,64]{2,1,0:T(2,128)} %param.21) | copy-start | bytes 1540
  8.8 10.9 %copy-start = (bf16[1,384,1024]{2,1,0:T(8,128)(2,1)S(1)}, bf16[1,384,1024]{2,1,0:T(8,128)(2,1)}, u32[]{:S(2)}) copy-start(bf16[1,384,1024]{2,1,0:T(8,128)(2,1)} %param.20) | copy-start | bytes 2359300
  8.8 133.9 %all-gather.10.cloned.1.call-start = ((), (), s32[]{:S(2)}) async-start(), calls=%async_computation.6 | async-start | bytes 10485760 | tf_op jit(solution)/shard_map/all_gather | solution.py:158
  9.5 192.9 %all-gather.12.cloned.1.call-start = ((), (), s32[]{:S(2)}) async-start(), calls=%async_computation.7 | async-start | bytes 10485760 | tf_op jit(solution)/shard_map/all_gather | solution.py:159
  10.1 311.8 %reduce-scatter.7.cloned.1.call-start = ((), (), s32[]{:S(2)}) async-start(), calls=%async_computation.9 | async-start | bytes 2621440 | tf_op jit(solution)/shard_map/reduce_scatter | solution.py:237
  91.9 0.9 copy-start.6
  96.1 120.8 %copy-start.2 = (f32[384,1024]{1,0:T(8,128)}, f32[384,1024]{1,0:T(8,128)S(1)}, u32[]{:S(2)}) copy-start(f32[384,1024]{1,0:T(8,128)S(1)} %get-tuple-element.583) | copy-start | bytes 4718596
  142.7 59.7 %copy-start.7 = (bf16[1,384,1024]{2,1,0:T(8,128)(2,1)S(1)}, bf16[1,384,1024]{2,1,0:T(8,128)(2,1)}, u32[]{:S(2)}) copy-start(bf16[1,384,1024]{2,1,0:T(8,128)(2,1)} %param.22) | copy-start | bytes 2359300
  202.4 10.6 %copy-start.24 = (bf16[1024,4096]{1,0:T(8,128)(2,1)S(1)}, bf16[1024,4096]{1,0:T(8,128)(2,1)}, u32[]{:S(2)}) copy-start(bf16[1024,4096]{1,0:T(8,128)(2,1)} %all-gather.10.cloned.1.call-done) | copy-start | bytes 25165828
  213.0 3.8 copy-start.25
  218.5 1.8 copy-start.10
  222.9 118.5 %reduce-scatter.5.cloned.1.call-start = ((), (), s32[]{:S(2)}) async-start(), calls=%async_computation.8 | async-start | bytes 7864320 | tf_op jit(solution)/shard_map/reduce_scatter | solution.py:234
  228.7 2.6 copy-start.4
  228.7 2.6 copy-start.11
  238.3 1.9 copy-start.5
  238.3 1.9 copy-start.12
  240.2 2.5 copy-start.4
  240.2 2.6 copy-start.11
  249.7 1.9 copy-start.5
  249.7 1.9 copy-start.12
  251.5 2.5 copy-start.4
  251.5 2.6 copy-start.11
  261.0 1.9 copy-start.5
  261.0 1.9 copy-start.12
  262.9 2.5 copy-start.4
  262.9 2.6 copy-start.11
  272.4 1.9 copy-start.5
  272.4 1.9 copy-start.12
  282.3 1.4 copy-start.3
  282.4 132.9 %reduce-scatter.9.cloned.1.call-start = ((), (), s32[]{:S(2)}) async-start(), calls=%async_computation.10 | async-start | bytes 10485760 | tf_op jit(solution)/shard_map/reduce_scatter | solution.py:238
  293.5 1.2 copy-start.8
  293.5 1.5 copy-start.1
  293.5 196.6 %reduce-scatter.11.cloned.1.call-start = ((), (), s32[]{:S(2)}) async-start(), calls=%async_computation.11 | async-start | bytes 10649600 | tf_op jit(solution)/shard_map/reduce_scatter | solution.py:231
  301.5 1.1 copy-start.9
  321.7 387.3 %all-reduce.4.cloned.1.call-start = ((), (), s32[]{:S(2)}) async-start(), calls=%async_computation.12 | async-start | bytes 12648448 | tf_op jit(solution)/shard_map/psum | solution.py:240
  496.1 0.7 copy-start.13
Sparse Core Ops, SparseCore 0:
  9.6 49.0 all-gather.5
  60.2 22.5 all-gather.7
  84.4 58.2 all-gather.9
  144.1 58.2 all-gather.11
  223.1 31.1 reduce-scatter.6
  282.5 58.8 reduce-scatter.4
  344.0 71.2 reduce-scatter.8
  417.9 72.2 reduce-scatter.10
  496.3 212.6 all-reduce.3

commit v3 on v2

--- a/solution.py
+++ b/solution.py
@@ -4,6 +4,7 @@
 import jax.numpy as jnp
 from jax import lax
 from jax.sharding import PartitionSpec as P
+
 
 HEADS = 16
 HDIM = 64
@@ -117,7 +118,46 @@
     )
 
 
-SMALL = ("ln1_gain", "ln1_bias", "q_bias", "v_bias", "b_out", "ln2_gain", "ln2_bias", "b_up", "b_down")
+def bit_steps(size):
+    assert size & (size - 1) == 0
+    return [1 << b for b in range(size.bit_length() - 1)]
+
+
+def chunk_order(size, steps):
+    places = []
+    for member in range(size):
+        place = 0
+        for step in steps:
+            place = place * 2 + (member // step) % 2
+        places.append(place)
+    order = [0] * size
+    for member, place in enumerate(places):
+        order[place] = member
+    return order
+
+
+def reorder_cols(matrix, order):
+    pieces = jnp.split(matrix, len(order), 1)
+    return jnp.concatenate([pieces[k] for k in order], 1)
+
+
+def halving(arrays, axis, size, steps):
+    index = lax.axis_index(axis)
+    for step in steps:
+        bit = (index // step) % 2
+        keeps, sends = [], []
+        for array in arrays:
+            pair = array.reshape(2, array.shape[0] // 2, *array.shape[1:])
+            keeps.append(lax.dynamic_index_in_dim(pair, bit, 0, keepdims=False))
+            sends.append(
+                lax.dynamic_index_in_dim(pair, 1 - bit, 0, keepdims=False).astype(jnp.bfloat16)
+            )
+        got = lax.ppermute(jnp.concatenate(sends, 0), axis, [(a, a ^ step) for a in range(size)])
+        arrays, offset = [], 0
+        for keep in keeps:
+            arrays.append(keep + got[offset : offset + keep.shape[0]].astype(jnp.float32))
+            offset += keep.shape[0]
+    return arrays
 
 
 def gather_small(pieces):
@@ -131,7 +171,7 @@
     return fulls
 
 
-def body(
+def body_inner(
     tokens,
     cont_segment,
     cotangent,
@@ -158,7 +198,7 @@
     full_up = lax.all_gather(w_up, "shard", axis=1, tiled=True)
     full_down = lax.all_gather(w_down, "shard", axis=0, tiled=True)
     inputs = tokens[0].astype(jnp.float32)
-    length, model_width = inputs.shape
+    _, model_width = inputs.shape
     distance, allowed = layout(cont_segment[0])
     normed = normalize(inputs, full_g1.astype(jnp.float32), full_s1.astype(jnp.float32)).astype(
         jnp.bfloat16
@@ -186,18 +226,25 @@
     back_g1, back_qkv, back_out, back_g2, back_up, back_down = (
         full_g1, full_qkv, full_out, full_g2, full_up, full_down
     )
+    shard_steps = bit_steps(shard_count)
+    order = chunk_order(shard_count, shard_steps)
     cot_low = cotangent[0]
     cot_full = cot_low.astype(jnp.float32)
     zero_shift = jnp.zeros((model_width,), jnp.float32)
     grad_bd = jnp.sum(cot_full, 0)
     grad_act = jnp.einsum("to,fo->tf", cot_low, back_down, preferred_element_type=jnp.float32)
-    gelu_value, gelu_pull = jax.vjp(partial(jax.nn.gelu, approximate=True), pre_act)
+    _, gelu_pull = jax.vjp(partial(jax.nn.gelu, approximate=True), pre_act)
     grad_pre = gelu_pull(grad_act)[0].astype(jnp.bfloat16)
     grad_bu = jnp.sum(grad_pre.astype(jnp.float32), 0)
+    grad_down = jnp.einsum(
+        "tf,to->fo", reorder_cols(activated, order), cot_low, preferred_element_type=jnp.float32
+    )
+    grad_up_t = jnp.einsum(
+        "tf,ti->fi", reorder_cols(grad_pre, order), normed_two, preferred_element_type=jnp.float32
+    )
+    down_own, up_own = halving([grad_down, grad_up_t], "shard", shard_count, shard_steps)
     grad_normed_two = jnp.einsum("tf,if->ti", grad_pre, back_up, preferred_element_type=jnp.float32)
-    norm_value_two, norm_pull_two = jax.vjp(
-        normalize, middle, back_g2.astype(jnp.float32), zero_shift
-    )
+    _, norm_pull_two = jax.vjp(normalize, middle, back_g2.astype(jnp.float32), zero_shift)
     grad_mid_part, grad_g2, grad_s2 = norm_pull_two(grad_normed_two)
     grad_middle = cot_full + grad_mid_part
     grad_branch = grad_middle.astype(jnp.bfloat16)
@@ -205,6 +252,9 @@
     grad_mixed = jnp.einsum(
         "to,io->ti", grad_branch, back_out, preferred_element_type=jnp.float32
     ).astype(jnp.bfloat16)
+    grad_out = jnp.einsum(
+        "ti,to->io", reorder_cols(mixed, order), grad_branch, preferred_element_type=jnp.float32
+    )
     grad_q, grad_k, grad_v = attend_backward(
         queries, key_rows, values, grad_mixed, log_norms, distance, allowed
     )
@@ -212,42 +262,32 @@
     grad_qb = jnp.sum(grad_q.astype(jnp.float32), 0)
     grad_vb = jnp.sum(grad_v.astype(jnp.float32), 0)
     grad_normed = jnp.einsum("tc,ic->ti", grad_proj, back_qkv, preferred_element_type=jnp.float32)
-    norm_value_one, norm_pull_one = jax.vjp(
-        normalize, inputs, back_g1.astype(jnp.float32), zero_shift
-    )
+    _, norm_pull_one = jax.vjp(normalize, inputs, back_g1.astype(jnp.float32), zero_shift)
     grad_in_part, grad_g1, grad_s1 = norm_pull_one(grad_normed)
     grad_inputs = grad_middle + grad_in_part
-    grad_down = jnp.einsum("tf,to->fo", activated, cot_low, preferred_element_type=jnp.float32)
-    grad_up = jnp.einsum("ti,tf->if", normed_two, grad_pre, preferred_element_type=jnp.float32)
-    grad_out = jnp.einsum("ti,to->io", mixed, grad_branch, preferred_element_type=jnp.float32)
-    grad_qkv_t = jnp.einsum("tc,ti->ci", grad_proj, normed, preferred_element_type=jnp.float32)
+    grad_qkv_t = jnp.einsum(
+        "tc,ti->ci", reorder_cols(grad_proj, order), normed, preferred_element_type=jnp.float32
+    )
     smalls = [grad_g1, grad_s1, grad_qb, grad_vb, grad_bo, grad_g2, grad_s2, grad_bu, grad_bd]
     small_rows = jnp.concatenate([g.reshape(shard_count, -1) for g in smalls], 1)
     small_rows = small_rows.reshape(shard_count, -1, model_width)
     small_rows = jnp.pad(small_rows, ((0, 0), (0, 16 - small_rows.shape[1]), (0, 0)))
-    down_rows = grad_down.reshape(shard_count, -1, model_width)
-    down_height = down_rows.shape[1]
-    joined = jnp.concatenate([down_rows, small_rows], 1).reshape(-1, model_width)
-    joined_own = lax.psum_scatter(
-        joined.astype(jnp.bfloat16), "shard", scatter_dimension=0, tiled=True
-    )
-    qkv_own = lax.psum_scatter(
-        grad_qkv_t.astype(jnp.bfloat16), "shard", scatter_dimension=0, tiled=True
-    )
-    out_own = lax.psum_scatter(grad_out.astype(jnp.bfloat16), "shard", scatter_dimension=0, tiled=True)
-    up_own = lax.psum_scatter(grad_up.astype(jnp.bfloat16), "shard", scatter_dimension=1, tiled=True)
-    owned = [qkv_own, out_own, up_own, joined_own]
-    total = lax.psum(jnp.concatenate(owned, 0), "rep")
+    small_rows = jnp.concatenate([small_rows[k] for k in order], 0)
+    out_own, qkv_own, small_own = halving(
+        [grad_out, grad_qkv_t, small_rows], "shard", shard_count, shard_steps
+    )
+    owned = [down_own, up_own, out_own, qkv_own, small_own]
+    total = lax.psum(jnp.concatenate([o.astype(jnp.bfloat16) for o in owned], 0), "rep")
     pieces, offset = [], 0
     for o in owned:
         pieces.append(total[offset : offset + o.shape[0]])
         offset += o.shape[0]
-    qkv_fin, out_fin, up_fin, joined_fin = pieces
+    down_fin, up_fin, out_fin, qkv_fin, small_fin_rows = pieces
+    down_fin = down_fin.astype(jnp.float32)
+    up_fin = up_fin.astype(jnp.float32).T
+    out_fin = out_fin.astype(jnp.float32)
     qkv_fin = qkv_fin.astype(jnp.float32).T
-    out_fin = out_fin.astype(jnp.float32)
-    up_fin = up_fin.astype(jnp.float32)
-    down_fin = joined_fin[:down_height].astype(jnp.float32)
-    small_flat = joined_fin[down_height:].reshape(-1).astype(jnp.float32)
+    small_flat = small_fin_rows.reshape(-1).astype(jnp.float32)
     small_fin, offset = [], 0
     for g in smalls:
         width = g.shape[0] // shard_count
@@ -275,7 +315,7 @@
 
 def solution(mesh):
     return jax.shard_map(
-        body,
+        body_inner,
         mesh=mesh,
         in_specs=(
             P(("rep", "shard"), None, None),

time: 735 us -> 763 us (1.038)
  waiting for transfers between devices: 502 us -> 459 us
  other arithmetic: 39.3 us -> 81 us
  local copies, waits for them, and re-layouts: 49.9 us -> 84.7 us
    reduce_scatter x4 -> x0, waiting for transfers between devices: 168 us -> none  [the longest x1 74.9 us: body(): lax.psum_scatter(joined.astype(jnp.bfloat16), 'shard', scatter_dimension=...]
    ppermute x0 -> x4, waiting for transfers between devices: none -> 117 us  [halving(): lax.ppermute(jnp.concatenate(sends, 0), axis, [(a, a ^ step) for a in ran...]
    add x0 -> x4, other arithmetic: none -> 20.6 us  [halving(): arrays.append(keep + got[offset:offset + keep.shape[0]].astype(jnp.float32))]
    convert_element_type x0 -> x9, local copies, waits for them, and re-layouts: none -> 16.9 us  [halving(): lax.dynamic_index_in_dim(pair, 1 - bit, 0, keepdims=False)]
    unnamed x4 -> x10, other arithmetic: 1.37 us -> 16.9 us
    unnamed x74 -> x153, local copies, waits for them, and re-layouts: 12.1 us -> 24 us
    concatenate x2 -> x7, other arithmetic: 9.76 us -> 16.7 us  [the longest x4 14.9 us: halving(): jnp.concatenate(sends, 0)]
  transfers between devices with their start and end apart: 9 -> 9, of which waited for: 7 -> 6; matrix products, arithmetic and copies ran while one was open for 19% -> 21% of each run, Pallas kernels for 0% -> 0%
where the time goes in v3:
time: 763 us; the launch traced here: 758 us
  waiting for transfers between devices  459 us (60%)
  matrix products  91 us (12%)
  local copies, waits for them, and re-layouts  84.7 us (11%)
  other arithmetic  81 us (11%)
  loops' own time  19 us (2%)
  between operations  15.1 us (2%)
    psum x1, waiting for transfers between devices, body_inner(): lax.psum(jnp.concatenate([o.astype(jnp.bfloat16) for o in owned], 0), 'rep')  203 us
    ppermute x4, waiting for transfers between devices, halving(): lax.ppermute(jnp.concatenate(sends, 0), axis, [(a, a ^ step) for a in ran...  117 us
    all_gather x1, waiting for transfers between devices, body_inner(): full_up = lax.all_gather(w_up, 'shard', axis=1, tiled=True)  49.6 us
    all_gather x1, waiting for transfers between devices, body_inner(): full_down = lax.all_gather(w_down, 'shard', axis=0, tiled=True)  48.4 us
    all_gather x1, waiting for transfers between devices, body_inner(): full_qkv = lax.all_gather(w_qkv, 'shard', axis=1, tiled=True)  38.4 us
    unnamed x153, local copies, waits for them, and re-layouts  24 us
    add x4, other arithmetic, halving(): arrays.append(keep + got[offset:offset + keep.shape[0]].astype(jnp.float32))  20.6 us
    unnamed x10, other arithmetic  16.9 us
  transfers between devices with their start and end apart: 9, of which 6 were waited for; matrix products, arithmetic and copies ran while one was open for 21% of the time, Pallas kernels for 0%

profile of v3, /device:TPU:0, one launch (start us, length us, event | category | flops | bytes accessed | tf_op | source)
XLA Modules:
  0.0 758.5 jit_solution(5887336189648716953)
XLA Ops:
  12.2 6.3 all-gather
  20.3 38.4 %all-gather.6.cloned.1.call-done = bf16[1024,3072]{1,0:T(8,128)(2,1)} async-done(((bf16[1024,768]{1,0:T(8,128)(2,1)}), bf16[1024,3072]{1,0:T(8,128)(2,1)}) %all-gather.6.cloned.1.call-update) | async-done | bytes 6291472 | tf_op jit(solution)/shard_map/all_gather | solution.py:196
  58.7 5.1 fusion.85
  63.8 1.0 slice.234
  65.9 1.5 copy.85
  68.4 19.0 %while.32 = (s32[]{:T(128)}, bf16[4,384,256]{1,2,0:T(8,128)(2,1)}, f32[4,4,384]{2,1,0:T(4,128)S(1)}, s32[4]{0:T(128)S(1)}, bf16[384,1024]{0,1:T(8,128)(2,1)S(1)}...) while((s32[]{:T(128)}, bf16[4,384,256]{1,2,0:T(8,128)(2,1)}, ...), condition=%wide.region_6.7_spmd.clone, body=%wide.region_3.6_spmd.clone.sunk | while | flops 157776416 | bytes 10964623 | solution.py:74
  88.6 3.1 fusion.129
  92.1 1.1 fusion.127
  93.2 49.6 %all-gather.10.cloned.1.call-done = bf16[1024,4096]{1,0:T(8,128)(2,1)} async-done(((bf16[1024,1024]{1,0:T(8,128)(2,1)}), bf16[1024,4096]{1,0:T(8,128)(2,1)}) %all-gather.10.cloned.1.call-update) | async-done | bytes 8388624 | tf_op jit(solution)/shard_map/all_gather | solution.py:198
  142.8 11.3 %multiply_convert_fusion.1 = (bf16[384,4096]{1,0:T(8,128)(2,1)}, f32[384,4096]{1,0:T(8,128)}) fusion(f32[4096]{0:T(1024)S(1)} %bitcast.359, bf16[1024,4096]{1,0:T(8,128)(2,1)} %all-gather.10.cloned.1.call-done, f32[384,1024]{1,0:T(8,128)S(1)} %get-tuple-element.603, f32[1024]{0:T(1024)S(1)} %bitcast.366, f32[1024]{0:T(1024)S(1)} %bitcast.360, ...), kind=kOutput, calls=%fused_computation.58 | convolution fusion | flops 3238920192 | bytes 19426304 | tf_op jit(solution)/shard_map/dot_general | solution.py:218
  154.0 48.4 %all-gather.12.cloned.1.call-done = bf16[4096,1024]{1,0:T(8,128)(2,1)} async-done(((bf16[1024,1024]{1,0:T(8,128)(2,1)}), bf16[4096,1024]{1,0:T(8,128)(2,1)}) %all-gather.12.cloned.1.call-update) | async-done | bytes 8388624 | tf_op jit(solution)/shard_map/all_gather | solution.py:199
  202.5 10.8 %convert_reduce_fusion = (f32[4096]{0:T(1024)S(1)}, bf16[384,4096]{1,0:T(8,128)(2,1)S(1)}) fusion(f32[384,4096]{1,0:T(8,128)} %get-tuple-element.605, bf16[4096,1024]{1,0:T(8,128)(2,1)} %all-gather.12.cloned.1.call-done, bf16[1,384,1024]{2,1,0:T(8,128)(2,1)S(1)} %copy-done.18), kind=kOutput, calls=%fused_computation.56 | convolution fusion | flops 3255824384 | bytes 18628608 | tf_op jit(solution)/shard_map/to,fo->tf/dot_general | solution.py:235
  213.2 1.7 fusion.125
  215.0 3.8 multiply_reduce_fusion.1
  218.8 1.7 fusion.123
  221.7 1.8 maximum_bitcast_fusion
  223.5 3.4 copy.100
  227.0 9.4 %fusion.95 = f32[2,2048,1024]{2,1,0:T(8,128)} fusion(bf16[2,2048,384]{2,1,0:T(8,128)(2,1)S(1)} %bitcast.312, bf16[1,384,1024]{2,1,0:T(8,128)(2,1)} %param.22), kind=kOutput, calls=%fused_computation.169 | convolution fusion | flops 3221225472 | bytes 20709376 | tf_op jit(solution)/shard_map/tf,to->fo/dot_general | solution.py:239
  236.4 9.4 %fusion.32 = f32[4096,1024]{1,0:T(8,128)} fusion(bf16[384,1024]{1,0:T(8,128)(2,1)S(1)} %copy-done.31, bf16[384,1024]{1,0:T(8,128)(2,1)S(1)} %copy-done.32, bf16[384,1024]{1,0:T(8,128)(2,1)S(1)} %copy-done.33, bf16[384,1024]{1,0:T(8,128)(2,1)S(1)} %copy-done.30, f32[384,1024]{1,0:T(8,128)S(1)} %copy-done.7, f32[1024]{0:T(1024)S(1)} %bitcast.367, ...), kind=kOutput, calls=%fused_computation.79 | convolution fusion | flops 3235774464 | bytes 21507072 | tf_op jit(solution)/shard_map/tf,ti->fi/dot_general | solution.py:242
  245.8 10.5 %fusion.23 = (bf16[2048,1024]{1,0:T(8,128)(2,1)}, bf16[2048,1024]{1,0:T(8,128)(2,1)}) fusion(f32[2,2048,1024]{2,1,0:T(8,128)} %fusion.95, s32[]{:T(128)S(6)} %select_n.101, f32[2,2048,1024]{2,1,0:T(8,128)} %bitcast.327), kind=kLoop, calls=%fused_computation.63 | loop fusion | bytes 16777220 | tf_op jit(solution)/shard_map/convert_element_type | solution.py:153
  256.3 7.8 %pad_maximum_fusion = bf16[4096,1024]{1,0:T(8,128)(2,1)} fusion(bf16[2048,1024]{1,0:T(8,128)(2,1)} %get-tuple-element.613, bf16[2048,1024]{1,0:T(8,128)(2,1)} %get-tuple-element.612), kind=kLoop, calls=%fused_computation.39 | loop fusion | flops 16777216 | bytes 16777216 | tf_op jit(solution)/shard_map/concatenate | solution.py:155
  264.7 1.1 copy-done.27
  265.8 1.0 convolution_convert_fusion
  269.7 49.2 %while.33 = (s32[]{:T(128)}, bf16[4,384,256]{1,2,0:T(8,128)(2,1)}, bf16[4,384,256]{1,2,0:T(8,128)(2,1)}, bf16[4,384,256]{1,2,0:T(8,128)(2,1)}, s32[4]{0:T(128)S(...) while((s32[]{:T(128)}, bf16[4,384,256]{1,2,0:T(8,128)(2,1)}, ...), condition=%wide.region_13.14_spmd.clone, body=%wide.region_11.13_spmd.clone.sunk | while | flops 385251872 | bytes 30607116 | solution.py:113
  277.5 1.1 multiply_reduce_fusion.5
  284.4 1.0 constant_dynamic-slice_fusion.17
  289.8 1.1 multiply_reduce_fusion.5
  302.1 1.1 multiply_reduce_fusion.5
  314.3 1.1 multiply_reduce_fusion.5
  318.9 2.1 split.77
  321.0 2.0 split.76
  323.0 5.9 fusion.121
  329.0 1.1 copy-done.20
  330.9 3.3 convert_reduce_fusion.2
  334.3 1.6 convert_reduce_fusion.4
  336.3 1.2 fusion.87
  337.8 1.5 copy-done.13
  340.8 3.6 fusion.83
  345.0 2.7 pad_maximum_fusion.1
  347.7 2.6 copy-done
  350.5 14.4 %bitcast_add_fusion = (f32[2048,1024]{1,0:T(8,128)}, f32[2048,1024]{1,0:T(8,128)}) fusion(f32[2,2048,1024]{2,1,0:T(8,128)} %bitcast.328, s32[]{:T(128)S(6)} %select_n.100, bf16[4096,1024]{1,0:T(8,128)(2,1)} %collective-permute-done, f32[2,2048,1024]{2,1,0:T(8,128)} %fusion.95), kind=kLoop, calls=%fused_computation.40 | loop fusion | flops 8388608 | bytes 41943044 | tf_op jit(solution)/shard_map/add | solution.py:158
  364.9 2.7 fusion.53
  367.6 2.7 fusion.52
  370.3 2.6 pad_maximum_fusion.2
  373.2 1.0 bitcast_add_fusion.8
  374.3 1.7 bitcast_add_fusion.6
  376.1 3.5 bitcast_add_fusion.2
  379.9 1.8 pad_maximum_fusion.3
  381.7 1.3 copy-done.5
  382.9 1.5 collective-permute-start.3
  384.4 82.2 %collective-permute-done.1 = bf16[2048,1024]{1,0:T(8,128)(2,1)} collective-permute-done((bf16[2048,1024]{1,0:T(8,128)(2,1)}, bf16[2048,1024]{1,0:T(8,128)(2,1)}, u32[]{:S(2)}, u32[]{:S(2)}) %collective-permute-start.1) | collective-permute-done | bytes 4194336 | tf_op jit(solution)/shard_map/ppermute | solution.py:155
  466.7 5.1 fusion.54
  471.8 5.2 fusion.55
  476.9 35.0 %collective-permute-done.3 = bf16[1040,1024]{1,0:T(8,128)(2,1)} collective-permute-done((bf16[1040,1024]{1,0:T(8,128)(2,1)}, bf16[1040,1024]{1,0:T(8,128)(2,1)}, u32[]{:S(2)}, u32[]{:S(2)}) %collective-permute-start.3) | collective-permute-done | bytes 2129952 | tf_op jit(solution)/shard_map/ppermute | solution.py:155
  512.0 2.0 fusion.110
  514.0 3.2 fusion.74
  517.2 1.4 fusion.114
  520.0 8.8 %fusion.77 = bf16[1,384,1024]{2,1,0:T(8,128)(2,1)} fusion(f32[384,1024]{1,0:T(8,128)S(1)} %copy-done.8, bf16[384,4096]{1,0:T(8,128)(2,1)} %get-tuple-element.604, bf16[4096,1024]{1,0:T(8,128)(2,1)} %all-gather.12.cloned.1.call-done, f32[1024]{0:T(1024)S(1)} %bitcast.368), kind=kOutput, calls=%fused_computation.151 | convolution fusion | flops 3222405120 | bytes 13897728 | tf_op jit(solution)/shard_map/dot_general | solution.py:223
  528.8 202.6 %all-reduce.4.cloned.1.call-done = bf16[3088,1024]{1,0:T(8,128)(2,1)} async-done(((bf16[3088,1024]{1,0:T(8,128)(2,1)}), bf16[3088,1024]{1,0:T(8,128)(2,1)}) %all-reduce.4.cloned.1.call-update) | async-done | bytes 6324240 | tf_op jit(solution)/shard_map/psum | solution.py:280
  733.4 1.8 convert_bitcast_fusion.1
  735.2 2.4 copy.94
  737.6 6.7 slice_convert_fusion
  744.3 5.3 copy.95
  749.6 2.1 slice_convert_fusion.2
  (350 shorter events, 66.2 us)
Async XLA Ops:
  7.2 51.5 %all-gather.6.cloned.1.call-start = ((), (), s32[]{:S(2)}) async-start(), calls=%async_computation | async-start | bytes 7864320 | tf_op jit(solution)/shard_map/all_gather | solution.py:196
  7.9 2.3 copy-start.47
  7.9 2.5 copy-start.48
  7.9 2.7 copy-start.49
  7.9 2.9 copy-start.50
  8.0 3.1 copy-start.51
  8.0 3.4 copy-start.52
  8.0 3.6 copy-start.53
  8.0 3.8 copy-start.46
  8.0 4.0 copy-start.54
  8.0 79.5 %all-gather.8.cloned.1.call-start = ((), (), s32[]{:S(2)}) async-start(), calls=%async_computation.1 | async-start | bytes 2621440 | tf_op jit(solution)/shard_map/all_gather | solution.py:197
  8.8 10.3 %copy-start.1 = (bf16[1,384,1024]{2,1,0:T(8,128)(2,1)S(1)}, bf16[1,384,1024]{2,1,0:T(8,128)(2,1)}, u32[]{:S(2)}) copy-start(bf16[1,384,1024]{2,1,0:T(8,128)(2,1)} %param.20) | copy-start | bytes 2359300
  8.8 10.7 %copy-start.45 = (s32[1,2,64]{2,1,0:T(2,128)S(1)}, s32[1,2,64]{2,1,0:T(2,128)}, u32[]{:S(2)}) copy-start(s32[1,2,64]{2,1,0:T(2,128)} %param.21) | copy-start | bytes 1540
  8.8 134.0 %all-gather.10.cloned.1.call-start = ((), (), s32[]{:S(2)}) async-start(), calls=%async_computation.2 | async-start | bytes 10485760 | tf_op jit(solution)/shard_map/all_gather | solution.py:198
  9.5 192.9 %all-gather.12.cloned.1.call-start = ((), (), s32[]{:S(2)}) async-start(), calls=%async_computation.3 | async-start | bytes 10485760 | tf_op jit(solution)/shard_map/all_gather | solution.py:199
  10.1 721.3 %all-reduce.4.cloned.1.call-start = ((), (), s32[]{:S(2)}) async-start(), calls=%async_computation.4 | async-start | bytes 12648448 | tf_op jit(solution)/shard_map/psum | solution.py:280
  19.1 44.7 %copy-start.43 = (f32[1,2,4,128]{3,1,2,0:T(2,128)}, f32[1,2,4,128]{3,1,2,0:T(2,128)S(1)}, u32[]{:S(2)}) copy-start(f32[1,2,4,128]{3,1,2,0:T(2,128)S(1)} %copy.107) | copy-start | bytes 12292
  20.3 43.5 %copy-start.40 = (f32[384]{0:T(512)}, f32[384]{0:T(512)S(1)}, u32[]{:S(2)}) copy-start(f32[384]{0:T(512)S(1)} %fusion.67) | copy-start | bytes 4612
  20.3 43.5 %copy-start.38 = (f32[384]{0:T(512)}, f32[384]{0:T(512)S(1)}, u32[]{:S(2)}) copy-start(f32[384]{0:T(512)S(1)} %fusion.115) | copy-start | bytes 4612
  87.5 4.3 copy-start.16
  88.6 3.4 copy-start.17
  91.8 127.1 %copy-start.6 = (f32[384,1024]{1,0:T(8,128)}, f32[384,1024]{1,0:T(8,128)S(1)}, u32[]{:S(2)}) copy-start(f32[384,1024]{1,0:T(8,128)S(1)} %get-tuple-element.603) | copy-start | bytes 4718596
  142.8 59.7 %copy-start.18 = (bf16[1,384,1024]{2,1,0:T(8,128)(2,1)S(1)}, bf16[1,384,1024]{2,1,0:T(8,128)(2,1)}, u32[]{:S(2)}) copy-start(bf16[1,384,1024]{2,1,0:T(8,128)(2,1)} %param.22) | copy-start | bytes 2359300
  202.5 12.5 %copy-start.55 = (bf16[1024,4096]{1,0:T(8,128)(2,1)S(1)}, bf16[1024,4096]{1,0:T(8,128)(2,1)}, u32[]{:S(2)}) copy-start(bf16[1024,4096]{1,0:T(8,128)(2,1)} %all-gather.10.cloned.1.call-done) | copy-start | bytes 25165828
  218.8 2.5 copy-start.21
  226.9 9.4 %copy-start.7 = (f32[384,1024]{1,0:T(8,128)S(1)}, f32[384,1024]{1,0:T(8,128)}, u32[]{:S(2)}) copy-start(f32[384,1024]{1,0:T(8,128)} %copy-done.6) | copy-start | bytes 4718596
  226.9 9.4 %copy-start.30 = (bf16[384,1024]{1,0:T(8,128)(2,1)S(1)}, bf16[384,1024]{1,0:T(8,128)(2,1)}, u32[]{:S(2)}) copy-start(bf16[384,1024]{1,0:T(8,128)(2,1)} %get-tuple-element.568) | copy-start | bytes 2359300
  226.9 9.4 %copy-start.31 = (bf16[384,1024]{1,0:T(8,128)(2,1)S(1)}, bf16[384,1024]{1,0:T(8,128)(2,1)}, u32[]{:S(2)}) copy-start(bf16[384,1024]{1,0:T(8,128)(2,1)} %get-tuple-element.569) | copy-start | bytes 2359300
  227.0 9.4 %copy-start.32 = (bf16[384,1024]{1,0:T(8,128)(2,1)S(1)}, bf16[384,1024]{1,0:T(8,128)(2,1)}, u32[]{:S(2)}) copy-start(bf16[384,1024]{1,0:T(8,128)(2,1)} %get-tuple-element.570) | copy-start | bytes 2359300
  227.0 9.4 %copy-start.33 = (bf16[384,1024]{1,0:T(8,128)(2,1)S(1)}, bf16[384,1024]{1,0:T(8,128)(2,1)}, u32[]{:S(2)}) copy-start(bf16[384,1024]{1,0:T(8,128)(2,1)} %get-tuple-element.571) | copy-start | bytes 2359300
  256.3 8.1 %copy-start.9 = (f32[384,1024]{1,0:T(8,128)S(1)}, f32[384,1024]{1,0:T(8,128)}, u32[]{:S(2)}) copy-start(f32[384,1024]{1,0:T(8,128)} %get-tuple-element.553) | copy-start | bytes 4718596
  256.3 8.1 %copy-start.19 = (bf16[1,384,1024]{2,1,0:T(8,128)(2,1)S(1)}, bf16[1,384,1024]{2,1,0:T(8,128)(2,1)}, u32[]{:S(2)}) copy-start(bf16[1,384,1024]{2,1,0:T(8,128)(2,1)} %param.22) | copy-start | bytes 2359300
  264.1 86.4 %collective-permute-start = (bf16[4096,1024]{1,0:T(8,128)(2,1)}, bf16[4096,1024]{1,0:T(8,128)(2,1)}, u32[]{:S(2)}, u32[]{:S(2)}) collective-permute-start(bf16[4096,1024]{1,0:T(8,128)(2,1)} %pad_maximum_fusion), channel_id=1, source_target_pairs={{0,1},{1,0},{2,3},{3,2},{4,5},{5,4},{6,7},{7,6},{8,9},{9,8},{10,11... | collective-permute-start | bytes 25165832 | tf_op jit(solution)/shard_map/ppermute | solution.py:155
  264.6 2.2 copy-start.22
  269.7 3.5 copy-start.28
  280.1 1.9 copy-start.29
  281.9 3.5 copy-start.28
  294.2 3.5 copy-start.28
  304.6 1.9 copy-start.29
  306.5 3.5 copy-start.28
  318.9 4.1 copy-start.2
  318.9 4.1 copy-start.11
  318.9 4.1 copy-start.12
  323.0 6.0 copy-start.41
  323.0 7.1 copy-start.39
  329.0 2.0 copy-start.10
  334.2 2.0 copy-start.23
  334.2 2.0 copy-start.34
  334.2 2.0 copy-start.35
  334.2 2.1 copy-start.36
  334.2 2.1 copy-start.37
  337.6 3.0 copy-start.3
  337.6 2.5 copy-start.24
  344.4 5.8 copy-start
  350.2 23.0 %collective-permute-start.2 = (bf16[2080,1024]{1,0:T(8,128)(2,1)}, bf16[2080,1024]{1,0:T(8,128)(2,1)}, u32[]{:S(2)}, u32[]{:S(2)}) collective-permute-start(bf16[2080,1024]{1,0:T(8,128)(2,1)} %pad_maximum_fusion.1), channel_id=1, source_target_pairs={{0,1},{1,0},{2,3},{3,2},{4,5},{5,4},{6,7},{7,6},{8,9},{9,8},{10,11... | collective-permute-start | bytes 12779528 | tf_op jit(solution)/shard_map/ppermute | solution.py:155
  364.9 11.1 %slice-start = ((s8[12582912]{0:T(1024)(128)(4,1)}), s8[4194304]{0:T(1024)(128)(4,1)S(1)}, s32[]{:S(2)}) async-start(s8[12582912]{0:T(1024)(128)(4,1)} %bitcast.308), calls=%async_computation.5 | async-start | bytes 8388608
  367.6 8.5 %slice-start.1 = ((s8[12582912]{0:T(1024)(128)(4,1)}), s8[4194304]{0:T(1024)(128)(4,1)S(1)}, s32[]{:S(2)}) async-start(s8[12582912]{0:T(1024)(128)(4,1)} %bitcast.308), calls=%async_computation.6 | async-start | bytes 8388608
  370.3 4.0 copy-start.4
  370.3 5.8 slice-start.2
  372.9 93.8 %collective-permute-start.1 = (bf16[2048,1024]{1,0:T(8,128)(2,1)}, bf16[2048,1024]{1,0:T(8,128)(2,1)}, u32[]{:S(2)}, u32[]{:S(2)}) collective-permute-start(bf16[2048,1024]{1,0:T(8,128)(2,1)} %pad_maximum_fusion.2), channel_id=1, source_target_pairs={{0,2},{1,3},{2,0},{3,1},{4,6},{5,7},{6,4},{7,5},{8,10},{9,11},{10,... | collective-permute-start | bytes 12582920 | tf_op jit(solution)/shard_map/ppermute | solution.py:155
  379.6 3.3 copy-start.5
  382.9 129.1 %collective-permute-start.3 = (bf16[1040,1024]{1,0:T(8,128)(2,1)}, bf16[1040,1024]{1,0:T(8,128)(2,1)}, u32[]{:S(2)}, u32[]{:S(2)}) collective-permute-start(bf16[1040,1024]{1,0:T(8,128)(2,1)} %pad_maximum_fusion.3), channel_id=1, source_target_pairs={{0,2},{1,3},{2,0},{3,1},{4,6},{5,7},{6,4},{7,5},{8,10},{9,11},{10,... | collective-permute-start | bytes 6389768 | tf_op jit(solution)/shard_map/ppermute | solution.py:155
  466.7 47.3 %slice-start.3 = ((s8[6291456]{0:T(1024)(128)(4,1)}), s8[4194304]{0:T(1024)(128)(4,1)S(1)}, s32[]{:S(2)}) async-start(s8[6291456]{0:T(1024)(128)(4,1)} %bitcast.318), calls=%async_computation.8 | async-start | bytes 8388608
  471.8 42.2 %slice-start.4 = ((s8[6291456]{0:T(1024)(128)(4,1)}), s8[2097152]{0:T(1024)(128)(4,1)S(1)}, s32[]{:S(2)}) async-start(s8[6291456]{0:T(1024)(128)(4,1)} %bitcast.318), calls=%async_computation.9 | async-start | bytes 4194304
  (12 other events, 16.2 us)
Sparse Core Ops, SparseCore 0:
  9.6 49.0 all-gather.5
  60.2 22.6 all-gather.7
  84.5 58.2 all-gather.9
  144.2 58.2 all-gather.11
  518.7 212.6 all-reduce.3

commit v4 on v3

--- a/solution.py
+++ b/solution.py
@@ -160,6 +160,15 @@
     return arrays
 
 
+def doubling(buf, axis, size, steps):
+    index = lax.axis_index(axis)
+    for step in steps:
+        low = (index // step) % 2 == 0
+        got = lax.ppermute(buf, axis, [(a, a ^ step) for a in range(size)])
+        buf = jnp.concatenate([jnp.where(low, buf, got), jnp.where(low, got, buf)], 0)
+    return buf
+
+
 def gather_small(pieces):
     packed = jnp.concatenate(pieces)
     shards = lax.all_gather(packed, "shard", axis=0, tiled=False)
@@ -242,7 +251,6 @@
     grad_up_t = jnp.einsum(
         "tf,ti->fi", reorder_cols(grad_pre, order), normed_two, preferred_element_type=jnp.float32
     )
-    down_own, up_own = halving([grad_down, grad_up_t], "shard", shard_count, shard_steps)
     grad_normed_two = jnp.einsum("tf,if->ti", grad_pre, back_up, preferred_element_type=jnp.float32)
     _, norm_pull_two = jax.vjp(normalize, middle, back_g2.astype(jnp.float32), zero_shift)
     grad_mid_part, grad_g2, grad_s2 = norm_pull_two(grad_normed_two)
@@ -255,6 +263,11 @@
     grad_out = jnp.einsum(
         "ti,to->io", reorder_cols(mixed, order), grad_branch, preferred_element_type=jnp.float32
     )
+    down_own, up_own, out_own = halving(
+        [grad_down, grad_up_t, grad_out], "shard", shard_count, shard_steps
+    )
+    owned_a = [down_own, up_own, out_own]
+    total_a = lax.psum(jnp.concatenate([o.astype(jnp.bfloat16) for o in owned_a], 0), "rep")
     grad_q, grad_k, grad_v = attend_backward(
         queries, key_rows, values, grad_mixed, log_norms, distance, allowed
     )
@@ -269,25 +282,25 @@
         "tc,ti->ci", reorder_cols(grad_proj, order), normed, preferred_element_type=jnp.float32
     )
     smalls = [grad_g1, grad_s1, grad_qb, grad_vb, grad_bo, grad_g2, grad_s2, grad_bu, grad_bd]
+    reps = lax.psum(1, "rep")
+    rep_steps = bit_steps(reps)
+    qkv_rows = grad_qkv_t.shape[0] // shard_count
     small_rows = jnp.concatenate([g.reshape(shard_count, -1) for g in smalls], 1)
     small_rows = small_rows.reshape(shard_count, -1, model_width)
-    small_rows = jnp.pad(small_rows, ((0, 0), (0, 16 - small_rows.shape[1]), (0, 0)))
+    pad_to = small_rows.shape[1] + (-(qkv_rows + small_rows.shape[1]) % (8 * reps))
+    small_rows = jnp.pad(small_rows, ((0, 0), (0, pad_to - small_rows.shape[1]), (0, 0)))
     small_rows = jnp.concatenate([small_rows[k] for k in order], 0)
-    out_own, qkv_own, small_own = halving(
-        [grad_out, grad_qkv_t, small_rows], "shard", shard_count, shard_steps
-    )
-    owned = [down_own, up_own, out_own, qkv_own, small_own]
-    total = lax.psum(jnp.concatenate([o.astype(jnp.bfloat16) for o in owned], 0), "rep")
-    pieces, offset = [], 0
-    for o in owned:
-        pieces.append(total[offset : offset + o.shape[0]])
-        offset += o.shape[0]
-    down_fin, up_fin, out_fin, qkv_fin, small_fin_rows = pieces
-    down_fin = down_fin.astype(jnp.float32)
-    up_fin = up_fin.astype(jnp.float32).T
-    out_fin = out_fin.astype(jnp.float32)
-    qkv_fin = qkv_fin.astype(jnp.float32).T
-    small_flat = small_fin_rows.reshape(-1).astype(jnp.float32)
+    qkv_own, small_own = halving([grad_qkv_t, small_rows], "shard", shard_count, shard_steps)
+    joined_b = jnp.concatenate([qkv_own, small_own], 0)
+    (joined_b,) = halving([joined_b], "rep", reps, rep_steps)
+    total_b = doubling(joined_b.astype(jnp.bfloat16), "rep", reps, rep_steps[::-1])
+    down_rows = down_own.shape[0]
+    up_rows = up_own.shape[0]
+    down_fin = total_a[:down_rows].astype(jnp.float32)
+    up_fin = total_a[down_rows : down_rows + up_rows].astype(jnp.float32).T
+    out_fin = total_a[down_rows + up_rows :].astype(jnp.float32)
+    qkv_fin = total_b[:qkv_rows].astype(jnp.float32).T
+    small_flat = total_b[qkv_rows:].reshape(-1).astype(jnp.float32)
     small_fin, offset = [], 0
     for g in smalls:
         width = g.shape[0] // shard_count

time: 763 us -> 794 us (1.041)
  local copies, waits for them, and re-layouts: 84.7 us -> 96.4 us
  waiting for transfers between devices: 459 us -> 469 us
  starting transfers between devices: 2.52 us -> 11.2 us
    psum x1, waiting for transfers between devices: 203 us -> 82.6 us  [body_inner(): lax.psum(jnp.concatenate([o.astype(jnp.bfloat16) for o in owned_a], 0), '...]
    ppermute x4 -> x7, waiting for transfers between devices: 117 us -> 210 us  [halving(): lax.ppermute(jnp.concatenate(sends, 0), axis, [(a, a ^ step) for a in ran...]
    ppermute x0 -> x3, waiting for transfers between devices: none -> 40.9 us  [doubling(): got = lax.ppermute(buf, axis, [(a, a ^ step) for a in range(size)])]
    unnamed x10 -> x5, other arithmetic: 16.9 us -> 0.63 us
    convert_element_type x2 -> x5, other arithmetic: 8.83 us -> 16.3 us  [the longest x2 7.42 us: body_inner(): o.astype(jnp.bfloat16)]
    unnamed x153 -> x189, local copies, waits for them, and re-layouts: 24 us -> 31.2 us
    add x4 -> x8, other arithmetic: 20.6 us -> 26.9 us  [halving(): arrays.append(keep + got[offset:offset + keep.shape[0]].astype(jnp.float32))]
    convert_element_type x9 -> x12, local copies, waits for them, and re-layouts: 16.9 us -> 18.4 us  [halving(): lax.dynamic_index_in_dim(pair, 1 - bit, 0, keepdims=False)]
  transfers between devices with their start and end apart: 9 -> 15, of which waited for: 6 -> 12; matrix products, arithmetic and copies ran while one was open for 21% -> 17% of each run, Pallas kernels for 0% -> 0%
where the time goes in v4:
time: 794 us; the launch traced here: 789 us
  waiting for transfers between devices  469 us (59%)
  local copies, waits for them, and re-layouts  96.4 us (12%)
  matrix products  91.6 us (12%)
  other arithmetic  80.5 us (10%)
  loops' own time  18.7 us (2%)
  between operations  15.4 us (2%)
  starting transfers between devices  11.2 us (1%)
    ppermute x7, waiting for transfers between devices, halving(): lax.ppermute(jnp.concatenate(sends, 0), axis, [(a, a ^ step) for a in ran...  210 us
    psum x1, waiting for transfers between devices, body_inner(): lax.psum(jnp.concatenate([o.astype(jnp.bfloat16) for o in owned_a], 0), '...  82.6 us
    all_gather x1, waiting for transfers between devices, body_inner(): full_down = lax.all_gather(w_down, 'shard', axis=0, tiled=True)  48.4 us
    all_gather x1, waiting for transfers between devices, body_inner(): full_up = lax.all_gather(w_up, 'shard', axis=1, tiled=True)  47.1 us
    ppermute x3, waiting for transfers between devices, doubling(): got = lax.ppermute(buf, axis, [(a, a ^ step) for a in range(size)])  40.9 us
    all_gather x1, waiting for transfers between devices, body_inner(): full_qkv = lax.all_gather(w_qkv, 'shard', axis=1, tiled=True)  37.2 us
    unnamed x189, local copies, waits for them, and re-layouts  31.2 us
    add x8, other arithmetic, halving(): arrays.append(keep + got[offset:offset + keep.shape[0]].astype(jnp.float32))  26.9 us
  transfers between devices with their start and end apart: 15, of which 12 were waited for; matrix products, arithmetic and copies ran while one was open for 17% of the time, Pallas kernels for 0%

profile of v4, /device:TPU:0, one launch (start us, length us, event | category | flops | bytes accessed | tf_op | source)
XLA Modules:
  0.0 788.6 jit_solution(6758530482955465673)
XLA Ops:
  12.2 6.3 all-gather
  21.5 37.2 %all-gather.6.cloned.1.call-done = bf16[1024,3072]{1,0:T(8,128)(2,1)} async-done(((bf16[1024,768]{1,0:T(8,128)(2,1)}), bf16[1024,3072]{1,0:T(8,128)(2,1)}) %all-gather.6.cloned.1.call-update) | async-done | bytes 6291472 | tf_op jit(solution)/shard_map/all_gather | solution.py:205
  58.7 5.1 fusion.82
  66.0 1.5 copy.84
  68.5 21.3 %while.32 = (s32[]{:T(128)}, bf16[4,384,256]{1,2,0:T(8,128)(2,1)}, f32[4,4,384]{2,1,0:T(4,128)}, s32[4]{0:T(128)S(1)}, bf16[384,1024]{0,1:T(8,128)(2,1)S(1)}, /*...) while((s32[]{:T(128)}, bf16[4,384,256]{1,2,0:T(8,128)(2,1)}, ...), condition=%wide.region_6.7_spmd.clone, body=%wide.region_3.6_spmd.clone.sunk | while | flops 157776416 | bytes 10964623 | solution.py:74
  90.9 3.4 fusion.126
  95.6 47.1 %all-gather.10.cloned.1.call-done = bf16[1024,4096]{1,0:T(8,128)(2,1)} async-done(((bf16[1024,1024]{1,0:T(8,128)(2,1)}), bf16[1024,4096]{1,0:T(8,128)(2,1)}) %all-gather.10.cloned.1.call-update) | async-done | bytes 8388624 | tf_op jit(solution)/shard_map/all_gather | solution.py:207
  142.7 11.3 %multiply_convert_fusion.1 = (bf16[384,4096]{1,0:T(8,128)(2,1)}, f32[384,4096]{1,0:T(8,128)}) fusion(f32[4096]{0:T(1024)S(1)} %bitcast.370, bf16[1024,4096]{1,0:T(8,128)(2,1)} %all-gather.10.cloned.1.call-done, f32[384,1024]{1,0:T(8,128)S(1)} %get-tuple-element.611, f32[1024]{0:T(1024)S(1)} %bitcast.377, f32[1024]{0:T(1024)S(1)} %bitcast.371, ...), kind=kOutput, calls=%fused_computation.58 | convolution fusion | flops 3238920192 | bytes 19426304 | tf_op jit(solution)/shard_map/dot_general | solution.py:227
  154.0 48.4 %all-gather.12.cloned.1.call-done = bf16[4096,1024]{1,0:T(8,128)(2,1)} async-done(((bf16[1024,1024]{1,0:T(8,128)(2,1)}), bf16[4096,1024]{1,0:T(8,128)(2,1)}) %all-gather.12.cloned.1.call-update) | async-done | bytes 8388624 | tf_op jit(solution)/shard_map/all_gather | solution.py:208
  202.4 11.2 %convert_reduce_fusion = (f32[4096]{0:T(1024)}, bf16[384,4096]{1,0:T(8,128)(2,1)S(1)}) fusion(f32[384,4096]{1,0:T(8,128)} %get-tuple-element.613, bf16[4096,1024]{1,0:T(8,128)(2,1)} %all-gather.12.cloned.1.call-done, bf16[1,384,1024]{2,1,0:T(8,128)(2,1)S(1)} %copy-done.17), kind=kOutput, calls=%fused_computation.56 | convolution fusion | flops 3255824384 | bytes 18628608 | tf_op jit(solution)/shard_map/to,fo->tf/dot_general | solution.py:244
  213.6 1.7 fusion.123
  215.3 4.3 multiply_reduce_fusion.1
  219.7 1.7 fusion.120
  222.6 1.8 maximum_bitcast_fusion
  224.4 3.4 copy.99
  227.8 9.4 %fusion.92 = f32[2,2048,1024]{2,1,0:T(8,128)} fusion(bf16[2,2048,384]{2,1,0:T(8,128)(2,1)S(1)} %bitcast.315, bf16[1,384,1024]{2,1,0:T(8,128)(2,1)} %param.22), kind=kOutput, calls=%fused_computation.181 | convolution fusion | flops 3221225472 | bytes 20709376 | tf_op jit(solution)/shard_map/tf,to->fo/dot_general | solution.py:248
  238.3 1.2 fusion.84
  239.5 2.0 copy-done.3
  241.8 9.8 %fusion.32 = f32[4096,1024]{1,0:T(8,128)} fusion(bf16[384,1024]{1,0:T(8,128)(2,1)S(1)} %copy-done.36, bf16[384,1024]{1,0:T(8,128)(2,1)S(1)} %copy-done.37, bf16[384,1024]{1,0:T(8,128)(2,1)S(1)} %copy-done.38, bf16[384,1024]{1,0:T(8,128)(2,1)S(1)} %copy-done.35, f32[384,1024]{1,0:T(8,128)S(1)} %copy-done.6, f32[1024]{0:T(1024)S(1)} %bitcast.378, ...), kind=kOutput, calls=%fused_computation.81 | convolution fusion | flops 3235774464 | bytes 21507072 | tf_op jit(solution)/shard_map/tf,ti->fi/dot_general | solution.py:251
  251.6 10.5 %fusion.23 = (bf16[2048,1024]{1,0:T(8,128)(2,1)}, bf16[2048,1024]{1,0:T(8,128)(2,1)}) fusion(f32[2,2048,1024]{2,1,0:T(8,128)} %fusion.92, s32[]{:T(128)S(6)} %select_n.194, f32[2,2048,1024]{2,1,0:T(8,128)} %bitcast.334), kind=kLoop, calls=%fused_computation.64 | loop fusion | bytes 16777220 | tf_op jit(solution)/shard_map/convert_element_type | solution.py:153
  262.1 7.8 pad_maximum_fusion
  274.2 51.8 %while.33 = (s32[]{:T(128)}, bf16[4,384,256]{1,2,0:T(8,128)(2,1)}, bf16[4,384,256]{1,2,0:T(8,128)(2,1)}, bf16[4,384,256]{1,2,0:T(8,128)(2,1)}, s32[4]{0:T(128)S(...) while((s32[]{:T(128)}, bf16[4,384,256]{1,2,0:T(8,128)(2,1)}, ...), condition=%wide.region_13.14_spmd.clone, body=%wide.region_11.13_spmd.clone.sunk | while | flops 385251872 | bytes 30607116 | solution.py:113
  308.6 1.1 multiply_reduce_fusion.5
  326.0 2.1 split.65
  328.1 1.9 split.64
  330.1 5.9 fusion.118
  338.1 3.3 convert_reduce_fusion.2
  341.4 1.5 convert_reduce_fusion.4
  346.3 3.6 fusion.80
  349.9 4.5 copy-done
  355.0 2.1 pad_maximum_fusion.3
  357.1 6.2 collective-permute-done
  363.3 1.4 bitcast_add_fusion.10
  365.6 2.2 bitcast_add_fusion.6
  367.8 1.3 copy-done.19
  369.2 15.6 %bitcast_add_fusion.1 = (f32[2048,1024]{1,0:T(8,128)}, f32[2048,1024]{1,0:T(8,128)}) fusion(f32[2,2048,1024]{2,1,0:T(8,128)} %fusion.92, s32[]{:T(128)S(6)} %select_n.193, bf16[4608,1024]{1,0:T(8,128)(2,1)} %collective-permute-done.8, f32[2,2048,1024]{2,1,0:T(8,128)} %bitcast.335), kind=kLoop, calls=%fused_computation.41 | loop fusion | flops 8388608 | bytes 41943044 | tf_op jit(solution)/shard_map/add | solution.py:158
  384.8 3.3 fusion.52
  388.0 2.5 fusion.51
  390.6 2.7 pad_maximum_fusion.1
  394.2 1.6 bitcast_add_fusion.2
  396.3 2.2 copy-done.4
  399.6 134.2 %collective-permute-done.1 = bf16[832,1024]{1,0:T(8,128)(2,1)S(1)} collective-permute-done((bf16[832,1024]{1,0:T(8,128)(2,1)S(1)}, bf16[832,1024]{1,0:T(8,128)(2,1)S(1)}, u32[]{:S(2)}, u32[]{:S(2)}) %collective-permute-start.1) | collective-permute-done | bytes 1703968 | tf_op jit(solution)/shard_map/ppermute | solution.py:155
  534.8 2.4 bitcast_add_fusion.5
  538.7 1.5 collective-permute-start.2
  540.2 19.0 %collective-permute-done.2 = bf16[416,1024]{1,0:T(8,128)(2,1)} collective-permute-done((bf16[416,1024]{1,0:T(8,128)(2,1)}, bf16[416,1024]{1,0:T(8,128)(2,1)}, u32[]{:S(2)}, u32[]{:S(2)}) %collective-permute-start.2) | collective-permute-done | bytes 852000 | tf_op jit(solution)/shard_map/ppermute | solution.py:155
  559.1 2.6 bitcast_add_fusion.7
  561.7 1.2 fusion.75
  562.9 6.2 fusion.26
  569.2 2.7 pad_maximum_fusion.2
  571.9 1.4 copy-done.22
  573.4 1.5 collective-permute-start.3
  575.0 26.9 %collective-permute-done.3 = bf16[208,1024]{1,0:T(8,128)(2,1)S(1)} collective-permute-done((bf16[208,1024]{1,0:T(8,128)(2,1)S(1)}, bf16[208,1024]{1,0:T(8,128)(2,1)S(1)}, u32[]{:S(2)}, u32[]{:S(2)}) %collective-permute-start.3) | collective-permute-done | bytes 426016 | tf_op jit(solution)/shard_map/ppermute | solution.py:155
  602.0 4.4 collective-permute-start.4
  606.5 23.5 %collective-permute-done.4 = bf16[104,1024]{1,0:T(8,128)(2,1)S(1)} collective-permute-done((bf16[104,1024]{1,0:T(8,128)(2,1)S(1)}, bf16[104,1024]{1,0:T(8,128)(2,1)S(1)}, u32[]{:S(2)}, u32[]{:S(2)}) %collective-permute-start.4) | collective-permute-done | bytes 213024 | tf_op jit(solution)/shard_map/ppermute | solution.py:155
  630.1 17.9 %collective-permute-done.5 = bf16[104,1024]{1,0:T(8,128)(2,1)S(1)} collective-permute-done((bf16[104,1024]{1,0:T(8,128)(2,1)S(1)}, bf16[104,1024]{1,0:T(8,128)(2,1)S(1)}, u32[]{:S(2)}, u32[]{:S(2)}) %collective-permute-start.5) | collective-permute-done | bytes 213024 | tf_op jit(solution)/shard_map/ppermute | solution.py:167
  648.2 8.1 %collective-permute-done.6 = bf16[208,1024]{1,0:T(8,128)(2,1)S(1)} collective-permute-done((bf16[208,1024]{1,0:T(8,128)(2,1)S(1)}, bf16[208,1024]{1,0:T(8,128)(2,1)S(1)}, u32[]{:S(2)}, u32[]{:S(2)}) %collective-permute-start.6) | collective-permute-done | bytes 426016 | tf_op jit(solution)/shard_map/ppermute | solution.py:167
  656.5 1.4 collective-permute-start.7
  658.0 7.7 fusion.73
  665.6 15.0 %collective-permute-done.7 = bf16[416,1024]{1,0:T(8,128)(2,1)S(1)} collective-permute-done((bf16[416,1024]{1,0:T(8,128)(2,1)S(1)}, bf16[416,1024]{1,0:T(8,128)(2,1)S(1)}, u32[]{:S(2)}, u32[]{:S(2)}) %collective-permute-start.7) | collective-permute-done | bytes 852000 | tf_op jit(solution)/shard_map/ppermute | solution.py:167
  681.6 2.4 copy.93
  685.1 82.6 %all-reduce.4.cloned.1.call-done = bf16[2304,1024]{1,0:T(8,128)(2,1)} async-done(((bf16[2304,1024]{1,0:T(8,128)(2,1)}), bf16[2304,1024]{1,0:T(8,128)(2,1)}) %all-reduce.4.cloned.1.call-update) | async-done | bytes 4718608 | tf_op jit(solution)/shard_map/psum | solution.py:270
  767.7 6.7 slice_convert_fusion
  774.4 5.3 copy.94
  779.7 2.1 slice_convert_fusion.2
  (409 shorter events, 87.6 us)
Async XLA Ops:
  7.2 51.5 %all-gather.6.cloned.1.call-start = ((), (), s32[]{:S(2)}) async-start(), calls=%async_computation | async-start | bytes 7864320 | tf_op jit(solution)/shard_map/all_gather | solution.py:205
  8.0 3.6 copy-start.73
  8.0 3.8 copy-start.66
  8.0 4.0 copy-start.74
  8.0 81.8 %all-gather.8.cloned.1.call-start = ((), (), s32[]{:S(2)}) async-start(), calls=%async_computation.1 | async-start | bytes 2621440 | tf_op jit(solution)/shard_map/all_gather | solution.py:206
  8.8 10.3 %copy-start.1 = (bf16[1,384,1024]{2,1,0:T(8,128)(2,1)S(1)}, bf16[1,384,1024]{2,1,0:T(8,128)(2,1)}, u32[]{:S(2)}) copy-start(bf16[1,384,1024]{2,1,0:T(8,128)(2,1)} %param.20) | copy-start | bytes 2359300
  8.8 10.7 %copy-start.65 = (s32[1,2,64]{2,1,0:T(2,128)S(1)}, s32[1,2,64]{2,1,0:T(2,128)}, u32[]{:S(2)}) copy-start(s32[1,2,64]{2,1,0:T(2,128)} %param.21) | copy-start | bytes 1540
  8.8 133.9 %all-gather.10.cloned.1.call-start = ((), (), s32[]{:S(2)}) async-start(), calls=%async_computation.2 | async-start | bytes 10485760 | tf_op jit(solution)/shard_map/all_gather | solution.py:207
  9.5 192.9 %all-gather.12.cloned.1.call-start = ((), (), s32[]{:S(2)}) async-start(), calls=%async_computation.3 | async-start | bytes 10485760 | tf_op jit(solution)/shard_map/all_gather | solution.py:208
  10.1 757.6 %all-reduce.4.cloned.1.call-start = ((), (), s32[]{:S(2)}) async-start(), calls=%async_computation.4 | async-start | bytes 9437184 | tf_op jit(solution)/shard_map/psum | solution.py:270
  19.1 44.7 %copy-start.57 = (f32[1,2,4,128]{3,1,2,0:T(2,128)}, f32[1,2,4,128]{3,1,2,0:T(2,128)S(1)}, u32[]{:S(2)}) copy-start(f32[1,2,4,128]{3,1,2,0:T(2,128)S(1)} %copy.106) | copy-start | bytes 12292
  19.1 44.6 %copy-start.41 = (f32[1,2,4,128]{3,1,2,0:T(2,128)}, f32[1,2,4,128]{3,1,2,0:T(2,128)S(1)}, u32[]{:S(2)}) copy-start(f32[1,2,4,128]{3,1,2,0:T(2,128)S(1)} %copy.105) | copy-start | bytes 12292
  21.0 198.6 %copy-start.55 = (f32[1,2,4,128]{3,1,2,0:T(2,128)}, f32[1,2,4,128]{3,1,2,0:T(2,128)S(1)}, u32[]{:S(2)}) copy-start(f32[1,2,4,128]{3,1,2,0:T(2,128)S(1)} %copy.110) | copy-start | bytes 12292
  21.1 42.6 %copy-start.43 = (f32[384]{0:T(512)}, f32[384]{0:T(512)S(1)}, u32[]{:S(2)}) copy-start(f32[384]{0:T(512)S(1)} %broadcast_multiply_fusion.1) | copy-start | bytes 4612
  21.5 42.3 %copy-start.49 = (f32[384]{0:T(512)}, f32[384]{0:T(512)S(1)}, u32[]{:S(2)}) copy-start(f32[384]{0:T(512)S(1)} %fusion.64) | copy-start | bytes 4612
  21.5 42.3 %copy-start.45 = (f32[384]{0:T(512)}, f32[384]{0:T(512)S(1)}, u32[]{:S(2)}) copy-start(f32[384]{0:T(512)S(1)} %fusion.112) | copy-start | bytes 4612
  89.8 4.6 copy-start.15
  90.9 3.8 copy-start.16
  94.3 125.4 %copy-start.5 = (f32[384,1024]{1,0:T(8,128)}, f32[384,1024]{1,0:T(8,128)S(1)}, u32[]{:S(2)}) copy-start(f32[384,1024]{1,0:T(8,128)S(1)} %get-tuple-element.611) | copy-start | bytes 4718596
  94.3 48.4 %copy-start.54 = (f32[1,8,4,128]{3,1,2,0:T(8,128)S(1)}, f32[1,8,4,128]{3,1,2,0:T(8,128)}, u32[]{:S(2)}) copy-start(f32[1,8,4,128]{3,1,2,0:T(8,128)} %copy.124) | copy-start | bytes 49156
  94.3 48.4 %copy-start.62 = (f32[1,2,4,128]{3,1,2,0:T(2,128)S(1)}, f32[1,2,4,128]{3,1,2,0:T(2,128)}, u32[]{:S(2)}) copy-start(f32[1,2,4,128]{3,1,2,0:T(2,128)} %copy.111) | copy-start | bytes 12292
  94.4 125.3 %copy-start.47 = (f32[384]{0:T(512)}, f32[384]{0:T(512)S(1)}, u32[]{:S(2)}) copy-start(f32[384]{0:T(512)S(1)} %broadcast_multiply_fusion) | copy-start | bytes 4612
  94.7 125.0 %copy-start.59 = (f32[384]{0:T(512)}, f32[384]{0:T(512)S(1)}, u32[]{:S(2)}) copy-start(f32[384]{0:T(512)S(1)} %fusion.113) | copy-start | bytes 4612
  142.7 59.7 %copy-start.17 = (bf16[1,384,1024]{2,1,0:T(8,128)(2,1)S(1)}, bf16[1,384,1024]{2,1,0:T(8,128)(2,1)}, u32[]{:S(2)}) copy-start(bf16[1,384,1024]{2,1,0:T(8,128)(2,1)} %param.22) | copy-start | bytes 2359300
  202.4 12.9 %copy-start.75 = (bf16[1024,4096]{1,0:T(8,128)(2,1)S(1)}, bf16[1024,4096]{1,0:T(8,128)(2,1)}, u32[]{:S(2)}) copy-start(bf16[1024,4096]{1,0:T(8,128)(2,1)} %all-gather.10.cloned.1.call-done) | copy-start | bytes 25165828
  227.8 9.4 %copy-start.8 = (f32[384,1024]{1,0:T(8,128)S(1)}, f32[384,1024]{1,0:T(8,128)}, u32[]{:S(2)}) copy-start(f32[384,1024]{1,0:T(8,128)} %get-tuple-element.553) | copy-start | bytes 4718596
  227.8 9.4 %copy-start.18 = (bf16[1,384,1024]{2,1,0:T(8,128)(2,1)S(1)}, bf16[1,384,1024]{2,1,0:T(8,128)(2,1)}, u32[]{:S(2)}) copy-start(bf16[1,384,1024]{2,1,0:T(8,128)(2,1)} %param.22) | copy-start | bytes 2359300
  238.2 3.5 copy-start.6
  238.2 3.5 copy-start.35
  238.2 3.5 copy-start.36
  238.2 3.5 copy-start.37
  238.2 3.5 copy-start.38
  238.2 3.5 copy-start.48
  238.2 3.5 copy-start.56
  238.3 3.5 copy-start.60
  238.3 3.5 copy-start.63
  262.1 8.2 %copy-start.31 = (bf16[1024,1024]{1,0:T(8,128)(2,1)S(1)}, bf16[1024,1024]{1,0:T(8,128)(2,1)}, u32[]{:S(2)}) copy-start(bf16[1024,1024]{1,0:T(8,128)(2,1)} %all-gather.8.cloned.1.call-done) | copy-start | bytes 6291460
  269.8 95.7 %collective-permute-start.8 = (bf16[4608,1024]{1,0:T(8,128)(2,1)}, bf16[4608,1024]{1,0:T(8,128)(2,1)}, u32[]{:S(2)}, u32[]{:S(2)}) collective-permute-start(bf16[4608,1024]{1,0:T(8,128)(2,1)} %pad_maximum_fusion), channel_id=1, source_target_pairs={{0,1},{1,0},{2,3},{3,2},{4,5},{5,4},{6,7},{7,6},{8,9},{9,8},{10,11... | collective-permute-start | bytes 28311560 | tf_op jit(solution)/shard_map/ppermute | solution.py:155
  326.0 4.1 copy-start.2
  326.0 4.1 copy-start.10
  326.0 4.1 copy-start.11
  326.0 4.1 copy-start.42
  326.0 4.1 copy-start.44
  330.1 6.0 copy-start.50
  330.1 7.1 copy-start.46
  349.9 4.5 copy-start
  357.1 6.2 collective-permute-start
  363.3 4.4 copy-start.23
  369.1 24.5 %slice-start = ((s8[12582912]{0:T(1024)(128)(4,1)}), s8[4194304]{0:T(1024)(128)(4,1)S(1)}, s32[]{:S(2)}) async-start(s8[12582912]{0:T(1024)(128)(4,1)} %bitcast.311), calls=%async_computation.5 | async-start | bytes 8388608
  369.1 24.5 %slice-start.1 = ((s8[12582912]{0:T(1024)(128)(4,1)}), s8[4194304]{0:T(1024)(128)(4,1)S(1)}, s32[]{:S(2)}) async-start(s8[12582912]{0:T(1024)(128)(4,1)} %bitcast.311), calls=%async_computation.6 | async-start | bytes 8388608
  369.2 24.5 %slice-start.2 = ((s8[12582912]{0:T(1024)(128)(4,1)}), s8[4194304]{0:T(1024)(128)(4,1)S(1)}, s32[]{:S(2)}) async-start(s8[12582912]{0:T(1024)(128)(4,1)} %bitcast.311), calls=%async_computation.7 | async-start | bytes 8388608
  390.6 3.7 copy-start.24
  393.3 168.4 %collective-permute-start.9 = (bf16[2304,1024]{1,0:T(8,128)(2,1)}, bf16[2304,1024]{1,0:T(8,128)(2,1)}, u32[]{:S(2)}, u32[]{:S(2)}) collective-permute-start(bf16[2304,1024]{1,0:T(8,128)(2,1)} %pad_maximum_fusion.1), channel_id=1, source_target_pairs={{0,2},{1,3},{2,0},{3,1},{4,6},{5,7},{6,4},{7,5},{8,10},{9,11},{10,... | collective-permute-start | bytes 14155784 | tf_op jit(solution)/shard_map/ppermute | solution.py:155
  398.5 135.3 %collective-permute-start.1 = (bf16[832,1024]{1,0:T(8,128)(2,1)S(1)}, bf16[832,1024]{1,0:T(8,128)(2,1)S(1)}, u32[]{:S(2)}, u32[]{:S(2)}) collective-permute-start(bf16[832,1024]{1,0:T(8,128)(2,1)S(1)} %pad_maximum_fusion.5), channel_id=1, source_target_pairs={{0,2},{1,3},{2,0},{3,1},{4,6},{5,7},{6,4},{7,5},{8,10},{9,11},{10,... | collective-permute-start | bytes 5111816 | tf_op jit(solution)/shard_map/ppermute | solution.py:155
  538.7 20.4 %collective-permute-start.2 = (bf16[416,1024]{1,0:T(8,128)(2,1)}, bf16[416,1024]{1,0:T(8,128)(2,1)}, u32[]{:S(2)}, u32[]{:S(2)}) collective-permute-start(bf16[416,1024]{1,0:T(8,128)(2,1)} %fusion.77), channel_id=1, source_target_pairs={{0,4},{4,0},{8,12},{12,8},{16,20},{20,16},{24,28},{28,24},{1,5},{5... | collective-permute-start | bytes 2555912 | tf_op jit(solution)/shard_map/ppermute | solution.py:155
  540.2 21.6 %copy-start.20 = (f32[512,1024]{1,0:T(8,128)S(1)}, f32[512,1024]{1,0:T(8,128)}, u32[]{:S(2)}) copy-start(f32[512,1024]{1,0:T(8,128)} %copy-done.19) | copy-start | bytes 6291460
  573.4 28.5 %collective-permute-start.3 = (bf16[208,1024]{1,0:T(8,128)(2,1)S(1)}, bf16[208,1024]{1,0:T(8,128)(2,1)S(1)}, u32[]{:S(2)}, u32[]{:S(2)}) collective-permute-start(bf16[208,1024]{1,0:T(8,128)(2,1)S(1)} %fusion.107), channel_id=1, source_target_pairs={{0,8},{4,12},{8,0},{12,4},{16,24},{20,28},{24,16},{28,20},{1,9},{5... | collective-permute-start | bytes 1277960 | tf_op jit(solution)/shard_map/ppermute | solution.py:155
  574.9 73.2 %copy-start.52 = (f32[1,2,4,128]{3,2,1,0:T(4,128)S(1)}, f32[1,2,4,128]{3,2,1,0:T(4,128)}, u32[]{:S(2)}) copy-start(f32[1,2,4,128]{3,2,1,0:T(4,128)} %get-tuple-element.602) | copy-start | bytes 12292
  602.0 27.9 %collective-permute-start.4 = (bf16[104,1024]{1,0:T(8,128)(2,1)S(1)}, bf16[104,1024]{1,0:T(8,128)(2,1)S(1)}, u32[]{:S(2)}, u32[]{:S(2)}) collective-permute-start(bf16[104,1024]{1,0:T(8,128)(2,1)S(1)} %fusion.110), channel_id=1, source_target_pairs={{0,16},{4,20},{8,24},{12,28},{16,0},{20,4},{24,8},{28,12},{1,17},{... | collective-permute-start | bytes 638984 | tf_op jit(solution)/shard_map/ppermute | solution.py:155
  630.0 18.0 %collective-permute-start.5 = (bf16[104,1024]{1,0:T(8,128)(2,1)S(1)}, bf16[104,1024]{1,0:T(8,128)(2,1)S(1)}, u32[]{:S(2)}, u32[]{:S(2)}) collective-permute-start(bf16[104,1024]{1,0:T(8,128)(2,1)S(1)} %fusion.108), channel_id=1, source_target_pairs={{0,16},{4,20},{8,24},{12,28},{16,0},{20,4},{24,8},{28,12},{1,17},{... | collective-permute-start | bytes 638984 | tf_op jit(solution)/shard_map/ppermute | solution.py:167
  630.1 27.9 %copy-start.7 = (f32[384,1024]{1,0:T(8,128)S(1)}, f32[384,1024]{1,0:T(8,128)}, u32[]{:S(2)}) copy-start(f32[384,1024]{1,0:T(8,128)} %copy-done.5) | copy-start | bytes 4718596
  648.0 8.2 %collective-permute-start.6 = (bf16[208,1024]{1,0:T(8,128)(2,1)S(1)}, bf16[208,1024]{1,0:T(8,128)(2,1)S(1)}, u32[]{:S(2)}, u32[]{:S(2)}) collective-permute-start(bf16[208,1024]{1,0:T(8,128)(2,1)S(1)} %pad_maximum_fusion.9), channel_id=1, source_target_pairs={{0,8},{4,12},{8,0},{12,4},{16,24},{20,28},{24,16},{28,20},{1,9},{5... | collective-permute-start | bytes 1277960 | tf_op jit(solution)/shard_map/ppermute | solution.py:167
  648.1 9.8 %copy-start.27 = (bf16[384,4096]{1,0:T(8,128)(2,1)S(1)}, bf16[384,4096]{1,0:T(8,128)(2,1)}, u32[]{:S(2)}) copy-start(bf16[384,4096]{1,0:T(8,128)(2,1)} %get-tuple-element.612) | copy-start | bytes 9437188
  656.5 24.1 %collective-permute-start.7 = (bf16[416,1024]{1,0:T(8,128)(2,1)S(1)}, bf16[416,1024]{1,0:T(8,128)(2,1)S(1)}, u32[]{:S(2)}, u32[]{:S(2)}) collective-permute-start(bf16[416,1024]{1,0:T(8,128)(2,1)S(1)} %pad_maximum_fusion.8), channel_id=1, source_target_pairs={{0,4},{4,0},{8,12},{12,8},{16,20},{20,16},{24,28},{28,24},{1,5},{5... | collective-permute-start | bytes 2555912 | tf_op jit(solution)/shard_map/ppermute | solution.py:167
  (36 other events, 72.3 us)
Sparse Core Ops, SparseCore 0:
  9.6 49.0 all-gather.5
  60.2 22.5 all-gather.7
  84.4 58.2 all-gather.9
  144.1 58.2 all-gather.11
  572.0 195.6 all-reduce.3

commit v5 on v4

--- a/solution.py
+++ b/solution.py
@@ -160,13 +160,23 @@
     return arrays
 
 
-def doubling(buf, axis, size, steps):
+def direct_reduce(buf, axis, size):
     index = lax.axis_index(axis)
-    for step in steps:
-        low = (index // step) % 2 == 0
-        got = lax.ppermute(buf, axis, [(a, a ^ step) for a in range(size)])
-        buf = jnp.concatenate([jnp.where(low, buf, got), jnp.where(low, got, buf)], 0)
-    return buf
+    chunks = buf.reshape(size, buf.shape[0] // size, *buf.shape[1:])
+    total = lax.dynamic_index_in_dim(chunks, index, 0, keepdims=False)
+    for shift in range(1, size):
+        send = lax.dynamic_index_in_dim(chunks, (index + shift) % size, 0, keepdims=False)
+        got = lax.ppermute(
+            send.astype(jnp.bfloat16), axis, [(a, (a + shift) % size) for a in range(size)]
+        )
+        total = total + got.astype(jnp.float32)
+    mine = total.astype(jnp.bfloat16)
+    result = jnp.zeros((size, *mine.shape), jnp.bfloat16)
+    result = lax.dynamic_update_index_in_dim(result, mine, index, 0)
+    for shift in range(1, size):
+        got = lax.ppermute(mine, axis, [(a, (a + shift) % size) for a in range(size)])
+        result = lax.dynamic_update_index_in_dim(result, got, (index - shift) % size, 0)
+    return result.reshape(buf.shape)
 
 
 def gather_small(pieces):
@@ -248,6 +258,8 @@
     grad_down = jnp.einsum(
         "tf,to->fo", reorder_cols(activated, order), cot_low, preferred_element_type=jnp.float32
     )
+    (down_own,) = halving([grad_down], "shard", shard_count, shard_steps)
+    total_a1 = lax.psum(down_own.astype(jnp.bfloat16), "rep")
     grad_up_t = jnp.einsum(
         "tf,ti->fi", reorder_cols(grad_pre, order), normed_two, preferred_element_type=jnp.float32
     )
@@ -263,11 +275,11 @@
     grad_out = jnp.einsum(
         "ti,to->io", reorder_cols(mixed, order), grad_branch, preferred_element_type=jnp.float32
     )
-    down_own, up_own, out_own = halving(
-        [grad_down, grad_up_t, grad_out], "shard", shard_count, shard_steps
-    )
-    owned_a = [down_own, up_own, out_own]
-    total_a = lax.psum(jnp.concatenate([o.astype(jnp.bfloat16) for o in owned_a], 0), "rep")
+    up_own, out_own = halving([grad_up_t, grad_out], "shard", shard_count, shard_steps)
+    owned_a = [up_own, out_own]
+    joined_a = jnp.concatenate([o.astype(jnp.bfloat16) for o in owned_a], 0)
+    total_a1, joined_a = lax.optimization_barrier((total_a1, joined_a))
+    total_a = lax.psum(joined_a, "rep")
     grad_q, grad_k, grad_v = attend_backward(
         queries, key_rows, values, grad_mixed, log_norms, distance, allowed
     )
@@ -283,7 +295,6 @@
     )
     smalls = [grad_g1, grad_s1, grad_qb, grad_vb, grad_bo, grad_g2, grad_s2, grad_bu, grad_bd]
     reps = lax.psum(1, "rep")
-    rep_steps = bit_steps(reps)
     qkv_rows = grad_qkv_t.shape[0] // shard_count
     small_rows = jnp.concatenate([g.reshape(shard_count, -1) for g in smalls], 1)
     small_rows = small_rows.reshape(shard_count, -1, model_width)
@@ -292,13 +303,11 @@
     small_rows = jnp.concatenate([small_rows[k] for k in order], 0)
     qkv_own, small_own = halving([grad_qkv_t, small_rows], "shard", shard_count, shard_steps)
     joined_b = jnp.concatenate([qkv_own, small_own], 0)
-    (joined_b,) = halving([joined_b], "rep", reps, rep_steps)
-    total_b = doubling(joined_b.astype(jnp.bfloat16), "rep", reps, rep_steps[::-1])
-    down_rows = down_own.shape[0]
+    total_b = direct_reduce(joined_b, "rep", reps)
     up_rows = up_own.shape[0]
-    down_fin = total_a[:down_rows].astype(jnp.float32)
-    up_fin = total_a[down_rows : down_rows + up_rows].astype(jnp.float32).T
-    out_fin = total_a[down_rows + up_rows :].astype(jnp.float32)
+    down_fin = total_a1.astype(jnp.float32)
+    up_fin = total_a[:up_rows].astype(jnp.float32).T
+    out_fin = total_a[up_rows:].astype(jnp.float32)
     qkv_fin = total_b[:qkv_rows].astype(jnp.float32).T
     small_flat = total_b[qkv_rows:].reshape(-1).astype(jnp.float32)
     small_fin, offset = [], 0

time: 794 us -> 755 us (0.951)
  waiting for transfers between devices: 469 us -> 379 us
  starting transfers between devices: 11.2 us -> 64.7 us
    ppermute x7 -> x6, waiting for transfers between devices: 210 us -> 54.5 us  [halving(): lax.ppermute(jnp.concatenate(sends, 0), axis, [(a, a ^ step) for a in ran...]
    ppermute x3 -> x14, starting transfers between devices: 1.59 us -> 60 us  [the longest x7 44.7 us: direct_reduce(): lax.ppermute(send.astype(jnp.bfloat16), axis, [(a, (a + shift) % size) fo...]
    psum x1 -> x2, waiting for transfers between devices: 82.6 us -> 130 us  [the longest x1 81 us: body_inner(): total_a = lax.psum(joined_a, 'rep')]
    ppermute x3 -> x14, waiting for transfers between devices: 40.9 us -> 58.9 us  [the longest x7 38.2 us: direct_reduce(): lax.ppermute(mine, axis, [(a, (a + shift) % size) for a in range(size)])]
    convert_element_type x12 -> x10, local copies, waits for them, and re-layouts: 18.4 us -> 13.2 us  [halving(): lax.dynamic_index_in_dim(pair, 1 - bit, 0, keepdims=False)]
    unnamed x189 -> x199, local copies, waits for them, and re-layouts: 31.2 us -> 34.7 us
    add x8 -> x7, other arithmetic: 26.9 us -> 25.7 us  [halving(): arrays.append(keep + got[offset:offset + keep.shape[0]].astype(jnp.float32))]
  transfers between devices with their start and end apart: 15 -> 26, of which waited for: 12 -> 17; matrix products, arithmetic and copies ran while one was open for 17% -> 20% of each run, Pallas kernels for 0% -> 0%
where the time goes in v5:
time: 755 us; the launch traced here: 750 us
  waiting for transfers between devices  379 us (50%)
  matrix products  92.1 us (12%)
  local copies, waits for them, and re-layouts  91.2 us (12%)
  other arithmetic  81.6 us (11%)
  starting transfers between devices  64.7 us (9%)
  loops' own time  19.5 us (3%)
  between operations  15.8 us (2%)
    psum x1, waiting for transfers between devices, body_inner(): total_a = lax.psum(joined_a, 'rep')  81 us
    ppermute x6, waiting for transfers between devices, halving(): lax.ppermute(jnp.concatenate(sends, 0), axis, [(a, a ^ step) for a in ran...  54.5 us
    psum x1, waiting for transfers between devices, body_inner(): total_a1 = lax.psum(down_own.astype(jnp.bfloat16), 'rep')  48.7 us
    all_gather x1, waiting for transfers between devices, body_inner(): full_down = lax.all_gather(w_down, 'shard', axis=0, tiled=True)  48.4 us
    all_gather x1, waiting for transfers between devices, body_inner(): full_up = lax.all_gather(w_up, 'shard', axis=1, tiled=True)  47 us
    ppermute x7, starting transfers between devices, direct_reduce(): lax.ppermute(send.astype(jnp.bfloat16), axis, [(a, (a + shift) % size) fo...  44.7 us
    all_gather x1, waiting for transfers between devices, body_inner(): full_qkv = lax.all_gather(w_qkv, 'shard', axis=1, tiled=True)  38.3 us
    ppermute x7, waiting for transfers between devices, direct_reduce(): lax.ppermute(mine, axis, [(a, (a + shift) % size) for a in range(size)])  38.2 us
  transfers between devices with their start and end apart: 26, of which 17 were waited for; matrix products, arithmetic and copies ran while one was open for 20% of the time, Pallas kernels for 0%

profile of v5, /device:TPU:0, one launch (start us, length us, event | category | flops | bytes accessed | tf_op | source)
XLA Modules:
  0.0 750.4 jit_solution(16494111892341805396)
XLA Ops:
  12.2 6.3 all-gather
  20.3 38.3 %all-gather.6.cloned.1.call-done = bf16[1024,3072]{1,0:T(8,128)(2,1)} async-done(((bf16[1024,768]{1,0:T(8,128)(2,1)}), bf16[1024,3072]{1,0:T(8,128)(2,1)}) %all-gather.6.cloned.1.call-update) | async-done | bytes 6291472 | tf_op jit(solution)/shard_map/all_gather | solution.py:215
  58.7 5.1 fusion.81
  68.5 21.3 %while.32 = (s32[]{:T(128)}, bf16[4,384,256]{1,2,0:T(8,128)(2,1)}, f32[4,4,384]{2,1,0:T(4,128)}, s32[4]{0:T(128)S(1)}, bf16[384,1024]{0,1:T(8,128)(2,1)S(1)}, /*...) while((s32[]{:T(128)}, bf16[4,384,256]{1,2,0:T(8,128)(2,1)}, ...), condition=%wide.region_6.7_spmd.clone, body=%wide.region_3.6_spmd.clone.sunk | while | flops 157776416 | bytes 10964623 | solution.py:74
  91.0 3.4 fusion.137
  95.7 47.0 %all-gather.10.cloned.1.call-done = bf16[1024,4096]{1,0:T(8,128)(2,1)} async-done(((bf16[1024,1024]{1,0:T(8,128)(2,1)}), bf16[1024,4096]{1,0:T(8,128)(2,1)}) %all-gather.10.cloned.1.call-update) | async-done | bytes 8388624 | tf_op jit(solution)/shard_map/all_gather | solution.py:217
  142.7 11.3 %multiply_convert_fusion.1 = (bf16[384,4096]{1,0:T(8,128)(2,1)}, f32[384,4096]{1,0:T(8,128)}) fusion(f32[4096]{0:T(1024)S(1)} %bitcast.398, bf16[1024,4096]{1,0:T(8,128)(2,1)} %all-gather.10.cloned.1.call-done, f32[384,1024]{1,0:T(8,128)S(1)} %get-tuple-element.612, f32[1024]{0:T(1024)S(1)} %bitcast.405, f32[1024]{0:T(1024)S(1)} %bitcast.399, ...), kind=kOutput, calls=%fused_computation.57 | convolution fusion | flops 3238920192 | bytes 19426304 | tf_op jit(solution)/shard_map/dot_general | solution.py:237
  154.0 48.4 %all-gather.12.cloned.1.call-done = bf16[4096,1024]{1,0:T(8,128)(2,1)} async-done(((bf16[1024,1024]{1,0:T(8,128)(2,1)}), bf16[4096,1024]{1,0:T(8,128)(2,1)}) %all-gather.12.cloned.1.call-update) | async-done | bytes 8388624 | tf_op jit(solution)/shard_map/all_gather | solution.py:218
  202.4 11.2 %convert_reduce_fusion = (f32[4096]{0:T(1024)}, bf16[384,4096]{1,0:T(8,128)(2,1)S(1)}) fusion(f32[384,4096]{1,0:T(8,128)} %get-tuple-element.614, bf16[4096,1024]{1,0:T(8,128)(2,1)} %all-gather.12.cloned.1.call-done, bf16[1,384,1024]{2,1,0:T(8,128)(2,1)S(1)} %copy-done.20), kind=kOutput, calls=%fused_computation.55 | convolution fusion | flops 3255824384 | bytes 18628608 | tf_op jit(solution)/shard_map/to,fo->tf/dot_general | solution.py:254
  215.3 4.3 multiply_reduce_fusion.1
  226.6 51.6 %while.33 = (s32[]{:T(128)}, bf16[4,384,256]{1,2,0:T(8,128)(2,1)}, bf16[4,384,256]{1,2,0:T(8,128)(2,1)}, bf16[4,384,256]{1,2,0:T(8,128)(2,1)}, s32[4]{0:T(128)S(...) while((s32[]{:T(128)}, bf16[4,384,256]{1,2,0:T(8,128)(2,1)}, ...), condition=%wide.region_13.14_spmd.clone, body=%wide.region_11.13_spmd.clone.sunk | while | flops 385251872 | bytes 36901940 | solution.py:113
  278.3 1.9 convert_reduce_fusion.4
  280.2 1.9 split.65
  283.1 5.7 fusion.128
  294.1 3.6 fusion.79
  298.9 3.6 copy-done
  303.1 2.1 pad_maximum_fusion.1
  306.6 1.8 maximum_bitcast_fusion
  308.4 3.4 copy.114
  311.9 9.5 %fusion.91 = f32[2,2048,1024]{2,1,0:T(8,128)} fusion(bf16[2,2048,384]{2,1,0:T(8,128)(2,1)S(1)} %bitcast.345, bf16[1,384,1024]{2,1,0:T(8,128)(2,1)} %param.22), kind=kOutput, calls=%fused_computation.171 | convolution fusion | flops 3221225472 | bytes 20709376 | tf_op jit(solution)/shard_map/tf,to->fo/dot_general | solution.py:258
  322.8 2.0 copy-done.3
  325.1 9.4 %fusion.32 = f32[4096,1024]{1,0:T(8,128)} fusion(bf16[384,1024]{1,0:T(8,128)(2,1)S(1)} %copy-done.39, bf16[384,1024]{1,0:T(8,128)(2,1)S(1)} %copy-done.40, bf16[384,1024]{1,0:T(8,128)(2,1)S(1)} %copy-done.41, bf16[384,1024]{1,0:T(8,128)(2,1)S(1)} %copy-done.38, f32[384,1024]{1,0:T(8,128)S(1)} %copy-done.9, f32[1024]{0:T(1024)S(1)} %bitcast.406, ...), kind=kOutput, calls=%fused_computation.79 | convolution fusion | flops 3235774464 | bytes 21507072 | tf_op jit(solution)/shard_map/tf,ti->fi/dot_general | solution.py:263
  334.5 4.0 fusion.24
  338.5 2.9 pad_maximum_fusion
  341.7 6.1 fusion.23
  349.9 4.7 bitcast_add_fusion.2
  355.0 2.2 copy-done.7
  357.6 6.0 bitcast_add_fusion.1
  367.0 1.9 copy-done.4
  370.7 6.6 bitcast_add_fusion
  377.6 2.1 pad_maximum_fusion.3
  383.1 14.3 %collective-permute-done.1 = bf16[832,1024]{1,0:T(8,128)(2,1)} collective-permute-done((bf16[832,1024]{1,0:T(8,128)(2,1)S(1)}, bf16[832,1024]{1,0:T(8,128)(2,1)}, u32[]{:S(2)}, u32[]{:S(2)}) %collective-permute-start.1) | collective-permute-done | bytes 1703968 | tf_op jit(solution)/shard_map/ppermute | solution.py:155
  397.4 4.8 bitcast_add_fusion.5
  402.2 40.1 %collective-permute-done.17 = bf16[1024,1024]{1,0:T(8,128)(2,1)} collective-permute-done((bf16[1024,1024]{1,0:T(8,128)(2,1)}, bf16[1024,1024]{1,0:T(8,128)(2,1)}, u32[]{:S(2)}, u32[]{:S(2)}) %collective-permute-start.17) | collective-permute-done | bytes 2097184 | tf_op jit(solution)/shard_map/ppermute | solution.py:155
  442.3 4.9 fusion.26
  448.2 2.2 pad_maximum_fusion.2
  453.1 4.2 collective-permute-start.8
  457.8 2.9 collective-permute-start.5
  460.8 6.7 collective-permute-done.8
  467.5 4.6 collective-permute-start.4
  472.1 7.8 %collective-permute-done.7 = bf16[104,1024]{1,0:T(8,128)(2,1)S(1)} collective-permute-done((bf16[104,1024]{1,0:T(8,128)(2,1)S(1)}, bf16[104,1024]{1,0:T(8,128)(2,1)S(1)}, u32[]{:S(2)}, u32[]{:S(2)}) %collective-permute-start.7) | collective-permute-done | bytes 213024 | tf_op jit(solution)/shard_map/ppermute | solution.py:169
  479.9 21.7 %collective-permute-start.3 = (bf16[104,1024]{1,0:T(8,128)(2,1)S(1)}, bf16[104,1024]{1,0:T(8,128)(2,1)S(1)}, u32[]{:S(2)}, u32[]{:S(2)}) collective-permute-start(bf16[104,1024]{1,0:T(8,128)(2,1)S(1)} %get-tuple-element.576), channel_id=1, source_target_pairs={{0,8},{4,12},{8,16},{12,20},{16,24},{20,28},{24,0},{28,4},{1,9},{5... | collective-permute-start | bytes 638984 | tf_op jit(solution)/shard_map/ppermute | solution.py:169
  501.6 10.7 %collective-permute-start.2 = (bf16[104,1024]{1,0:T(8,128)(2,1)S(1)}, bf16[104,1024]{1,0:T(8,128)(2,1)}, u32[]{:S(2)}, u32[]{:S(2)}) collective-permute-start(bf16[104,1024]{1,0:T(8,128)(2,1)S(1)} %get-tuple-element.570), channel_id=1, source_target_pairs={{0,4},{4,8},{8,12},{12,16},{16,20},{20,24},{24,28},{28,0},{1,5},{5... | collective-permute-start | bytes 638984 | tf_op jit(solution)/shard_map/ppermute | solution.py:169
  512.3 2.6 collective-permute-done.5
  517.1 2.8 collective-permute-done.2
  520.1 2.5 bitcast_dynamic-update-slice_fusion.8
  522.6 2.8 collective-permute-start.9
  526.6 3.6 fusion.25
  532.0 48.7 %all-reduce.5.cloned.1.call-done = bf16[1024,1024]{1,0:T(8,128)(2,1)} async-done(((bf16[1024,1024]{1,0:T(8,128)(2,1)}), bf16[1024,1024]{1,0:T(8,128)(2,1)}) %all-reduce.5.cloned.1.call-update) | async-done | bytes 2097168 | tf_op jit(solution)/shard_map/psum | solution.py:262
  580.7 8.6 %fusion.73 = bf16[1,384,1024]{2,1,0:T(8,128)(2,1)} fusion(f32[384,1024]{1,0:T(8,128)S(1)} %copy-done.9, bf16[384,4096]{1,0:T(8,128)(2,1)} %get-tuple-element.613, bf16[4096,1024]{1,0:T(8,128)(2,1)} %all-gather.12.cloned.1.call-done, f32[1024]{0:T(1024)S(1)} %bitcast.407), kind=kOutput, calls=%fused_computation.152 | convolution fusion | flops 3222405120 | bytes 13897728 | tf_op jit(solution)/shard_map/dot_general | solution.py:242
  590.4 2.1 collective-permute-start.11
  592.5 2.1 collective-permute-start.12
  595.3 2.5 collective-permute-start.14
  597.8 6.2 collective-permute-done.10
  604.0 4.0 collective-permute-start.15
  608.0 17.5 %collective-permute-done.11 = bf16[104,1024]{1,0:T(8,128)(2,1)S(1)} collective-permute-done((bf16[104,1024]{1,0:T(8,128)(2,1)}, bf16[104,1024]{1,0:T(8,128)(2,1)S(1)}, u32[]{:S(2)}, u32[]{:S(2)}) %collective-permute-start.11) | collective-permute-done | bytes 213024 | tf_op jit(solution)/shard_map/ppermute | solution.py:177
  625.5 6.4 collective-permute-done.12
  632.2 7.9 %collective-permute-done.15 = bf16[104,1024]{1,0:T(8,128)(2,1)S(1)} collective-permute-done((bf16[104,1024]{1,0:T(8,128)(2,1)}, bf16[104,1024]{1,0:T(8,128)(2,1)S(1)}, u32[]{:S(2)}, u32[]{:S(2)}) %collective-permute-start.15) | collective-permute-done | bytes 213024 | tf_op jit(solution)/shard_map/ppermute | solution.py:177
  643.2 2.4 copy.108
  646.7 4.1 convert_element_type.524
  650.8 81.0 %all-reduce.7.cloned.1.call-done = bf16[1280,1024]{1,0:T(8,128)(2,1)} async-done(((bf16[1280,1024]{1,0:T(8,128)(2,1)}), bf16[1280,1024]{1,0:T(8,128)(2,1)}) %all-reduce.7.cloned.1.call-update) | async-done | bytes 2621456 | tf_op jit(solution)/shard_map/psum | solution.py:282
  731.8 4.1 convert_bitcast_fusion
  735.8 5.3 copy.109
  741.2 2.1 slice_convert_fusion.1
  (492 shorter events, 114.1 us)
Async XLA Ops:
  7.2 51.5 %all-gather.6.cloned.1.call-start = ((), (), s32[]{:S(2)}) async-start(), calls=%async_computation | async-start | bytes 7864320 | tf_op jit(solution)/shard_map/all_gather | solution.py:215
  8.0 81.8 %all-gather.8.cloned.1.call-start = ((), (), s32[]{:S(2)}) async-start(), calls=%async_computation.1 | async-start | bytes 2621440 | tf_op jit(solution)/shard_map/all_gather | solution.py:216
  8.8 10.3 %copy-start.1 = (bf16[1,384,1024]{2,1,0:T(8,128)(2,1)S(1)}, bf16[1,384,1024]{2,1,0:T(8,128)(2,1)}, u32[]{:S(2)}) copy-start(bf16[1,384,1024]{2,1,0:T(8,128)(2,1)} %param.20) | copy-start | bytes 2359300
  8.8 10.7 %copy-start.77 = (s32[1,2,64]{2,1,0:T(2,128)S(1)}, s32[1,2,64]{2,1,0:T(2,128)}, u32[]{:S(2)}) copy-start(s32[1,2,64]{2,1,0:T(2,128)} %param.21) | copy-start | bytes 1540
  8.8 133.9 %all-gather.10.cloned.1.call-start = ((), (), s32[]{:S(2)}) async-start(), calls=%async_computation.2 | async-start | bytes 10485760 | tf_op jit(solution)/shard_map/all_gather | solution.py:217
  9.5 192.9 %all-gather.12.cloned.1.call-start = ((), (), s32[]{:S(2)}) async-start(), calls=%async_computation.3 | async-start | bytes 10485760 | tf_op jit(solution)/shard_map/all_gather | solution.py:218
  10.1 570.6 %all-reduce.5.cloned.1.call-start = ((), (), s32[]{:S(2)}) async-start(), calls=%async_computation.4 | async-start | bytes 4194304 | tf_op jit(solution)/shard_map/psum | solution.py:262
  19.1 44.7 %copy-start.69 = (f32[1,2,4,128]{3,1,2,0:T(2,128)}, f32[1,2,4,128]{3,1,2,0:T(2,128)S(1)}, u32[]{:S(2)}) copy-start(f32[1,2,4,128]{3,1,2,0:T(2,128)S(1)} %copy.121) | copy-start | bytes 12292
  19.1 44.7 %copy-start.50 = (f32[1,2,4,128]{3,1,2,0:T(2,128)}, f32[1,2,4,128]{3,1,2,0:T(2,128)S(1)}, u32[]{:S(2)}) copy-start(f32[1,2,4,128]{3,1,2,0:T(2,128)S(1)} %copy.120) | copy-start | bytes 12292
  19.8 122.9 %copy-start.73 = (f32[1,2,4,128]{3,1,2,0:T(2,128)}, f32[1,2,4,128]{3,1,2,0:T(2,128)S(1)}, u32[]{:S(2)}) copy-start(f32[1,2,4,128]{3,1,2,0:T(2,128)S(1)} %copy.126) | copy-start | bytes 12292
  19.9 199.8 %copy-start.67 = (f32[1,2,4,128]{3,1,2,0:T(2,128)}, f32[1,2,4,128]{3,1,2,0:T(2,128)S(1)}, u32[]{:S(2)}) copy-start(f32[1,2,4,128]{3,1,2,0:T(2,128)S(1)} %copy.125) | copy-start | bytes 12292
  20.0 43.8 %copy-start.52 = (f32[384]{0:T(512)}, f32[384]{0:T(512)S(1)}, u32[]{:S(2)}) copy-start(f32[384]{0:T(512)S(1)} %broadcast_multiply_fusion.1) | copy-start | bytes 4612
  20.3 43.5 %copy-start.62 = (f32[384]{0:T(512)}, f32[384]{0:T(512)S(1)}, u32[]{:S(2)}) copy-start(f32[384]{0:T(512)S(1)} %fusion.64) | copy-start | bytes 4612
  20.3 43.5 %copy-start.56 = (f32[384]{0:T(512)}, f32[384]{0:T(512)S(1)}, u32[]{:S(2)}) copy-start(f32[384]{0:T(512)S(1)} %fusion.122) | copy-start | bytes 4612
  94.4 125.2 %copy-start.8 = (f32[384,1024]{1,0:T(8,128)}, f32[384,1024]{1,0:T(8,128)S(1)}, u32[]{:S(2)}) copy-start(f32[384,1024]{1,0:T(8,128)S(1)} %get-tuple-element.612) | copy-start | bytes 4718596
  94.4 125.2 %copy-start.60 = (f32[384]{0:T(512)}, f32[384]{0:T(512)S(1)}, u32[]{:S(2)}) copy-start(f32[384]{0:T(512)S(1)} %broadcast_multiply_fusion) | copy-start | bytes 4612
  94.8 124.9 %copy-start.71 = (f32[384]{0:T(512)}, f32[384]{0:T(512)S(1)}, u32[]{:S(2)}) copy-start(f32[384]{0:T(512)S(1)} %fusion.123) | copy-start | bytes 4612
  142.7 59.7 %copy-start.20 = (bf16[1,384,1024]{2,1,0:T(8,128)(2,1)S(1)}, bf16[1,384,1024]{2,1,0:T(8,128)(2,1)}, u32[]{:S(2)}) copy-start(bf16[1,384,1024]{2,1,0:T(8,128)(2,1)} %param.22) | copy-start | bytes 2359300
  202.4 12.9 %copy-start.87 = (bf16[1024,4096]{1,0:T(8,128)(2,1)S(1)}, bf16[1024,4096]{1,0:T(8,128)(2,1)}, u32[]{:S(2)}) copy-start(bf16[1024,4096]{1,0:T(8,128)(2,1)} %all-gather.10.cloned.1.call-done) | copy-start | bytes 25165828
  226.6 5.7 copy-start.54
  226.6 5.7 copy-start.88
  239.4 5.8 copy-start.54
  239.4 5.8 copy-start.88
  252.2 5.8 copy-start.54
  252.2 5.8 copy-start.88
  265.0 5.8 copy-start.54
  265.0 5.8 copy-start.88
  283.0 5.7 copy-start.63
  283.0 5.7 copy-start.57
  297.7 4.9 copy-start
  305.2 42.9 %collective-permute-start = (bf16[1664,1024]{1,0:T(8,128)(2,1)}, bf16[1664,1024]{1,0:T(8,128)(2,1)}, u32[]{:S(2)}, u32[]{:S(2)}) collective-permute-start(bf16[1664,1024]{1,0:T(8,128)(2,1)} %pad_maximum_fusion.1), channel_id=1, source_target_pairs={{0,1},{1,0},{2,3},{3,2},{4,5},{5,4},{6,7},{7,6},{8,9},{9,8},{10,11... | collective-permute-start | bytes 10223624 | tf_op jit(solution)/shard_map/ppermute | solution.py:155
  311.9 9.6 %copy-start.29 = (bf16[384,1024]{1,0:T(8,128)(2,1)S(1)}, bf16[384,1024]{1,0:T(8,128)(2,1)}, u32[]{:S(2)}) copy-start(bf16[384,1024]{1,0:T(8,128)(2,1)} %copy-done.28) | copy-start | bytes 2359300
  311.9 9.6 %copy-start.42 = (bf16[384,256]{0,1:T(8,128)(2,1)S(1)}, bf16[384,256]{0,1:T(8,128)(2,1)}, u32[]{:S(2)}) copy-start(bf16[384,256]{0,1:T(8,128)(2,1)} %get-tuple-element.586) | copy-start | bytes 589828
  311.9 9.6 %copy-start.43 = (bf16[384,256]{0,1:T(8,128)(2,1)S(1)}, bf16[384,256]{0,1:T(8,128)(2,1)}, u32[]{:S(2)}) copy-start(bf16[384,256]{0,1:T(8,128)(2,1)} %get-tuple-element.587) | copy-start | bytes 589828
  311.9 9.5 %copy-start.44 = (bf16[384,256]{0,1:T(8,128)(2,1)S(1)}, bf16[384,256]{0,1:T(8,128)(2,1)}, u32[]{:S(2)}) copy-start(bf16[384,256]{0,1:T(8,128)(2,1)} %get-tuple-element.588) | copy-start | bytes 589828
  341.4 6.6 copy-start.26
  341.4 25.5 %collective-permute-start.18 = (bf16[2560,1024]{1,0:T(8,128)(2,1)}, bf16[2560,1024]{1,0:T(8,128)(2,1)}, u32[]{:S(2)}, u32[]{:S(2)}) collective-permute-start(bf16[2560,1024]{1,0:T(8,128)(2,1)} %pad_maximum_fusion), channel_id=1, source_target_pairs={{0,1},{1,0},{2,3},{3,2},{4,5},{5,4},{6,7},{7,6},{8,9},{9,8},{10,11... | collective-permute-start | bytes 15728648 | tf_op jit(solution)/shard_map/ppermute | solution.py:155
  347.8 9.7 %collective-permute-start.16 = (bf16[2048,1024]{1,0:T(8,128)(2,1)}, bf16[2048,1024]{1,0:T(8,128)(2,1)}, u32[]{:S(2)}, u32[]{:S(2)}) collective-permute-start(bf16[2048,1024]{1,0:T(8,128)(2,1)} %fusion.23), channel_id=1, source_target_pairs={{0,1},{1,0},{2,3},{3,2},{4,5},{5,4},{6,7},{7,6},{8,9},{9,8},{10,11... | collective-permute-start | bytes 12582920 | tf_op jit(solution)/shard_map/ppermute | solution.py:155
  357.2 40.2 %collective-permute-start.1 = (bf16[832,1024]{1,0:T(8,128)(2,1)S(1)}, bf16[832,1024]{1,0:T(8,128)(2,1)}, u32[]{:S(2)}, u32[]{:S(2)}) collective-permute-start(bf16[832,1024]{1,0:T(8,128)(2,1)S(1)} %pad_maximum_fusion.5), channel_id=1, source_target_pairs={{0,2},{1,3},{2,0},{3,1},{4,6},{5,7},{6,4},{7,5},{8,10},{9,11},{10,... | collective-permute-start | bytes 5111816 | tf_op jit(solution)/shard_map/ppermute | solution.py:155
  363.6 7.0 copy-start.6
  363.6 5.3 copy-start.4
  365.3 77.0 %collective-permute-start.17 = (bf16[1024,1024]{1,0:T(8,128)(2,1)}, bf16[1024,1024]{1,0:T(8,128)(2,1)}, u32[]{:S(2)}, u32[]{:S(2)}) collective-permute-start(bf16[1024,1024]{1,0:T(8,128)(2,1)} %fusion.51), channel_id=1, source_target_pairs={{0,2},{1,3},{2,0},{3,1},{4,6},{5,7},{6,4},{7,5},{8,10},{9,11},{10,... | collective-permute-start | bytes 6291464 | tf_op jit(solution)/shard_map/ppermute | solution.py:155
  370.6 6.7 copy-start.23
  381.4 144.0 %collective-permute-start.19 = (bf16[1280,1024]{1,0:T(8,128)(2,1)}, bf16[1280,1024]{1,0:T(8,128)(2,1)}, u32[]{:S(2)}, u32[]{:S(2)}) collective-permute-start(bf16[1280,1024]{1,0:T(8,128)(2,1)} %pad_maximum_fusion.3), channel_id=1, source_target_pairs={{0,2},{1,3},{2,0},{3,1},{4,6},{5,7},{6,4},{7,5},{8,10},{9,11},{10,... | collective-permute-start | bytes 7864328 | tf_op jit(solution)/shard_map/ppermute | solution.py:155
  402.2 45.1 %copy-start.35 = (f32[128,1024]{1,0:T(8,128)S(1)}, f32[128,1024]{1,0:T(8,128)}, u32[]{:S(2)}) copy-start(f32[128,1024]{1,0:T(8,128)} %copy-done.34) | copy-start | bytes 1572868
  447.2 284.5 %all-reduce.7.cloned.1.call-start = ((), (), s32[]{:S(2)}) async-start(), calls=%async_computation.5 | async-start | bytes 5242880 | tf_op jit(solution)/shard_map/psum | solution.py:282
  450.4 61.9 %copy-start.65 = (f32[1,2,4,128]{3,2,1,0:T(4,128)S(1)}, f32[1,2,4,128]{3,2,1,0:T(4,128)}, u32[]{:S(2)}) copy-start(f32[1,2,4,128]{3,2,1,0:T(4,128)} %get-tuple-element.603) | copy-start | bytes 12292
  453.1 14.4 %collective-permute-start.8 = (bf16[104,1024]{1,0:T(8,128)(2,1)S(1)}, bf16[104,1024]{1,0:T(8,128)(2,1)S(1)}, u32[]{:S(2)}, u32[]{:S(2)}) collective-permute-start(bf16[104,1024]{1,0:T(8,128)(2,1)S(1)} %get-tuple-element.571), channel_id=1, source_target_pairs={{0,28},{4,0},{8,4},{12,8},{16,12},{20,16},{24,20},{28,24},{1,29},{... | collective-permute-start | bytes 638984 | tf_op jit(solution)/shard_map/ppermute | solution.py:169
  457.3 22.6 %collective-permute-start.7 = (bf16[104,1024]{1,0:T(8,128)(2,1)S(1)}, bf16[104,1024]{1,0:T(8,128)(2,1)S(1)}, u32[]{:S(2)}, u32[]{:S(2)}) collective-permute-start(bf16[104,1024]{1,0:T(8,128)(2,1)S(1)} %get-tuple-element.572), channel_id=1, source_target_pairs={{0,24},{4,28},{8,0},{12,4},{16,8},{20,12},{24,16},{28,20},{1,25},{... | collective-permute-start | bytes 638984 | tf_op jit(solution)/shard_map/ppermute | solution.py:169
  457.8 43.8 %collective-permute-start.6 = (bf16[104,1024]{1,0:T(8,128)(2,1)S(1)}, bf16[104,1024]{1,0:T(8,128)(2,1)S(1)}, u32[]{:S(2)}, u32[]{:S(2)}) collective-permute-start(bf16[104,1024]{1,0:T(8,128)(2,1)S(1)} %get-tuple-element.573), channel_id=1, source_target_pairs={{0,20},{4,24},{8,28},{12,0},{16,4},{20,8},{24,12},{28,16},{1,21},{... | collective-permute-start | bytes 638984 | tf_op jit(solution)/shard_map/ppermute | solution.py:169
  457.8 57.1 %collective-permute-start.5 = (bf16[104,1024]{1,0:T(8,128)(2,1)}, bf16[104,1024]{1,0:T(8,128)(2,1)S(1)}, u32[]{:S(2)}, u32[]{:S(2)}) collective-permute-start(bf16[104,1024]{1,0:T(8,128)(2,1)} %get-tuple-element.574), channel_id=1, source_target_pairs={{0,16},{4,20},{8,24},{12,28},{16,0},{20,4},{24,8},{28,12},{1,17},{... | collective-permute-start | bytes 638984 | tf_op jit(solution)/shard_map/ppermute | solution.py:169
  467.5 48.2 %collective-permute-start.4 = (bf16[104,1024]{1,0:T(8,128)(2,1)S(1)}, bf16[104,1024]{1,0:T(8,128)(2,1)S(1)}, u32[]{:S(2)}, u32[]{:S(2)}) collective-permute-start(bf16[104,1024]{1,0:T(8,128)(2,1)S(1)} %get-tuple-element.575), channel_id=1, source_target_pairs={{0,12},{4,16},{8,20},{12,24},{16,28},{20,0},{24,4},{28,8},{1,13},{... | collective-permute-start | bytes 638984 | tf_op jit(solution)/shard_map/ppermute | solution.py:169
  479.9 35.8 %copy-start.45 = (bf16[104,1024]{1,0:T(8,128)(2,1)}, bf16[104,1024]{1,0:T(8,128)(2,1)S(1)}, u32[]{:S(2)}) copy-start(bf16[104,1024]{1,0:T(8,128)(2,1)S(1)} %collective-permute-done.7) | copy-start | bytes 638980
  479.9 35.8 %collective-permute-start.3 = (bf16[104,1024]{1,0:T(8,128)(2,1)S(1)}, bf16[104,1024]{1,0:T(8,128)(2,1)S(1)}, u32[]{:S(2)}, u32[]{:S(2)}) collective-permute-start(bf16[104,1024]{1,0:T(8,128)(2,1)S(1)} %get-tuple-element.576), channel_id=1, source_target_pairs={{0,8},{4,12},{8,16},{12,20},{16,24},{20,28},{24,0},{28,4},{1,9},{5... | collective-permute-start | bytes 638984 | tf_op jit(solution)/shard_map/ppermute | solution.py:169
  501.6 14.1 %copy-start.46 = (bf16[104,1024]{1,0:T(8,128)(2,1)}, bf16[104,1024]{1,0:T(8,128)(2,1)S(1)}, u32[]{:S(2)}) copy-start(bf16[104,1024]{1,0:T(8,128)(2,1)S(1)} %collective-permute-done.6) | copy-start | bytes 638980
  501.6 18.2 %collective-permute-start.2 = (bf16[104,1024]{1,0:T(8,128)(2,1)S(1)}, bf16[104,1024]{1,0:T(8,128)(2,1)}, u32[]{:S(2)}, u32[]{:S(2)}) collective-permute-start(bf16[104,1024]{1,0:T(8,128)(2,1)S(1)} %get-tuple-element.570), channel_id=1, source_target_pairs={{0,4},{4,8},{8,12},{12,16},{16,20},{20,24},{24,28},{28,0},{1,5},{5... | collective-permute-start | bytes 638984 | tf_op jit(solution)/shard_map/ppermute | solution.py:169
  512.3 13.0 %copy-start.24 = (f32[512,1024]{1,0:T(8,128)S(1)}, f32[512,1024]{1,0:T(8,128)}, u32[]{:S(2)}) copy-start(f32[512,1024]{1,0:T(8,128)} %copy-done.23) | copy-start | bytes 6291460
  522.6 72.7 %collective-permute-start.9 = (bf16[104,1024]{1,0:T(8,128)(2,1)}, bf16[104,1024]{1,0:T(8,128)(2,1)S(1)}, u32[]{:S(2)}, u32[]{:S(2)}) collective-permute-start(bf16[104,1024]{1,0:T(8,128)(2,1)} %get-tuple-element.555), channel_id=1, source_target_pairs={{0,4},{4,8},{8,12},{12,16},{16,20},{20,24},{24,28},{28,0},{1,5},{5... | collective-permute-start | bytes 638984 | tf_op jit(solution)/shard_map/ppermute | solution.py:177
  589.3 14.7 %collective-permute-start.10 = (bf16[104,1024]{1,0:T(8,128)(2,1)}, bf16[104,1024]{1,0:T(8,128)(2,1)S(1)}, u32[]{:S(2)}, u32[]{:S(2)}) collective-permute-start(bf16[104,1024]{1,0:T(8,128)(2,1)} %get-tuple-element.555), channel_id=1, source_target_pairs={{0,8},{4,12},{8,16},{12,20},{16,24},{20,28},{24,0},{28,4},{1,9},{5... | collective-permute-start | bytes 638984 | tf_op jit(solution)/shard_map/ppermute | solution.py:177
  590.4 35.1 %collective-permute-start.11 = (bf16[104,1024]{1,0:T(8,128)(2,1)}, bf16[104,1024]{1,0:T(8,128)(2,1)S(1)}, u32[]{:S(2)}, u32[]{:S(2)}) collective-permute-start(bf16[104,1024]{1,0:T(8,128)(2,1)} %get-tuple-element.555), channel_id=1, source_target_pairs={{0,12},{4,16},{8,20},{12,24},{16,28},{20,0},{24,4},{28,8},{1,13},{... | collective-permute-start | bytes 638984 | tf_op jit(solution)/shard_map/ppermute | solution.py:177
  592.5 39.4 %collective-permute-start.12 = (bf16[104,1024]{1,0:T(8,128)(2,1)}, bf16[104,1024]{1,0:T(8,128)(2,1)S(1)}, u32[]{:S(2)}, u32[]{:S(2)}) collective-permute-start(bf16[104,1024]{1,0:T(8,128)(2,1)} %get-tuple-element.555), channel_id=1, source_target_pairs={{0,16},{4,20},{8,24},{12,28},{16,0},{20,4},{24,8},{28,12},{1,17},{... | collective-permute-start | bytes 638984 | tf_op jit(solution)/shard_map/ppermute | solution.py:177
  594.6 37.3 %collective-permute-start.13 = (bf16[104,1024]{1,0:T(8,128)(2,1)}, bf16[104,1024]{1,0:T(8,128)(2,1)S(1)}, u32[]{:S(2)}, u32[]{:S(2)}) collective-permute-start(bf16[104,1024]{1,0:T(8,128)(2,1)} %get-tuple-element.555), channel_id=1, source_target_pairs={{0,20},{4,24},{8,28},{12,0},{16,4},{20,8},{24,12},{28,16},{1,21},{... | collective-permute-start | bytes 638984 | tf_op jit(solution)/shard_map/ppermute | solution.py:177
  595.3 36.9 %collective-permute-start.14 = (bf16[104,1024]{1,0:T(8,128)(2,1)}, bf16[104,1024]{1,0:T(8,128)(2,1)S(1)}, u32[]{:S(2)}, u32[]{:S(2)}) collective-permute-start(bf16[104,1024]{1,0:T(8,128)(2,1)} %get-tuple-element.555), channel_id=1, source_target_pairs={{0,24},{4,28},{8,0},{12,4},{16,8},{20,12},{24,16},{28,20},{1,25},{... | collective-permute-start | bytes 638984 | tf_op jit(solution)/shard_map/ppermute | solution.py:177
  604.0 36.1 %collective-permute-start.15 = (bf16[104,1024]{1,0:T(8,128)(2,1)}, bf16[104,1024]{1,0:T(8,128)(2,1)S(1)}, u32[]{:S(2)}, u32[]{:S(2)}) collective-permute-start(bf16[104,1024]{1,0:T(8,128)(2,1)} %get-tuple-element.555), channel_id=1, source_target_pairs={{0,28},{4,0},{8,4},{12,8},{16,12},{20,16},{24,20},{28,24},{1,29},{... | collective-permute-start | bytes 638984 | tf_op jit(solution)/shard_map/ppermute | solution.py:177
  (76 other events, 189.7 us)
Sparse Core Ops, SparseCore 0:
  9.6 49.0 all-gather.5
  60.2 22.5 all-gather.7
  84.4 58.2 all-gather.9
  144.1 58.2 all-gather.11
  447.4 133.2 all-reduce.4
  584.8 146.9 all-reduce.6

commit v6 on v5

--- a/solution.py
+++ b/solution.py
@@ -179,6 +179,23 @@
     return result.reshape(buf.shape)
 
 
+def gather_pieces(piece, axis, size, steps, dim):
+    index = lax.axis_index(axis)
+    results = []
+    buf = piece
+    for step in steps:
+        low = (index // step) % 2 == 0
+        got = lax.ppermute(buf, axis, [(a, a ^ step) for a in range(size)])
+        results.append(got)
+        buf = jnp.concatenate([jnp.where(low, buf, got), jnp.where(low, got, buf)], dim)
+    return buf, results[0]
+
+
+def unpermute(full, order, dim):
+    pieces = jnp.split(full, len(order), dim)
+    return jnp.concatenate([pieces[order.index(k)] for k in range(len(order))], dim)
+
+
 def gather_small(pieces):
     packed = jnp.concatenate(pieces)
     shards = lax.all_gather(packed, "shard", axis=0, tiled=False)
@@ -212,10 +229,19 @@
     full_g1, full_s1, full_qb, full_vb, full_bo, full_g2, full_s2, full_bu, full_bd = gather_small(
         [ln1_gain, ln1_bias, q_bias, v_bias, b_out, ln2_gain, ln2_bias, b_up, b_down]
     )
-    full_qkv = lax.all_gather(w_qkv, "shard", axis=1, tiled=True)
-    full_out = lax.all_gather(w_out, "shard", axis=0, tiled=True)
-    full_up = lax.all_gather(w_up, "shard", axis=1, tiled=True)
-    full_down = lax.all_gather(w_down, "shard", axis=0, tiled=True)
+    shard_steps = bit_steps(shard_count)
+    order = chunk_order(shard_count, shard_steps)
+    gather_steps = shard_steps[::-1]
+    full_qkv, first = gather_pieces(w_qkv, "shard", shard_count, gather_steps, 1)
+    first, w_out = lax.optimization_barrier((first, w_out))
+    full_out, first = gather_pieces(w_out, "shard", shard_count, gather_steps, 0)
+    first, full_qkv, w_up = lax.optimization_barrier((first, full_qkv, w_up))
+    full_up, first = gather_pieces(w_up, "shard", shard_count, gather_steps, 1)
+    first, full_out, w_down = lax.optimization_barrier((first, full_out, w_down))
+    full_down, first = gather_pieces(w_down, "shard", shard_count, gather_steps, 0)
+    full_qkv = unpermute(full_qkv, order, 1)
+    full_out = unpermute(full_out, order, 0)
+    full_bu = reorder_cols(full_bu.reshape(1, -1), order).reshape(-1)
     inputs = tokens[0].astype(jnp.float32)
     _, model_width = inputs.shape
     distance, allowed = layout(cont_segment[0])
@@ -245,8 +271,6 @@
     back_g1, back_qkv, back_out, back_g2, back_up, back_down = (
         full_g1, full_qkv, full_out, full_g2, full_up, full_down
     )
-    shard_steps = bit_steps(shard_count)
-    order = chunk_order(shard_count, shard_steps)
     cot_low = cotangent[0]
     cot_full = cot_low.astype(jnp.float32)
     zero_shift = jnp.zeros((model_width,), jnp.float32)
@@ -254,14 +278,15 @@
     grad_act = jnp.einsum("to,fo->tf", cot_low, back_down, preferred_element_type=jnp.float32)
     _, gelu_pull = jax.vjp(partial(jax.nn.gelu, approximate=True), pre_act)
     grad_pre = gelu_pull(grad_act)[0].astype(jnp.bfloat16)
-    grad_bu = jnp.sum(grad_pre.astype(jnp.float32), 0)
+    grad_bu = jnp.sum(grad_pre.astype(jnp.float32), 0).reshape(1, -1)
+    grad_bu = unpermute(grad_bu, order, 1).reshape(-1)
     grad_down = jnp.einsum(
-        "tf,to->fo", reorder_cols(activated, order), cot_low, preferred_element_type=jnp.float32
+        "tf,to->fo", activated, cot_low, preferred_element_type=jnp.float32
     )
     (down_own,) = halving([grad_down], "shard", shard_count, shard_steps)
     total_a1 = lax.psum(down_own.astype(jnp.bfloat16), "rep")
     grad_up_t = jnp.einsum(
-        "tf,ti->fi", reorder_cols(grad_pre, order), normed_two, preferred_element_type=jnp.float32
+        "tf,ti->fi", grad_pre, normed_two, preferred_element_type=jnp.float32
     )
     grad_normed_two = jnp.einsum("tf,if->ti", grad_pre, back_up, preferred_element_type=jnp.float32)
     _, norm_pull_two = jax.vjp(normalize, middle, back_g2.astype(jnp.float32), zero_shift)

time: 755 us -> 709 us (0.939)
  waiting for transfers between devices: 379 us -> 303 us
  other arithmetic: 81.6 us -> 109 us
  local copies, waits for them, and re-layouts: 91.2 us -> 99 us
    all_gather x4 -> x0, waiting for transfers between devices: 134 us -> none  [the longest x1 48.4 us: body_inner(): full_down = lax.all_gather(w_down, 'shard', axis=0, tiled=True)]
    ppermute x0 -> x8, waiting for transfers between devices: none -> 93.6 us  [gather_pieces(): got = lax.ppermute(buf, axis, [(a, a ^ step) for a in range(size)])]
    psum x1, waiting for transfers between devices: 48.7 us -> 20.9 us  [body_inner(): total_a1 = lax.psum(down_own.astype(jnp.bfloat16), 'rep')]
    select_n x0 -> x8, other arithmetic: none -> 26.4 us  [gather_pieces(): jnp.where(low, buf, got)]
    concatenate x0 -> x7, other arithmetic: none -> 12.8 us  [the longest x6 12.2 us: gather_pieces(): jnp.concatenate([jnp.where(low, buf, got), jnp.where(low, got, buf)], dim)]
    dynamic_slice x28, local copies, waits for them, and re-layouts: 8.84 us -> 20.3 us  [head_slice(): part = lax.dynamic_slice_in_dim(matrix, block * block_width, block_width, 1)]
    ppermute x0 -> x8, starting transfers between devices: none -> 7.88 us  [gather_pieces(): got = lax.ppermute(buf, axis, [(a, a ^ step) for a in range(size)])]
    unnamed x199 -> x222, local copies, waits for them, and re-layouts: 34.7 us -> 31.9 us
  transfers between devices with their start and end apart: 26 -> 30, of which waited for: 17 -> 16; matrix products, arithmetic and copies ran while one was open for 20% -> 37% of each run, Pallas kernels for 0% -> 0%
where the time goes in v6:
time: 709 us; the launch traced here: 703 us
  waiting for transfers between devices  303 us (43%)
  other arithmetic  109 us (15%)
  local copies, waits for them, and re-layouts  99 us (14%)
  matrix products  84.9 us (12%)
  starting transfers between devices  68 us (10%)
  loops' own time  18.8 us (3%)
  between operations  16 us (2%)
    ppermute x8, waiting for transfers between devices, gather_pieces(): got = lax.ppermute(buf, axis, [(a, a ^ step) for a in range(size)])  93.6 us
    psum x1, waiting for transfers between devices, body_inner(): total_a = lax.psum(joined_a, 'rep')  81.5 us
    ppermute x6, waiting for transfers between devices, halving(): lax.ppermute(jnp.concatenate(sends, 0), axis, [(a, a ^ step) for a in ran...  57.1 us
    ppermute x7, starting transfers between devices, direct_reduce(): lax.ppermute(send.astype(jnp.bfloat16), axis, [(a, (a + shift) % size) fo...  38.3 us
    ppermute x7, waiting for transfers between devices, direct_reduce(): lax.ppermute(mine, axis, [(a, (a + shift) % size) for a in range(size)])  36.2 us
    unnamed x222, local copies, waits for them, and re-layouts  31.9 us
    select_n x8, other arithmetic, gather_pieces(): jnp.where(low, buf, got)  26.4 us
    add x7, other arithmetic, halving(): arrays.append(keep + got[offset:offset + keep.shape[0]].astype(jnp.float32))  22.6 us
  transfers between devices with their start and end apart: 30, of which 16 were waited for; matrix products, arithmetic and copies ran while one was open for 37% of the time, Pallas kernels for 0%

profile of v6, /device:TPU:0, one launch (start us, length us, event | category | flops | bytes accessed | tf_op | source)
XLA Modules:
  0.0 703.4 jit_solution(8492846567188163198)
XLA Ops:
  7.2 3.1 collective-permute-start
  10.3 34.7 %collective-permute-done = bf16[1024,768]{1,0:T(8,128)(2,1)} collective-permute-done((bf16[1024,768]{1,0:T(8,128)(2,1)}, bf16[1024,768]{1,0:T(8,128)(2,1)}, u32[]{:S(2)}, u32[]{:S(2)}) %collective-permute-start) | collective-permute-done | bytes 1572896 | tf_op jit(solution)/shard_map/ppermute | solution.py:188
  51.3 5.4 all-gather
  60.2 12.0 %collective-permute-done.1 = bf16[256,1024]{1,0:T(8,128)(2,1)} collective-permute-done((bf16[256,1024]{1,0:T(8,128)(2,1)S(1)}, bf16[256,1024]{1,0:T(8,128)(2,1)}, u32[]{:S(2)}, u32[]{:S(2)}) %collective-permute-start.1) | collective-permute-done | bytes 524320 | tf_op jit(solution)/shard_map/ppermute | solution.py:188
  74.5 3.9 broadcast_select_fusion.5
  78.4 2.6 pad_maximum_fusion.2
  86.5 2.7 fusion.84
  93.3 36.1 %collective-permute-done.3 = bf16[1024,1024]{1,0:T(8,128)(2,1)} collective-permute-done((bf16[1024,1024]{1,0:T(8,128)(2,1)}, bf16[1024,1024]{1,0:T(8,128)(2,1)}, u32[]{:S(2)}, u32[]{:S(2)}) %collective-permute-start.3) | collective-permute-done | bytes 2097184 | tf_op jit(solution)/shard_map/ppermute | solution.py:188
  131.1 2.5 broadcast_select_fusion.9
  133.6 2.7 pad_maximum_fusion.9
  137.2 26.7 %while.32 = (s32[]{:T(128)}, bf16[4,384,256]{1,2,0:T(8,128)(2,1)}, f32[4,4,384]{2,1,0:T(4,128)S(1)}, s32[4]{0:T(128)S(1)}, bf16[384,1024]{0,1:T(8,128)(2,1)}, /*...) while((s32[]{:T(128)}, bf16[4,384,256]{1,2,0:T(8,128)(2,1)}, ...), condition=%wide.region_6.7_spmd.clone, body=%wide.region_3.6_spmd.clone.sunk | while | flops 157776416 | bytes 10964623 | solution.py:74
  166.2 10.8 %collective-permute-done.6 = bf16[1024,1024]{1,0:T(8,128)(2,1)} collective-permute-done((bf16[1024,1024]{1,0:T(8,128)(2,1)}, bf16[1024,1024]{1,0:T(8,128)(2,1)}, u32[]{:S(2)}, u32[]{:S(2)}) %collective-permute-start.6) | collective-permute-done | bytes 2097184 | tf_op jit(solution)/shard_map/ppermute | solution.py:188
  177.0 2.5 broadcast_select_fusion.7
  179.5 2.5 pad_maximum_fusion.10
  185.7 3.9 broadcast_select_fusion.3
  189.6 8.8 %fusion.28 = (bf16[4096,384]{0,1:T(8,128)(2,1)}, f32[384,4096]{1,0:T(8,128)}) fusion(f32[4096]{0:T(1024)S(1)} %maximum_convert_fusion, bf16[1024,2048]{1,0:T(8,128)(2,1)S(1)} %get-tuple-element.583, bf16[1024,2048]{1,0:T(8,128)(2,1)S(1)} %get-tuple-element.582, f32[384,1024]{1,0:T(8,128)S(1)} %get-tuple-element.646, f32[1024]{0:T(1024)S(1)} %bitcast.408, ...), kind=kOutput, calls=%fused_computation.64 | convolution fusion | flops 3255697408 | bytes 19426304 | tf_op jit(solution)/shard_map/dot_general | solution.py:263
  198.5 3.4 copy.114
  201.9 5.7 fusion.101
  207.6 2.7 fusion.37
  212.8 8.4 %broadcast_select_fusion.1 = (bf16[2048,1024]{1,0:T(8,128)(2,1)}, bf16[2048,1024]{1,0:T(8,128)(2,1)}) fusion(bf16[2048,1024]{1,0:T(8,128)(2,1)} %collective-permute-done.7, pred[]{:T(512)S(6)} %eq.69, bf16[1024,1024]{1,0:T(8,128)(2,1)S(1)} %copy-done.14, bf16[1024,1024]{1,0:T(8,128)(2,1)S(1)} %copy-done.12), kind=kLoop, calls=%fused_computation.95 | loop fusion | flops 12582912 | bytes 16777216 | tf_op jit(solution)/shard_map/jit(_where)/select_n | solution.py:190
  221.3 13.4 %convert_reduce_fusion = (f32[4096]{0:T(1024)}, bf16[384,4096]{1,0:T(8,128)(2,1)S(1)}) fusion(f32[384,4096]{1,0:T(8,128)} %get-tuple-element.652, bf16[1,384,1024]{2,1,0:T(8,128)(2,1)S(1)} %copy-done.25, bf16[2048,1024]{1,0:T(8,128)(2,1)} %get-tuple-element.585, bf16[2048,1024]{1,0:T(8,128)(2,1)} %get-tuple-element.584), kind=kOutput, calls=%fused_computation.73 | convolution fusion | flops 3272601600 | bytes 18628608 | tf_op jit(solution)/shard_map/to,fo->tf/dot_general | solution.py:278
  234.7 4.3 multiply_reduce_fusion.1
  239.0 8.5 %fusion.145 = f32[4096,1024]{1,0:T(8,128)} fusion(bf16[384,4096]{1,0:T(8,128)(2,1)S(1)} %get-tuple-element.650, f32[384,1024]{1,0:T(8,128)S(1)} %copy-done.20, f32[1024]{0:T(1024)S(1)} %bitcast.409, f32[1024]{0:T(1024)S(1)} %bitcast.401, f32[384]{0:T(512)S(1)} %fusion.130, f32[384]{0:T(512)S(1)} %broadcast_multiply_fusion), kind=kOutput, calls=%fused_computation.317 | convolution fusion | flops 3223191552 | bytes 21507072 | tf_op jit(solution)/shard_map/tf,ti->fi/dot_general | solution.py:288
  254.1 49.2 %while.33 = (s32[]{:T(128)}, bf16[4,384,256]{1,2,0:T(8,128)(2,1)}, bf16[4,384,256]{1,2,0:T(8,128)(2,1)}, bf16[4,384,256]{1,2,0:T(8,128)(2,1)}, s32[4]{0:T(128)S(...) while((s32[]{:T(128)}, bf16[4,384,256]{1,2,0:T(8,128)(2,1)}, ...), condition=%wide.region_13.14_spmd.clone, body=%wide.region_11.13_spmd.clone.sunk | while | flops 385251872 | bytes 30607116 | solution.py:113
  303.3 2.5 convert_reduce_fusion.4
  308.6 5.6 fusion.146
  325.8 2.3 fusion.93
  330.2 4.0 fusion.38
  334.4 3.0 pad_maximum_fusion.8
  339.9 3.6 fusion.90
  343.6 4.6 copy-done.1
  350.9 6.0 bitcast_add_fusion.1
  360.3 4.4 bitcast_add_fusion.2
  365.1 2.3 copy-done.8
  369.1 6.0 bitcast_add_fusion
  375.1 2.3 bitcast_add_fusion.6
  381.6 25.8 %collective-permute-done.25 = bf16[1024,1024]{1,0:T(8,128)(2,1)} collective-permute-done((bf16[1024,1024]{1,0:T(8,128)(2,1)}, bf16[1024,1024]{1,0:T(8,128)(2,1)}, u32[]{:S(2)}, u32[]{:S(2)}) %collective-permute-start.25) | collective-permute-done | bytes 2097184 | tf_op jit(solution)/shard_map/ppermute | solution.py:155
  407.4 4.9 fusion.40
  412.7 31.3 %collective-permute-done.9 = bf16[832,1024]{1,0:T(8,128)(2,1)} collective-permute-done((bf16[832,1024]{1,0:T(8,128)(2,1)S(1)}, bf16[832,1024]{1,0:T(8,128)(2,1)}, u32[]{:S(2)}, u32[]{:S(2)}) %collective-permute-start.9) | collective-permute-done | bytes 1703968 | tf_op jit(solution)/shard_map/ppermute | solution.py:155
  443.9 2.9 bitcast_add_fusion.5
  449.3 4.6 collective-permute-start.16
  454.3 3.0 collective-permute-start.13
  457.3 3.8 collective-permute-done.16
  462.8 5.0 collective-permute-done.15
  467.8 19.8 %collective-permute-start.11 = (bf16[104,1024]{1,0:T(8,128)(2,1)}, bf16[104,1024]{1,0:T(8,128)(2,1)}, u32[]{:S(2)}, u32[]{:S(2)}) collective-permute-start(bf16[104,1024]{1,0:T(8,128)(2,1)} %get-tuple-element.604), channel_id=1, source_target_pairs={{0,8},{4,12},{8,16},{12,20},{16,24},{20,28},{24,0},{28,4},{1,9},{5... | collective-permute-start | bytes 638984 | tf_op jit(solution)/shard_map/ppermute | solution.py:169
  487.6 8.8 %collective-permute-start.10 = (bf16[104,1024]{1,0:T(8,128)(2,1)}, bf16[104,1024]{1,0:T(8,128)(2,1)}, u32[]{:S(2)}, u32[]{:S(2)}) collective-permute-start(bf16[104,1024]{1,0:T(8,128)(2,1)} %get-tuple-element.598), channel_id=1, source_target_pairs={{0,4},{4,8},{8,12},{12,16},{16,20},{20,24},{24,28},{28,0},{1,5},{5... | collective-permute-start | bytes 638984 | tf_op jit(solution)/shard_map/ppermute | solution.py:169
  496.4 4.6 collective-permute-done.13
  501.1 2.4 bitcast_dynamic-update-slice_fusion.8
  506.4 4.1 fusion.39
  512.2 20.9 %all-reduce.5.cloned.1.call-done = bf16[1024,1024]{1,0:T(8,128)(2,1)} async-done(((bf16[1024,1024]{1,0:T(8,128)(2,1)}), bf16[1024,1024]{1,0:T(8,128)(2,1)}) %all-reduce.5.cloned.1.call-update) | async-done | bytes 2097168 | tf_op jit(solution)/shard_map/psum | solution.py:287
  533.2 10.2 %fusion.83 = bf16[1,384,1024]{2,1,0:T(8,128)(2,1)} fusion(f32[384,1024]{1,0:T(8,128)S(1)} %copy-done.21, bf16[2048,1024]{1,0:T(8,128)(2,1)} %get-tuple-element.585, bf16[2048,1024]{1,0:T(8,128)(2,1)} %get-tuple-element.584, f32[384,4096]{1,0:T(8,128)} %get-tuple-element.652, f32[1024]{0:T(1024)S(1)} %bitcast.411), kind=kOutput, calls=%fused_computation.185 | convolution fusion | flops 3253338112 | bytes 17043456 | tf_op jit(solution)/shard_map/dot_general | solution.py:268
  544.5 2.6 collective-permute-start.19
  547.1 3.2 collective-permute-start.20
  550.3 2.4 collective-permute-start.22
  552.7 5.3 collective-permute-done.18
  558.1 6.0 collective-permute-start.23
  564.1 16.9 %collective-permute-done.19 = bf16[104,1024]{1,0:T(8,128)(2,1)S(1)} collective-permute-done((bf16[104,1024]{1,0:T(8,128)(2,1)}, bf16[104,1024]{1,0:T(8,128)(2,1)S(1)}, u32[]{:S(2)}, u32[]{:S(2)}) %collective-permute-start.19) | collective-permute-done | bytes 213024 | tf_op jit(solution)/shard_map/ppermute | solution.py:177
  581.0 5.0 collective-permute-done.20
  586.6 8.4 %collective-permute-done.23 = bf16[104,1024]{1,0:T(8,128)(2,1)S(1)} collective-permute-done((bf16[104,1024]{1,0:T(8,128)(2,1)}, bf16[104,1024]{1,0:T(8,128)(2,1)S(1)}, u32[]{:S(2)}, u32[]{:S(2)}) %collective-permute-start.23) | collective-permute-done | bytes 213024 | tf_op jit(solution)/shard_map/ppermute | solution.py:177
  595.5 2.4 copy.108
  599.0 4.1 convert_element_type.524
  603.1 81.5 %all-reduce.7.cloned.1.call-done = bf16[1280,1024]{1,0:T(8,128)(2,1)} async-done(((bf16[1280,1024]{1,0:T(8,128)(2,1)}), bf16[1280,1024]{1,0:T(8,128)(2,1)}) %all-reduce.7.cloned.1.call-update) | async-done | bytes 2621456 | tf_op jit(solution)/shard_map/psum | solution.py:307
  684.6 4.0 convert_bitcast_fusion
  688.7 5.3 copy.109
  (487 shorter events, 142.4 us)
Async XLA Ops:
  7.2 526.0 %all-reduce.5.cloned.1.call-start = ((), (), s32[]{:S(2)}) async-start(), calls=%async_computation | async-start | bytes 4194304 | tf_op jit(solution)/shard_map/psum | solution.py:287
  7.2 37.8 %collective-permute-start = (bf16[1024,768]{1,0:T(8,128)(2,1)}, bf16[1024,768]{1,0:T(8,128)(2,1)}, u32[]{:S(2)}, u32[]{:S(2)}) collective-permute-start(bf16[1024,768]{1,0:T(8,128)(2,1)} %param.25), channel_id=1, source_target_pairs={{0,2},{1,3},{2,0},{3,1},{4,6},{5,7},{6,4},{7,5},{8,10},{9,11},{10,... | collective-permute-start | bytes 4718600 | tf_op jit(solution)/shard_map/ppermute | solution.py:188
  47.2 9.5 %copy-start.85 = (s32[1,2,64]{2,1,0:T(2,128)S(1)}, s32[1,2,64]{2,1,0:T(2,128)}, u32[]{:S(2)}) copy-start(s32[1,2,64]{2,1,0:T(2,128)} %param.21) | copy-start | bytes 1540
  47.2 9.9 %copy-start.6 = (bf16[1,384,1024]{2,1,0:T(8,128)(2,1)S(1)}, bf16[1,384,1024]{2,1,0:T(8,128)(2,1)}, u32[]{:S(2)}) copy-start(bf16[1,384,1024]{2,1,0:T(8,128)(2,1)} %param.20) | copy-start | bytes 2359300
  47.2 10.7 %copy-start.54 = (bf16[256,1024]{1,0:T(8,128)(2,1)S(1)}, bf16[256,1024]{1,0:T(8,128)(2,1)}, u32[]{:S(2)}) copy-start(bf16[256,1024]{1,0:T(8,128)(2,1)} %param.28) | copy-start | bytes 1572868
  49.3 25.2 %collective-permute-start.2 = (bf16[1024,1536]{1,0:T(8,128)(2,1)}, bf16[1024,1536]{1,0:T(8,128)(2,1)}, u32[]{:S(2)}, u32[]{:S(2)}) collective-permute-start(bf16[1024,1536]{1,0:T(8,128)(2,1)} %pad_maximum_fusion.15), channel_id=1, source_target_pairs={{0,1},{1,0},{2,3},{3,2},{4,5},{5,4},{6,7},{7,6},{8,9},{9,8},{10,11... | collective-permute-start | bytes 9437192 | tf_op jit(solution)/shard_map/ppermute | solution.py:188
  57.3 29.2 %copy-start.67 = (f32[384]{0:T(512)}, f32[384]{0:T(512)S(1)}, u32[]{:S(2)}) copy-start(f32[384]{0:T(512)S(1)} %broadcast_multiply_fusion.1) | copy-start | bytes 4612
  57.9 14.3 %collective-permute-start.1 = (bf16[256,1024]{1,0:T(8,128)(2,1)S(1)}, bf16[256,1024]{1,0:T(8,128)(2,1)}, u32[]{:S(2)}, u32[]{:S(2)}) collective-permute-start(bf16[256,1024]{1,0:T(8,128)(2,1)S(1)} %copy-done.54), channel_id=1, source_target_pairs={{0,2},{1,3},{2,0},{3,1},{4,6},{5,7},{6,4},{7,5},{8,10},{9,11},{10,... | collective-permute-start | bytes 1572872 | tf_op jit(solution)/shard_map/ppermute | solution.py:188
  59.6 26.9 %copy-start.83 = (f32[1,2,4,128]{3,1,2,0:T(2,128)}, f32[1,2,4,128]{3,1,2,0:T(2,128)S(1)}, u32[]{:S(2)}) copy-start(f32[1,2,4,128]{3,1,2,0:T(2,128)S(1)} %copy.121) | copy-start | bytes 12292
  59.6 26.9 %copy-start.63 = (f32[1,2,4,128]{3,1,2,0:T(2,128)}, f32[1,2,4,128]{3,1,2,0:T(2,128)S(1)}, u32[]{:S(2)}) copy-start(f32[1,2,4,128]{3,1,2,0:T(2,128)S(1)} %copy.120) | copy-start | bytes 12292
  59.8 14.7 %copy-start.16 = (bf16[1024,768]{1,0:T(8,128)(2,1)S(1)}, bf16[1024,768]{1,0:T(8,128)(2,1)}, u32[]{:S(2)}) copy-start(bf16[1024,768]{1,0:T(8,128)(2,1)} %copy-done.15) | copy-start | bytes 4718596
  60.2 18.2 %copy-start.73 = (f32[384]{0:T(512)}, f32[384]{0:T(512)S(1)}, u32[]{:S(2)}) copy-start(f32[384]{0:T(512)S(1)} %fusion.74) | copy-start | bytes 4612
  60.2 26.3 %copy-start.70 = (f32[384]{0:T(512)}, f32[384]{0:T(512)S(1)}, u32[]{:S(2)}) copy-start(f32[384]{0:T(512)S(1)} %fusion.129) | copy-start | bytes 4612
  74.5 8.2 %collective-permute-start.4 = (bf16[512,1024]{1,0:T(8,128)(2,1)}, bf16[512,1024]{1,0:T(8,128)(2,1)}, u32[]{:S(2)}, u32[]{:S(2)}) collective-permute-start(bf16[512,1024]{1,0:T(8,128)(2,1)} %pad_maximum_fusion.27), channel_id=1, source_target_pairs={{0,1},{1,0},{2,3},{3,2},{4,5},{5,4},{6,7},{7,6},{8,9},{9,8},{10,11... | collective-permute-start | bytes 3145736 | tf_op jit(solution)/shard_map/ppermute | solution.py:188
  81.1 48.4 %collective-permute-start.3 = (bf16[1024,1024]{1,0:T(8,128)(2,1)}, bf16[1024,1024]{1,0:T(8,128)(2,1)}, u32[]{:S(2)}, u32[]{:S(2)}) collective-permute-start(bf16[1024,1024]{1,0:T(8,128)(2,1)} %param.32), channel_id=1, source_target_pairs={{0,2},{1,3},{2,0},{3,1},{4,6},{5,7},{6,4},{7,5},{8,10},{9,11},{10,... | collective-permute-start | bytes 6291464 | tf_op jit(solution)/shard_map/ppermute | solution.py:188
  129.5 47.5 %collective-permute-start.6 = (bf16[1024,1024]{1,0:T(8,128)(2,1)}, bf16[1024,1024]{1,0:T(8,128)(2,1)}, u32[]{:S(2)}, u32[]{:S(2)}) collective-permute-start(bf16[1024,1024]{1,0:T(8,128)(2,1)} %param.34), channel_id=1, source_target_pairs={{0,2},{1,3},{2,0},{3,1},{4,6},{5,7},{6,4},{7,5},{8,10},{9,11},{10,... | collective-permute-start | bytes 6291464 | tf_op jit(solution)/shard_map/ppermute | solution.py:188
  136.3 49.3 %collective-permute-start.5 = (bf16[1024,2048]{1,0:T(8,128)(2,1)}, bf16[1024,2048]{1,0:T(8,128)(2,1)}, u32[]{:S(2)}, u32[]{:S(2)}) collective-permute-start(bf16[1024,2048]{1,0:T(8,128)(2,1)} %pad_maximum_fusion.9), channel_id=1, source_target_pairs={{0,1},{1,0},{2,3},{3,2},{4,5},{5,4},{6,7},{7,6},{8,9},{9,8},{10,11... | collective-permute-start | bytes 12582920 | tf_op jit(solution)/shard_map/ppermute | solution.py:188
  182.9 27.8 %collective-permute-start.7 = (bf16[2048,1024]{1,0:T(8,128)(2,1)}, bf16[2048,1024]{1,0:T(8,128)(2,1)}, u32[]{:S(2)}, u32[]{:S(2)}) collective-permute-start(bf16[2048,1024]{1,0:T(8,128)(2,1)} %pad_maximum_fusion.10), channel_id=1, source_target_pairs={{0,1},{1,0},{2,3},{3,2},{4,5},{5,4},{6,7},{7,6},{8,9},{9,8},{10,11... | collective-permute-start | bytes 12582920 | tf_op jit(solution)/shard_map/ppermute | solution.py:188
  189.6 8.9 %copy-start.31 = (bf16[1024,2048]{1,0:T(8,128)(2,1)}, bf16[1024,2048]{1,0:T(8,128)(2,1)S(1)}, u32[]{:S(2)}) copy-start(bf16[1024,2048]{1,0:T(8,128)(2,1)S(1)} %get-tuple-element.582) | copy-start | bytes 12582916
  189.6 8.9 %copy-start.33 = (bf16[1024,2048]{1,0:T(8,128)(2,1)}, bf16[1024,2048]{1,0:T(8,128)(2,1)S(1)}, u32[]{:S(2)}) copy-start(bf16[1024,2048]{1,0:T(8,128)(2,1)S(1)} %get-tuple-element.583) | copy-start | bytes 12582916
  207.6 13.6 %copy-start = (f32[2,2048,1024]{2,1,0:T(8,128)}, f32[2,2048,1024]{2,1,0:T(8,128)S(1)}, u32[]{:S(2)}) copy-start(f32[2,2048,1024]{2,1,0:T(8,128)S(1)} %fusion.101) | copy-start | bytes 50331652
  210.3 10.9 %copy-start.25 = (bf16[1,384,1024]{2,1,0:T(8,128)(2,1)S(1)}, bf16[1,384,1024]{2,1,0:T(8,128)(2,1)}, u32[]{:S(2)}) copy-start(bf16[1,384,1024]{2,1,0:T(8,128)(2,1)} %param.22) | copy-start | bytes 2359300
  210.3 140.6 %collective-permute-start.24 = (bf16[2048,1024]{1,0:T(8,128)(2,1)}, bf16[2048,1024]{1,0:T(8,128)(2,1)}, u32[]{:S(2)}, u32[]{:S(2)}) collective-permute-start(bf16[2048,1024]{1,0:T(8,128)(2,1)} %fusion.37), channel_id=1, source_target_pairs={{0,1},{1,0},{2,3},{3,2},{4,5},{5,4},{6,7},{7,6},{8,9},{9,8},{10,11... | collective-permute-start | bytes 12582920 | tf_op jit(solution)/shard_map/ppermute | solution.py:155
  221.2 13.4 %copy-start.20 = (f32[384,1024]{1,0:T(8,128)S(1)}, f32[384,1024]{1,0:T(8,128)}, u32[]{:S(2)}) copy-start(f32[384,1024]{1,0:T(8,128)} %copy-done.19) | copy-start | bytes 4718596
  221.2 13.4 %copy-start.32 = (bf16[1024,2048]{1,0:T(8,128)(2,1)S(1)}, bf16[1024,2048]{1,0:T(8,128)(2,1)}, u32[]{:S(2)}) copy-start(bf16[1024,2048]{1,0:T(8,128)(2,1)} %copy-done.31) | copy-start | bytes 12582916
  221.3 13.4 %copy-start.34 = (bf16[1024,2048]{1,0:T(8,128)(2,1)S(1)}, bf16[1024,2048]{1,0:T(8,128)(2,1)}, u32[]{:S(2)}) copy-start(bf16[1024,2048]{1,0:T(8,128)(2,1)} %copy-done.33) | copy-start | bytes 12582916
  303.2 5.3 copy-start.7
  303.2 5.3 copy-start.23
  303.2 5.3 copy-start.40
  303.3 5.3 copy-start.64
  308.6 5.6 copy-start.74
  308.6 5.6 copy-start.71
  315.8 10.0 %copy-start.38 = (bf16[384,1024]{1,0:T(8,128)(2,1)S(1)}, bf16[384,1024]{1,0:T(8,128)(2,1)}, u32[]{:S(2)}) copy-start(bf16[384,1024]{1,0:T(8,128)(2,1)} %copy-done.37) | copy-start | bytes 2359300
  315.8 10.0 %copy-start.52 = (bf16[384,256]{0,1:T(8,128)(2,1)S(1)}, bf16[384,256]{0,1:T(8,128)(2,1)}, u32[]{:S(2)}) copy-start(bf16[384,256]{0,1:T(8,128)(2,1)} %get-tuple-element.615) | copy-start | bytes 589828
  315.8 10.0 %copy-start.53 = (bf16[384,256]{0,1:T(8,128)(2,1)S(1)}, bf16[384,256]{0,1:T(8,128)(2,1)}, u32[]{:S(2)}) copy-start(bf16[384,256]{0,1:T(8,128)(2,1)} %get-tuple-element.616) | copy-start | bytes 589828
  337.4 31.7 %collective-permute-start.26 = (bf16[2560,1024]{1,0:T(8,128)(2,1)}, bf16[2560,1024]{1,0:T(8,128)(2,1)}, u32[]{:S(2)}, u32[]{:S(2)}) collective-permute-start(bf16[2560,1024]{1,0:T(8,128)(2,1)} %pad_maximum_fusion.8), channel_id=1, source_target_pairs={{0,1},{1,0},{2,3},{3,2},{4,5},{5,4},{6,7},{7,6},{8,9},{9,8},{10,11... | collective-permute-start | bytes 15728648 | tf_op jit(solution)/shard_map/ppermute | solution.py:155
  339.6 9.1 %copy-start.35 = (f32[256,1024]{1,0:T(8,128)}, f32[256,1024]{1,0:T(8,128)S(1)}, u32[]{:S(2)}) copy-start(f32[256,1024]{1,0:T(8,128)S(1)} %pad_maximum_fusion.28) | copy-start | bytes 3145732
  350.8 9.4 %collective-permute-start.8 = (bf16[1664,1024]{1,0:T(8,128)(2,1)}, bf16[1664,1024]{1,0:T(8,128)(2,1)S(1)}, u32[]{:S(2)}, u32[]{:S(2)}) collective-permute-start(bf16[1664,1024]{1,0:T(8,128)(2,1)} %pad_maximum_fusion.11), channel_id=1, source_target_pairs={{0,1},{1,0},{2,3},{3,2},{4,5},{5,4},{6,7},{7,6},{8,9},{9,8},{10,11... | collective-permute-start | bytes 10223624 | tf_op jit(solution)/shard_map/ppermute | solution.py:155
  356.9 7.8 %copy-start.5 = (f32[2048,1024]{1,0:T(8,128)}, f32[2048,1024]{1,0:T(8,128)S(1)}, u32[]{:S(2)}) copy-start(f32[2048,1024]{1,0:T(8,128)S(1)} %bitcast_add_fusion.1) | copy-start | bytes 25165828
  358.6 48.8 %collective-permute-start.25 = (bf16[1024,1024]{1,0:T(8,128)(2,1)}, bf16[1024,1024]{1,0:T(8,128)(2,1)}, u32[]{:S(2)}, u32[]{:S(2)}) collective-permute-start(bf16[1024,1024]{1,0:T(8,128)(2,1)} %fusion.61), channel_id=1, source_target_pairs={{0,2},{1,3},{2,0},{3,1},{4,6},{5,7},{6,4},{7,5},{8,10},{9,11},{10,... | collective-permute-start | bytes 6291464 | tf_op jit(solution)/shard_map/ppermute | solution.py:155
  367.4 7.7 %copy-start.3 = (f32[1024,1024]{1,0:T(8,128)S(1)}, f32[1024,1024]{1,0:T(8,128)}, u32[]{:S(2)}) copy-start(f32[1024,1024]{1,0:T(8,128)} %copy-done.2) | copy-start | bytes 12582916
  367.4 76.5 %collective-permute-start.9 = (bf16[832,1024]{1,0:T(8,128)(2,1)S(1)}, bf16[832,1024]{1,0:T(8,128)(2,1)}, u32[]{:S(2)}, u32[]{:S(2)}) collective-permute-start(bf16[832,1024]{1,0:T(8,128)(2,1)S(1)} %pad_maximum_fusion.20), channel_id=1, source_target_pairs={{0,2},{1,3},{2,0},{3,1},{4,6},{5,7},{6,4},{7,5},{8,10},{9,11},{10,... | collective-permute-start | bytes 5111816 | tf_op jit(solution)/shard_map/ppermute | solution.py:155
  375.1 6.0 copy-start.4
  381.1 124.0 %collective-permute-start.27 = (bf16[1280,1024]{1,0:T(8,128)(2,1)}, bf16[1280,1024]{1,0:T(8,128)(2,1)}, u32[]{:S(2)}, u32[]{:S(2)}) collective-permute-start(bf16[1280,1024]{1,0:T(8,128)(2,1)} %pad_maximum_fusion.16), channel_id=1, source_target_pairs={{0,2},{1,3},{2,0},{3,1},{4,6},{5,7},{6,4},{7,5},{8,10},{9,11},{10,... | collective-permute-start | bytes 7864328 | tf_op jit(solution)/shard_map/ppermute | solution.py:155
  412.3 34.5 %copy-start.45 = (f32[128,1024]{1,0:T(8,128)S(1)}, f32[128,1024]{1,0:T(8,128)}, u32[]{:S(2)}) copy-start(f32[128,1024]{1,0:T(8,128)} %copy-done.44) | copy-start | bytes 1572868
  412.4 272.3 %all-reduce.7.cloned.1.call-start = ((), (), s32[]{:S(2)}) async-start(), calls=%async_computation.1 | async-start | bytes 5242880 | tf_op jit(solution)/shard_map/psum | solution.py:307
  448.2 48.2 %copy-start.77 = (f32[1,2,4,128]{3,2,1,0:T(4,128)S(1)}, f32[1,2,4,128]{3,2,1,0:T(4,128)}, u32[]{:S(2)}) copy-start(f32[1,2,4,128]{3,2,1,0:T(4,128)} %get-tuple-element.633) | copy-start | bytes 12292
  449.3 11.8 %collective-permute-start.16 = (bf16[104,1024]{1,0:T(8,128)(2,1)S(1)}, bf16[104,1024]{1,0:T(8,128)(2,1)}, u32[]{:S(2)}, u32[]{:S(2)}) collective-permute-start(bf16[104,1024]{1,0:T(8,128)(2,1)S(1)} %get-tuple-element.599), channel_id=1, source_target_pairs={{0,28},{4,0},{8,4},{12,8},{16,12},{20,16},{24,20},{28,24},{1,29},{... | collective-permute-start | bytes 638984 | tf_op jit(solution)/shard_map/ppermute | solution.py:169
  453.8 14.0 %collective-permute-start.15 = (bf16[104,1024]{1,0:T(8,128)(2,1)S(1)}, bf16[104,1024]{1,0:T(8,128)(2,1)}, u32[]{:S(2)}, u32[]{:S(2)}) collective-permute-start(bf16[104,1024]{1,0:T(8,128)(2,1)S(1)} %get-tuple-element.600), channel_id=1, source_target_pairs={{0,24},{4,28},{8,0},{12,4},{16,8},{20,12},{24,16},{28,20},{1,25},{... | collective-permute-start | bytes 638984 | tf_op jit(solution)/shard_map/ppermute | solution.py:169
  454.3 33.3 %collective-permute-start.14 = (bf16[104,1024]{1,0:T(8,128)(2,1)S(1)}, bf16[104,1024]{1,0:T(8,128)(2,1)}, u32[]{:S(2)}, u32[]{:S(2)}) collective-permute-start(bf16[104,1024]{1,0:T(8,128)(2,1)S(1)} %get-tuple-element.601), channel_id=1, source_target_pairs={{0,20},{4,24},{8,28},{12,0},{16,4},{20,8},{24,12},{28,16},{1,21},{... | collective-permute-start | bytes 638984 | tf_op jit(solution)/shard_map/ppermute | solution.py:169
  454.3 46.6 %collective-permute-start.13 = (bf16[104,1024]{1,0:T(8,128)(2,1)}, bf16[104,1024]{1,0:T(8,128)(2,1)}, u32[]{:S(2)}, u32[]{:S(2)}) collective-permute-start(bf16[104,1024]{1,0:T(8,128)(2,1)} %get-tuple-element.602), channel_id=1, source_target_pairs={{0,16},{4,20},{8,24},{12,28},{16,0},{20,4},{24,8},{28,12},{1,17},{... | collective-permute-start | bytes 638984 | tf_op jit(solution)/shard_map/ppermute | solution.py:169
  461.1 39.9 %collective-permute-start.12 = (bf16[104,1024]{1,0:T(8,128)(2,1)}, bf16[104,1024]{1,0:T(8,128)(2,1)}, u32[]{:S(2)}, u32[]{:S(2)}) collective-permute-start(bf16[104,1024]{1,0:T(8,128)(2,1)} %get-tuple-element.603), channel_id=1, source_target_pairs={{0,12},{4,16},{8,20},{12,24},{16,28},{20,0},{24,4},{28,8},{1,13},{... | collective-permute-start | bytes 638984 | tf_op jit(solution)/shard_map/ppermute | solution.py:169
  467.8 33.1 %collective-permute-start.11 = (bf16[104,1024]{1,0:T(8,128)(2,1)}, bf16[104,1024]{1,0:T(8,128)(2,1)}, u32[]{:S(2)}, u32[]{:S(2)}) collective-permute-start(bf16[104,1024]{1,0:T(8,128)(2,1)} %get-tuple-element.604), channel_id=1, source_target_pairs={{0,8},{4,12},{8,16},{12,20},{16,24},{20,28},{24,0},{28,4},{1,9},{5... | collective-permute-start | bytes 638984 | tf_op jit(solution)/shard_map/ppermute | solution.py:169
  487.6 13.3 %collective-permute-start.10 = (bf16[104,1024]{1,0:T(8,128)(2,1)}, bf16[104,1024]{1,0:T(8,128)(2,1)}, u32[]{:S(2)}, u32[]{:S(2)}) collective-permute-start(bf16[104,1024]{1,0:T(8,128)(2,1)} %get-tuple-element.598), channel_id=1, source_target_pairs={{0,4},{4,8},{8,12},{12,16},{16,20},{20,24},{24,28},{28,0},{1,5},{5... | collective-permute-start | bytes 638984 | tf_op jit(solution)/shard_map/ppermute | solution.py:169
  496.4 8.8 %copy-start.30 = (f32[512,1024]{1,0:T(8,128)S(1)}, f32[512,1024]{1,0:T(8,128)}, u32[]{:S(2)}) copy-start(f32[512,1024]{1,0:T(8,128)} %copy-done.29) | copy-start | bytes 6291460
  503.5 46.8 %collective-permute-start.17 = (bf16[104,1024]{1,0:T(8,128)(2,1)}, bf16[104,1024]{1,0:T(8,128)(2,1)S(1)}, u32[]{:S(2)}, u32[]{:S(2)}) collective-permute-start(bf16[104,1024]{1,0:T(8,128)(2,1)} %get-tuple-element.569), channel_id=1, source_target_pairs={{0,4},{4,8},{8,12},{12,16},{16,20},{20,24},{24,28},{28,0},{1,5},{5... | collective-permute-start | bytes 638984 | tf_op jit(solution)/shard_map/ppermute | solution.py:177
  512.2 21.0 %copy-start.21 = (f32[384,1024]{1,0:T(8,128)S(1)}, f32[384,1024]{1,0:T(8,128)}, u32[]{:S(2)}) copy-start(f32[384,1024]{1,0:T(8,128)} %copy-done.19) | copy-start | bytes 4718596
  533.2 19.5 %copy-start.28 = (bf16[8,104,1024]{2,1,0:T(8,128)(2,1)S(1)}, bf16[8,104,1024]{2,1,0:T(8,128)(2,1)}, u32[]{:S(2)}) copy-start(bf16[8,104,1024]{2,1,0:T(8,128)(2,1)} %copy-done.27) | copy-start | bytes 5111812
  543.4 14.7 %collective-permute-start.18 = (bf16[104,1024]{1,0:T(8,128)(2,1)}, bf16[104,1024]{1,0:T(8,128)(2,1)S(1)}, u32[]{:S(2)}, u32[]{:S(2)}) collective-permute-start(bf16[104,1024]{1,0:T(8,128)(2,1)} %get-tuple-element.569), channel_id=1, source_target_pairs={{0,8},{4,12},{8,16},{12,20},{16,24},{20,28},{24,0},{28,4},{1,9},{5... | collective-permute-start | bytes 638984 | tf_op jit(solution)/shard_map/ppermute | solution.py:177
  544.5 36.5 %collective-permute-start.19 = (bf16[104,1024]{1,0:T(8,128)(2,1)}, bf16[104,1024]{1,0:T(8,128)(2,1)S(1)}, u32[]{:S(2)}, u32[]{:S(2)}) collective-permute-start(bf16[104,1024]{1,0:T(8,128)(2,1)} %get-tuple-element.569), channel_id=1, source_target_pairs={{0,12},{4,16},{8,20},{12,24},{16,28},{20,0},{24,4},{28,8},{1,13},{... | collective-permute-start | bytes 638984 | tf_op jit(solution)/shard_map/ppermute | solution.py:177
  547.1 38.9 %collective-permute-start.20 = (bf16[104,1024]{1,0:T(8,128)(2,1)}, bf16[104,1024]{1,0:T(8,128)(2,1)S(1)}, u32[]{:S(2)}, u32[]{:S(2)}) collective-permute-start(bf16[104,1024]{1,0:T(8,128)(2,1)} %get-tuple-element.569), channel_id=1, source_target_pairs={{0,16},{4,20},{8,24},{12,28},{16,0},{20,4},{24,8},{28,12},{1,17},{... | collective-permute-start | bytes 638984 | tf_op jit(solution)/shard_map/ppermute | solution.py:177
  550.3 35.7 %collective-permute-start.21 = (bf16[104,1024]{1,0:T(8,128)(2,1)}, bf16[104,1024]{1,0:T(8,128)(2,1)S(1)}, u32[]{:S(2)}, u32[]{:S(2)}) collective-permute-start(bf16[104,1024]{1,0:T(8,128)(2,1)} %get-tuple-element.569), channel_id=1, source_target_pairs={{0,20},{4,24},{8,28},{12,0},{16,4},{20,8},{24,12},{28,16},{1,21},{... | collective-permute-start | bytes 638984 | tf_op jit(solution)/shard_map/ppermute | solution.py:177
  550.3 36.2 %collective-permute-start.22 = (bf16[104,1024]{1,0:T(8,128)(2,1)}, bf16[104,1024]{1,0:T(8,128)(2,1)S(1)}, u32[]{:S(2)}, u32[]{:S(2)}) collective-permute-start(bf16[104,1024]{1,0:T(8,128)(2,1)} %get-tuple-element.569), channel_id=1, source_target_pairs={{0,24},{4,28},{8,0},{12,4},{16,8},{20,12},{24,16},{28,20},{1,25},{... | collective-permute-start | bytes 638984 | tf_op jit(solution)/shard_map/ppermute | solution.py:177
  558.1 36.9 %collective-permute-start.23 = (bf16[104,1024]{1,0:T(8,128)(2,1)}, bf16[104,1024]{1,0:T(8,128)(2,1)S(1)}, u32[]{:S(2)}, u32[]{:S(2)}) collective-permute-start(bf16[104,1024]{1,0:T(8,128)(2,1)} %get-tuple-element.569), channel_id=1, source_target_pairs={{0,28},{4,0},{8,4},{12,8},{16,12},{20,16},{24,20},{28,24},{1,29},{... | collective-permute-start | bytes 638984 | tf_op jit(solution)/shard_map/ppermute | solution.py:177
  (67 other events, 180.3 us)
Sparse Core Ops, SparseCore 0:
  412.5 120.6 all-reduce.4
  536.8 147.7 all-reduce.6

commit v7 on v5

--- a/solution.py
+++ b/solution.py
@@ -71,7 +71,9 @@
         mixed = jnp.einsum("hqk,khd->qhd", attn_probs, v_part, preferred_element_type=jnp.float32)
         return (mixed.reshape(length, 4 * HDIM), (peak + jnp.log(row_totals))[:, :, 0])
 
-    mixed, log_norms = lax.map(head_block, jnp.arange(HEADS // 4, dtype=jnp.int32))
+    blocks = [head_block(block) for block in range(HEADS // 4)]
+    mixed = jnp.stack([b[0] for b in blocks])
+    log_norms = jnp.stack([b[1] for b in blocks])
     return (side_by_side(mixed).astype(jnp.bfloat16), log_norms)
 
 
@@ -110,7 +112,8 @@
             grad_v.reshape(length, block_width),
         )
 
-    grad_q, grad_k, grad_v = lax.map(head_block, jnp.arange(HEADS // 4, dtype=jnp.int32))
+    blocks = [head_block(block) for block in range(HEADS // 4)]
+    grad_q, grad_k, grad_v = (jnp.stack([b[i] for b in blocks]) for i in range(3))
     return (
         side_by_side(grad_q).astype(jnp.bfloat16),
         side_by_side(grad_k).astype(jnp.bfloat16),

time: 755 us -> 730 us (0.967)
  loops' own time: 19.5 us -> 0 us
  local copies, waits for them, and re-layouts: 91.2 us -> 77.8 us
  matrix products: 92.1 us -> 104 us
    another operation x2 -> x0, loops' own time: 19.5 us -> none  [the longest x1 14.1 us: attend_backward(): lax.map(head_block, jnp.arange(HEADS // 4, dtype=jnp.int32))]
    dynamic_update_slice x12 -> x0, local copies, waits for them, and re-layouts: 8.76 us -> none  [attend_forward(): lax.map(head_block, jnp.arange(HEADS // 4, dtype=jnp.int32))]
    dot_general x4, matrix products: 2.16 us -> 9.72 us  [head_block(): jnp.einsum('hqk,qhd->khd', attn_probs.astype(jnp.bfloat16), g_part, prefe...]
    unnamed x199 -> x324, local copies, waits for them, and re-layouts: 34.7 us -> 41.3 us
  transfers between devices with their start and end apart: 26 -> 26, of which waited for: 17 -> 18; matrix products, arithmetic and copies ran while one was open for 20% -> 21% of each run, Pallas kernels for 0% -> 0%
where the time goes in v7:
time: 730 us; the launch traced here: 726 us
  waiting for transfers between devices  378 us (52%)
  matrix products  104 us (14%)
  other arithmetic  79.5 us (11%)
  local copies, waits for them, and re-layouts  77.8 us (11%)
  starting transfers between devices  64.5 us (9%)
  between operations  16.4 us (2%)
    psum x1, waiting for transfers between devices, body_inner(): total_a = lax.psum(joined_a, 'rep')  81 us
    ppermute x6, waiting for transfers between devices, halving(): lax.ppermute(jnp.concatenate(sends, 0), axis, [(a, a ^ step) for a in ran...  54.5 us
    all_gather x1, waiting for transfers between devices, body_inner(): full_up = lax.all_gather(w_up, 'shard', axis=1, tiled=True)  52.6 us
    psum x1, waiting for transfers between devices, body_inner(): total_a1 = lax.psum(down_own.astype(jnp.bfloat16), 'rep')  48.7 us
    all_gather x1, waiting for transfers between devices, body_inner(): full_down = lax.all_gather(w_down, 'shard', axis=0, tiled=True)  46 us
    ppermute x7, starting transfers between devices, direct_reduce(): lax.ppermute(send.astype(jnp.bfloat16), axis, [(a, (a + shift) % size) fo...  44.6 us
    unnamed x324, local copies, waits for them, and re-layouts  41.3 us
    ppermute x7, waiting for transfers between devices, direct_reduce(): lax.ppermute(mine, axis, [(a, (a + shift) % size) for a in range(size)])  38.2 us
  transfers between devices with their start and end apart: 26, of which 18 were waited for; matrix products, arithmetic and copies ran while one was open for 21% of the time, Pallas kernels for 0%

profile of v7, /device:TPU:0, one launch (start us, length us, event | category | flops | bytes accessed | tf_op | source)
XLA Modules:
  0.0 725.9 jit_solution(9637894228335845173)
XLA Ops:
  12.2 6.6 all-gather
  25.7 33.0 %all-gather.6.cloned.1.call-done = bf16[1024,3072]{1,0:T(8,128)(2,1)} async-done(((bf16[1024,768]{1,0:T(8,128)(2,1)}), bf16[1024,3072]{1,0:T(8,128)(2,1)}) %all-gather.6.cloned.1.call-update) | async-done | bytes 6291472 | tf_op jit(solution)/shard_map/all_gather | solution.py:218
  58.7 6.9 fusion.159
  82.9 3.5 fusion.164
  90.1 52.6 %all-gather.10.cloned.1.call-done = bf16[1024,4096]{1,0:T(8,128)(2,1)} async-done(((bf16[1024,1024]{1,0:T(8,128)(2,1)}), bf16[1024,4096]{1,0:T(8,128)(2,1)}) %all-gather.10.cloned.1.call-update) | async-done | bytes 8388624 | tf_op jit(solution)/shard_map/all_gather | solution.py:220
  142.8 13.7 %multiply_convert_fusion = (bf16[384,4096]{1,0:T(8,128)(2,1)}, f32[384,4096]{1,0:T(8,128)}) fusion(f32[4096]{0:T(1024)S(1)} %bitcast.444, bf16[1024,4096]{1,0:T(8,128)(2,1)} %all-gather.10.cloned.1.call-done, f32[384,1024]{1,0:T(8,128)} %copy-done.16, f32[1024]{0:T(1024)S(1)} %bitcast.451, f32[1024]{0:T(1024)S(1)} %bitcast.445, f32[384]{0:T(512)S(1)} %fusion.142, ...), kind=kOutput, calls=%fused_computation.20 | convolution fusion | flops 3238920192 | bytes 19426304 | tf_op jit(solution)/shard_map/dot_general | solution.py:240
  156.5 46.0 %all-gather.12.cloned.1.call-done = bf16[4096,1024]{1,0:T(8,128)(2,1)} async-done(((bf16[1024,1024]{1,0:T(8,128)(2,1)}), bf16[4096,1024]{1,0:T(8,128)(2,1)}) %all-gather.12.cloned.1.call-update) | async-done | bytes 8388624 | tf_op jit(solution)/shard_map/all_gather | solution.py:221
  202.5 11.3 %convert_reduce_fusion = (f32[4096]{0:T(1024)}, bf16[384,4096]{1,0:T(8,128)(2,1)S(1)}) fusion(f32[384,4096]{1,0:T(8,128)} %get-tuple-element.168, bf16[4096,1024]{1,0:T(8,128)(2,1)} %all-gather.12.cloned.1.call-done, bf16[1,384,1024]{2,1,0:T(8,128)(2,1)} %param.18), kind=kOutput, calls=%fused_computation.18 | convolution fusion | flops 3255824384 | bytes 18628608 | tf_op jit(solution)/shard_map/to,fo->tf/dot_general | solution.py:257
  213.8 4.3 multiply_reduce_fusion.4
  224.0 3.1 fusion.68
  227.0 2.5 multiply_reduce_fusion
  230.7 3.1 fusion.70
  233.8 2.5 multiply_reduce_fusion.1
  237.4 3.1 fusion.72
  240.5 2.5 multiply_reduce_fusion.2
  261.3 2.9 fusion.147
  269.7 3.6 fusion.97
  274.6 3.6 copy-done
  278.8 2.1 pad_maximum_fusion.1
  284.1 3.4 copy.226
  287.6 9.3 %fusion.109 = f32[2,2048,1024]{2,1,0:T(8,128)} fusion(bf16[2,2048,384]{2,1,0:T(8,128)(2,1)S(1)} %bitcast.351, bf16[1,384,1024]{2,1,0:T(8,128)(2,1)} %param.18), kind=kOutput, calls=%fused_computation.197 | convolution fusion | flops 3221225472 | bytes 20709376 | tf_op jit(solution)/shard_map/tf,to->fo/dot_general | solution.py:261
  298.3 2.0 copy-done.11
  300.6 9.5 %fusion.18 = f32[4096,1024]{1,0:T(8,128)} fusion(bf16[384,1024]{1,0:T(8,128)(2,1)S(1)} %copy-done.50, bf16[384,1024]{1,0:T(8,128)(2,1)S(1)} %copy-done.51, bf16[384,1024]{1,0:T(8,128)(2,1)S(1)} %copy-done.52, bf16[384,1024]{1,0:T(8,128)(2,1)S(1)} %copy-done.49, f32[384,1024]{1,0:T(8,128)S(1)} %copy-done.18, f32[1024]{0:T(1024)S(1)} %bitcast.452, ...), kind=kOutput, calls=%fused_computation.42 | convolution fusion | flops 3235774464 | bytes 21507072 | tf_op jit(solution)/shard_map/tf,ti->fi/dot_general | solution.py:266
  310.1 4.0 fusion.10
  314.2 2.8 pad_maximum_fusion
  317.2 6.1 fusion.9
  325.5 4.7 bitcast_add_fusion.2
  330.6 2.2 copy-done.15
  333.1 6.0 bitcast_add_fusion.1
  346.2 6.6 bitcast_add_fusion
  353.1 2.1 pad_maximum_fusion.3
  358.6 14.3 %collective-permute-done.1 = bf16[832,1024]{1,0:T(8,128)(2,1)} collective-permute-done((bf16[832,1024]{1,0:T(8,128)(2,1)S(1)}, bf16[832,1024]{1,0:T(8,128)(2,1)}, u32[]{:S(2)}, u32[]{:S(2)}) %collective-permute-start.1) | collective-permute-done | bytes 1703968 | tf_op jit(solution)/shard_map/ppermute | solution.py:158
  372.9 4.8 bitcast_add_fusion.5
  377.7 40.1 %collective-permute-done.17 = bf16[1024,1024]{1,0:T(8,128)(2,1)} collective-permute-done((bf16[1024,1024]{1,0:T(8,128)(2,1)}, bf16[1024,1024]{1,0:T(8,128)(2,1)}, u32[]{:S(2)}, u32[]{:S(2)}) %collective-permute-start.17) | collective-permute-done | bytes 2097184 | tf_op jit(solution)/shard_map/ppermute | solution.py:158
  417.9 4.9 fusion.12
  423.8 2.2 pad_maximum_fusion.2
  428.6 4.2 collective-permute-start.8
  433.4 2.9 collective-permute-start.5
  436.3 6.7 collective-permute-done.8
  443.0 4.6 collective-permute-start.4
  447.6 7.9 %collective-permute-done.7 = bf16[104,1024]{1,0:T(8,128)(2,1)S(1)} collective-permute-done((bf16[104,1024]{1,0:T(8,128)(2,1)S(1)}, bf16[104,1024]{1,0:T(8,128)(2,1)S(1)}, u32[]{:S(2)}, u32[]{:S(2)}) %collective-permute-start.7) | collective-permute-done | bytes 213024 | tf_op jit(solution)/shard_map/ppermute | solution.py:172
  455.5 21.6 %collective-permute-start.3 = (bf16[104,1024]{1,0:T(8,128)(2,1)S(1)}, bf16[104,1024]{1,0:T(8,128)(2,1)S(1)}, u32[]{:S(2)}, u32[]{:S(2)}) collective-permute-start(bf16[104,1024]{1,0:T(8,128)(2,1)S(1)} %get-tuple-element.104), channel_id=1, source_target_pairs={{0,8},{4,12},{8,16},{12,20},{16,24},{20,28},{24,0},{28,4},{1,9},{5... | collective-permute-start | bytes 638984 | tf_op jit(solution)/shard_map/ppermute | solution.py:172
  477.1 10.7 %collective-permute-start.2 = (bf16[104,1024]{1,0:T(8,128)(2,1)S(1)}, bf16[104,1024]{1,0:T(8,128)(2,1)}, u32[]{:S(2)}, u32[]{:S(2)}) collective-permute-start(bf16[104,1024]{1,0:T(8,128)(2,1)S(1)} %get-tuple-element.98), channel_id=1, source_target_pairs={{0,4},{4,8},{8,12},{12,16},{16,20},{20,24},{24,28},{28,0},{1,5},{5... | collective-permute-start | bytes 638984 | tf_op jit(solution)/shard_map/ppermute | solution.py:172
  487.9 2.6 collective-permute-done.5
  492.6 2.8 collective-permute-done.2
  495.6 2.5 bitcast_dynamic-update-slice_fusion.7
  498.1 2.8 collective-permute-start.9
  502.1 3.6 fusion.11
  507.5 48.7 %all-reduce.5.cloned.1.call-done = bf16[1024,1024]{1,0:T(8,128)(2,1)} async-done(((bf16[1024,1024]{1,0:T(8,128)(2,1)}), bf16[1024,1024]{1,0:T(8,128)(2,1)}) %all-reduce.5.cloned.1.call-update) | async-done | bytes 2097168 | tf_op jit(solution)/shard_map/psum | solution.py:265
  556.2 8.6 %fusion.67 = bf16[1,384,1024]{2,1,0:T(8,128)(2,1)} fusion(f32[384,1024]{1,0:T(8,128)S(1)} %copy-done.18, bf16[384,4096]{1,0:T(8,128)(2,1)} %get-tuple-element.167, bf16[4096,1024]{1,0:T(8,128)(2,1)} %all-gather.12.cloned.1.call-done, f32[1024]{0:T(1024)S(1)} %bitcast.453), kind=kOutput, calls=%fused_computation.148 | convolution fusion | flops 3222405120 | bytes 13897728 | tf_op jit(solution)/shard_map/dot_general | solution.py:245
  566.0 2.1 collective-permute-start.11
  568.1 2.1 collective-permute-start.12
  570.8 2.5 collective-permute-start.14
  573.4 6.2 collective-permute-done.10
  579.6 4.0 collective-permute-start.15
  583.6 17.4 %collective-permute-done.11 = bf16[104,1024]{1,0:T(8,128)(2,1)S(1)} collective-permute-done((bf16[104,1024]{1,0:T(8,128)(2,1)}, bf16[104,1024]{1,0:T(8,128)(2,1)S(1)}, u32[]{:S(2)}, u32[]{:S(2)}) %collective-permute-start.11) | collective-permute-done | bytes 213024 | tf_op jit(solution)/shard_map/ppermute | solution.py:180
  601.1 6.4 collective-permute-done.12
  607.7 7.9 %collective-permute-done.15 = bf16[104,1024]{1,0:T(8,128)(2,1)S(1)} collective-permute-done((bf16[104,1024]{1,0:T(8,128)(2,1)}, bf16[104,1024]{1,0:T(8,128)(2,1)S(1)}, u32[]{:S(2)}, u32[]{:S(2)}) %collective-permute-start.15) | collective-permute-done | bytes 213024 | tf_op jit(solution)/shard_map/ppermute | solution.py:180
  618.7 2.4 copy.208
  622.3 4.1 convert_element_type.568
  626.4 81.0 %all-reduce.7.cloned.1.call-done = bf16[1280,1024]{1,0:T(8,128)(2,1)} async-done(((bf16[1280,1024]{1,0:T(8,128)(2,1)}), bf16[1280,1024]{1,0:T(8,128)(2,1)}) %all-reduce.7.cloned.1.call-update) | async-done | bytes 2621456 | tf_op jit(solution)/shard_map/psum | solution.py:285
  707.3 4.1 convert_bitcast_fusion
  711.4 5.3 copy.209
  716.7 2.1 slice_convert_fusion
  (492 shorter events, 99.5 us)
Async XLA Ops:
  7.2 51.5 %all-gather.6.cloned.1.call-start = ((), (), s32[]{:S(2)}) async-start(), calls=%async_computation | async-start | bytes 7864320 | tf_op jit(solution)/shard_map/all_gather | solution.py:218
  8.0 11.4 %copy-start.131 = (s32[1,2,64]{2,1,0:T(2,128)S(1)}, s32[1,2,64]{2,1,0:T(2,128)}, u32[]{:S(2)}) copy-start(s32[1,2,64]{2,1,0:T(2,128)} %param.17) | copy-start | bytes 1540
  8.0 74.9 %all-gather.8.cloned.1.call-start = ((), (), s32[]{:S(2)}) async-start(), calls=%async_computation.1 | async-start | bytes 2621440 | tf_op jit(solution)/shard_map/all_gather | solution.py:219
  8.8 14.6 %copy-start.10 = (bf16[1,384,1024]{2,1,0:T(8,128)(2,1)S(1)}, bf16[1,384,1024]{2,1,0:T(8,128)(2,1)}, u32[]{:S(2)}) copy-start(bf16[1,384,1024]{2,1,0:T(8,128)(2,1)} %param.16) | copy-start | bytes 2359300
  8.8 134.0 %all-gather.10.cloned.1.call-start = ((), (), s32[]{:S(2)}) async-start(), calls=%async_computation.2 | async-start | bytes 10485760 | tf_op jit(solution)/shard_map/all_gather | solution.py:220
  9.5 192.9 %all-gather.12.cloned.1.call-start = ((), (), s32[]{:S(2)}) async-start(), calls=%async_computation.3 | async-start | bytes 10485760 | tf_op jit(solution)/shard_map/all_gather | solution.py:221
  10.1 546.1 %all-reduce.5.cloned.1.call-start = ((), (), s32[]{:S(2)}) async-start(), calls=%async_computation.4 | async-start | bytes 4194304 | tf_op jit(solution)/shard_map/psum | solution.py:265
  19.3 46.3 %copy-start.123 = (f32[1,2,4,128]{3,1,2,0:T(2,128)}, f32[1,2,4,128]{3,1,2,0:T(2,128)S(1)}, u32[]{:S(2)}) copy-start(f32[1,2,4,128]{3,1,2,0:T(2,128)S(1)} %copy.232) | copy-start | bytes 12292
  19.3 46.3 %copy-start.88 = (f32[1,2,4,128]{3,1,2,0:T(2,128)}, f32[1,2,4,128]{3,1,2,0:T(2,128)S(1)}, u32[]{:S(2)}) copy-start(f32[1,2,4,128]{3,1,2,0:T(2,128)S(1)} %copy.231) | copy-start | bytes 12292
  23.5 42.1 %copy-start.90 = (f32[384]{0:T(512)}, f32[384]{0:T(512)S(1)}, u32[]{:S(2)}) copy-start(f32[384]{0:T(512)S(1)} %broadcast_multiply_fusion.1) | copy-start | bytes 4612
  23.9 41.8 %copy-start.115 = (f32[384]{0:T(512)}, f32[384]{0:T(512)S(1)}, u32[]{:S(2)}) copy-start(f32[384]{0:T(512)S(1)} %fusion.58) | copy-start | bytes 4612
  23.9 41.8 %copy-start.92 = (f32[384]{0:T(512)}, f32[384]{0:T(512)S(1)}, u32[]{:S(2)}) copy-start(f32[384]{0:T(512)S(1)} %fusion.141) | copy-start | bytes 4612
  66.6 5.8 copy-start.64
  68.2 6.0 copy-start.70
  70.7 10.5 %copy-start.43 = (bf16[384,256]{0,1:T(8,128)(2,1)}, bf16[384,256]{0,1:T(8,128)(2,1)S(1)}, u32[]{:S(2)}) copy-start(bf16[384,256]{0,1:T(8,128)(2,1)S(1)} %copy.172) | copy-start | bytes 589828
  82.9 5.7 copy-start.100
  82.9 5.7 copy-start.102
  82.9 6.3 copy-start.104
  82.9 6.3 copy-start.106
  82.9 6.3 copy-start.108
  82.9 6.3 copy-start.110
  82.9 6.3 copy-start.25
  86.5 56.3 %copy-start.120 = (f32[1,8,4,128]{3,1,2,0:T(8,128)S(1)}, f32[1,8,4,128]{3,1,2,0:T(8,128)}, u32[]{:S(2)}) copy-start(f32[1,8,4,128]{3,1,2,0:T(8,128)} %copy.250) | copy-start | bytes 49156
  86.5 56.3 %copy-start.121 = (f32[1,2,4,128]{3,1,2,0:T(2,128)S(1)}, f32[1,2,4,128]{3,1,2,0:T(2,128)}, u32[]{:S(2)}) copy-start(f32[1,2,4,128]{3,1,2,0:T(2,128)} %copy.236) | copy-start | bytes 12292
  86.5 56.3 %copy-start.127 = (f32[1,2,4,128]{3,1,2,0:T(2,128)S(1)}, f32[1,2,4,128]{3,1,2,0:T(2,128)}, u32[]{:S(2)}) copy-start(f32[1,2,4,128]{3,1,2,0:T(2,128)} %copy.237) | copy-start | bytes 12292
  86.5 131.6 %copy-start.113 = (f32[384]{0:T(512)}, f32[384]{0:T(512)S(1)}, u32[]{:S(2)}) copy-start(f32[384]{0:T(512)S(1)} %broadcast_multiply_fusion) | copy-start | bytes 4612
  87.9 130.2 %copy-start.125 = (f32[384]{0:T(512)}, f32[384]{0:T(512)S(1)}, u32[]{:S(2)}) copy-start(f32[384]{0:T(512)S(1)} %fusion.142) | copy-start | bytes 4612
  202.5 11.3 %copy-start.17 = (f32[384,1024]{1,0:T(8,128)S(1)}, f32[384,1024]{1,0:T(8,128)}, u32[]{:S(2)}) copy-start(f32[384,1024]{1,0:T(8,128)} %copy-done.16) | copy-start | bytes 4718596
  202.5 11.3 %copy-start.141 = (bf16[1024,4096]{1,0:T(8,128)(2,1)S(1)}, bf16[1024,4096]{1,0:T(8,128)(2,1)}, u32[]{:S(2)}) copy-start(bf16[1024,4096]{1,0:T(8,128)(2,1)} %all-gather.10.cloned.1.call-done) | copy-start | bytes 25165828
  254.5 6.7 slice-start
  280.9 42.8 %collective-permute-start = (bf16[1664,1024]{1,0:T(8,128)(2,1)}, bf16[1664,1024]{1,0:T(8,128)(2,1)}, u32[]{:S(2)}, u32[]{:S(2)}) collective-permute-start(bf16[1664,1024]{1,0:T(8,128)(2,1)} %pad_maximum_fusion.1), channel_id=1, source_target_pairs={{0,1},{1,0},{2,3},{3,2},{4,5},{5,4},{6,7},{7,6},{8,9},{9,8},{10,11... | collective-permute-start | bytes 10223624 | tf_op jit(solution)/shard_map/ppermute | solution.py:158
  287.5 9.4 %copy-start.37 = (bf16[384,1024]{1,0:T(8,128)(2,1)S(1)}, bf16[384,1024]{1,0:T(8,128)(2,1)}, u32[]{:S(2)}) copy-start(bf16[384,1024]{1,0:T(8,128)(2,1)} %copy-done.36) | copy-start | bytes 2359300
  287.5 9.4 %copy-start.72 = (bf16[384,256]{0,1:T(8,128)(2,1)S(1)}, bf16[384,256]{0,1:T(8,128)(2,1)}, u32[]{:S(2)}) copy-start(bf16[384,256]{0,1:T(8,128)(2,1)} %get-tuple-element.117) | copy-start | bytes 589828
  287.6 9.4 %copy-start.73 = (bf16[384,256]{0,1:T(8,128)(2,1)S(1)}, bf16[384,256]{0,1:T(8,128)(2,1)}, u32[]{:S(2)}) copy-start(bf16[384,256]{0,1:T(8,128)(2,1)} %get-tuple-element.118) | copy-start | bytes 589828
  287.6 9.4 %copy-start.74 = (bf16[384,256]{0,1:T(8,128)(2,1)S(1)}, bf16[384,256]{0,1:T(8,128)(2,1)}, u32[]{:S(2)}) copy-start(bf16[384,256]{0,1:T(8,128)(2,1)} %get-tuple-element.119) | copy-start | bytes 589828
  287.6 9.4 %copy-start.75 = (bf16[384,256]{0,1:T(8,128)(2,1)S(1)}, bf16[384,256]{0,1:T(8,128)(2,1)}, u32[]{:S(2)}) copy-start(bf16[384,256]{0,1:T(8,128)(2,1)} %get-tuple-element.120) | copy-start | bytes 589828
  317.0 6.6 copy-start.32
  317.0 25.5 %collective-permute-start.18 = (bf16[2560,1024]{1,0:T(8,128)(2,1)}, bf16[2560,1024]{1,0:T(8,128)(2,1)}, u32[]{:S(2)}, u32[]{:S(2)}) collective-permute-start(bf16[2560,1024]{1,0:T(8,128)(2,1)} %pad_maximum_fusion), channel_id=1, source_target_pairs={{0,1},{1,0},{2,3},{3,2},{4,5},{5,4},{6,7},{7,6},{8,9},{9,8},{10,11... | collective-permute-start | bytes 15728648 | tf_op jit(solution)/shard_map/ppermute | solution.py:158
  323.4 9.7 %collective-permute-start.16 = (bf16[2048,1024]{1,0:T(8,128)(2,1)}, bf16[2048,1024]{1,0:T(8,128)(2,1)}, u32[]{:S(2)}, u32[]{:S(2)}) collective-permute-start(bf16[2048,1024]{1,0:T(8,128)(2,1)} %fusion.9), channel_id=1, source_target_pairs={{0,1},{1,0},{2,3},{3,2},{4,5},{5,4},{6,7},{7,6},{8,9},{9,8},{10,11... | collective-permute-start | bytes 12582920 | tf_op jit(solution)/shard_map/ppermute | solution.py:158
  332.7 40.2 %collective-permute-start.1 = (bf16[832,1024]{1,0:T(8,128)(2,1)S(1)}, bf16[832,1024]{1,0:T(8,128)(2,1)}, u32[]{:S(2)}, u32[]{:S(2)}) collective-permute-start(bf16[832,1024]{1,0:T(8,128)(2,1)S(1)} %pad_maximum_fusion.5), channel_id=1, source_target_pairs={{0,2},{1,3},{2,0},{3,1},{4,6},{5,7},{6,4},{7,5},{8,10},{9,11},{10,... | collective-permute-start | bytes 5111816 | tf_op jit(solution)/shard_map/ppermute | solution.py:158
  339.1 7.0 copy-start.14
  340.8 77.1 %collective-permute-start.17 = (bf16[1024,1024]{1,0:T(8,128)(2,1)}, bf16[1024,1024]{1,0:T(8,128)(2,1)}, u32[]{:S(2)}, u32[]{:S(2)}) collective-permute-start(bf16[1024,1024]{1,0:T(8,128)(2,1)} %fusion.37), channel_id=1, source_target_pairs={{0,2},{1,3},{2,0},{3,1},{4,6},{5,7},{6,4},{7,5},{8,10},{9,11},{10,... | collective-permute-start | bytes 6291464 | tf_op jit(solution)/shard_map/ppermute | solution.py:158
  346.1 6.7 copy-start.29
  356.9 144.0 %collective-permute-start.19 = (bf16[1280,1024]{1,0:T(8,128)(2,1)}, bf16[1280,1024]{1,0:T(8,128)(2,1)}, u32[]{:S(2)}, u32[]{:S(2)}) collective-permute-start(bf16[1280,1024]{1,0:T(8,128)(2,1)} %pad_maximum_fusion.3), channel_id=1, source_target_pairs={{0,2},{1,3},{2,0},{3,1},{4,6},{5,7},{6,4},{7,5},{8,10},{9,11},{10,... | collective-permute-start | bytes 7864328 | tf_op jit(solution)/shard_map/ppermute | solution.py:158
  377.7 45.1 %copy-start.42 = (f32[128,1024]{1,0:T(8,128)S(1)}, f32[128,1024]{1,0:T(8,128)}, u32[]{:S(2)}) copy-start(f32[128,1024]{1,0:T(8,128)} %copy-done.41) | copy-start | bytes 1572868
  422.8 284.5 %all-reduce.7.cloned.1.call-start = ((), (), s32[]{:S(2)}) async-start(), calls=%async_computation.5 | async-start | bytes 5242880 | tf_op jit(solution)/shard_map/psum | solution.py:285
  426.0 61.9 %copy-start.118 = (f32[1,2,4,128]{3,2,1,0:T(4,128)S(1)}, f32[1,2,4,128]{3,2,1,0:T(4,128)}, u32[]{:S(2)}) copy-start(f32[1,2,4,128]{3,2,1,0:T(4,128)} %get-tuple-element.147) | copy-start | bytes 12292
  428.6 14.4 %collective-permute-start.8 = (bf16[104,1024]{1,0:T(8,128)(2,1)S(1)}, bf16[104,1024]{1,0:T(8,128)(2,1)S(1)}, u32[]{:S(2)}, u32[]{:S(2)}) collective-permute-start(bf16[104,1024]{1,0:T(8,128)(2,1)S(1)} %get-tuple-element.99), channel_id=1, source_target_pairs={{0,28},{4,0},{8,4},{12,8},{16,12},{20,16},{24,20},{28,24},{1,29},{... | collective-permute-start | bytes 638984 | tf_op jit(solution)/shard_map/ppermute | solution.py:172
  432.8 22.7 %collective-permute-start.7 = (bf16[104,1024]{1,0:T(8,128)(2,1)S(1)}, bf16[104,1024]{1,0:T(8,128)(2,1)S(1)}, u32[]{:S(2)}, u32[]{:S(2)}) collective-permute-start(bf16[104,1024]{1,0:T(8,128)(2,1)S(1)} %get-tuple-element.100), channel_id=1, source_target_pairs={{0,24},{4,28},{8,0},{12,4},{16,8},{20,12},{24,16},{28,20},{1,25},{... | collective-permute-start | bytes 638984 | tf_op jit(solution)/shard_map/ppermute | solution.py:172
  433.4 43.8 %collective-permute-start.6 = (bf16[104,1024]{1,0:T(8,128)(2,1)S(1)}, bf16[104,1024]{1,0:T(8,128)(2,1)S(1)}, u32[]{:S(2)}, u32[]{:S(2)}) collective-permute-start(bf16[104,1024]{1,0:T(8,128)(2,1)S(1)} %get-tuple-element.101), channel_id=1, source_target_pairs={{0,20},{4,24},{8,28},{12,0},{16,4},{20,8},{24,12},{28,16},{1,21},{... | collective-permute-start | bytes 638984 | tf_op jit(solution)/shard_map/ppermute | solution.py:172
  433.4 57.1 %collective-permute-start.5 = (bf16[104,1024]{1,0:T(8,128)(2,1)}, bf16[104,1024]{1,0:T(8,128)(2,1)S(1)}, u32[]{:S(2)}, u32[]{:S(2)}) collective-permute-start(bf16[104,1024]{1,0:T(8,128)(2,1)} %get-tuple-element.102), channel_id=1, source_target_pairs={{0,16},{4,20},{8,24},{12,28},{16,0},{20,4},{24,8},{28,12},{1,17},{... | collective-permute-start | bytes 638984 | tf_op jit(solution)/shard_map/ppermute | solution.py:172
  443.0 48.2 %collective-permute-start.4 = (bf16[104,1024]{1,0:T(8,128)(2,1)S(1)}, bf16[104,1024]{1,0:T(8,128)(2,1)S(1)}, u32[]{:S(2)}, u32[]{:S(2)}) collective-permute-start(bf16[104,1024]{1,0:T(8,128)(2,1)S(1)} %get-tuple-element.103), channel_id=1, source_target_pairs={{0,12},{4,16},{8,20},{12,24},{16,28},{20,0},{24,4},{28,8},{1,13},{... | collective-permute-start | bytes 638984 | tf_op jit(solution)/shard_map/ppermute | solution.py:172
  455.5 35.7 %copy-start.78 = (bf16[104,1024]{1,0:T(8,128)(2,1)}, bf16[104,1024]{1,0:T(8,128)(2,1)S(1)}, u32[]{:S(2)}) copy-start(bf16[104,1024]{1,0:T(8,128)(2,1)S(1)} %collective-permute-done.7) | copy-start | bytes 638980
  455.5 35.7 %collective-permute-start.3 = (bf16[104,1024]{1,0:T(8,128)(2,1)S(1)}, bf16[104,1024]{1,0:T(8,128)(2,1)S(1)}, u32[]{:S(2)}, u32[]{:S(2)}) collective-permute-start(bf16[104,1024]{1,0:T(8,128)(2,1)S(1)} %get-tuple-element.104), channel_id=1, source_target_pairs={{0,8},{4,12},{8,16},{12,20},{16,24},{20,28},{24,0},{28,4},{1,9},{5... | collective-permute-start | bytes 638984 | tf_op jit(solution)/shard_map/ppermute | solution.py:172
  477.1 14.1 %copy-start.79 = (bf16[104,1024]{1,0:T(8,128)(2,1)}, bf16[104,1024]{1,0:T(8,128)(2,1)S(1)}, u32[]{:S(2)}) copy-start(bf16[104,1024]{1,0:T(8,128)(2,1)S(1)} %collective-permute-done.6) | copy-start | bytes 638980
  477.1 18.2 %collective-permute-start.2 = (bf16[104,1024]{1,0:T(8,128)(2,1)S(1)}, bf16[104,1024]{1,0:T(8,128)(2,1)}, u32[]{:S(2)}, u32[]{:S(2)}) collective-permute-start(bf16[104,1024]{1,0:T(8,128)(2,1)S(1)} %get-tuple-element.98), channel_id=1, source_target_pairs={{0,4},{4,8},{8,12},{12,16},{16,20},{20,24},{24,28},{28,0},{1,5},{5... | collective-permute-start | bytes 638984 | tf_op jit(solution)/shard_map/ppermute | solution.py:172
  487.9 13.0 %copy-start.30 = (f32[512,1024]{1,0:T(8,128)S(1)}, f32[512,1024]{1,0:T(8,128)}, u32[]{:S(2)}) copy-start(f32[512,1024]{1,0:T(8,128)} %copy-done.29) | copy-start | bytes 6291460
  498.1 72.8 %collective-permute-start.9 = (bf16[104,1024]{1,0:T(8,128)(2,1)}, bf16[104,1024]{1,0:T(8,128)(2,1)S(1)}, u32[]{:S(2)}, u32[]{:S(2)}) collective-permute-start(bf16[104,1024]{1,0:T(8,128)(2,1)} %get-tuple-element.87), channel_id=1, source_target_pairs={{0,4},{4,8},{8,12},{12,16},{16,20},{20,24},{24,28},{28,0},{1,5},{5... | collective-permute-start | bytes 638984 | tf_op jit(solution)/shard_map/ppermute | solution.py:180
  564.9 14.7 %collective-permute-start.10 = (bf16[104,1024]{1,0:T(8,128)(2,1)}, bf16[104,1024]{1,0:T(8,128)(2,1)S(1)}, u32[]{:S(2)}, u32[]{:S(2)}) collective-permute-start(bf16[104,1024]{1,0:T(8,128)(2,1)} %get-tuple-element.87), channel_id=1, source_target_pairs={{0,8},{4,12},{8,16},{12,20},{16,24},{20,28},{24,0},{28,4},{1,9},{5... | collective-permute-start | bytes 638984 | tf_op jit(solution)/shard_map/ppermute | solution.py:180
  566.0 35.1 %collective-permute-start.11 = (bf16[104,1024]{1,0:T(8,128)(2,1)}, bf16[104,1024]{1,0:T(8,128)(2,1)S(1)}, u32[]{:S(2)}, u32[]{:S(2)}) collective-permute-start(bf16[104,1024]{1,0:T(8,128)(2,1)} %get-tuple-element.87), channel_id=1, source_target_pairs={{0,12},{4,16},{8,20},{12,24},{16,28},{20,0},{24,4},{28,8},{1,13},{... | collective-permute-start | bytes 638984 | tf_op jit(solution)/shard_map/ppermute | solution.py:180
  568.1 39.4 %collective-permute-start.12 = (bf16[104,1024]{1,0:T(8,128)(2,1)}, bf16[104,1024]{1,0:T(8,128)(2,1)S(1)}, u32[]{:S(2)}, u32[]{:S(2)}) collective-permute-start(bf16[104,1024]{1,0:T(8,128)(2,1)} %get-tuple-element.87), channel_id=1, source_target_pairs={{0,16},{4,20},{8,24},{12,28},{16,0},{20,4},{24,8},{28,12},{1,17},{... | collective-permute-start | bytes 638984 | tf_op jit(solution)/shard_map/ppermute | solution.py:180
  570.2 37.3 %collective-permute-start.13 = (bf16[104,1024]{1,0:T(8,128)(2,1)}, bf16[104,1024]{1,0:T(8,128)(2,1)S(1)}, u32[]{:S(2)}, u32[]{:S(2)}) collective-permute-start(bf16[104,1024]{1,0:T(8,128)(2,1)} %get-tuple-element.87), channel_id=1, source_target_pairs={{0,20},{4,24},{8,28},{12,0},{16,4},{20,8},{24,12},{28,16},{1,21},{... | collective-permute-start | bytes 638984 | tf_op jit(solution)/shard_map/ppermute | solution.py:180
  570.8 36.9 %collective-permute-start.14 = (bf16[104,1024]{1,0:T(8,128)(2,1)}, bf16[104,1024]{1,0:T(8,128)(2,1)S(1)}, u32[]{:S(2)}, u32[]{:S(2)}) collective-permute-start(bf16[104,1024]{1,0:T(8,128)(2,1)} %get-tuple-element.87), channel_id=1, source_target_pairs={{0,24},{4,28},{8,0},{12,4},{16,8},{20,12},{24,16},{28,20},{1,25},{... | collective-permute-start | bytes 638984 | tf_op jit(solution)/shard_map/ppermute | solution.py:180
  579.6 36.1 %collective-permute-start.15 = (bf16[104,1024]{1,0:T(8,128)(2,1)}, bf16[104,1024]{1,0:T(8,128)(2,1)S(1)}, u32[]{:S(2)}, u32[]{:S(2)}) collective-permute-start(bf16[104,1024]{1,0:T(8,128)(2,1)} %get-tuple-element.87), channel_id=1, source_target_pairs={{0,28},{4,0},{8,4},{12,8},{16,12},{20,16},{24,20},{28,24},{1,29},{... | collective-permute-start | bytes 638984 | tf_op jit(solution)/shard_map/ppermute | solution.py:180
  (108 other events, 275.9 us)
Sparse Core Ops, SparseCore 0:
  9.6 49.1 all-gather.5
  60.3 22.5 all-gather.7
  84.5 58.2 all-gather.9
  144.2 58.2 all-gather.11
  422.9 133.2 all-reduce.4
  560.3 146.9 all-reduce.6

commit v8 on v5

--- a/solution.py
+++ b/solution.py
@@ -276,9 +276,9 @@
         "ti,to->io", reorder_cols(mixed, order), grad_branch, preferred_element_type=jnp.float32
     )
     up_own, out_own = halving([grad_up_t, grad_out], "shard", shard_count, shard_steps)
-    owned_a = [up_own, out_own]
-    joined_a = jnp.concatenate([o.astype(jnp.bfloat16) for o in owned_a], 0)
-    total_a1, joined_a = lax.optimization_barrier((total_a1, joined_a))
+    owned_a = [up_own.astype(jnp.bfloat16).T, out_own.astype(jnp.bfloat16)]
+    joined_a = jnp.concatenate(owned_a, 0)
+    down_fin, joined_a = lax.optimization_barrier((total_a1.astype(jnp.float32), joined_a))
     total_a = lax.psum(joined_a, "rep")
     grad_q, grad_k, grad_v = attend_backward(
         queries, key_rows, values, grad_mixed, log_norms, distance, allowed
@@ -305,8 +305,7 @@
     joined_b = jnp.concatenate([qkv_own, small_own], 0)
     total_b = direct_reduce(joined_b, "rep", reps)
     up_rows = up_own.shape[0]
-    down_fin = total_a1.astype(jnp.float32)
-    up_fin = total_a[:up_rows].astype(jnp.float32).T
+    up_fin = total_a[:up_rows].astype(jnp.float32)
     out_fin = total_a[up_rows:].astype(jnp.float32)
     qkv_fin = total_b[:qkv_rows].astype(jnp.float32).T
     small_flat = total_b[qkv_rows:].reshape(-1).astype(jnp.float32)

time: 755 us -> 749 us (level)
  waiting for transfers between devices: 379 us -> 371 us
    unnamed x199 -> x198, local copies, waits for them, and re-layouts: 34.7 us -> 29.9 us
  transfers between devices with their start and end apart: 26 -> 26, of which waited for: 17 -> 16; matrix products, arithmetic and copies ran while one was open for 20% -> 21% of each run, Pallas kernels for 0% -> 0%
where the time goes in v8:
time: 749 us; the launch traced here: 744 us
  waiting for transfers between devices  371 us (50%)
  matrix products  92.1 us (12%)
  local copies, waits for them, and re-layouts  90.5 us (12%)
  other arithmetic  83.4 us (11%)
  starting transfers between devices  65.2 us (9%)
  loops' own time  19.5 us (3%)
  between operations  15.8 us (2%)
    psum x1, waiting for transfers between devices, body_inner(): total_a = lax.psum(joined_a, 'rep')  79.4 us
    ppermute x6, waiting for transfers between devices, halving(): lax.ppermute(jnp.concatenate(sends, 0), axis, [(a, a ^ step) for a in ran...  54.5 us
    all_gather x1, waiting for transfers between devices, body_inner(): full_down = lax.all_gather(w_down, 'shard', axis=0, tiled=True)  48.4 us
    all_gather x1, waiting for transfers between devices, body_inner(): full_up = lax.all_gather(w_up, 'shard', axis=1, tiled=True)  47 us
    ppermute x7, starting transfers between devices, direct_reduce(): lax.ppermute(send.astype(jnp.bfloat16), axis, [(a, (a + shift) % size) fo...  44.7 us
    psum x1, waiting for transfers between devices, body_inner(): total_a1 = lax.psum(down_own.astype(jnp.bfloat16), 'rep')  43.1 us
    all_gather x1, waiting for transfers between devices, body_inner(): full_qkv = lax.all_gather(w_qkv, 'shard', axis=1, tiled=True)  38.3 us
    ppermute x7, waiting for transfers between devices, direct_reduce(): lax.ppermute(mine, axis, [(a, (a + shift) % size) for a in range(size)])  37.2 us
  transfers between devices with their start and end apart: 26, of which 16 were waited for; matrix products, arithmetic and copies ran while one was open for 21% of the time, Pallas kernels for 0%

profile of v8, /device:TPU:0, one launch (start us, length us, event | category | flops | bytes accessed | tf_op | source)
XLA Modules:
  0.0 743.9 jit_solution(13247085026568980798)
XLA Ops:
  12.2 6.3 all-gather
  20.3 38.3 %all-gather.6.cloned.1.call-done = bf16[1024,3072]{1,0:T(8,128)(2,1)} async-done(((bf16[1024,768]{1,0:T(8,128)(2,1)}), bf16[1024,3072]{1,0:T(8,128)(2,1)}) %all-gather.6.cloned.1.call-update) | async-done | bytes 6291472 | tf_op jit(solution)/shard_map/all_gather | solution.py:215
  58.7 5.1 fusion.82
  68.5 21.3 %while.32 = (s32[]{:T(128)}, bf16[4,384,256]{1,2,0:T(8,128)(2,1)}, f32[4,4,384]{2,1,0:T(4,128)}, s32[4]{0:T(128)S(1)}, bf16[384,1024]{0,1:T(8,128)(2,1)S(1)}, /*...) while((s32[]{:T(128)}, bf16[4,384,256]{1,2,0:T(8,128)(2,1)}, ...), condition=%wide.region_6.7_spmd.clone, body=%wide.region_3.6_spmd.clone.sunk | while | flops 157776416 | bytes 10964623 | solution.py:74
  91.0 3.4 fusion.138
  95.7 47.0 %all-gather.10.cloned.1.call-done = bf16[1024,4096]{1,0:T(8,128)(2,1)} async-done(((bf16[1024,1024]{1,0:T(8,128)(2,1)}), bf16[1024,4096]{1,0:T(8,128)(2,1)}) %all-gather.10.cloned.1.call-update) | async-done | bytes 8388624 | tf_op jit(solution)/shard_map/all_gather | solution.py:217
  142.7 11.3 %multiply_convert_fusion.1 = (bf16[384,4096]{1,0:T(8,128)(2,1)}, f32[384,4096]{1,0:T(8,128)}) fusion(f32[4096]{0:T(1024)S(1)} %bitcast.400, bf16[1024,4096]{1,0:T(8,128)(2,1)} %all-gather.10.cloned.1.call-done, f32[384,1024]{1,0:T(8,128)S(1)} %get-tuple-element.597, f32[1024]{0:T(1024)S(1)} %bitcast.407, f32[1024]{0:T(1024)S(1)} %bitcast.401, ...), kind=kOutput, calls=%fused_computation.57 | convolution fusion | flops 3238920192 | bytes 19426304 | tf_op jit(solution)/shard_map/dot_general | solution.py:237
  154.0 48.4 %all-gather.12.cloned.1.call-done = bf16[4096,1024]{1,0:T(8,128)(2,1)} async-done(((bf16[1024,1024]{1,0:T(8,128)(2,1)}), bf16[4096,1024]{1,0:T(8,128)(2,1)}) %all-gather.12.cloned.1.call-update) | async-done | bytes 8388624 | tf_op jit(solution)/shard_map/all_gather | solution.py:218
  202.4 11.2 %convert_reduce_fusion = (f32[4096]{0:T(1024)}, bf16[384,4096]{1,0:T(8,128)(2,1)S(1)}) fusion(f32[384,4096]{1,0:T(8,128)} %get-tuple-element.599, bf16[4096,1024]{1,0:T(8,128)(2,1)} %all-gather.12.cloned.1.call-done, bf16[1,384,1024]{2,1,0:T(8,128)(2,1)S(1)} %copy-done.21), kind=kOutput, calls=%fused_computation.55 | convolution fusion | flops 3255824384 | bytes 18628608 | tf_op jit(solution)/shard_map/to,fo->tf/dot_general | solution.py:254
  215.3 4.3 multiply_reduce_fusion.1
  226.6 51.6 %while.33 = (s32[]{:T(128)}, bf16[4,384,256]{1,2,0:T(8,128)(2,1)}, bf16[4,384,256]{1,2,0:T(8,128)(2,1)}, bf16[4,384,256]{1,2,0:T(8,128)(2,1)}, s32[4]{0:T(128)S(...) while((s32[]{:T(128)}, bf16[4,384,256]{1,2,0:T(8,128)(2,1)}, ...), condition=%wide.region_13.14_spmd.clone, body=%wide.region_11.13_spmd.clone.sunk | while | flops 385251872 | bytes 36901940 | solution.py:113
  278.3 1.9 convert_reduce_fusion.4
  280.2 1.9 split.65
  283.1 5.7 fusion.129
  294.1 3.6 fusion.80
  298.9 3.6 copy-done
  303.1 2.1 pad_maximum_fusion.1
  306.6 1.8 maximum_bitcast_fusion
  308.4 3.4 copy.114
  311.9 9.5 %fusion.92 = f32[2,2048,1024]{2,1,0:T(8,128)} fusion(bf16[2,2048,384]{2,1,0:T(8,128)(2,1)S(1)} %bitcast.347, bf16[1,384,1024]{2,1,0:T(8,128)(2,1)} %param.22), kind=kOutput, calls=%fused_computation.172 | convolution fusion | flops 3221225472 | bytes 20709376 | tf_op jit(solution)/shard_map/tf,to->fo/dot_general | solution.py:258
  322.8 2.0 copy-done.3
  325.1 9.4 %fusion.32 = f32[4096,1024]{1,0:T(8,128)} fusion(bf16[384,1024]{1,0:T(8,128)(2,1)S(1)} %copy-done.39, bf16[384,1024]{1,0:T(8,128)(2,1)S(1)} %copy-done.40, bf16[384,1024]{1,0:T(8,128)(2,1)S(1)} %copy-done.41, bf16[384,1024]{1,0:T(8,128)(2,1)S(1)} %copy-done.38, f32[384,1024]{1,0:T(8,128)S(1)} %copy-done.9, f32[1024]{0:T(1024)S(1)} %bitcast.408, ...), kind=kOutput, calls=%fused_computation.78 | convolution fusion | flops 3235774464 | bytes 21507072 | tf_op jit(solution)/shard_map/tf,ti->fi/dot_general | solution.py:263
  334.5 4.0 fusion.24
  338.5 2.9 pad_maximum_fusion
  341.7 6.1 fusion.23
  349.9 4.7 bitcast_add_fusion.2
  355.0 2.2 copy-done.7
  357.6 6.0 bitcast_add_fusion.1
  367.0 1.9 copy-done.4
  370.7 6.6 bitcast_add_fusion
  377.6 2.1 pad_maximum_fusion.3
  383.1 14.3 %collective-permute-done.1 = bf16[832,1024]{1,0:T(8,128)(2,1)} collective-permute-done((bf16[832,1024]{1,0:T(8,128)(2,1)S(1)}, bf16[832,1024]{1,0:T(8,128)(2,1)}, u32[]{:S(2)}, u32[]{:S(2)}) %collective-permute-start.1) | collective-permute-done | bytes 1703968 | tf_op jit(solution)/shard_map/ppermute | solution.py:155
  397.4 4.8 bitcast_add_fusion.5
  402.2 40.1 %collective-permute-done.17 = bf16[1024,1024]{1,0:T(8,128)(2,1)} collective-permute-done((bf16[1024,1024]{1,0:T(8,128)(2,1)}, bf16[1024,1024]{1,0:T(8,128)(2,1)}, u32[]{:S(2)}, u32[]{:S(2)}) %collective-permute-start.17) | collective-permute-done | bytes 2097184 | tf_op jit(solution)/shard_map/ppermute | solution.py:155
  442.3 4.9 fusion.26
  448.2 2.2 pad_maximum_fusion.2
  453.1 4.2 collective-permute-start.8
  457.8 2.9 collective-permute-start.5
  460.8 6.7 collective-permute-done.8
  467.5 4.6 collective-permute-start.4
  472.1 7.8 %collective-permute-done.7 = bf16[104,1024]{1,0:T(8,128)(2,1)S(1)} collective-permute-done((bf16[104,1024]{1,0:T(8,128)(2,1)S(1)}, bf16[104,1024]{1,0:T(8,128)(2,1)S(1)}, u32[]{:S(2)}, u32[]{:S(2)}) %collective-permute-start.7) | collective-permute-done | bytes 213024 | tf_op jit(solution)/shard_map/ppermute | solution.py:169
  479.9 21.7 %collective-permute-start.3 = (bf16[104,1024]{1,0:T(8,128)(2,1)S(1)}, bf16[104,1024]{1,0:T(8,128)(2,1)S(1)}, u32[]{:S(2)}, u32[]{:S(2)}) collective-permute-start(bf16[104,1024]{1,0:T(8,128)(2,1)S(1)} %get-tuple-element.561), channel_id=1, source_target_pairs={{0,8},{4,12},{8,16},{12,20},{16,24},{20,28},{24,0},{28,4},{1,9},{5... | collective-permute-start | bytes 638984 | tf_op jit(solution)/shard_map/ppermute | solution.py:169
  501.6 10.7 %collective-permute-start.2 = (bf16[104,1024]{1,0:T(8,128)(2,1)S(1)}, bf16[104,1024]{1,0:T(8,128)(2,1)}, u32[]{:S(2)}, u32[]{:S(2)}) collective-permute-start(bf16[104,1024]{1,0:T(8,128)(2,1)S(1)} %get-tuple-element.555), channel_id=1, source_target_pairs={{0,4},{4,8},{8,12},{12,16},{16,20},{20,24},{24,28},{28,0},{1,5},{5... | collective-permute-start | bytes 638984 | tf_op jit(solution)/shard_map/ppermute | solution.py:169
  512.3 2.6 collective-permute-done.5
  517.1 2.8 collective-permute-done.2
  520.1 2.5 bitcast_dynamic-update-slice_fusion.8
  522.6 2.6 collective-permute-start.9
  525.2 5.0 fusion.53
  530.2 4.1 copy.108
  538.2 43.1 %all-reduce.5.cloned.1.call-done = bf16[1024,1024]{1,0:T(8,128)(2,1)} async-done(((bf16[1024,1024]{1,0:T(8,128)(2,1)}), bf16[1024,1024]{1,0:T(8,128)(2,1)}) %all-reduce.5.cloned.1.call-update) | async-done | bytes 2097168 | tf_op jit(solution)/shard_map/psum | solution.py:262
  581.3 4.1 convert_element_type.511
  585.4 8.6 %fusion.74 = bf16[1,384,1024]{2,1,0:T(8,128)(2,1)} fusion(f32[384,1024]{1,0:T(8,128)S(1)} %copy-done.9, bf16[384,4096]{1,0:T(8,128)(2,1)} %get-tuple-element.598, bf16[4096,1024]{1,0:T(8,128)(2,1)} %all-gather.12.cloned.1.call-done, f32[1024]{0:T(1024)S(1)} %bitcast.409), kind=kOutput, calls=%fused_computation.153 | convolution fusion | flops 3222405120 | bytes 13897728 | tf_op jit(solution)/shard_map/dot_general | solution.py:242
  595.1 2.1 collective-permute-start.11
  597.2 2.1 collective-permute-start.12
  600.0 2.5 collective-permute-start.14
  602.5 6.2 collective-permute-done.10
  608.7 4.7 collective-permute-start.15
  613.5 17.3 %collective-permute-done.11 = bf16[104,1024]{1,0:T(8,128)(2,1)S(1)} collective-permute-done((bf16[104,1024]{1,0:T(8,128)(2,1)}, bf16[104,1024]{1,0:T(8,128)(2,1)S(1)}, u32[]{:S(2)}, u32[]{:S(2)}) %collective-permute-start.11) | collective-permute-done | bytes 213024 | tf_op jit(solution)/shard_map/ppermute | solution.py:177
  630.8 5.2 collective-permute-done.12
  636.1 8.5 %collective-permute-done.15 = bf16[104,1024]{1,0:T(8,128)(2,1)S(1)} collective-permute-done((bf16[104,1024]{1,0:T(8,128)(2,1)}, bf16[104,1024]{1,0:T(8,128)(2,1)S(1)}, u32[]{:S(2)}, u32[]{:S(2)}) %collective-permute-start.15) | collective-permute-done | bytes 213024 | tf_op jit(solution)/shard_map/ppermute | solution.py:177
  647.7 2.4 copy.109
  651.2 79.4 %all-reduce.7.cloned.1.call-done = bf16[1280,1024]{1,0:T(8,128)(2,1)} async-done(((bf16[1280,1024]{1,0:T(8,128)(2,1)}), bf16[1280,1024]{1,0:T(8,128)(2,1)}) %all-reduce.7.cloned.1.call-update) | async-done | bytes 2621456 | tf_op jit(solution)/shard_map/psum | solution.py:282
  730.6 2.1 slice_convert_fusion.2
  732.7 4.1 slice_convert_fusion
  (492 shorter events, 114.8 us)
Async XLA Ops:
  7.2 51.5 %all-gather.6.cloned.1.call-start = ((), (), s32[]{:S(2)}) async-start(), calls=%async_computation | async-start | bytes 7864320 | tf_op jit(solution)/shard_map/all_gather | solution.py:215
  8.0 81.8 %all-gather.8.cloned.1.call-start = ((), (), s32[]{:S(2)}) async-start(), calls=%async_computation.1 | async-start | bytes 2621440 | tf_op jit(solution)/shard_map/all_gather | solution.py:216
  8.8 10.3 %copy-start.1 = (bf16[1,384,1024]{2,1,0:T(8,128)(2,1)S(1)}, bf16[1,384,1024]{2,1,0:T(8,128)(2,1)}, u32[]{:S(2)}) copy-start(bf16[1,384,1024]{2,1,0:T(8,128)(2,1)} %param.20) | copy-start | bytes 2359300
  8.8 10.7 %copy-start.77 = (s32[1,2,64]{2,1,0:T(2,128)S(1)}, s32[1,2,64]{2,1,0:T(2,128)}, u32[]{:S(2)}) copy-start(s32[1,2,64]{2,1,0:T(2,128)} %param.21) | copy-start | bytes 1540
  8.8 133.9 %all-gather.10.cloned.1.call-start = ((), (), s32[]{:S(2)}) async-start(), calls=%async_computation.2 | async-start | bytes 10485760 | tf_op jit(solution)/shard_map/all_gather | solution.py:217
  9.5 192.9 %all-gather.12.cloned.1.call-start = ((), (), s32[]{:S(2)}) async-start(), calls=%async_computation.3 | async-start | bytes 10485760 | tf_op jit(solution)/shard_map/all_gather | solution.py:218
  10.1 571.2 %all-reduce.5.cloned.1.call-start = ((), (), s32[]{:S(2)}) async-start(), calls=%async_computation.4 | async-start | bytes 4194304 | tf_op jit(solution)/shard_map/psum | solution.py:262
  19.1 44.7 %copy-start.69 = (f32[1,2,4,128]{3,1,2,0:T(2,128)}, f32[1,2,4,128]{3,1,2,0:T(2,128)S(1)}, u32[]{:S(2)}) copy-start(f32[1,2,4,128]{3,1,2,0:T(2,128)S(1)} %copy.121) | copy-start | bytes 12292
  19.1 44.7 %copy-start.50 = (f32[1,2,4,128]{3,1,2,0:T(2,128)}, f32[1,2,4,128]{3,1,2,0:T(2,128)S(1)}, u32[]{:S(2)}) copy-start(f32[1,2,4,128]{3,1,2,0:T(2,128)S(1)} %copy.120) | copy-start | bytes 12292
  19.8 122.9 %copy-start.73 = (f32[1,2,4,128]{3,1,2,0:T(2,128)}, f32[1,2,4,128]{3,1,2,0:T(2,128)S(1)}, u32[]{:S(2)}) copy-start(f32[1,2,4,128]{3,1,2,0:T(2,128)S(1)} %copy.126) | copy-start | bytes 12292
  19.9 199.8 %copy-start.67 = (f32[1,2,4,128]{3,1,2,0:T(2,128)}, f32[1,2,4,128]{3,1,2,0:T(2,128)S(1)}, u32[]{:S(2)}) copy-start(f32[1,2,4,128]{3,1,2,0:T(2,128)S(1)} %copy.125) | copy-start | bytes 12292
  20.0 43.8 %copy-start.52 = (f32[384]{0:T(512)}, f32[384]{0:T(512)S(1)}, u32[]{:S(2)}) copy-start(f32[384]{0:T(512)S(1)} %broadcast_multiply_fusion.1) | copy-start | bytes 4612
  20.3 43.5 %copy-start.62 = (f32[384]{0:T(512)}, f32[384]{0:T(512)S(1)}, u32[]{:S(2)}) copy-start(f32[384]{0:T(512)S(1)} %fusion.65) | copy-start | bytes 4612
  20.3 43.5 %copy-start.56 = (f32[384]{0:T(512)}, f32[384]{0:T(512)S(1)}, u32[]{:S(2)}) copy-start(f32[384]{0:T(512)S(1)} %fusion.123) | copy-start | bytes 4612
  94.4 125.2 %copy-start.8 = (f32[384,1024]{1,0:T(8,128)}, f32[384,1024]{1,0:T(8,128)S(1)}, u32[]{:S(2)}) copy-start(f32[384,1024]{1,0:T(8,128)S(1)} %get-tuple-element.597) | copy-start | bytes 4718596
  94.4 125.2 %copy-start.60 = (f32[384]{0:T(512)}, f32[384]{0:T(512)S(1)}, u32[]{:S(2)}) copy-start(f32[384]{0:T(512)S(1)} %broadcast_multiply_fusion) | copy-start | bytes 4612
  94.8 124.9 %copy-start.71 = (f32[384]{0:T(512)}, f32[384]{0:T(512)S(1)}, u32[]{:S(2)}) copy-start(f32[384]{0:T(512)S(1)} %fusion.124) | copy-start | bytes 4612
  142.7 59.7 %copy-start.21 = (bf16[1,384,1024]{2,1,0:T(8,128)(2,1)S(1)}, bf16[1,384,1024]{2,1,0:T(8,128)(2,1)}, u32[]{:S(2)}) copy-start(bf16[1,384,1024]{2,1,0:T(8,128)(2,1)} %param.22) | copy-start | bytes 2359300
  202.4 12.9 %copy-start.87 = (bf16[1024,4096]{1,0:T(8,128)(2,1)S(1)}, bf16[1024,4096]{1,0:T(8,128)(2,1)}, u32[]{:S(2)}) copy-start(bf16[1024,4096]{1,0:T(8,128)(2,1)} %all-gather.10.cloned.1.call-done) | copy-start | bytes 25165828
  226.6 5.7 copy-start.54
  226.6 5.7 copy-start.88
  239.4 5.8 copy-start.54
  239.4 5.8 copy-start.88
  252.2 5.8 copy-start.54
  252.2 5.8 copy-start.88
  265.0 5.8 copy-start.54
  265.0 5.8 copy-start.88
  278.3 4.8 copy-start.2
  283.0 5.7 copy-start.63
  283.0 5.7 copy-start.57
  297.7 4.9 copy-start
  305.2 42.9 %collective-permute-start = (bf16[1664,1024]{1,0:T(8,128)(2,1)}, bf16[1664,1024]{1,0:T(8,128)(2,1)}, u32[]{:S(2)}, u32[]{:S(2)}) collective-permute-start(bf16[1664,1024]{1,0:T(8,128)(2,1)} %pad_maximum_fusion.1), channel_id=1, source_target_pairs={{0,1},{1,0},{2,3},{3,2},{4,5},{5,4},{6,7},{7,6},{8,9},{9,8},{10,11... | collective-permute-start | bytes 10223624 | tf_op jit(solution)/shard_map/ppermute | solution.py:155
  311.9 9.6 %copy-start.29 = (bf16[384,1024]{1,0:T(8,128)(2,1)S(1)}, bf16[384,1024]{1,0:T(8,128)(2,1)}, u32[]{:S(2)}) copy-start(bf16[384,1024]{1,0:T(8,128)(2,1)} %copy-done.28) | copy-start | bytes 2359300
  311.9 9.6 %copy-start.42 = (bf16[384,256]{0,1:T(8,128)(2,1)S(1)}, bf16[384,256]{0,1:T(8,128)(2,1)}, u32[]{:S(2)}) copy-start(bf16[384,256]{0,1:T(8,128)(2,1)} %get-tuple-element.571) | copy-start | bytes 589828
  311.9 9.6 %copy-start.43 = (bf16[384,256]{0,1:T(8,128)(2,1)S(1)}, bf16[384,256]{0,1:T(8,128)(2,1)}, u32[]{:S(2)}) copy-start(bf16[384,256]{0,1:T(8,128)(2,1)} %get-tuple-element.572) | copy-start | bytes 589828
  311.9 9.5 %copy-start.44 = (bf16[384,256]{0,1:T(8,128)(2,1)S(1)}, bf16[384,256]{0,1:T(8,128)(2,1)}, u32[]{:S(2)}) copy-start(bf16[384,256]{0,1:T(8,128)(2,1)} %get-tuple-element.573) | copy-start | bytes 589828
  341.4 6.6 copy-start.26
  341.4 25.5 %collective-permute-start.18 = (bf16[2560,1024]{1,0:T(8,128)(2,1)}, bf16[2560,1024]{1,0:T(8,128)(2,1)}, u32[]{:S(2)}, u32[]{:S(2)}) collective-permute-start(bf16[2560,1024]{1,0:T(8,128)(2,1)} %pad_maximum_fusion), channel_id=1, source_target_pairs={{0,1},{1,0},{2,3},{3,2},{4,5},{5,4},{6,7},{7,6},{8,9},{9,8},{10,11... | collective-permute-start | bytes 15728648 | tf_op jit(solution)/shard_map/ppermute | solution.py:155
  347.8 9.7 %collective-permute-start.16 = (bf16[2048,1024]{1,0:T(8,128)(2,1)}, bf16[2048,1024]{1,0:T(8,128)(2,1)}, u32[]{:S(2)}, u32[]{:S(2)}) collective-permute-start(bf16[2048,1024]{1,0:T(8,128)(2,1)} %fusion.23), channel_id=1, source_target_pairs={{0,1},{1,0},{2,3},{3,2},{4,5},{5,4},{6,7},{7,6},{8,9},{9,8},{10,11... | collective-permute-start | bytes 12582920 | tf_op jit(solution)/shard_map/ppermute | solution.py:155
  357.2 40.2 %collective-permute-start.1 = (bf16[832,1024]{1,0:T(8,128)(2,1)S(1)}, bf16[832,1024]{1,0:T(8,128)(2,1)}, u32[]{:S(2)}, u32[]{:S(2)}) collective-permute-start(bf16[832,1024]{1,0:T(8,128)(2,1)S(1)} %pad_maximum_fusion.5), channel_id=1, source_target_pairs={{0,2},{1,3},{2,0},{3,1},{4,6},{5,7},{6,4},{7,5},{8,10},{9,11},{10,... | collective-permute-start | bytes 5111816 | tf_op jit(solution)/shard_map/ppermute | solution.py:155
  363.6 7.0 copy-start.6
  363.6 5.3 copy-start.4
  365.3 77.0 %collective-permute-start.17 = (bf16[1024,1024]{1,0:T(8,128)(2,1)}, bf16[1024,1024]{1,0:T(8,128)(2,1)}, u32[]{:S(2)}, u32[]{:S(2)}) collective-permute-start(bf16[1024,1024]{1,0:T(8,128)(2,1)} %fusion.51), channel_id=1, source_target_pairs={{0,2},{1,3},{2,0},{3,1},{4,6},{5,7},{6,4},{7,5},{8,10},{9,11},{10,... | collective-permute-start | bytes 6291464 | tf_op jit(solution)/shard_map/ppermute | solution.py:155
  370.6 6.7 copy-start.24
  381.4 143.8 %collective-permute-start.19 = (bf16[1280,1024]{1,0:T(8,128)(2,1)}, bf16[1280,1024]{1,0:T(8,128)(2,1)}, u32[]{:S(2)}, u32[]{:S(2)}) collective-permute-start(bf16[1280,1024]{1,0:T(8,128)(2,1)} %pad_maximum_fusion.3), channel_id=1, source_target_pairs={{0,2},{1,3},{2,0},{3,1},{4,6},{5,7},{6,4},{7,5},{8,10},{9,11},{10,... | collective-permute-start | bytes 7864328 | tf_op jit(solution)/shard_map/ppermute | solution.py:155
  402.2 45.1 %copy-start.35 = (f32[128,1024]{1,0:T(8,128)S(1)}, f32[128,1024]{1,0:T(8,128)}, u32[]{:S(2)}) copy-start(f32[128,1024]{1,0:T(8,128)} %copy-done.34) | copy-start | bytes 1572868
  447.2 283.4 %all-reduce.7.cloned.1.call-start = ((), (), s32[]{:S(2)}) async-start(), calls=%async_computation.5 | async-start | bytes 5242880 | tf_op jit(solution)/shard_map/psum | solution.py:282
  450.4 61.9 %copy-start.65 = (f32[1,2,4,128]{3,2,1,0:T(4,128)S(1)}, f32[1,2,4,128]{3,2,1,0:T(4,128)}, u32[]{:S(2)}) copy-start(f32[1,2,4,128]{3,2,1,0:T(4,128)} %get-tuple-element.588) | copy-start | bytes 12292
  453.1 14.4 %collective-permute-start.8 = (bf16[104,1024]{1,0:T(8,128)(2,1)S(1)}, bf16[104,1024]{1,0:T(8,128)(2,1)S(1)}, u32[]{:S(2)}, u32[]{:S(2)}) collective-permute-start(bf16[104,1024]{1,0:T(8,128)(2,1)S(1)} %get-tuple-element.556), channel_id=1, source_target_pairs={{0,28},{4,0},{8,4},{12,8},{16,12},{20,16},{24,20},{28,24},{1,29},{... | collective-permute-start | bytes 638984 | tf_op jit(solution)/shard_map/ppermute | solution.py:169
  457.3 22.6 %collective-permute-start.7 = (bf16[104,1024]{1,0:T(8,128)(2,1)S(1)}, bf16[104,1024]{1,0:T(8,128)(2,1)S(1)}, u32[]{:S(2)}, u32[]{:S(2)}) collective-permute-start(bf16[104,1024]{1,0:T(8,128)(2,1)S(1)} %get-tuple-element.557), channel_id=1, source_target_pairs={{0,24},{4,28},{8,0},{12,4},{16,8},{20,12},{24,16},{28,20},{1,25},{... | collective-permute-start | bytes 638984 | tf_op jit(solution)/shard_map/ppermute | solution.py:169
  457.8 43.8 %collective-permute-start.6 = (bf16[104,1024]{1,0:T(8,128)(2,1)S(1)}, bf16[104,1024]{1,0:T(8,128)(2,1)S(1)}, u32[]{:S(2)}, u32[]{:S(2)}) collective-permute-start(bf16[104,1024]{1,0:T(8,128)(2,1)S(1)} %get-tuple-element.558), channel_id=1, source_target_pairs={{0,20},{4,24},{8,28},{12,0},{16,4},{20,8},{24,12},{28,16},{1,21},{... | collective-permute-start | bytes 638984 | tf_op jit(solution)/shard_map/ppermute | solution.py:169
  457.8 57.1 %collective-permute-start.5 = (bf16[104,1024]{1,0:T(8,128)(2,1)}, bf16[104,1024]{1,0:T(8,128)(2,1)S(1)}, u32[]{:S(2)}, u32[]{:S(2)}) collective-permute-start(bf16[104,1024]{1,0:T(8,128)(2,1)} %get-tuple-element.559), channel_id=1, source_target_pairs={{0,16},{4,20},{8,24},{12,28},{16,0},{20,4},{24,8},{28,12},{1,17},{... | collective-permute-start | bytes 638984 | tf_op jit(solution)/shard_map/ppermute | solution.py:169
  467.5 48.2 %collective-permute-start.4 = (bf16[104,1024]{1,0:T(8,128)(2,1)S(1)}, bf16[104,1024]{1,0:T(8,128)(2,1)S(1)}, u32[]{:S(2)}, u32[]{:S(2)}) collective-permute-start(bf16[104,1024]{1,0:T(8,128)(2,1)S(1)} %get-tuple-element.560), channel_id=1, source_target_pairs={{0,12},{4,16},{8,20},{12,24},{16,28},{20,0},{24,4},{28,8},{1,13},{... | collective-permute-start | bytes 638984 | tf_op jit(solution)/shard_map/ppermute | solution.py:169
  479.9 35.8 %copy-start.45 = (bf16[104,1024]{1,0:T(8,128)(2,1)}, bf16[104,1024]{1,0:T(8,128)(2,1)S(1)}, u32[]{:S(2)}) copy-start(bf16[104,1024]{1,0:T(8,128)(2,1)S(1)} %collective-permute-done.7) | copy-start | bytes 638980
  479.9 35.8 %collective-permute-start.3 = (bf16[104,1024]{1,0:T(8,128)(2,1)S(1)}, bf16[104,1024]{1,0:T(8,128)(2,1)S(1)}, u32[]{:S(2)}, u32[]{:S(2)}) collective-permute-start(bf16[104,1024]{1,0:T(8,128)(2,1)S(1)} %get-tuple-element.561), channel_id=1, source_target_pairs={{0,8},{4,12},{8,16},{12,20},{16,24},{20,28},{24,0},{28,4},{1,9},{5... | collective-permute-start | bytes 638984 | tf_op jit(solution)/shard_map/ppermute | solution.py:169
  501.6 14.1 %copy-start.46 = (bf16[104,1024]{1,0:T(8,128)(2,1)}, bf16[104,1024]{1,0:T(8,128)(2,1)S(1)}, u32[]{:S(2)}) copy-start(bf16[104,1024]{1,0:T(8,128)(2,1)S(1)} %collective-permute-done.6) | copy-start | bytes 638980
  501.6 18.2 %collective-permute-start.2 = (bf16[104,1024]{1,0:T(8,128)(2,1)S(1)}, bf16[104,1024]{1,0:T(8,128)(2,1)}, u32[]{:S(2)}, u32[]{:S(2)}) collective-permute-start(bf16[104,1024]{1,0:T(8,128)(2,1)S(1)} %get-tuple-element.555), channel_id=1, source_target_pairs={{0,4},{4,8},{8,12},{12,16},{16,20},{20,24},{24,28},{28,0},{1,5},{5... | collective-permute-start | bytes 638984 | tf_op jit(solution)/shard_map/ppermute | solution.py:169
  522.6 77.4 %collective-permute-start.9 = (bf16[104,1024]{1,0:T(8,128)(2,1)}, bf16[104,1024]{1,0:T(8,128)(2,1)S(1)}, u32[]{:S(2)}, u32[]{:S(2)}) collective-permute-start(bf16[104,1024]{1,0:T(8,128)(2,1)} %get-tuple-element.540), channel_id=1, source_target_pairs={{0,4},{4,8},{8,12},{12,16},{16,20},{20,24},{24,28},{28,0},{1,5},{5... | collective-permute-start | bytes 638984 | tf_op jit(solution)/shard_map/ppermute | solution.py:177
  594.0 14.7 %collective-permute-start.10 = (bf16[104,1024]{1,0:T(8,128)(2,1)}, bf16[104,1024]{1,0:T(8,128)(2,1)S(1)}, u32[]{:S(2)}, u32[]{:S(2)}) collective-permute-start(bf16[104,1024]{1,0:T(8,128)(2,1)} %get-tuple-element.540), channel_id=1, source_target_pairs={{0,8},{4,12},{8,16},{12,20},{16,24},{20,28},{24,0},{28,4},{1,9},{5... | collective-permute-start | bytes 638984 | tf_op jit(solution)/shard_map/ppermute | solution.py:177
  595.1 35.7 %collective-permute-start.11 = (bf16[104,1024]{1,0:T(8,128)(2,1)}, bf16[104,1024]{1,0:T(8,128)(2,1)S(1)}, u32[]{:S(2)}, u32[]{:S(2)}) collective-permute-start(bf16[104,1024]{1,0:T(8,128)(2,1)} %get-tuple-element.540), channel_id=1, source_target_pairs={{0,12},{4,16},{8,20},{12,24},{16,28},{20,0},{24,4},{28,8},{1,13},{... | collective-permute-start | bytes 638984 | tf_op jit(solution)/shard_map/ppermute | solution.py:177
  597.2 38.8 %collective-permute-start.12 = (bf16[104,1024]{1,0:T(8,128)(2,1)}, bf16[104,1024]{1,0:T(8,128)(2,1)S(1)}, u32[]{:S(2)}, u32[]{:S(2)}) collective-permute-start(bf16[104,1024]{1,0:T(8,128)(2,1)} %get-tuple-element.540), channel_id=1, source_target_pairs={{0,16},{4,20},{8,24},{12,28},{16,0},{20,4},{24,8},{28,12},{1,17},{... | collective-permute-start | bytes 638984 | tf_op jit(solution)/shard_map/ppermute | solution.py:177
  599.3 36.7 %collective-permute-start.13 = (bf16[104,1024]{1,0:T(8,128)(2,1)}, bf16[104,1024]{1,0:T(8,128)(2,1)S(1)}, u32[]{:S(2)}, u32[]{:S(2)}) collective-permute-start(bf16[104,1024]{1,0:T(8,128)(2,1)} %get-tuple-element.540), channel_id=1, source_target_pairs={{0,20},{4,24},{8,28},{12,0},{16,4},{20,8},{24,12},{28,16},{1,21},{... | collective-permute-start | bytes 638984 | tf_op jit(solution)/shard_map/ppermute | solution.py:177
  600.0 36.1 %collective-permute-start.14 = (bf16[104,1024]{1,0:T(8,128)(2,1)}, bf16[104,1024]{1,0:T(8,128)(2,1)S(1)}, u32[]{:S(2)}, u32[]{:S(2)}) collective-permute-start(bf16[104,1024]{1,0:T(8,128)(2,1)} %get-tuple-element.540), channel_id=1, source_target_pairs={{0,24},{4,28},{8,0},{12,4},{16,8},{20,12},{24,16},{28,20},{1,25},{... | collective-permute-start | bytes 638984 | tf_op jit(solution)/shard_map/ppermute | solution.py:177
  608.7 35.9 %collective-permute-start.15 = (bf16[104,1024]{1,0:T(8,128)(2,1)}, bf16[104,1024]{1,0:T(8,128)(2,1)S(1)}, u32[]{:S(2)}, u32[]{:S(2)}) collective-permute-start(bf16[104,1024]{1,0:T(8,128)(2,1)} %get-tuple-element.540), channel_id=1, source_target_pairs={{0,28},{4,0},{8,4},{12,8},{16,12},{20,16},{24,20},{28,24},{1,29},{... | collective-permute-start | bytes 638984 | tf_op jit(solution)/shard_map/ppermute | solution.py:177
  (76 other events, 187.1 us)
Sparse Core Ops, SparseCore 0:
  9.6 49.0 all-gather.5
  60.2 22.5 all-gather.7
  84.4 58.2 all-gather.9
  144.1 58.2 all-gather.11
  447.4 133.8 all-reduce.4
  585.5 145.0 all-reduce.6

commit v9 on v8

--- a/solution.py
+++ b/solution.py
@@ -238,6 +238,14 @@
         jnp.float32
     )
     activated = jax.nn.gelu(pre_act, approximate=True).astype(jnp.bfloat16)
+    cot_low = cotangent[0]
+    shard_steps = bit_steps(shard_count)
+    order = chunk_order(shard_count, shard_steps)
+    grad_down = jnp.einsum(
+        "tf,to->fo", reorder_cols(activated, order), cot_low, preferred_element_type=jnp.float32
+    )
+    down_half = halving([grad_down], "shard", shard_count, shard_steps[:1])
+    down_half, full_down = lax.optimization_barrier((down_half, full_down))
     outputs = middle + (
         jnp.dot(activated, full_down, preferred_element_type=jnp.float32)
         + full_bd.astype(jnp.float32)
@@ -245,9 +253,6 @@
     back_g1, back_qkv, back_out, back_g2, back_up, back_down = (
         full_g1, full_qkv, full_out, full_g2, full_up, full_down
     )
-    shard_steps = bit_steps(shard_count)
-    order = chunk_order(shard_count, shard_steps)
-    cot_low = cotangent[0]
     cot_full = cot_low.astype(jnp.float32)
     zero_shift = jnp.zeros((model_width,), jnp.float32)
     grad_bd = jnp.sum(cot_full, 0)
@@ -255,10 +260,7 @@
     _, gelu_pull = jax.vjp(partial(jax.nn.gelu, approximate=True), pre_act)
     grad_pre = gelu_pull(grad_act)[0].astype(jnp.bfloat16)
     grad_bu = jnp.sum(grad_pre.astype(jnp.float32), 0)
-    grad_down = jnp.einsum(
-        "tf,to->fo", reorder_cols(activated, order), cot_low, preferred_element_type=jnp.float32
-    )
-    (down_own,) = halving([grad_down], "shard", shard_count, shard_steps)
+    (down_own,) = halving(down_half, "shard", shard_count, shard_steps[1:])
     total_a1 = lax.psum(down_own.astype(jnp.bfloat16), "rep")
     grad_up_t = jnp.einsum(
         "tf,ti->fi", reorder_cols(grad_pre, order), normed_two, preferred_element_type=jnp.float32
@@ -284,31 +286,32 @@
         queries, key_rows, values, grad_mixed, log_norms, distance, allowed
     )
     grad_proj = jnp.concatenate([grad_q, grad_k, grad_v], 1)
+    reps = lax.psum(1, "rep")
+    grad_qkv_t = jnp.einsum(
+        "tc,ti->ci", reorder_cols(grad_proj, order), normed, preferred_element_type=jnp.float32
+    )
+    (qkv_own,) = halving([grad_qkv_t], "shard", shard_count, shard_steps)
+    total_b = direct_reduce(qkv_own, "rep", reps)
+    grad_qkv_t, grad_proj = lax.optimization_barrier((grad_qkv_t, grad_proj))
     grad_qb = jnp.sum(grad_q.astype(jnp.float32), 0)
     grad_vb = jnp.sum(grad_v.astype(jnp.float32), 0)
     grad_normed = jnp.einsum("tc,ic->ti", grad_proj, back_qkv, preferred_element_type=jnp.float32)
     _, norm_pull_one = jax.vjp(normalize, inputs, back_g1.astype(jnp.float32), zero_shift)
     grad_in_part, grad_g1, grad_s1 = norm_pull_one(grad_normed)
     grad_inputs = grad_middle + grad_in_part
-    grad_qkv_t = jnp.einsum(
-        "tc,ti->ci", reorder_cols(grad_proj, order), normed, preferred_element_type=jnp.float32
-    )
     smalls = [grad_g1, grad_s1, grad_qb, grad_vb, grad_bo, grad_g2, grad_s2, grad_bu, grad_bd]
-    reps = lax.psum(1, "rep")
-    qkv_rows = grad_qkv_t.shape[0] // shard_count
     small_rows = jnp.concatenate([g.reshape(shard_count, -1) for g in smalls], 1)
     small_rows = small_rows.reshape(shard_count, -1, model_width)
-    pad_to = small_rows.shape[1] + (-(qkv_rows + small_rows.shape[1]) % (8 * reps))
+    pad_to = small_rows.shape[1] + (-small_rows.shape[1] % reps)
     small_rows = jnp.pad(small_rows, ((0, 0), (0, pad_to - small_rows.shape[1]), (0, 0)))
     small_rows = jnp.concatenate([small_rows[k] for k in order], 0)
-    qkv_own, small_own = halving([grad_qkv_t, small_rows], "shard", shard_count, shard_steps)
-    joined_b = jnp.concatenate([qkv_own, small_own], 0)
-    total_b = direct_reduce(joined_b, "rep", reps)
+    (small_own,) = halving([small_rows], "shard", shard_count, shard_steps)
+    total_s = direct_reduce(small_own, "rep", reps)
     up_rows = up_own.shape[0]
     up_fin = total_a[:up_rows].astype(jnp.float32)
     out_fin = total_a[up_rows:].astype(jnp.float32)
-    qkv_fin = total_b[:qkv_rows].astype(jnp.float32).T
-    small_flat = total_b[qkv_rows:].reshape(-1).astype(jnp.float32)
+    qkv_fin = total_b.astype(jnp.float32).T
+    small_flat = total_s.reshape(-1).astype(jnp.float32)
     small_fin, offset = [], 0
     for g in smalls:
         width = g.shape[0] // shard_count

time: 749 us -> 682 us (0.911)
  waiting for transfers between devices: 371 us -> 315 us
  other arithmetic: 83.4 us -> 71.4 us
  starting transfers between devices: 65.2 us -> 55.1 us
    all_gather x1, waiting for transfers between devices: 48.4 us -> 9.33 us  [body_inner(): full_down = lax.all_gather(w_down, 'shard', axis=0, tiled=True)]
    ppermute x6 -> x8, waiting for transfers between devices: 54.5 us -> 23.7 us  [halving(): lax.ppermute(jnp.concatenate(sends, 0), axis, [(a, a ^ step) for a in ran...]
    psum x1, waiting for transfers between devices: 43.1 us -> 67.4 us  [body_inner(): total_a1 = lax.psum(down_own.astype(jnp.bfloat16), 'rep')]
    ppermute x7 -> x14, starting transfers between devices: 44.7 us -> 20.9 us  [direct_reduce(): lax.ppermute(send.astype(jnp.bfloat16), axis, [(a, (a + shift) % size) fo...]
    ppermute x7 -> x14, waiting for transfers between devices: 20.7 us -> 43.6 us  [direct_reduce(): lax.ppermute(send.astype(jnp.bfloat16), axis, [(a, (a + shift) % size) fo...]
    psum x1, waiting for transfers between devices: 79.4 us -> 60.4 us  [body_inner(): total_a = lax.psum(joined_a, 'rep')]
    ppermute x7 -> x14, waiting for transfers between devices: 37.2 us -> 21.7 us  [direct_reduce(): lax.ppermute(mine, axis, [(a, (a + shift) % size) for a in range(size)])]
    ppermute x7 -> x14, starting transfers between devices: 15.8 us -> 29 us  [direct_reduce(): lax.ppermute(mine, axis, [(a, (a + shift) % size) for a in range(size)])]
  transfers between devices with their start and end apart: 26 -> 42, of which waited for: 16 -> 16; matrix products, arithmetic and copies ran while one was open for 21% -> 20% of each run, Pallas kernels for 0% -> 0%
where the time goes in v9:
time: 682 us; the launch traced here: 677 us
  waiting for transfers between devices  315 us (46%)
  matrix products  99.1 us (15%)
  local copies, waits for them, and re-layouts  95.2 us (14%)
  other arithmetic  71.4 us (10%)
  starting transfers between devices  55.1 us (8%)
  loops' own time  18.9 us (3%)
  between operations  15.9 us (2%)
    psum x1, waiting for transfers between devices, body_inner(): total_a1 = lax.psum(down_own.astype(jnp.bfloat16), 'rep')  67.4 us
    psum x1, waiting for transfers between devices, body_inner(): total_a = lax.psum(joined_a, 'rep')  60.4 us
    all_gather x1, waiting for transfers between devices, body_inner(): full_up = lax.all_gather(w_up, 'shard', axis=1, tiled=True)  48.2 us
    ppermute x14, waiting for transfers between devices, direct_reduce(): lax.ppermute(send.astype(jnp.bfloat16), axis, [(a, (a + shift) % size) fo...  43.6 us
    all_gather x1, waiting for transfers between devices, body_inner(): full_qkv = lax.all_gather(w_qkv, 'shard', axis=1, tiled=True)  38.1 us
    unnamed x193, local copies, waits for them, and re-layouts  29.2 us
    ppermute x14, starting transfers between devices, direct_reduce(): lax.ppermute(mine, axis, [(a, (a + shift) % size) for a in range(size)])  29 us
    add x6, other arithmetic, halving(): arrays.append(keep + got[offset:offset + keep.shape[0]].astype(jnp.float32))  26.8 us
  transfers between devices with their start and end apart: 42, of which 16 were waited for; matrix products, arithmetic and copies ran while one was open for 20% of the time, Pallas kernels for 0%

profile of v9, /device:TPU:0, one launch (start us, length us, event | category | flops | bytes accessed | tf_op | source)
XLA Modules:
  0.0 677.3 jit_solution(1244024390977771272)
XLA Ops:
  12.2 6.6 all-gather
  20.6 38.1 %all-gather.6.cloned.1.call-done = bf16[1024,3072]{1,0:T(8,128)(2,1)} async-done(((bf16[1024,768]{1,0:T(8,128)(2,1)}), bf16[1024,3072]{1,0:T(8,128)(2,1)}) %all-gather.6.cloned.1.call-update) | async-done | bytes 6291472 | tf_op jit(solution)/shard_map/all_gather | solution.py:215
  58.7 4.9 fusion.135
  68.3 21.3 %while.32 = (s32[]{:T(128)}, bf16[4,384,256]{1,2,0:T(8,128)(2,1)}, f32[4,4,384]{2,1,0:T(4,128)}, s32[4]{0:T(128)S(1)}, bf16[384,1024]{0,1:T(8,128)(2,1)S(1)}, /*...) while((s32[]{:T(128)}, bf16[4,384,256]{1,2,0:T(8,128)(2,1)}, ...), condition=%wide.region_6.7_spmd.clone, body=%wide.region_3.6_spmd.clone.sunk | while | flops 157776416 | bytes 10964623 | solution.py:74
  90.8 3.3 fusion.147
  94.5 48.2 %all-gather.10.cloned.1.call-done = bf16[1024,4096]{1,0:T(8,128)(2,1)} async-done(((bf16[1024,1024]{1,0:T(8,128)(2,1)}), bf16[1024,4096]{1,0:T(8,128)(2,1)}) %all-gather.10.cloned.1.call-update) | async-done | bytes 8388624 | tf_op jit(solution)/shard_map/all_gather | solution.py:217
  142.7 10.6 %multiply_convert_fusion.1 = (bf16[384,4096]{1,0:T(8,128)(2,1)S(1)}, f32[384,4096]{1,0:T(8,128)}) fusion(f32[4096]{0:T(1024)S(1)} %bitcast.426, bf16[1024,4096]{1,0:T(8,128)(2,1)} %all-gather.10.cloned.1.call-done, f32[384,1024]{1,0:T(8,128)S(1)} %get-tuple-element.611, f32[1024]{0:T(1024)S(1)} %bitcast.433, f32[1024]{0:T(1024)S(1)} %bitcast.427, ...), kind=kOutput, calls=%fused_computation.62 | convolution fusion | flops 3238920192 | bytes 19426304 | tf_op jit(solution)/shard_map/dot_general | solution.py:237
  154.9 1.8 maximum_bitcast_fusion
  156.7 4.0 copy.111
  160.7 5.7 fusion.95
  166.4 5.8 copy-done
  172.2 2.7 fusion.26
  176.0 6.8 collective-permute-done
  182.8 10.3 %bitcast_add_fusion.1 = f32[2048,1024]{1,0:T(8,128)} fusion(bf16[2048,1024]{1,0:T(8,128)(2,1)} %collective-permute-done, f32[2,2048,1024]{2,1,0:T(8,128)} %copy-done, s32[]{:T(128)S(6)} %select_n.262), kind=kLoop, calls=%fused_computation.40 | loop fusion | flops 4194304 | bytes 20971524 | tf_op jit(solution)/shard_map/add | solution.py:158
  193.1 9.3 %all-gather.12.cloned.1.call-done = bf16[4096,1024]{1,0:T(8,128)(2,1)} async-done(((bf16[1024,1024]{1,0:T(8,128)(2,1)}), bf16[4096,1024]{1,0:T(8,128)(2,1)}) %all-gather.12.cloned.1.call-update) | async-done | bytes 8388624 | tf_op jit(solution)/shard_map/all_gather | solution.py:218
  202.4 10.8 %convert_reduce_fusion = (f32[4096]{0:T(1024)}, bf16[384,4096]{1,0:T(8,128)(2,1)S(1)}) fusion(f32[384,4096]{1,0:T(8,128)} %get-tuple-element.613, bf16[4096,1024]{1,0:T(8,128)(2,1)} %all-gather.12.cloned.1.call-done, bf16[1,384,1024]{2,1,0:T(8,128)(2,1)S(1)} %copy-done.18), kind=kOutput, calls=%fused_computation.61 | convolution fusion | flops 3255824384 | bytes 18628608 | tf_op jit(solution)/shard_map/to,fo->tf/dot_general | solution.py:259
  213.2 1.7 fusion.143
  215.6 7.0 %multiply_reduce_fusion.1 = (f32[1024]{0:T(1024)}, f32[384]{0:T(512)S(1)}, f32[1024]{0:T(1024)}, f32[384,1024]{1,0:T(8,128)S(1)}) fusion(f32[384,1024]{1,0:T(8,128)S(1)} %copy-done.7, f32[384]{0:T(512)S(1)} %fusion.129, f32[384]{0:T(512)S(1)} %broadcast_multiply_fusion, f32[1024]{0:T(1024)S(1)} %bitcast.428, bf16[384,4096]{1,0:T(8,128)(2,1)S(1)} %get-tuple-element.617, ...), kind=kOutput, calls=%fused_computation.141 | convolution fusion | flops 3224368640 | bytes 14696960 | tf_op jit(solution)/shard_map/tf,if->ti/dot_general | solution.py:268
  229.6 54.7 %while.33 = (s32[]{:T(128)}, bf16[4,384,256]{1,2,0:T(8,128)(2,1)}, bf16[4,384,256]{1,2,0:T(8,128)(2,1)}, bf16[4,384,256]{1,2,0:T(8,128)(2,1)}, s32[4]{0:T(128)S(...) while((s32[]{:T(128)}, bf16[4,384,256]{1,2,0:T(8,128)(2,1)}, ...), condition=%wide.region_13.14_spmd.clone, body=%wide.region_11.13_spmd.clone.sunk | while | flops 385251872 | bytes 30610428 | solution.py:113
  287.9 14.3 %fusion.47 = f32[3072,1024]{1,0:T(8,128)} fusion(bf16[384,1024]{0,1:T(8,128)(2,1)S(1)} %bitcast.408, bf16[384,1024]{0,1:T(8,128)(2,1)S(1)} %bitcast.389, bf16[384,1024]{0,1:T(8,128)(2,1)S(1)} %bitcast.392, bf16[384,768]{0,1:T(8,128)(2,1)S(1)} %split.69, bf16[384,768]{0,1:T(8,128)(2,1)S(1)} %split.68, bf16[1,384,1024]{2,1,0:T(8,128)(2,1)S(1)} %copy-done.4, ...), kind=kOutput, calls=%fused_computation.100 | convolution fusion | flops 2444230656 | bytes 16919552 | tf_op jit(solution)/shard_map/tc,ti->ci/dot_general | solution.py:290
  303.7 2.0 copy-done.1
  306.0 9.5 %fusion.35 = f32[4096,1024]{1,0:T(8,128)} fusion(bf16[384,1024]{1,0:T(8,128)(2,1)S(1)} %copy-done.32, bf16[384,1024]{1,0:T(8,128)(2,1)S(1)} %copy-done.33, bf16[384,1024]{1,0:T(8,128)(2,1)S(1)} %copy-done.34, bf16[384,1024]{1,0:T(8,128)(2,1)S(1)} %copy-done.31, f32[384,1024]{1,0:T(8,128)S(1)} %copy-done.8, f32[1024]{0:T(1024)S(1)} %bitcast.434, ...), kind=kOutput, calls=%fused_computation.81 | convolution fusion | flops 3235774464 | bytes 21507072 | tf_op jit(solution)/shard_map/tf,ti->fi/dot_general | solution.py:265
  315.4 4.0 fusion.27
  319.5 3.0 pad_maximum_fusion
  322.7 5.1 fusion.138
  333.4 2.5 fusion.62
  335.9 1.8 collective-permute-start.33
  337.7 4.3 collective-permute-start.9
  342.6 5.1 fusion.34
  347.7 3.0 collective-permute-start.6
  351.2 7.9 %fusion.81 = bf16[1,384,1024]{2,1,0:T(8,128)(2,1)} fusion(f32[384,1024]{1,0:T(8,128)S(1)} %copy-done.8, bf16[384,4096]{1,0:T(8,128)(2,1)S(1)} %copy-done.24, bf16[4096,1024]{1,0:T(8,128)(2,1)} %all-gather.12.cloned.1.call-done, f32[1024]{0:T(1024)S(1)} %bitcast.435), kind=kOutput, calls=%fused_computation.151 | convolution fusion | flops 3222405120 | bytes 13897728 | tf_op jit(solution)/shard_map/dot_general | solution.py:250
  359.0 1.9 collective-permute-start.4
  361.9 3.4 collective-permute-done.4
  365.3 2.0 collective-permute-done.3
  367.4 16.1 %collective-permute-done.33 = bf16[1024,1024]{1,0:T(8,128)(2,1)S(1)} collective-permute-done((bf16[1024,1024]{1,0:T(8,128)(2,1)S(1)}, bf16[1024,1024]{1,0:T(8,128)(2,1)S(1)}, u32[]{:S(2)}, u32[]{:S(2)}) %collective-permute-start.33) | collective-permute-done | bytes 2097184 | tf_op jit(solution)/shard_map/ppermute | solution.py:155
  383.5 2.1 fusion.29
  385.7 2.2 bitcast_add_fusion.6
  389.3 6.4 bitcast_add_fusion
  396.3 2.7 copy-done.2
  400.7 4.9 bitcast_add_fusion.2
  412.1 2.4 collective-permute-start.12
  416.3 2.2 collective-permute-start.14
  422.1 67.4 %all-reduce.5.cloned.1.call-done = bf16[1024,1024]{1,0:T(8,128)(2,1)} async-done(((bf16[1024,1024]{1,0:T(8,128)(2,1)}), bf16[1024,1024]{1,0:T(8,128)(2,1)}) %all-reduce.5.cloned.1.call-update) | async-done | bytes 2097168 | tf_op jit(solution)/shard_map/psum | solution.py:264
  489.5 4.2 convert_element_type.581
  493.8 3.0 bitcast_add_fusion.5
  499.6 2.5 collective-permute-start.25
  503.8 1.9 collective-permute-start.22
  505.7 3.8 fusion.64
  509.5 2.9 copy.104
  513.9 1.7 pad_maximum_fusion.2
  517.9 2.0 collective-permute-start.20
  520.8 38.2 %collective-permute-done.22 = bf16[96,1024]{1,0:T(8,128)(2,1)S(1)} collective-permute-done((bf16[96,1024]{1,0:T(8,128)(2,1)}, bf16[96,1024]{1,0:T(8,128)(2,1)S(1)}, u32[]{:S(2)}, u32[]{:S(2)}) %collective-permute-start.22) | collective-permute-done | bytes 196640 | tf_op jit(solution)/shard_map/ppermute | solution.py:169
  561.4 6.7 collective-permute-start.27
  568.2 3.4 collective-permute-start.28
  571.6 1.9 collective-permute-start.29
  574.5 2.4 collective-permute-start.31
  576.9 3.0 collective-permute-start.32
  579.9 16.7 %collective-permute-done.28 = bf16[96,1024]{1,0:T(8,128)(2,1)S(1)} collective-permute-done((bf16[96,1024]{1,0:T(8,128)(2,1)S(1)}, bf16[96,1024]{1,0:T(8,128)(2,1)S(1)}, u32[]{:S(2)}, u32[]{:S(2)}) %collective-permute-start.28) | collective-permute-done | bytes 196640 | tf_op jit(solution)/shard_map/ppermute | solution.py:177
  596.6 2.2 collective-permute-done.29
  598.9 1.9 collective-permute-done.32
  601.3 2.4 copy.105
  603.7 60.4 %all-reduce.7.cloned.1.call-done = bf16[1280,1024]{1,0:T(8,128)(2,1)} async-done(((bf16[1280,1024]{1,0:T(8,128)(2,1)}), bf16[1280,1024]{1,0:T(8,128)(2,1)}) %all-reduce.7.cloned.1.call-update) | async-done | bytes 2621456 | tf_op jit(solution)/shard_map/psum | solution.py:284
  664.0 2.1 slice_convert_fusion.2
  666.2 4.1 slice_convert_fusion
  (512 shorter events, 121.5 us)
Async XLA Ops:
  7.2 51.5 %all-gather.6.cloned.1.call-start = ((), (), s32[]{:S(2)}) async-start(), calls=%async_computation | async-start | bytes 7864320 | tf_op jit(solution)/shard_map/all_gather | solution.py:215
  8.0 81.6 %all-gather.8.cloned.1.call-start = ((), (), s32[]{:S(2)}) async-start(), calls=%async_computation.1 | async-start | bytes 2621440 | tf_op jit(solution)/shard_map/all_gather | solution.py:216
  8.8 10.7 %copy-start.3 = (bf16[1,384,1024]{2,1,0:T(8,128)(2,1)S(1)}, bf16[1,384,1024]{2,1,0:T(8,128)(2,1)}, u32[]{:S(2)}) copy-start(bf16[1,384,1024]{2,1,0:T(8,128)(2,1)} %param.20) | copy-start | bytes 2359300
  8.8 133.9 %all-gather.10.cloned.1.call-start = ((), (), s32[]{:S(2)}) async-start(), calls=%async_computation.2 | async-start | bytes 10485760 | tf_op jit(solution)/shard_map/all_gather | solution.py:217
  9.5 10.7 %copy-start.70 = (s32[1,2,64]{2,1,0:T(2,128)S(1)}, s32[1,2,64]{2,1,0:T(2,128)}, u32[]{:S(2)}) copy-start(s32[1,2,64]{2,1,0:T(2,128)} %param.21) | copy-start | bytes 1540
  9.5 192.9 %all-gather.12.cloned.1.call-start = ((), (), s32[]{:S(2)}) async-start(), calls=%async_computation.3 | async-start | bytes 10485760 | tf_op jit(solution)/shard_map/all_gather | solution.py:218
  10.1 479.4 %all-reduce.5.cloned.1.call-start = ((), (), s32[]{:S(2)}) async-start(), calls=%async_computation.4 | async-start | bytes 4194304 | tf_op jit(solution)/shard_map/psum | solution.py:264
  19.4 44.2 %copy-start.64 = (f32[1,2,4,128]{3,1,2,0:T(2,128)}, f32[1,2,4,128]{3,1,2,0:T(2,128)S(1)}, u32[]{:S(2)}) copy-start(f32[1,2,4,128]{3,1,2,0:T(2,128)S(1)} %copy.118) | copy-start | bytes 12292
  19.4 44.2 %copy-start.43 = (f32[1,2,4,128]{3,1,2,0:T(2,128)}, f32[1,2,4,128]{3,1,2,0:T(2,128)S(1)}, u32[]{:S(2)}) copy-start(f32[1,2,4,128]{3,1,2,0:T(2,128)S(1)} %copy.117) | copy-start | bytes 12292
  19.6 44.0 %copy-start.45 = (f32[384]{0:T(512)}, f32[384]{0:T(512)S(1)}, u32[]{:S(2)}) copy-start(f32[384]{0:T(512)S(1)} %broadcast_multiply_fusion.1) | copy-start | bytes 4612
  20.0 43.7 %copy-start.52 = (f32[384]{0:T(512)}, f32[384]{0:T(512)S(1)}, u32[]{:S(2)}) copy-start(f32[384]{0:T(512)S(1)} %fusion.76) | copy-start | bytes 4612
  20.0 43.7 %copy-start.47 = (f32[384]{0:T(512)}, f32[384]{0:T(512)S(1)}, u32[]{:S(2)}) copy-start(f32[384]{0:T(512)S(1)} %fusion.128) | copy-start | bytes 4612
  20.5 122.2 %copy-start.66 = (f32[1,2,4,128]{3,1,2,0:T(2,128)}, f32[1,2,4,128]{3,1,2,0:T(2,128)S(1)}, u32[]{:S(2)}) copy-start(f32[1,2,4,128]{3,1,2,0:T(2,128)S(1)} %copy.123) | copy-start | bytes 12292
  20.6 202.1 %copy-start.60 = (f32[1,2,4,128]{3,1,2,0:T(2,128)}, f32[1,2,4,128]{3,1,2,0:T(2,128)S(1)}, u32[]{:S(2)}) copy-start(f32[1,2,4,128]{3,1,2,0:T(2,128)S(1)} %copy.122) | copy-start | bytes 12292
  94.2 59.1 %copy-start.6 = (f32[384,1024]{1,0:T(8,128)}, f32[384,1024]{1,0:T(8,128)S(1)}, u32[]{:S(2)}) copy-start(f32[384,1024]{1,0:T(8,128)S(1)} %get-tuple-element.611) | copy-start | bytes 4718596
  94.2 128.5 %copy-start.50 = (f32[384]{0:T(512)}, f32[384]{0:T(512)S(1)}, u32[]{:S(2)}) copy-start(f32[384]{0:T(512)S(1)} %broadcast_multiply_fusion) | copy-start | bytes 4612
  94.5 128.1 %copy-start.62 = (f32[384]{0:T(512)}, f32[384]{0:T(512)S(1)}, u32[]{:S(2)}) copy-start(f32[384]{0:T(512)S(1)} %fusion.129) | copy-start | bytes 4612
  174.9 7.9 %collective-permute-start = (bf16[2048,1024]{1,0:T(8,128)(2,1)}, bf16[2048,1024]{1,0:T(8,128)(2,1)}, u32[]{:S(2)}, u32[]{:S(2)}) collective-permute-start(bf16[2048,1024]{1,0:T(8,128)(2,1)} %fusion.26), channel_id=1, source_target_pairs={{0,1},{1,0},{2,3},{3,2},{4,5},{5,4},{6,7},{7,6},{8,9},{9,8},{10,11... | collective-permute-start | bytes 12582920 | tf_op jit(solution)/shard_map/ppermute | solution.py:155
  176.0 26.4 %copy-start.18 = (bf16[1,384,1024]{2,1,0:T(8,128)(2,1)S(1)}, bf16[1,384,1024]{2,1,0:T(8,128)(2,1)}, u32[]{:S(2)}) copy-start(bf16[1,384,1024]{2,1,0:T(8,128)(2,1)} %param.22) | copy-start | bytes 2359300
  287.9 14.4 %copy-start.26 = (bf16[384,1024]{1,0:T(8,128)(2,1)S(1)}, bf16[384,1024]{1,0:T(8,128)(2,1)}, u32[]{:S(2)}) copy-start(bf16[384,1024]{1,0:T(8,128)(2,1)} %copy-done.25) | copy-start | bytes 2359300
  287.9 14.4 %copy-start.35 = (bf16[384,256]{0,1:T(8,128)(2,1)S(1)}, bf16[384,256]{0,1:T(8,128)(2,1)}, u32[]{:S(2)}) copy-start(bf16[384,256]{0,1:T(8,128)(2,1)} %get-tuple-element.579) | copy-start | bytes 589828
  287.9 14.4 %copy-start.36 = (bf16[384,256]{0,1:T(8,128)(2,1)S(1)}, bf16[384,256]{0,1:T(8,128)(2,1)}, u32[]{:S(2)}) copy-start(bf16[384,256]{0,1:T(8,128)(2,1)} %get-tuple-element.580) | copy-start | bytes 589828
  287.9 14.4 %copy-start.37 = (bf16[384,256]{0,1:T(8,128)(2,1)S(1)}, bf16[384,256]{0,1:T(8,128)(2,1)}, u32[]{:S(2)}) copy-start(bf16[384,256]{0,1:T(8,128)(2,1)} %get-tuple-element.581) | copy-start | bytes 589828
  322.4 63.3 %collective-permute-start.34 = (bf16[2560,1024]{1,0:T(8,128)(2,1)}, bf16[2560,1024]{1,0:T(8,128)(2,1)}, u32[]{:S(2)}, u32[]{:S(2)}) collective-permute-start(bf16[2560,1024]{1,0:T(8,128)(2,1)} %pad_maximum_fusion), channel_id=1, source_target_pairs={{0,1},{1,0},{2,3},{3,2},{4,5},{5,4},{6,7},{7,6},{8,9},{9,8},{10,11... | collective-permute-start | bytes 15728648 | tf_op jit(solution)/shard_map/ppermute | solution.py:155
  331.7 1.3 collective-permute-start.1
  333.0 4.7 collective-permute-start.2
  335.9 47.6 %collective-permute-start.33 = (bf16[1024,1024]{1,0:T(8,128)(2,1)S(1)}, bf16[1024,1024]{1,0:T(8,128)(2,1)S(1)}, u32[]{:S(2)}, u32[]{:S(2)}) collective-permute-start(bf16[1024,1024]{1,0:T(8,128)(2,1)S(1)} %fusion.62), channel_id=1, source_target_pairs={{0,2},{1,3},{2,0},{3,1},{4,6},{5,7},{6,4},{7,5},{8,10},{9,11},{10,... | collective-permute-start | bytes 6291464 | tf_op jit(solution)/shard_map/ppermute | solution.py:155
  337.7 9.9 %collective-permute-start.9 = (bf16[1,1024]{1,0:T(2,128)(2,1)S(1)}, bf16[1,1024]{1,0:T(2,128)(2,1)S(1)}, u32[]{:S(2)}, u32[]{:S(2)}) collective-permute-start(bf16[1,1024]{1,0:T(2,128)(2,1)S(1)} %get-tuple-element.596), channel_id=1, source_target_pairs={{0,28},{4,0},{8,4},{12,8},{16,12},{20,16},{24,20},{28,24},{1,29},{... | collective-permute-start | bytes 6152 | tf_op jit(solution)/shard_map/ppermute | solution.py:169
  342.0 5.7 collective-permute-start.8
  342.6 8.1 %collective-permute-start.7 = (bf16[1,1024]{1,0:T(2,128)(2,1)S(1)}, bf16[1,1024]{1,0:T(2,128)(2,1)S(1)}, u32[]{:S(2)}, u32[]{:S(2)}) collective-permute-start(bf16[1,1024]{1,0:T(2,128)(2,1)S(1)} %get-tuple-element.598), channel_id=1, source_target_pairs={{0,20},{4,24},{8,28},{12,0},{16,4},{20,8},{24,12},{28,16},{1,21},{... | collective-permute-start | bytes 6152 | tf_op jit(solution)/shard_map/ppermute | solution.py:169
  342.6 8.6 %copy-start.24 = (bf16[384,4096]{1,0:T(8,128)(2,1)S(1)}, bf16[384,4096]{1,0:T(8,128)(2,1)}, u32[]{:S(2)}) copy-start(bf16[384,4096]{1,0:T(8,128)(2,1)} %copy-done.23) | copy-start | bytes 9437188
  347.7 53.0 %collective-permute-start.17 = (bf16[1536,1024]{1,0:T(8,128)(2,1)}, bf16[1536,1024]{1,0:T(8,128)(2,1)}, u32[]{:S(2)}, u32[]{:S(2)}) collective-permute-start(bf16[1536,1024]{1,0:T(8,128)(2,1)} %fusion.34), channel_id=1, source_target_pairs={{0,1},{1,0},{2,3},{3,2},{4,5},{5,4},{6,7},{7,6},{8,9},{9,8},{10,11... | collective-permute-start | bytes 9437192 | tf_op jit(solution)/shard_map/ppermute | solution.py:155
  347.7 11.4 %collective-permute-start.6 = (bf16[1,1024]{1,0:T(2,128)(2,1)S(1)}, bf16[1,1024]{1,0:T(2,128)(2,1)S(1)}, u32[]{:S(2)}, u32[]{:S(2)}) collective-permute-start(bf16[1,1024]{1,0:T(2,128)(2,1)S(1)} %get-tuple-element.599), channel_id=1, source_target_pairs={{0,16},{4,20},{8,24},{12,28},{16,0},{20,4},{24,8},{28,12},{1,17},{... | collective-permute-start | bytes 6152 | tf_op jit(solution)/shard_map/ppermute | solution.py:169
  350.7 10.3 %collective-permute-start.5 = (bf16[1,1024]{1,0:T(2,128)(2,1)S(1)}, bf16[1,1024]{1,0:T(2,128)(2,1)S(1)}, u32[]{:S(2)}, u32[]{:S(2)}) collective-permute-start(bf16[1,1024]{1,0:T(2,128)(2,1)S(1)} %get-tuple-element.600), channel_id=1, source_target_pairs={{0,12},{4,16},{8,20},{12,24},{16,28},{20,0},{24,4},{28,8},{1,13},{... | collective-permute-start | bytes 6152 | tf_op jit(solution)/shard_map/ppermute | solution.py:169
  351.2 32.4 %slice-start = ((s8[8388608]{0:T(1024)(128)(4,1)}), s8[4194304]{0:T(1024)(128)(4,1)S(1)}, s32[]{:S(2)}) async-start(s8[8388608]{0:T(1024)(128)(4,1)} %bitcast.374), calls=%async_computation.6 | async-start | bytes 8388608
  351.2 32.4 %slice-start.1 = ((s8[8388608]{0:T(1024)(128)(4,1)}), s8[4194304]{0:T(1024)(128)(4,1)S(1)}, s32[]{:S(2)}) async-start(s8[8388608]{0:T(1024)(128)(4,1)} %bitcast.374), calls=%async_computation.7 | async-start | bytes 8388608
  359.0 6.2 collective-permute-start.4
  361.0 6.3 collective-permute-start.3
  367.3 47.2 %collective-permute-start.10 = (bf16[1,1024]{1,0:T(2,128)(2,1)S(1)}, bf16[1,1024]{1,0:T(2,128)(2,1)S(1)}, u32[]{:S(2)}, u32[]{:S(2)}) collective-permute-start(bf16[1,1024]{1,0:T(2,128)(2,1)S(1)} %get-tuple-element.548), channel_id=1, source_target_pairs={{0,4},{4,8},{8,12},{12,16},{16,20},{20,24},{24,28},{28,0},{1,5},{5... | collective-permute-start | bytes 6152 | tf_op jit(solution)/shard_map/ppermute | solution.py:177
  385.7 278.4 %all-reduce.7.cloned.1.call-start = ((), (), s32[]{:S(2)}) async-start(), calls=%async_computation.5 | async-start | bytes 5242880 | tf_op jit(solution)/shard_map/psum | solution.py:284
  399.0 104.8 %collective-permute-start.35 = (bf16[1280,1024]{1,0:T(8,128)(2,1)S(1)}, bf16[1280,1024]{1,0:T(8,128)(2,1)}, u32[]{:S(2)}, u32[]{:S(2)}) collective-permute-start(bf16[1280,1024]{1,0:T(8,128)(2,1)S(1)} %pad_maximum_fusion.1), channel_id=1, source_target_pairs={{0,2},{1,3},{2,0},{3,1},{4,6},{5,7},{6,4},{7,5},{8,10},{9,11},{10,... | collective-permute-start | bytes 7864328 | tf_op jit(solution)/shard_map/ppermute | solution.py:155
  407.1 86.7 %collective-permute-start.18 = (bf16[768,1024]{1,0:T(8,128)(2,1)}, bf16[768,1024]{1,0:T(8,128)(2,1)}, u32[]{:S(2)}, u32[]{:S(2)}) collective-permute-start(bf16[768,1024]{1,0:T(8,128)(2,1)} %fusion.78), channel_id=1, source_target_pairs={{0,2},{1,3},{2,0},{3,1},{4,6},{5,7},{6,4},{7,5},{8,10},{9,11},{10,... | collective-permute-start | bytes 4718600 | tf_op jit(solution)/shard_map/ppermute | solution.py:155
  410.6 5.6 collective-permute-start.11
  412.1 6.3 collective-permute-start.12
  414.5 5.6 collective-permute-start.13
  416.3 5.2 collective-permute-start.14
  418.5 3.7 collective-permute-start.15
  420.1 95.5 %collective-permute-start.16 = (bf16[1,1024]{1,0:T(2,128)(2,1)S(1)}, bf16[1,1024]{1,0:T(2,128)(2,1)S(1)}, u32[]{:S(2)}, u32[]{:S(2)}) collective-permute-start(bf16[1,1024]{1,0:T(2,128)(2,1)S(1)} %get-tuple-element.548), channel_id=1, source_target_pairs={{0,28},{4,0},{8,4},{12,8},{16,12},{20,16},{24,20},{28,24},{1,29},{... | collective-permute-start | bytes 6152 | tf_op jit(solution)/shard_map/ppermute | solution.py:177
  489.5 16.2 %slice-start.2 = ((s8[8388608]{0:T(1024)(128)(4,1)}), s8[4194304]{0:T(1024)(128)(4,1)S(1)}, s32[]{:S(2)}) async-start(s8[8388608]{0:T(1024)(128)(4,1)} %bitcast.378), calls=%async_computation.8 | async-start | bytes 8388608
  493.8 11.9 %slice-start.3 = ((s8[8388608]{0:T(1024)(128)(4,1)}), s8[4194304]{0:T(1024)(128)(4,1)S(1)}, s32[]{:S(2)}) async-start(s8[8388608]{0:T(1024)(128)(4,1)} %bitcast.378), calls=%async_computation.9 | async-start | bytes 8388608
  499.6 18.3 %collective-permute-start.25 = (bf16[96,1024]{1,0:T(8,128)(2,1)}, bf16[96,1024]{1,0:T(8,128)(2,1)}, u32[]{:S(2)}, u32[]{:S(2)}) collective-permute-start(bf16[96,1024]{1,0:T(8,128)(2,1)} %get-tuple-element.568), channel_id=1, source_target_pairs={{0,28},{4,0},{8,4},{12,8},{16,12},{20,16},{24,20},{28,24},{1,29},{... | collective-permute-start | bytes 589832 | tf_op jit(solution)/shard_map/ppermute | solution.py:169
  502.1 17.8 %collective-permute-start.24 = (bf16[96,1024]{1,0:T(8,128)(2,1)}, bf16[96,1024]{1,0:T(8,128)(2,1)}, u32[]{:S(2)}, u32[]{:S(2)}) collective-permute-start(bf16[96,1024]{1,0:T(8,128)(2,1)} %get-tuple-element.569), channel_id=1, source_target_pairs={{0,24},{4,28},{8,0},{12,4},{16,8},{20,12},{24,16},{28,20},{1,25},{... | collective-permute-start | bytes 589832 | tf_op jit(solution)/shard_map/ppermute | solution.py:169
  503.6 17.2 %collective-permute-start.23 = (bf16[96,1024]{1,0:T(8,128)(2,1)}, bf16[96,1024]{1,0:T(8,128)(2,1)}, u32[]{:S(2)}, u32[]{:S(2)}) collective-permute-start(bf16[96,1024]{1,0:T(8,128)(2,1)} %get-tuple-element.570), channel_id=1, source_target_pairs={{0,20},{4,24},{8,28},{12,0},{16,4},{20,8},{24,12},{28,16},{1,21},{... | collective-permute-start | bytes 589832 | tf_op jit(solution)/shard_map/ppermute | solution.py:169
  503.8 55.2 %collective-permute-start.22 = (bf16[96,1024]{1,0:T(8,128)(2,1)}, bf16[96,1024]{1,0:T(8,128)(2,1)S(1)}, u32[]{:S(2)}, u32[]{:S(2)}) collective-permute-start(bf16[96,1024]{1,0:T(8,128)(2,1)} %get-tuple-element.571), channel_id=1, source_target_pairs={{0,16},{4,20},{8,24},{12,28},{16,0},{20,4},{24,8},{28,12},{1,17},{... | collective-permute-start | bytes 589832 | tf_op jit(solution)/shard_map/ppermute | solution.py:169
  516.5 42.5 %collective-permute-start.21 = (bf16[96,1024]{1,0:T(8,128)(2,1)S(1)}, bf16[96,1024]{1,0:T(8,128)(2,1)S(1)}, u32[]{:S(2)}, u32[]{:S(2)}) collective-permute-start(bf16[96,1024]{1,0:T(8,128)(2,1)S(1)} %copy-done.40), channel_id=1, source_target_pairs={{0,12},{4,16},{8,20},{12,24},{16,28},{20,0},{24,4},{28,8},{1,13},{... | collective-permute-start | bytes 589832 | tf_op jit(solution)/shard_map/ppermute | solution.py:169
  517.9 41.2 %collective-permute-start.20 = (bf16[96,1024]{1,0:T(8,128)(2,1)S(1)}, bf16[96,1024]{1,0:T(8,128)(2,1)S(1)}, u32[]{:S(2)}, u32[]{:S(2)}) collective-permute-start(bf16[96,1024]{1,0:T(8,128)(2,1)S(1)} %copy-done.39), channel_id=1, source_target_pairs={{0,8},{4,12},{8,16},{12,20},{16,24},{20,28},{24,0},{28,4},{1,9},{5... | collective-permute-start | bytes 589832 | tf_op jit(solution)/shard_map/ppermute | solution.py:169
  519.9 39.2 %collective-permute-start.19 = (bf16[96,1024]{1,0:T(8,128)(2,1)S(1)}, bf16[96,1024]{1,0:T(8,128)(2,1)S(1)}, u32[]{:S(2)}, u32[]{:S(2)}) collective-permute-start(bf16[96,1024]{1,0:T(8,128)(2,1)S(1)} %copy-done.38), channel_id=1, source_target_pairs={{0,4},{4,8},{8,12},{12,16},{16,20},{20,24},{24,28},{28,0},{1,5},{5... | collective-permute-start | bytes 589832 | tf_op jit(solution)/shard_map/ppermute | solution.py:169
  560.8 13.7 %collective-permute-start.26 = (bf16[96,1024]{1,0:T(8,128)(2,1)S(1)}, bf16[96,1024]{1,0:T(8,128)(2,1)S(1)}, u32[]{:S(2)}, u32[]{:S(2)}) collective-permute-start(bf16[96,1024]{1,0:T(8,128)(2,1)S(1)} %get-tuple-element.546), channel_id=1, source_target_pairs={{0,4},{4,8},{8,12},{12,16},{16,20},{20,24},{24,28},{28,0},{1,5},{5... | collective-permute-start | bytes 589832 | tf_op jit(solution)/shard_map/ppermute | solution.py:177
  561.4 15.4 %collective-permute-start.27 = (bf16[96,1024]{1,0:T(8,128)(2,1)S(1)}, bf16[96,1024]{1,0:T(8,128)(2,1)S(1)}, u32[]{:S(2)}, u32[]{:S(2)}) collective-permute-start(bf16[96,1024]{1,0:T(8,128)(2,1)S(1)} %get-tuple-element.546), channel_id=1, source_target_pairs={{0,8},{4,12},{8,16},{12,20},{16,24},{20,28},{24,0},{28,4},{1,9},{5... | collective-permute-start | bytes 589832 | tf_op jit(solution)/shard_map/ppermute | solution.py:177
  568.2 28.4 %collective-permute-start.28 = (bf16[96,1024]{1,0:T(8,128)(2,1)S(1)}, bf16[96,1024]{1,0:T(8,128)(2,1)S(1)}, u32[]{:S(2)}, u32[]{:S(2)}) collective-permute-start(bf16[96,1024]{1,0:T(8,128)(2,1)S(1)} %get-tuple-element.546), channel_id=1, source_target_pairs={{0,12},{4,16},{8,20},{12,24},{16,28},{20,0},{24,4},{28,8},{1,13},{... | collective-permute-start | bytes 589832 | tf_op jit(solution)/shard_map/ppermute | solution.py:177
  571.6 27.2 %collective-permute-start.29 = (bf16[96,1024]{1,0:T(8,128)(2,1)S(1)}, bf16[96,1024]{1,0:T(8,128)(2,1)S(1)}, u32[]{:S(2)}, u32[]{:S(2)}) collective-permute-start(bf16[96,1024]{1,0:T(8,128)(2,1)S(1)} %get-tuple-element.546), channel_id=1, source_target_pairs={{0,16},{4,20},{8,24},{12,28},{16,0},{20,4},{24,8},{28,12},{1,17},{... | collective-permute-start | bytes 589832 | tf_op jit(solution)/shard_map/ppermute | solution.py:177
  573.5 25.4 %collective-permute-start.30 = (bf16[96,1024]{1,0:T(8,128)(2,1)S(1)}, bf16[96,1024]{1,0:T(8,128)(2,1)S(1)}, u32[]{:S(2)}, u32[]{:S(2)}) collective-permute-start(bf16[96,1024]{1,0:T(8,128)(2,1)S(1)} %get-tuple-element.546), channel_id=1, source_target_pairs={{0,20},{4,24},{8,28},{12,0},{16,4},{20,8},{24,12},{28,16},{1,21},{... | collective-permute-start | bytes 589832 | tf_op jit(solution)/shard_map/ppermute | solution.py:177
  574.5 24.4 %collective-permute-start.31 = (bf16[96,1024]{1,0:T(8,128)(2,1)S(1)}, bf16[96,1024]{1,0:T(8,128)(2,1)S(1)}, u32[]{:S(2)}, u32[]{:S(2)}) collective-permute-start(bf16[96,1024]{1,0:T(8,128)(2,1)S(1)} %get-tuple-element.546), channel_id=1, source_target_pairs={{0,24},{4,28},{8,0},{12,4},{16,8},{20,12},{24,16},{28,20},{1,25},{... | collective-permute-start | bytes 589832 | tf_op jit(solution)/shard_map/ppermute | solution.py:177
  576.9 23.9 %collective-permute-start.32 = (bf16[96,1024]{1,0:T(8,128)(2,1)S(1)}, bf16[96,1024]{1,0:T(8,128)(2,1)S(1)}, u32[]{:S(2)}, u32[]{:S(2)}) collective-permute-start(bf16[96,1024]{1,0:T(8,128)(2,1)S(1)} %get-tuple-element.546), channel_id=1, source_target_pairs={{0,28},{4,0},{8,4},{12,8},{16,12},{20,16},{24,20},{28,24},{1,29},{... | collective-permute-start | bytes 589832 | tf_op jit(solution)/shard_map/ppermute | solution.py:177
  (82 other events, 254.1 us)
Sparse Core Ops, SparseCore 0:
  9.6 49.0 all-gather.5
  60.3 22.5 all-gather.7
  84.4 58.2 all-gather.9
  144.1 58.2 all-gather.11
  385.8 103.6 all-reduce.4
  515.7 148.2 all-reduce.6

commit v10 on v9

--- a/solution.py
+++ b/solution.py
@@ -290,9 +290,10 @@
     grad_qkv_t = jnp.einsum(
         "tc,ti->ci", reorder_cols(grad_proj, order), normed, preferred_element_type=jnp.float32
     )
-    (qkv_own,) = halving([grad_qkv_t], "shard", shard_count, shard_steps)
+    qkv_half = halving([grad_qkv_t], "shard", shard_count, shard_steps[:1])
+    qkv_half, grad_proj = lax.optimization_barrier((qkv_half, grad_proj))
+    (qkv_own,) = halving(qkv_half, "shard", shard_count, shard_steps[1:])
     total_b = direct_reduce(qkv_own, "rep", reps)
-    grad_qkv_t, grad_proj = lax.optimization_barrier((grad_qkv_t, grad_proj))
     grad_qb = jnp.sum(grad_q.astype(jnp.float32), 0)
     grad_vb = jnp.sum(grad_v.astype(jnp.float32), 0)
     grad_normed = jnp.einsum("tc,ic->ti", grad_proj, back_qkv, preferred_element_type=jnp.float32)

time: 682 us -> 662 us (0.971)
  waiting for transfers between devices: 315 us -> 302 us
  matrix products: 99.1 us -> 88.7 us
  starting transfers between devices: 55.1 us -> 45.4 us
  local copies, waits for them, and re-layouts: 95.2 us -> 103 us
    ppermute x8, waiting for transfers between devices: 23.7 us -> 9.51 us  [halving(): lax.ppermute(jnp.concatenate(sends, 0), axis, [(a, a ^ step) for a in ran...]
    ppermute x14, starting transfers between devices: 29 us -> 18 us  [direct_reduce(): lax.ppermute(mine, axis, [(a, (a + shift) % size) for a in range(size)])]
    dot_general x1, matrix products: 14.3 us -> 3.63 us  [body_inner(): jnp.einsum('tc,ti->ci', reorder_cols(grad_proj, order), normed, preferred...]
    psum x1, waiting for transfers between devices: 67.4 us -> 57.8 us  [body_inner(): total_a1 = lax.psum(down_own.astype(jnp.bfloat16), 'rep')]
    psum x1, waiting for transfers between devices: 60.4 us -> 68.3 us  [body_inner(): total_a = lax.psum(joined_a, 'rep')]
    unnamed x193 -> x209, local copies, waits for them, and re-layouts: 29.2 us -> 32.4 us
  transfers between devices with their start and end apart: 42 -> 42, of which waited for: 16 -> 17; matrix products, arithmetic and copies ran while one was open for 20% -> 25% of each run, Pallas kernels for 0% -> 0%
where the time goes in v10:
time: 662 us; the launch traced here: 658 us
  waiting for transfers between devices  302 us (46%)
  local copies, waits for them, and re-layouts  103 us (16%)
  matrix products  88.7 us (13%)
  other arithmetic  77.6 us (12%)
  starting transfers between devices  45.4 us (7%)
  loops' own time  18.9 us (3%)
  between operations  15.8 us (2%)
    psum x1, waiting for transfers between devices, body_inner(): total_a = lax.psum(joined_a, 'rep')  68.3 us
    psum x1, waiting for transfers between devices, body_inner(): total_a1 = lax.psum(down_own.astype(jnp.bfloat16), 'rep')  57.8 us
    all_gather x1, waiting for transfers between devices, body_inner(): full_up = lax.all_gather(w_up, 'shard', axis=1, tiled=True)  48.3 us
    ppermute x14, waiting for transfers between devices, direct_reduce(): lax.ppermute(send.astype(jnp.bfloat16), axis, [(a, (a + shift) % size) fo...  42.2 us
    all_gather x1, waiting for transfers between devices, body_inner(): full_qkv = lax.all_gather(w_qkv, 'shard', axis=1, tiled=True)  38.7 us
    unnamed x209, local copies, waits for them, and re-layouts  32.4 us
    add x6, other arithmetic, halving(): arrays.append(keep + got[offset:offset + keep.shape[0]].astype(jnp.float32))  27.2 us
    ppermute x14, waiting for transfers between devices, direct_reduce(): lax.ppermute(mine, axis, [(a, (a + shift) % size) for a in range(size)])  24.7 us
  transfers between devices with their start and end apart: 42, of which 17 were waited for; matrix products, arithmetic and copies ran while one was open for 25% of the time, Pallas kernels for 0%

profile of v10, /device:TPU:0, one launch (start us, length us, event | category | flops | bytes accessed | tf_op | source)
XLA Modules:
  0.0 657.7 jit_solution(8594248362266508695)
XLA Ops:
  12.2 6.4 all-gather
  20.0 38.7 %all-gather.6.cloned.1.call-done = bf16[1024,3072]{1,0:T(8,128)(2,1)} async-done(((bf16[1024,768]{1,0:T(8,128)(2,1)}), bf16[1024,3072]{1,0:T(8,128)(2,1)}) %all-gather.6.cloned.1.call-update) | async-done | bytes 6291472 | tf_op jit(solution)/shard_map/all_gather | solution.py:215
  58.7 4.9 fusion.79
  68.3 21.3 %while.32 = (s32[]{:T(128)}, bf16[4,384,256]{1,2,0:T(8,128)(2,1)}, f32[4,4,384]{2,1,0:T(4,128)}, s32[4]{0:T(128)S(1)}, bf16[384,1024]{0,1:T(8,128)(2,1)S(1)}, /*...) while((s32[]{:T(128)}, bf16[4,384,256]{1,2,0:T(8,128)(2,1)}, ...), condition=%wide.region_6.7_spmd.clone, body=%wide.region_3.6_spmd.clone.sunk | while | flops 157776416 | bytes 10964623 | solution.py:74
  90.8 3.3 fusion.142
  94.4 48.3 %all-gather.10.cloned.1.call-done = bf16[1024,4096]{1,0:T(8,128)(2,1)} async-done(((bf16[1024,1024]{1,0:T(8,128)(2,1)}), bf16[1024,4096]{1,0:T(8,128)(2,1)}) %all-gather.10.cloned.1.call-update) | async-done | bytes 8388624 | tf_op jit(solution)/shard_map/all_gather | solution.py:217
  142.7 10.6 %multiply_convert_fusion.1 = (bf16[384,4096]{1,0:T(8,128)(2,1)S(1)}, f32[384,4096]{1,0:T(8,128)}) fusion(f32[4096]{0:T(1024)S(1)} %bitcast.430, bf16[1024,4096]{1,0:T(8,128)(2,1)} %all-gather.10.cloned.1.call-done, f32[384,1024]{1,0:T(8,128)S(1)} %get-tuple-element.615, f32[1024]{0:T(1024)S(1)} %bitcast.437, f32[1024]{0:T(1024)S(1)} %bitcast.431, ...), kind=kOutput, calls=%fused_computation.62 | convolution fusion | flops 3238920192 | bytes 19426304 | tf_op jit(solution)/shard_map/dot_general | solution.py:237
  154.9 1.8 maximum_bitcast_fusion
  156.7 3.7 copy.119
  160.4 5.7 fusion.89
  166.1 5.8 copy-done
  171.9 2.7 fusion.26
  176.4 6.1 collective-permute-done
  182.5 10.3 %bitcast_add_fusion.1 = f32[2048,1024]{1,0:T(8,128)} fusion(bf16[2048,1024]{1,0:T(8,128)(2,1)} %collective-permute-done, f32[2,2048,1024]{2,1,0:T(8,128)} %copy-done, s32[]{:T(128)S(6)} %select_n.262), kind=kLoop, calls=%fused_computation.40 | loop fusion | flops 4194304 | bytes 20971524 | tf_op jit(solution)/shard_map/add | solution.py:158
  192.8 9.6 %all-gather.12.cloned.1.call-done = bf16[4096,1024]{1,0:T(8,128)(2,1)} async-done(((bf16[1024,1024]{1,0:T(8,128)(2,1)}), bf16[4096,1024]{1,0:T(8,128)(2,1)}) %all-gather.12.cloned.1.call-update) | async-done | bytes 8388624 | tf_op jit(solution)/shard_map/all_gather | solution.py:218
  202.4 10.9 %convert_reduce_fusion = (f32[4096]{0:T(1024)}, bf16[384,4096]{1,0:T(8,128)(2,1)S(1)}) fusion(f32[384,4096]{1,0:T(8,128)} %get-tuple-element.617, bf16[4096,1024]{1,0:T(8,128)(2,1)} %all-gather.12.cloned.1.call-done, bf16[1,384,1024]{2,1,0:T(8,128)(2,1)S(1)} %copy-done.18), kind=kOutput, calls=%fused_computation.60 | convolution fusion | flops 3255824384 | bytes 18628608 | tf_op jit(solution)/shard_map/to,fo->tf/dot_general | solution.py:259
  213.3 8.4 %multiply_reduce_fusion.1 = (f32[1024]{0:T(1024)}, f32[384]{0:T(512)S(1)}, f32[1024]{0:T(1024)}, f32[384,1024]{1,0:T(8,128)S(1)}) fusion(f32[384,1024]{1,0:T(8,128)S(1)} %copy-done.7, f32[384]{0:T(512)S(1)} %fusion.129, f32[384]{0:T(512)S(1)} %broadcast_multiply_fusion, f32[1024]{0:T(1024)S(1)} %bitcast.432, bf16[384,4096]{1,0:T(8,128)(2,1)S(1)} %get-tuple-element.621, ...), kind=kOutput, calls=%fused_computation.136 | convolution fusion | flops 3224368640 | bytes 14696960 | tf_op jit(solution)/shard_map/tf,if->ti/dot_general | solution.py:268
  228.7 54.6 %while.33 = (s32[]{:T(128)}, bf16[4,384,256]{1,2,0:T(8,128)(2,1)}, bf16[4,384,256]{1,2,0:T(8,128)(2,1)}, bf16[4,384,256]{1,2,0:T(8,128)(2,1)}, s32[4]{0:T(128)S(...) while((s32[]{:T(128)}, bf16[4,384,256]{1,2,0:T(8,128)(2,1)}, ...), condition=%wide.region_13.14_spmd.clone, body=%wide.region_11.13_spmd.clone.sunk | while | flops 385251872 | bytes 30610428 | solution.py:113
  285.9 2.3 pad_maximum_fusion.3
  288.2 3.6 fusion.77
  291.9 4.6 copy-done.1
  296.5 2.1 fusion.34
  301.9 3.8 fusion.48
  307.4 2.0 copy-done.4
  312.0 9.7 %fusion.35 = f32[4096,1024]{1,0:T(8,128)} fusion(bf16[384,1024]{1,0:T(8,128)(2,1)S(1)} %get-tuple-element.566, bf16[384,1024]{1,0:T(8,128)(2,1)S(1)} %get-tuple-element.567, bf16[384,1024]{1,0:T(8,128)(2,1)S(1)} %get-tuple-element.568, bf16[384,1024]{1,0:T(8,128)(2,1)S(1)} %get-tuple-element.565, f32[384,1024]{1,0:T(8,128)S(1)} %copy-done.8, ...), kind=kOutput, calls=%fused_computation.81 | convolution fusion | flops 3235774464 | bytes 21507072 | tf_op jit(solution)/shard_map/tf,ti->fi/dot_general | solution.py:265
  321.7 6.2 fusion.27
  327.9 5.5 pad_maximum_fusion
  335.1 5.8 bitcast_add_fusion.2
  340.9 2.9 fusion.133
  346.7 8.8 %fusion.71 = bf16[1,384,1024]{2,1,0:T(8,128)(2,1)} fusion(f32[384,1024]{1,0:T(8,128)S(1)} %copy-done.8, bf16[384,4096]{1,0:T(8,128)(2,1)} %copy-done.23, bf16[4096,1024]{1,0:T(8,128)(2,1)} %all-gather.12.cloned.1.call-done, f32[1024]{0:T(1024)S(1)} %bitcast.439), kind=kOutput, calls=%fused_computation.146 | convolution fusion | flops 3222405120 | bytes 13897728 | tf_op jit(solution)/shard_map/dot_general | solution.py:250
  355.5 1.7 collective-permute-start.3
  357.3 3.8 fusion.29
  361.2 4.3 collective-permute-start.10
  366.3 2.3 bitcast_add_fusion.6
  370.0 5.9 bitcast_add_fusion
  376.6 2.8 copy-done.5
  380.0 3.3 collective-permute-start.7
  383.3 1.9 collective-permute-start.5
  385.9 3.3 fusion.68
  389.2 1.7 collective-permute-start.18
  394.4 2.4 collective-permute-start.12
  406.1 57.8 %all-reduce.5.cloned.1.call-done = bf16[1024,1024]{1,0:T(8,128)(2,1)} async-done(((bf16[1024,1024]{1,0:T(8,128)(2,1)}), bf16[1024,1024]{1,0:T(8,128)(2,1)}) %all-reduce.5.cloned.1.call-update) | async-done | bytes 2097168 | tf_op jit(solution)/shard_map/psum | solution.py:264
  463.9 4.2 convert_element_type.589
  468.1 3.4 collective-permute-done.18
  471.5 2.9 bitcast_add_fusion.5
  474.4 1.7 copy-done.16
  478.7 3.5 collective-permute-start.24
  482.2 3.8 fusion.50
  486.0 2.9 copy.112
  490.4 1.7 pad_maximum_fusion.2
  493.0 2.9 collective-permute-start.21
  495.9 2.0 collective-permute-start.20
  499.2 41.4 %collective-permute-done.22 = bf16[96,1024]{1,0:T(8,128)(2,1)S(1)} collective-permute-done((bf16[96,1024]{1,0:T(8,128)(2,1)}, bf16[96,1024]{1,0:T(8,128)(2,1)S(1)}, u32[]{:S(2)}, u32[]{:S(2)}) %collective-permute-start.22) | collective-permute-done | bytes 196640 | tf_op jit(solution)/shard_map/ppermute | solution.py:169
  543.0 1.9 collective-permute-start.28
  544.8 3.5 collective-permute-start.29
  548.3 4.8 collective-permute-done.26
  553.1 3.7 collective-permute-start.32
  556.8 8.7 %collective-permute-done.28 = bf16[96,1024]{1,0:T(8,128)(2,1)S(1)} collective-permute-done((bf16[96,1024]{1,0:T(8,128)(2,1)S(1)}, bf16[96,1024]{1,0:T(8,128)(2,1)S(1)}, u32[]{:S(2)}, u32[]{:S(2)}) %collective-permute-start.28) | collective-permute-done | bytes 196640 | tf_op jit(solution)/shard_map/ppermute | solution.py:177
  565.5 5.3 collective-permute-done.29
  571.0 2.3 collective-permute-done.32
  573.8 2.4 copy.113
  576.1 68.3 %all-reduce.7.cloned.1.call-done = bf16[1280,1024]{1,0:T(8,128)(2,1)} async-done(((bf16[1280,1024]{1,0:T(8,128)(2,1)}), bf16[1280,1024]{1,0:T(8,128)(2,1)}) %all-reduce.7.cloned.1.call-update) | async-done | bytes 2621456 | tf_op jit(solution)/shard_map/psum | solution.py:284
  644.5 2.1 slice_convert_fusion.2
  646.6 4.1 slice_convert_fusion
  (530 shorter events, 120.1 us)
Async XLA Ops:
  7.2 51.5 %all-gather.6.cloned.1.call-start = ((), (), s32[]{:S(2)}) async-start(), calls=%async_computation | async-start | bytes 7864320 | tf_op jit(solution)/shard_map/all_gather | solution.py:215
  8.0 81.6 %all-gather.8.cloned.1.call-start = ((), (), s32[]{:S(2)}) async-start(), calls=%async_computation.1 | async-start | bytes 2621440 | tf_op jit(solution)/shard_map/all_gather | solution.py:216
  8.8 133.9 %all-gather.10.cloned.1.call-start = ((), (), s32[]{:S(2)}) async-start(), calls=%async_computation.2 | async-start | bytes 10485760 | tf_op jit(solution)/shard_map/all_gather | solution.py:217
  9.5 192.9 %all-gather.12.cloned.1.call-start = ((), (), s32[]{:S(2)}) async-start(), calls=%async_computation.3 | async-start | bytes 10485760 | tf_op jit(solution)/shard_map/all_gather | solution.py:218
  10.1 453.8 %all-reduce.5.cloned.1.call-start = ((), (), s32[]{:S(2)}) async-start(), calls=%async_computation.4 | async-start | bytes 4194304 | tf_op jit(solution)/shard_map/psum | solution.py:264
  18.7 44.9 %copy-start.64 = (f32[1,2,4,128]{3,1,2,0:T(2,128)}, f32[1,2,4,128]{3,1,2,0:T(2,128)S(1)}, u32[]{:S(2)}) copy-start(f32[1,2,4,128]{3,1,2,0:T(2,128)S(1)} %copy.126) | copy-start | bytes 12292
  18.7 44.9 %copy-start.40 = (f32[1,2,4,128]{3,1,2,0:T(2,128)}, f32[1,2,4,128]{3,1,2,0:T(2,128)S(1)}, u32[]{:S(2)}) copy-start(f32[1,2,4,128]{3,1,2,0:T(2,128)S(1)} %copy.125) | copy-start | bytes 12292
  18.9 44.7 %copy-start.44 = (f32[384]{0:T(512)}, f32[384]{0:T(512)S(1)}, u32[]{:S(2)}) copy-start(f32[384]{0:T(512)S(1)} %broadcast_multiply_fusion.1) | copy-start | bytes 4612
  19.3 44.3 %copy-start.51 = (f32[384]{0:T(512)}, f32[384]{0:T(512)S(1)}, u32[]{:S(2)}) copy-start(f32[384]{0:T(512)S(1)} %fusion.62) | copy-start | bytes 4612
  19.3 44.3 %copy-start.46 = (f32[384]{0:T(512)}, f32[384]{0:T(512)S(1)}, u32[]{:S(2)}) copy-start(f32[384]{0:T(512)S(1)} %fusion.128) | copy-start | bytes 4612
  19.9 122.8 %copy-start.68 = (f32[1,2,4,128]{3,1,2,0:T(2,128)}, f32[1,2,4,128]{3,1,2,0:T(2,128)S(1)}, u32[]{:S(2)}) copy-start(f32[1,2,4,128]{3,1,2,0:T(2,128)S(1)} %copy.131) | copy-start | bytes 12292
  19.9 201.9 %copy-start.62 = (f32[1,2,4,128]{3,1,2,0:T(2,128)}, f32[1,2,4,128]{3,1,2,0:T(2,128)S(1)}, u32[]{:S(2)}) copy-start(f32[1,2,4,128]{3,1,2,0:T(2,128)S(1)} %copy.130) | copy-start | bytes 12292
  94.1 59.2 %copy-start.6 = (f32[384,1024]{1,0:T(8,128)}, f32[384,1024]{1,0:T(8,128)S(1)}, u32[]{:S(2)}) copy-start(f32[384,1024]{1,0:T(8,128)S(1)} %get-tuple-element.615) | copy-start | bytes 4718596
  94.1 127.7 %copy-start.49 = (f32[384]{0:T(512)}, f32[384]{0:T(512)S(1)}, u32[]{:S(2)}) copy-start(f32[384]{0:T(512)S(1)} %broadcast_multiply_fusion) | copy-start | bytes 4612
  94.4 127.4 %copy-start.66 = (f32[384]{0:T(512)}, f32[384]{0:T(512)S(1)}, u32[]{:S(2)}) copy-start(f32[384]{0:T(512)S(1)} %fusion.129) | copy-start | bytes 4612
  174.6 7.9 %collective-permute-start = (bf16[2048,1024]{1,0:T(8,128)(2,1)}, bf16[2048,1024]{1,0:T(8,128)(2,1)}, u32[]{:S(2)}, u32[]{:S(2)}) collective-permute-start(bf16[2048,1024]{1,0:T(8,128)(2,1)} %fusion.26), channel_id=1, source_target_pairs={{0,1},{1,0},{2,3},{3,2},{4,5},{5,4},{6,7},{7,6},{8,9},{9,8},{10,11... | collective-permute-start | bytes 12582920 | tf_op jit(solution)/shard_map/ppermute | solution.py:155
  176.4 26.0 %copy-start.18 = (bf16[1,384,1024]{2,1,0:T(8,128)(2,1)S(1)}, bf16[1,384,1024]{2,1,0:T(8,128)(2,1)}, u32[]{:S(2)}) copy-start(bf16[1,384,1024]{2,1,0:T(8,128)(2,1)} %param.22) | copy-start | bytes 2359300
  202.4 10.9 %copy-start.7 = (f32[384,1024]{1,0:T(8,128)S(1)}, f32[384,1024]{1,0:T(8,128)}, u32[]{:S(2)}) copy-start(f32[384,1024]{1,0:T(8,128)} %copy-done.6) | copy-start | bytes 4718596
  298.6 36.5 %collective-permute-start.1 = (bf16[1536,1024]{1,0:T(8,128)(2,1)}, bf16[1536,1024]{1,0:T(8,128)(2,1)}, u32[]{:S(2)}, u32[]{:S(2)}) collective-permute-start(bf16[1536,1024]{1,0:T(8,128)(2,1)} %fusion.34), channel_id=1, source_target_pairs={{0,1},{1,0},{2,3},{3,2},{4,5},{5,4},{6,7},{7,6},{8,9},{9,8},{10,11... | collective-permute-start | bytes 9437192 | tf_op jit(solution)/shard_map/ppermute | solution.py:155
  305.8 51.5 %collective-permute-start.33 = (bf16[1024,1024]{1,0:T(8,128)(2,1)}, bf16[1024,1024]{1,0:T(8,128)(2,1)}, u32[]{:S(2)}, u32[]{:S(2)}) collective-permute-start(bf16[1024,1024]{1,0:T(8,128)(2,1)} %fusion.48), channel_id=1, source_target_pairs={{0,2},{1,3},{2,0},{3,1},{4,6},{5,7},{6,4},{7,5},{8,10},{9,11},{10,... | collective-permute-start | bytes 6291464 | tf_op jit(solution)/shard_map/ppermute | solution.py:155
  312.0 23.1 %slice-start = ((s8[12582912]{0:T(1024)(128)(4,1)}), s8[4194304]{0:T(1024)(128)(4,1)S(1)}, s32[]{:S(2)}) async-start(s8[12582912]{0:T(1024)(128)(4,1)} %bitcast.376), calls=%async_computation.6 | async-start | bytes 8388608
  312.0 23.1 %slice-start.1 = ((s8[12582912]{0:T(1024)(128)(4,1)}), s8[4194304]{0:T(1024)(128)(4,1)S(1)}, s32[]{:S(2)}) async-start(s8[12582912]{0:T(1024)(128)(4,1)} %bitcast.376), calls=%async_computation.7 | async-start | bytes 8388608
  321.7 13.4 %slice-start.2 = ((s8[12582912]{0:T(1024)(128)(4,1)}), s8[4194304]{0:T(1024)(128)(4,1)S(1)}, s32[]{:S(2)}) async-start(s8[12582912]{0:T(1024)(128)(4,1)} %bitcast.376), calls=%async_computation.8 | async-start | bytes 8388608
  333.4 32.9 %collective-permute-start.34 = (bf16[2560,1024]{1,0:T(8,128)(2,1)}, bf16[2560,1024]{1,0:T(8,128)(2,1)}, u32[]{:S(2)}, u32[]{:S(2)}) collective-permute-start(bf16[2560,1024]{1,0:T(8,128)(2,1)} %pad_maximum_fusion), channel_id=1, source_target_pairs={{0,1},{1,0},{2,3},{3,2},{4,5},{5,4},{6,7},{7,6},{8,9},{9,8},{10,11... | collective-permute-start | bytes 15728648 | tf_op jit(solution)/shard_map/ppermute | solution.py:155
  346.2 9.4 %collective-permute-start.2 = (bf16[16,1024]{1,0:T(8,128)(2,1)S(1)}, bf16[16,1024]{1,0:T(8,128)(2,1)S(1)}, u32[]{:S(2)}, u32[]{:S(2)}) collective-permute-start(bf16[16,1024]{1,0:T(8,128)(2,1)S(1)} %fusion.116), channel_id=1, source_target_pairs={{0,1},{1,0},{2,3},{3,2},{4,5},{5,4},{6,7},{7,6},{8,9},{9,8},{10,11... | collective-permute-start | bytes 98312 | tf_op jit(solution)/shard_map/ppermute | solution.py:155
  355.5 5.6 collective-permute-start.3
  361.1 283.3 %all-reduce.7.cloned.1.call-start = ((), (), s32[]{:S(2)}) async-start(), calls=%async_computation.5 | async-start | bytes 5242880 | tf_op jit(solution)/shard_map/psum | solution.py:284
  361.2 22.0 %collective-permute-start.10 = (bf16[1,1024]{1,0:T(2,128)(2,1)S(1)}, bf16[1,1024]{1,0:T(2,128)(2,1)S(1)}, u32[]{:S(2)}, u32[]{:S(2)}) collective-permute-start(bf16[1,1024]{1,0:T(2,128)(2,1)S(1)} %get-tuple-element.600), channel_id=1, source_target_pairs={{0,28},{4,0},{8,4},{12,8},{16,12},{20,16},{24,20},{28,24},{1,29},{... | collective-permute-start | bytes 6152 | tf_op jit(solution)/shard_map/ppermute | solution.py:169
  365.5 17.8 %collective-permute-start.9 = (bf16[1,1024]{1,0:T(2,128)(2,1)S(1)}, bf16[1,1024]{1,0:T(2,128)(2,1)S(1)}, u32[]{:S(2)}, u32[]{:S(2)}) collective-permute-start(bf16[1,1024]{1,0:T(2,128)(2,1)S(1)} %get-tuple-element.601), channel_id=1, source_target_pairs={{0,24},{4,28},{8,0},{12,4},{16,8},{20,12},{24,16},{28,20},{1,25},{... | collective-permute-start | bytes 6152 | tf_op jit(solution)/shard_map/ppermute | solution.py:169
  366.1 19.2 %collective-permute-start.8 = (bf16[1,1024]{1,0:T(2,128)(2,1)S(1)}, bf16[1,1024]{1,0:T(2,128)(2,1)S(1)}, u32[]{:S(2)}, u32[]{:S(2)}) collective-permute-start(bf16[1,1024]{1,0:T(2,128)(2,1)S(1)} %get-tuple-element.602), channel_id=1, source_target_pairs={{0,20},{4,24},{8,28},{12,0},{16,4},{20,8},{24,12},{28,16},{1,21},{... | collective-permute-start | bytes 6152 | tf_op jit(solution)/shard_map/ppermute | solution.py:169
  376.3 16.5 %copy-start.22 = (f32[384,1024]{1,0:T(8,128)S(1)}, f32[384,1024]{1,0:T(8,128)}, u32[]{:S(2)}) copy-start(f32[384,1024]{1,0:T(8,128)} %copy-done.21) | copy-start | bytes 4718596
  379.3 13.4 %copy-start.10 = (f32[384,1024]{1,0:T(8,128)S(1)}, f32[384,1024]{1,0:T(8,128)}, u32[]{:S(2)}) copy-start(f32[384,1024]{1,0:T(8,128)} %copy-done.9) | copy-start | bytes 4718596
  379.3 13.4 %copy-start.19 = (bf16[1,384,1024]{2,1,0:T(8,128)(2,1)S(1)}, bf16[1,384,1024]{2,1,0:T(8,128)(2,1)}, u32[]{:S(2)}) copy-start(bf16[1,384,1024]{2,1,0:T(8,128)(2,1)} %param.22) | copy-start | bytes 2359300
  379.4 13.4 %copy-start.48 = (f32[384]{0:T(512)S(1)}, f32[384]{0:T(512)}, u32[]{:S(2)}) copy-start(f32[384]{0:T(512)} %copy-done.46) | copy-start | bytes 4612
  379.4 13.4 %copy-start.54 = (f32[384]{0:T(512)S(1)}, f32[384]{0:T(512)}, u32[]{:S(2)}) copy-start(f32[384]{0:T(512)} %copy-done.53) | copy-start | bytes 4612
  379.4 102.8 %collective-permute-start.35 = (bf16[1280,1024]{1,0:T(8,128)(2,1)S(1)}, bf16[1280,1024]{1,0:T(8,128)(2,1)}, u32[]{:S(2)}, u32[]{:S(2)}) collective-permute-start(bf16[1280,1024]{1,0:T(8,128)(2,1)S(1)} %pad_maximum_fusion.1), channel_id=1, source_target_pairs={{0,2},{1,3},{2,0},{3,1},{4,6},{5,7},{6,4},{7,5},{8,10},{9,11},{10,... | collective-permute-start | bytes 7864328 | tf_op jit(solution)/shard_map/ppermute | solution.py:155
  380.0 9.2 %collective-permute-start.7 = (bf16[1,1024]{1,0:T(2,128)(2,1)S(1)}, bf16[1,1024]{1,0:T(2,128)(2,1)S(1)}, u32[]{:S(2)}, u32[]{:S(2)}) collective-permute-start(bf16[1,1024]{1,0:T(2,128)(2,1)S(1)} %get-tuple-element.603), channel_id=1, source_target_pairs={{0,16},{4,20},{8,24},{12,28},{16,0},{20,4},{24,8},{28,12},{1,17},{... | collective-permute-start | bytes 6152 | tf_op jit(solution)/shard_map/ppermute | solution.py:169
  383.3 7.7 %collective-permute-start.6 = (bf16[1,1024]{1,0:T(2,128)(2,1)S(1)}, bf16[1,1024]{1,0:T(2,128)(2,1)S(1)}, u32[]{:S(2)}, u32[]{:S(2)}) collective-permute-start(bf16[1,1024]{1,0:T(2,128)(2,1)S(1)} %get-tuple-element.604), channel_id=1, source_target_pairs={{0,12},{4,16},{8,20},{12,24},{16,28},{20,0},{24,4},{28,8},{1,13},{... | collective-permute-start | bytes 6152 | tf_op jit(solution)/shard_map/ppermute | solution.py:169
  383.3 7.6 %collective-permute-start.5 = (bf16[1,1024]{1,0:T(2,128)(2,1)S(1)}, bf16[1,1024]{1,0:T(2,128)(2,1)S(1)}, u32[]{:S(2)}, u32[]{:S(2)}) collective-permute-start(bf16[1,1024]{1,0:T(2,128)(2,1)S(1)} %get-tuple-element.605), channel_id=1, source_target_pairs={{0,8},{4,12},{8,16},{12,20},{16,24},{20,28},{24,0},{28,4},{1,9},{5... | collective-permute-start | bytes 6152 | tf_op jit(solution)/shard_map/ppermute | solution.py:169
  385.2 6.5 collective-permute-start.4
  389.2 82.2 %collective-permute-start.18 = (bf16[768,1024]{1,0:T(8,128)(2,1)}, bf16[768,1024]{1,0:T(8,128)(2,1)}, u32[]{:S(2)}, u32[]{:S(2)}) collective-permute-start(bf16[768,1024]{1,0:T(8,128)(2,1)} %fusion.68), channel_id=1, source_target_pairs={{0,2},{1,3},{2,0},{3,1},{4,6},{5,7},{6,4},{7,5},{8,10},{9,11},{10,... | collective-permute-start | bytes 4718600 | tf_op jit(solution)/shard_map/ppermute | solution.py:155
  391.8 6.4 collective-permute-start.11
  394.4 5.4 collective-permute-start.12
  396.8 5.6 collective-permute-start.13
  398.2 5.7 collective-permute-start.14
  399.8 5.3 collective-permute-start.15
  402.4 3.7 collective-permute-start.16
  403.8 88.3 %collective-permute-start.17 = (bf16[1,1024]{1,0:T(2,128)(2,1)S(1)}, bf16[1,1024]{1,0:T(2,128)(2,1)S(1)}, u32[]{:S(2)}, u32[]{:S(2)}) collective-permute-start(bf16[1,1024]{1,0:T(2,128)(2,1)S(1)} %get-tuple-element.550), channel_id=1, source_target_pairs={{0,28},{4,0},{8,4},{12,8},{16,12},{20,16},{24,20},{28,24},{1,29},{... | collective-permute-start | bytes 6152 | tf_op jit(solution)/shard_map/ppermute | solution.py:177
  463.9 18.3 %slice-start.5 = ((s8[8388608]{0:T(1024)(128)(4,1)}), s8[4194304]{0:T(1024)(128)(4,1)S(1)}, s32[]{:S(2)}) async-start(s8[8388608]{0:T(1024)(128)(4,1)} %bitcast.386), calls=%async_computation.11 | async-start | bytes 8388608
  468.1 14.1 %slice-start.6 = ((s8[8388608]{0:T(1024)(128)(4,1)}), s8[4194304]{0:T(1024)(128)(4,1)S(1)}, s32[]{:S(2)}) async-start(s8[8388608]{0:T(1024)(128)(4,1)} %bitcast.386), calls=%async_computation.12 | async-start | bytes 8388608
  477.1 18.8 %collective-permute-start.25 = (bf16[96,1024]{1,0:T(8,128)(2,1)}, bf16[96,1024]{1,0:T(8,128)(2,1)}, u32[]{:S(2)}, u32[]{:S(2)}) collective-permute-start(bf16[96,1024]{1,0:T(8,128)(2,1)} %get-tuple-element.570), channel_id=1, source_target_pairs={{0,28},{4,0},{8,4},{12,8},{16,12},{20,16},{24,20},{28,24},{1,29},{... | collective-permute-start | bytes 589832 | tf_op jit(solution)/shard_map/ppermute | solution.py:169
  478.7 19.2 %collective-permute-start.24 = (bf16[96,1024]{1,0:T(8,128)(2,1)}, bf16[96,1024]{1,0:T(8,128)(2,1)}, u32[]{:S(2)}, u32[]{:S(2)}) collective-permute-start(bf16[96,1024]{1,0:T(8,128)(2,1)} %get-tuple-element.571), channel_id=1, source_target_pairs={{0,24},{4,28},{8,0},{12,4},{16,8},{20,12},{24,16},{28,20},{1,25},{... | collective-permute-start | bytes 589832 | tf_op jit(solution)/shard_map/ppermute | solution.py:169
  482.2 17.0 %collective-permute-start.23 = (bf16[96,1024]{1,0:T(8,128)(2,1)}, bf16[96,1024]{1,0:T(8,128)(2,1)}, u32[]{:S(2)}, u32[]{:S(2)}) collective-permute-start(bf16[96,1024]{1,0:T(8,128)(2,1)} %get-tuple-element.572), channel_id=1, source_target_pairs={{0,20},{4,24},{8,28},{12,0},{16,4},{20,8},{24,12},{28,16},{1,21},{... | collective-permute-start | bytes 589832 | tf_op jit(solution)/shard_map/ppermute | solution.py:169
  482.2 58.4 %collective-permute-start.22 = (bf16[96,1024]{1,0:T(8,128)(2,1)}, bf16[96,1024]{1,0:T(8,128)(2,1)S(1)}, u32[]{:S(2)}, u32[]{:S(2)}) collective-permute-start(bf16[96,1024]{1,0:T(8,128)(2,1)} %get-tuple-element.573), channel_id=1, source_target_pairs={{0,16},{4,20},{8,24},{12,28},{16,0},{20,4},{24,8},{28,12},{1,17},{... | collective-permute-start | bytes 589832 | tf_op jit(solution)/shard_map/ppermute | solution.py:169
  493.0 47.5 %collective-permute-start.21 = (bf16[96,1024]{1,0:T(8,128)(2,1)S(1)}, bf16[96,1024]{1,0:T(8,128)(2,1)S(1)}, u32[]{:S(2)}, u32[]{:S(2)}) collective-permute-start(bf16[96,1024]{1,0:T(8,128)(2,1)S(1)} %copy-done.38), channel_id=1, source_target_pairs={{0,12},{4,16},{8,20},{12,24},{16,28},{20,0},{24,4},{28,8},{1,13},{... | collective-permute-start | bytes 589832 | tf_op jit(solution)/shard_map/ppermute | solution.py:169
  495.9 44.6 %collective-permute-start.20 = (bf16[96,1024]{1,0:T(8,128)(2,1)S(1)}, bf16[96,1024]{1,0:T(8,128)(2,1)S(1)}, u32[]{:S(2)}, u32[]{:S(2)}) collective-permute-start(bf16[96,1024]{1,0:T(8,128)(2,1)S(1)} %copy-done.37), channel_id=1, source_target_pairs={{0,8},{4,12},{8,16},{12,20},{16,24},{20,28},{24,0},{28,4},{1,9},{5... | collective-permute-start | bytes 589832 | tf_op jit(solution)/shard_map/ppermute | solution.py:169
  497.9 42.6 %collective-permute-start.19 = (bf16[96,1024]{1,0:T(8,128)(2,1)S(1)}, bf16[96,1024]{1,0:T(8,128)(2,1)S(1)}, u32[]{:S(2)}, u32[]{:S(2)}) collective-permute-start(bf16[96,1024]{1,0:T(8,128)(2,1)S(1)} %copy-done.36), channel_id=1, source_target_pairs={{0,4},{4,8},{8,12},{12,16},{16,20},{20,24},{24,28},{28,0},{1,5},{5... | collective-permute-start | bytes 589832 | tf_op jit(solution)/shard_map/ppermute | solution.py:169
  542.3 10.8 %collective-permute-start.26 = (bf16[96,1024]{1,0:T(8,128)(2,1)S(1)}, bf16[96,1024]{1,0:T(8,128)(2,1)S(1)}, u32[]{:S(2)}, u32[]{:S(2)}) collective-permute-start(bf16[96,1024]{1,0:T(8,128)(2,1)S(1)} %get-tuple-element.548), channel_id=1, source_target_pairs={{0,4},{4,8},{8,12},{12,16},{16,20},{20,24},{24,28},{28,0},{1,5},{5... | collective-permute-start | bytes 589832 | tf_op jit(solution)/shard_map/ppermute | solution.py:177
  543.0 10.2 %collective-permute-start.27 = (bf16[96,1024]{1,0:T(8,128)(2,1)S(1)}, bf16[96,1024]{1,0:T(8,128)(2,1)S(1)}, u32[]{:S(2)}, u32[]{:S(2)}) collective-permute-start(bf16[96,1024]{1,0:T(8,128)(2,1)S(1)} %get-tuple-element.548), channel_id=1, source_target_pairs={{0,8},{4,12},{8,16},{12,20},{16,24},{20,28},{24,0},{28,4},{1,9},{5... | collective-permute-start | bytes 589832 | tf_op jit(solution)/shard_map/ppermute | solution.py:177
  543.0 22.5 %collective-permute-start.28 = (bf16[96,1024]{1,0:T(8,128)(2,1)S(1)}, bf16[96,1024]{1,0:T(8,128)(2,1)S(1)}, u32[]{:S(2)}, u32[]{:S(2)}) collective-permute-start(bf16[96,1024]{1,0:T(8,128)(2,1)S(1)} %get-tuple-element.548), channel_id=1, source_target_pairs={{0,12},{4,16},{8,20},{12,24},{16,28},{20,0},{24,4},{28,8},{1,13},{... | collective-permute-start | bytes 589832 | tf_op jit(solution)/shard_map/ppermute | solution.py:177
  544.8 26.0 %collective-permute-start.29 = (bf16[96,1024]{1,0:T(8,128)(2,1)S(1)}, bf16[96,1024]{1,0:T(8,128)(2,1)S(1)}, u32[]{:S(2)}, u32[]{:S(2)}) collective-permute-start(bf16[96,1024]{1,0:T(8,128)(2,1)S(1)} %get-tuple-element.548), channel_id=1, source_target_pairs={{0,16},{4,20},{8,24},{12,28},{16,0},{20,4},{24,8},{28,12},{1,17},{... | collective-permute-start | bytes 589832 | tf_op jit(solution)/shard_map/ppermute | solution.py:177
  548.3 22.6 %collective-permute-start.30 = (bf16[96,1024]{1,0:T(8,128)(2,1)S(1)}, bf16[96,1024]{1,0:T(8,128)(2,1)S(1)}, u32[]{:S(2)}, u32[]{:S(2)}) collective-permute-start(bf16[96,1024]{1,0:T(8,128)(2,1)S(1)} %get-tuple-element.548), channel_id=1, source_target_pairs={{0,20},{4,24},{8,28},{12,0},{16,4},{20,8},{24,12},{28,16},{1,21},{... | collective-permute-start | bytes 589832 | tf_op jit(solution)/shard_map/ppermute | solution.py:177
  553.1 17.8 %collective-permute-start.31 = (bf16[96,1024]{1,0:T(8,128)(2,1)S(1)}, bf16[96,1024]{1,0:T(8,128)(2,1)S(1)}, u32[]{:S(2)}, u32[]{:S(2)}) collective-permute-start(bf16[96,1024]{1,0:T(8,128)(2,1)S(1)} %get-tuple-element.548), channel_id=1, source_target_pairs={{0,24},{4,28},{8,0},{12,4},{16,8},{20,12},{24,16},{28,20},{1,25},{... | collective-permute-start | bytes 589832 | tf_op jit(solution)/shard_map/ppermute | solution.py:177
  553.1 20.1 %collective-permute-start.32 = (bf16[96,1024]{1,0:T(8,128)(2,1)S(1)}, bf16[96,1024]{1,0:T(8,128)(2,1)S(1)}, u32[]{:S(2)}, u32[]{:S(2)}) collective-permute-start(bf16[96,1024]{1,0:T(8,128)(2,1)S(1)} %get-tuple-element.548), channel_id=1, source_target_pairs={{0,28},{4,0},{8,4},{12,8},{16,12},{20,16},{24,20},{28,24},{1,29},{... | collective-permute-start | bytes 589832 | tf_op jit(solution)/shard_map/ppermute | solution.py:177
  (90 other events, 335.8 us)
Sparse Core Ops, SparseCore 0:
  9.6 49.0 all-gather.5
  60.2 22.5 all-gather.7
  84.4 58.2 all-gather.9
  144.1 58.2 all-gather.11
  361.2 102.5 all-reduce.4
  492.2 152.1 all-reduce.6

commit v11 on v10

--- a/solution.py
+++ b/solution.py
@@ -290,10 +290,10 @@
     grad_qkv_t = jnp.einsum(
         "tc,ti->ci", reorder_cols(grad_proj, order), normed, preferred_element_type=jnp.float32
     )
+    qkv_rows = grad_qkv_t.shape[0] // shard_count
     qkv_half = halving([grad_qkv_t], "shard", shard_count, shard_steps[:1])
     qkv_half, grad_proj = lax.optimization_barrier((qkv_half, grad_proj))
     (qkv_own,) = halving(qkv_half, "shard", shard_count, shard_steps[1:])
-    total_b = direct_reduce(qkv_own, "rep", reps)
     grad_qb = jnp.sum(grad_q.astype(jnp.float32), 0)
     grad_vb = jnp.sum(grad_v.astype(jnp.float32), 0)
     grad_normed = jnp.einsum("tc,ic->ti", grad_proj, back_qkv, preferred_element_type=jnp.float32)
@@ -307,7 +307,9 @@
     small_rows = jnp.pad(small_rows, ((0, 0), (0, pad_to - small_rows.shape[1]), (0, 0)))
     small_rows = jnp.concatenate([small_rows[k] for k in order], 0)
     (small_own,) = halving([small_rows], "shard", shard_count, shard_steps)
-    total_s = direct_reduce(small_own, "rep", reps)
+    total_b = direct_reduce(jnp.concatenate([qkv_own, small_own], 0), "rep", reps)
+    total_s = total_b[qkv_rows:]
+    total_b = total_b[:qkv_rows]
     up_rows = up_own.shape[0]
     up_fin = total_a[:up_rows].astype(jnp.float32)
     out_fin = total_a[up_rows:].astype(jnp.float32)

time: 662 us -> 693 us (1.047)
  starting transfers between devices: 45.4 us -> 56.7 us
  other arithmetic: 77.6 us -> 88.2 us
  local copies, waits for them, and re-layouts: 103 us -> 111 us
  waiting for transfers between devices: 302 us -> 294 us
  matrix products: 88.7 us -> 96.6 us
    ppermute x14 -> x7, waiting for transfers between devices: 42.2 us -> 0.02 us  [direct_reduce(): lax.ppermute(send.astype(jnp.bfloat16), axis, [(a, (a + shift) % size) fo...]
    ppermute x8, waiting for transfers between devices: 9.51 us -> 46.3 us  [halving(): lax.ppermute(jnp.concatenate(sends, 0), axis, [(a, a ^ step) for a in ran...]
    psum x1, waiting for transfers between devices: 57.8 us -> 33.7 us  [body_inner(): total_a1 = lax.psum(down_own.astype(jnp.bfloat16), 'rep')]
    psum x1, waiting for transfers between devices: 68.3 us -> 86.3 us  [body_inner(): total_a = lax.psum(joined_a, 'rep')]
    ppermute x14 -> x7, starting transfers between devices: 21.5 us -> 37.2 us  [direct_reduce(): lax.ppermute(send.astype(jnp.bfloat16), axis, [(a, (a + shift) % size) fo...]
    dot_general x1, matrix products: 8.45 us -> 16.5 us  [body_inner(): jnp.einsum('tf,if->ti', grad_pre, back_up, preferred_element_type=jnp.flo...]
    ppermute x14 -> x7, waiting for transfers between devices: 24.7 us -> 29.6 us  [direct_reduce(): lax.ppermute(mine, axis, [(a, (a + shift) % size) for a in range(size)])]
    unnamed x209 -> x188, local copies, waits for them, and re-layouts: 32.4 us -> 27.7 us
  transfers between devices with their start and end apart: 42 -> 28, of which waited for: 17 -> 12; matrix products, arithmetic and copies ran while one was open for 25% -> 26% of each run, Pallas kernels for 0% -> 0%
where the time goes in v11:
time: 693 us; the launch traced here: 688 us
  waiting for transfers between devices  294 us (42%)
  local copies, waits for them, and re-layouts  111 us (16%)
  matrix products  96.6 us (14%)
  other arithmetic  88.2 us (13%)
  starting transfers between devices  56.7 us (8%)
  loops' own time  18.9 us (3%)
  between operations  15.9 us (2%)
    psum x1, waiting for transfers between devices, body_inner(): total_a = lax.psum(joined_a, 'rep')  86.3 us
    all_gather x1, waiting for transfers between devices, body_inner(): full_up = lax.all_gather(w_up, 'shard', axis=1, tiled=True)  48.2 us
    ppermute x8, waiting for transfers between devices, halving(): lax.ppermute(jnp.concatenate(sends, 0), axis, [(a, a ^ step) for a in ran...  46.3 us
    all_gather x1, waiting for transfers between devices, body_inner(): full_qkv = lax.all_gather(w_qkv, 'shard', axis=1, tiled=True)  38.1 us
    ppermute x7, starting transfers between devices, direct_reduce(): lax.ppermute(send.astype(jnp.bfloat16), axis, [(a, (a + shift) % size) fo...  37.2 us
    psum x1, waiting for transfers between devices, body_inner(): total_a1 = lax.psum(down_own.astype(jnp.bfloat16), 'rep')  33.7 us
    add x6, other arithmetic, halving(): arrays.append(keep + got[offset:offset + keep.shape[0]].astype(jnp.float32))  33.4 us
    ppermute x7, waiting for transfers between devices, direct_reduce(): lax.ppermute(mine, axis, [(a, (a + shift) % size) for a in range(size)])  29.6 us
  transfers between devices with their start and end apart: 28, of which 12 were waited for; matrix products, arithmetic and copies ran while one was open for 26% of the time, Pallas kernels for 0%

profile of v11, /device:TPU:0, one launch (start us, length us, event | category | flops | bytes accessed | tf_op | source)
XLA Modules:
  0.0 688.2 jit_solution(17859226481646958313)
XLA Ops:
  12.2 6.5 all-gather
  20.6 38.1 %all-gather.6.cloned.1.call-done = bf16[1024,3072]{1,0:T(8,128)(2,1)} async-done(((bf16[1024,768]{1,0:T(8,128)(2,1)}), bf16[1024,3072]{1,0:T(8,128)(2,1)}) %all-gather.6.cloned.1.call-update) | async-done | bytes 6291472 | tf_op jit(solution)/shard_map/all_gather | solution.py:215
  58.7 4.9 fusion.79
  68.3 21.3 %while.32 = (s32[]{:T(128)}, bf16[4,384,256]{1,2,0:T(8,128)(2,1)}, f32[4,4,384]{2,1,0:T(4,128)}, s32[4]{0:T(128)S(1)}, bf16[384,1024]{0,1:T(8,128)(2,1)S(1)}, /*...) while((s32[]{:T(128)}, bf16[4,384,256]{1,2,0:T(8,128)(2,1)}, ...), condition=%wide.region_6.7_spmd.clone, body=%wide.region_3.6_spmd.clone.sunk | while | flops 157776416 | bytes 10964623 | solution.py:74
  90.8 3.3 fusion.132
  94.4 48.2 %all-gather.10.cloned.1.call-done = bf16[1024,4096]{1,0:T(8,128)(2,1)} async-done(((bf16[1024,1024]{1,0:T(8,128)(2,1)}), bf16[1024,4096]{1,0:T(8,128)(2,1)}) %all-gather.10.cloned.1.call-update) | async-done | bytes 8388624 | tf_op jit(solution)/shard_map/all_gather | solution.py:217
  142.7 10.6 %multiply_convert_fusion.1 = (bf16[384,4096]{1,0:T(8,128)(2,1)S(1)}, f32[384,4096]{1,0:T(8,128)}) fusion(f32[4096]{0:T(1024)S(1)} %bitcast.408, bf16[1024,4096]{1,0:T(8,128)(2,1)} %all-gather.10.cloned.1.call-done, f32[384,1024]{1,0:T(8,128)S(1)} %get-tuple-element.606, f32[1024]{0:T(1024)S(1)} %bitcast.415, f32[1024]{0:T(1024)S(1)} %bitcast.409, ...), kind=kOutput, calls=%fused_computation.62 | convolution fusion | flops 3238920192 | bytes 19426304 | tf_op jit(solution)/shard_map/dot_general | solution.py:237
  154.9 1.8 maximum_bitcast_fusion
  156.7 3.8 copy.119
  160.5 5.7 fusion.89
  166.2 5.8 copy-done
  172.0 2.7 fusion.26
  175.8 6.8 collective-permute-done
  182.6 10.3 %bitcast_add_fusion.1 = f32[2048,1024]{1,0:T(8,128)} fusion(bf16[2048,1024]{1,0:T(8,128)(2,1)} %collective-permute-done, f32[2,2048,1024]{2,1,0:T(8,128)} %copy-done, s32[]{:T(128)S(6)} %select_n.216), kind=kLoop, calls=%fused_computation.40 | loop fusion | flops 4194304 | bytes 20971524 | tf_op jit(solution)/shard_map/add | solution.py:158
  192.8 9.6 %all-gather.12.cloned.1.call-done = bf16[4096,1024]{1,0:T(8,128)(2,1)} async-done(((bf16[1024,1024]{1,0:T(8,128)(2,1)}), bf16[4096,1024]{1,0:T(8,128)(2,1)}) %all-gather.12.cloned.1.call-update) | async-done | bytes 8388624 | tf_op jit(solution)/shard_map/all_gather | solution.py:218
  202.4 10.8 %convert_reduce_fusion = (f32[4096]{0:T(1024)}, bf16[384,4096]{1,0:T(8,128)(2,1)S(1)}) fusion(f32[384,4096]{1,0:T(8,128)} %get-tuple-element.608, bf16[4096,1024]{1,0:T(8,128)(2,1)} %all-gather.12.cloned.1.call-done, bf16[1,384,1024]{2,1,0:T(8,128)(2,1)S(1)} %copy-done.18), kind=kOutput, calls=%fused_computation.60 | convolution fusion | flops 3255824384 | bytes 18628608 | tf_op jit(solution)/shard_map/to,fo->tf/dot_general | solution.py:259
  213.2 1.8 fusion.128
  215.6 16.5 %multiply_reduce_fusion.1 = (f32[1024]{0:T(1024)}, f32[384]{0:T(512)S(1)}, f32[1024]{0:T(1024)}, f32[384,1024]{1,0:T(8,128)S(1)}) fusion(f32[384,1024]{1,0:T(8,128)S(1)} %copy-done.7, f32[384]{0:T(512)S(1)} %fusion.119, f32[384]{0:T(512)S(1)} %broadcast_multiply_fusion, f32[1024]{0:T(1024)S(1)} %bitcast.410, bf16[384,4096]{1,0:T(8,128)(2,1)S(1)} %get-tuple-element.612, ...), kind=kOutput, calls=%fused_computation.137 | convolution fusion | flops 3224368640 | bytes 14696960 | tf_op jit(solution)/shard_map/tf,if->ti/dot_general | solution.py:268
  239.1 54.6 %while.33 = (s32[]{:T(128)}, bf16[4,384,256]{1,2,0:T(8,128)(2,1)}, bf16[4,384,256]{1,2,0:T(8,128)(2,1)}, bf16[4,384,256]{1,2,0:T(8,128)(2,1)}, s32[4]{0:T(128)S(...) while((s32[]{:T(128)}, bf16[4,384,256]{1,2,0:T(8,128)(2,1)}, ...), condition=%wide.region_13.14_spmd.clone, body=%wide.region_11.13_spmd.clone.sunk | while | flops 385251872 | bytes 30610428 | solution.py:113
  296.3 2.4 pad_maximum_fusion.4
  298.7 3.6 fusion.77
  302.4 2.2 fusion.34
  306.2 3.5 copy-done.1
  309.6 2.0 copy-done.4
  311.9 9.6 %fusion.35 = f32[4096,1024]{1,0:T(8,128)} fusion(bf16[384,1024]{1,0:T(8,128)(2,1)S(1)} %copy-done.32, bf16[384,1024]{1,0:T(8,128)(2,1)S(1)} %copy-done.33, bf16[384,1024]{1,0:T(8,128)(2,1)S(1)} %copy-done.34, bf16[384,1024]{1,0:T(8,128)(2,1)S(1)} %copy-done.31, f32[384,1024]{1,0:T(8,128)S(1)} %copy-done.8, f32[1024]{0:T(1024)S(1)} %bitcast.416, ...), kind=kOutput, calls=%fused_computation.82 | convolution fusion | flops 3235774464 | bytes 21507072 | tf_op jit(solution)/shard_map/tf,ti->fi/dot_general | solution.py:265
  321.5 4.0 fusion.27
  325.7 2.9 pad_maximum_fusion
  328.9 4.0 fusion.48
  333.6 8.2 %bitcast_add_fusion.2 = f32[1536,1024]{1,0:T(8,128)} fusion(bf16[1536,1024]{1,0:T(8,128)(2,1)} %collective-permute-done.1, f32[2,1536,1024]{2,1,0:T(8,128)} %copy-done.1, s32[]{:T(128)S(6)} %select_n.216), kind=kLoop, calls=%fused_computation.54 | loop fusion | flops 3145728 | bytes 15728644 | tf_op jit(solution)/shard_map/add | solution.py:158
  341.8 2.9 fusion.123
  347.2 3.5 fusion.68
  355.9 10.3 %bitcast_add_fusion = f32[2048,1024]{1,0:T(8,128)} fusion(f32[2,2048,1024]{2,1,0:T(8,128)} %bitcast.380, s32[]{:T(128)S(6)} %select_n.216, bf16[2560,1024]{1,0:T(8,128)(2,1)} %collective-permute-done.20), kind=kLoop, calls=%fused_computation.39 | loop fusion | flops 4194304 | bytes 20971524 | tf_op jit(solution)/shard_map/add | solution.py:158
  366.2 2.5 fusion.49
  372.1 9.6 %collective-permute-done.19 = bf16[1024,1024]{1,0:T(8,128)(2,1)} collective-permute-done((bf16[1024,1024]{1,0:T(8,128)(2,1)}, bf16[1024,1024]{1,0:T(8,128)(2,1)}, u32[]{:S(2)}, u32[]{:S(2)}) %collective-permute-start.19) | collective-permute-done | bytes 2097184 | tf_op jit(solution)/shard_map/ppermute | solution.py:155
  381.7 3.7 fusion.29
  385.7 29.9 %collective-permute-done.4 = bf16[8,1024]{1,0:T(8,128)(2,1)S(1)} collective-permute-done((bf16[8,1024]{1,0:T(8,128)(2,1)S(1)}, bf16[8,1024]{1,0:T(8,128)(2,1)S(1)}, u32[]{:S(2)}, u32[]{:S(2)}) %collective-permute-start.4) | collective-permute-done | bytes 16416 | tf_op jit(solution)/shard_map/ppermute | solution.py:155
  415.7 2.9 bitcast_add_fusion.5
  418.6 2.0 pad_maximum_fusion.1
  420.7 4.2 reshape.437
  424.9 2.8 fusion.108
  427.6 4.1 collective-permute-start.11
  432.3 8.7 %fusion.71 = bf16[1,384,1024]{2,1,0:T(8,128)(2,1)} fusion(f32[384,1024]{1,0:T(8,128)S(1)} %copy-done.8, bf16[384,4096]{1,0:T(8,128)(2,1)} %copy-done.23, bf16[4096,1024]{1,0:T(8,128)(2,1)} %all-gather.12.cloned.1.call-done, f32[1024]{0:T(1024)S(1)} %bitcast.417), kind=kOutput, calls=%fused_computation.147 | convolution fusion | flops 3222405120 | bytes 13897728 | tf_op jit(solution)/shard_map/dot_general | solution.py:250
  441.0 2.9 collective-permute-start.8
  443.9 18.8 %collective-permute-start.6 = (bf16[97,1024]{1,0:T(8,128)(2,1)S(1)}, bf16[97,1024]{1,0:T(8,128)(2,1)S(1)}, u32[]{:S(2)}, u32[]{:S(2)}) collective-permute-start(bf16[97,1024]{1,0:T(8,128)(2,1)S(1)} %get-tuple-element.569), channel_id=1, source_target_pairs={{0,8},{4,12},{8,16},{12,20},{16,24},{20,28},{24,0},{28,4},{1,9},{5... | collective-permute-start | bytes 595976 | tf_op jit(solution)/shard_map/ppermute | solution.py:169
  462.7 10.9 %collective-permute-start.5 = (bf16[97,1024]{1,0:T(8,128)(2,1)S(1)}, bf16[97,1024]{1,0:T(8,128)(2,1)S(1)}, u32[]{:S(2)}, u32[]{:S(2)}) collective-permute-start(bf16[97,1024]{1,0:T(8,128)(2,1)S(1)} %get-tuple-element.563), channel_id=1, source_target_pairs={{0,4},{4,8},{8,12},{12,16},{16,20},{20,24},{24,28},{28,0},{1,5},{5... | collective-permute-start | bytes 595976 | tf_op jit(solution)/shard_map/ppermute | solution.py:169
  473.6 33.7 %all-reduce.5.cloned.1.call-done = bf16[1024,1024]{1,0:T(8,128)(2,1)} async-done(((bf16[1024,1024]{1,0:T(8,128)(2,1)}), bf16[1024,1024]{1,0:T(8,128)(2,1)}) %all-reduce.5.cloned.1.call-update) | async-done | bytes 2097168 | tf_op jit(solution)/shard_map/psum | solution.py:264
  507.2 4.1 convert_element_type.511
  512.7 2.0 bitcast_dynamic-update-slice_fusion.8
  516.2 5.0 fusion.50
  521.1 2.9 copy.112
  528.8 3.0 fusion.75
  534.0 2.8 collective-permute-start.15
  537.8 2.5 collective-permute-start.17
  542.0 4.1 collective-permute-done.13
  546.1 4.2 collective-permute-start.18
  550.9 15.2 %collective-permute-done.14 = bf16[97,1024]{1,0:T(8,128)(2,1)S(1)} collective-permute-done((bf16[97,1024]{1,0:T(8,128)(2,1)S(1)}, bf16[97,1024]{1,0:T(8,128)(2,1)S(1)}, u32[]{:S(2)}, u32[]{:S(2)}) %collective-permute-start.14) | collective-permute-done | bytes 198688 | tf_op jit(solution)/shard_map/ppermute | solution.py:177
  566.9 5.1 collective-permute-done.15
  574.1 5.1 collective-permute-done.18
  579.9 1.9 reshape.438
  583.0 1.8 convert_bitcast_fusion
  584.8 2.4 copy.113
  588.4 86.3 %all-reduce.7.cloned.1.call-done = bf16[1280,1024]{1,0:T(8,128)(2,1)} async-done(((bf16[1280,1024]{1,0:T(8,128)(2,1)}), bf16[1280,1024]{1,0:T(8,128)(2,1)}) %all-reduce.7.cloned.1.call-update) | async-done | bytes 2621456 | tf_op jit(solution)/shard_map/psum | solution.py:284
  674.7 2.1 slice_convert_fusion.2
  676.8 4.1 slice_convert_fusion
  (472 shorter events, 116.1 us)
Async XLA Ops:
  7.2 51.5 %all-gather.6.cloned.1.call-start = ((), (), s32[]{:S(2)}) async-start(), calls=%async_computation | async-start | bytes 7864320 | tf_op jit(solution)/shard_map/all_gather | solution.py:215
  8.0 81.7 %all-gather.8.cloned.1.call-start = ((), (), s32[]{:S(2)}) async-start(), calls=%async_computation.1 | async-start | bytes 2621440 | tf_op jit(solution)/shard_map/all_gather | solution.py:216
  8.8 10.6 %copy-start.2 = (bf16[1,384,1024]{2,1,0:T(8,128)(2,1)S(1)}, bf16[1,384,1024]{2,1,0:T(8,128)(2,1)}, u32[]{:S(2)}) copy-start(bf16[1,384,1024]{2,1,0:T(8,128)(2,1)} %param.20) | copy-start | bytes 2359300
  8.8 133.9 %all-gather.10.cloned.1.call-start = ((), (), s32[]{:S(2)}) async-start(), calls=%async_computation.2 | async-start | bytes 10485760 | tf_op jit(solution)/shard_map/all_gather | solution.py:217
  9.5 10.6 %copy-start.67 = (s32[1,2,64]{2,1,0:T(2,128)S(1)}, s32[1,2,64]{2,1,0:T(2,128)}, u32[]{:S(2)}) copy-start(s32[1,2,64]{2,1,0:T(2,128)} %param.21) | copy-start | bytes 1540
  9.5 192.9 %all-gather.12.cloned.1.call-start = ((), (), s32[]{:S(2)}) async-start(), calls=%async_computation.3 | async-start | bytes 10485760 | tf_op jit(solution)/shard_map/all_gather | solution.py:218
  10.1 497.1 %all-reduce.5.cloned.1.call-start = ((), (), s32[]{:S(2)}) async-start(), calls=%async_computation.4 | async-start | bytes 4194304 | tf_op jit(solution)/shard_map/psum | solution.py:264
  19.3 44.3 %copy-start.59 = (f32[1,2,4,128]{3,1,2,0:T(2,128)}, f32[1,2,4,128]{3,1,2,0:T(2,128)S(1)}, u32[]{:S(2)}) copy-start(f32[1,2,4,128]{3,1,2,0:T(2,128)S(1)} %copy.126) | copy-start | bytes 12292
  19.3 44.3 %copy-start.38 = (f32[1,2,4,128]{3,1,2,0:T(2,128)}, f32[1,2,4,128]{3,1,2,0:T(2,128)S(1)}, u32[]{:S(2)}) copy-start(f32[1,2,4,128]{3,1,2,0:T(2,128)S(1)} %copy.125) | copy-start | bytes 12292
  19.5 44.1 %copy-start.42 = (f32[384]{0:T(512)}, f32[384]{0:T(512)S(1)}, u32[]{:S(2)}) copy-start(f32[384]{0:T(512)S(1)} %broadcast_multiply_fusion.1) | copy-start | bytes 4612
  19.9 43.8 %copy-start.49 = (f32[384]{0:T(512)}, f32[384]{0:T(512)S(1)}, u32[]{:S(2)}) copy-start(f32[384]{0:T(512)S(1)} %fusion.62) | copy-start | bytes 4612
  19.9 43.8 %copy-start.44 = (f32[384]{0:T(512)}, f32[384]{0:T(512)S(1)}, u32[]{:S(2)}) copy-start(f32[384]{0:T(512)S(1)} %fusion.118) | copy-start | bytes 4612
  20.5 122.2 %copy-start.65 = (f32[1,2,4,128]{3,1,2,0:T(2,128)}, f32[1,2,4,128]{3,1,2,0:T(2,128)S(1)}, u32[]{:S(2)}) copy-start(f32[1,2,4,128]{3,1,2,0:T(2,128)S(1)} %copy.131) | copy-start | bytes 12292
  20.5 211.7 %copy-start.57 = (f32[1,2,4,128]{3,1,2,0:T(2,128)}, f32[1,2,4,128]{3,1,2,0:T(2,128)S(1)}, u32[]{:S(2)}) copy-start(f32[1,2,4,128]{3,1,2,0:T(2,128)S(1)} %copy.130) | copy-start | bytes 12292
  94.1 59.2 %copy-start.6 = (f32[384,1024]{1,0:T(8,128)}, f32[384,1024]{1,0:T(8,128)S(1)}, u32[]{:S(2)}) copy-start(f32[384,1024]{1,0:T(8,128)S(1)} %get-tuple-element.606) | copy-start | bytes 4718596
  94.1 138.0 %copy-start.47 = (f32[384]{0:T(512)}, f32[384]{0:T(512)S(1)}, u32[]{:S(2)}) copy-start(f32[384]{0:T(512)S(1)} %broadcast_multiply_fusion) | copy-start | bytes 4612
  94.4 137.7 %copy-start.61 = (f32[384]{0:T(512)}, f32[384]{0:T(512)S(1)}, u32[]{:S(2)}) copy-start(f32[384]{0:T(512)S(1)} %fusion.119) | copy-start | bytes 4612
  174.7 7.9 %collective-permute-start = (bf16[2048,1024]{1,0:T(8,128)(2,1)}, bf16[2048,1024]{1,0:T(8,128)(2,1)}, u32[]{:S(2)}, u32[]{:S(2)}) collective-permute-start(bf16[2048,1024]{1,0:T(8,128)(2,1)} %fusion.26), channel_id=1, source_target_pairs={{0,1},{1,0},{2,3},{3,2},{4,5},{5,4},{6,7},{7,6},{8,9},{9,8},{10,11... | collective-permute-start | bytes 12582920 | tf_op jit(solution)/shard_map/ppermute | solution.py:155
  175.8 26.6 %copy-start.18 = (bf16[1,384,1024]{2,1,0:T(8,128)(2,1)S(1)}, bf16[1,384,1024]{2,1,0:T(8,128)(2,1)}, u32[]{:S(2)}) copy-start(bf16[1,384,1024]{2,1,0:T(8,128)(2,1)} %param.22) | copy-start | bytes 2359300
  239.1 6.6 copy-start.40
  239.1 6.6 copy-start.77
  252.7 6.7 copy-start.40
  252.7 6.7 copy-start.77
  266.4 6.7 copy-start.40
  266.4 6.7 copy-start.77
  280.1 6.7 copy-start.40
  280.1 6.7 copy-start.77
  302.3 7.3 %copy-start.1 = (f32[2,1536,1024]{2,1,0:T(8,128)}, f32[2,1536,1024]{2,1,0:T(8,128)S(1)}, u32[]{:S(2)}) copy-start(f32[2,1536,1024]{2,1,0:T(8,128)S(1)} %fusion.77) | copy-start | bytes 37748740
  304.6 29.1 %collective-permute-start.1 = (bf16[1536,1024]{1,0:T(8,128)(2,1)}, bf16[1536,1024]{1,0:T(8,128)(2,1)}, u32[]{:S(2)}, u32[]{:S(2)}) collective-permute-start(bf16[1536,1024]{1,0:T(8,128)(2,1)} %fusion.34), channel_id=1, source_target_pairs={{0,1},{1,0},{2,3},{3,2},{4,5},{5,4},{6,7},{7,6},{8,9},{9,8},{10,11... | collective-permute-start | bytes 9437192 | tf_op jit(solution)/shard_map/ppermute | solution.py:155
  304.8 7.0 %copy-start.8 = (f32[384,1024]{1,0:T(8,128)S(1)}, f32[384,1024]{1,0:T(8,128)}, u32[]{:S(2)}) copy-start(f32[384,1024]{1,0:T(8,128)} %copy-done.6) | copy-start | bytes 4718596
  304.8 7.0 %copy-start.31 = (bf16[384,1024]{1,0:T(8,128)(2,1)S(1)}, bf16[384,1024]{1,0:T(8,128)(2,1)}, u32[]{:S(2)}) copy-start(bf16[384,1024]{1,0:T(8,128)(2,1)} %get-tuple-element.570) | copy-start | bytes 2359300
  304.8 7.0 %copy-start.32 = (bf16[384,1024]{1,0:T(8,128)(2,1)S(1)}, bf16[384,1024]{1,0:T(8,128)(2,1)}, u32[]{:S(2)}) copy-start(bf16[384,1024]{1,0:T(8,128)(2,1)} %get-tuple-element.571) | copy-start | bytes 2359300
  304.8 7.0 %copy-start.33 = (bf16[384,1024]{1,0:T(8,128)(2,1)S(1)}, bf16[384,1024]{1,0:T(8,128)(2,1)}, u32[]{:S(2)}) copy-start(bf16[384,1024]{1,0:T(8,128)(2,1)} %get-tuple-element.572) | copy-start | bytes 2359300
  304.9 7.0 %copy-start.34 = (bf16[384,1024]{1,0:T(8,128)(2,1)S(1)}, bf16[384,1024]{1,0:T(8,128)(2,1)}, u32[]{:S(2)}) copy-start(bf16[384,1024]{1,0:T(8,128)(2,1)} %get-tuple-element.573) | copy-start | bytes 2359300
  304.9 7.0 %copy-start.48 = (f32[384]{0:T(512)S(1)}, f32[384]{0:T(512)}, u32[]{:S(2)}) copy-start(f32[384]{0:T(512)} %copy-done.47) | copy-start | bytes 4612
  304.9 7.0 %copy-start.58 = (f32[1,2,4,128]{3,1,2,0:T(2,128)S(1)}, f32[1,2,4,128]{3,1,2,0:T(2,128)}, u32[]{:S(2)}) copy-start(f32[1,2,4,128]{3,1,2,0:T(2,128)} %copy-done.57) | copy-start | bytes 12292
  304.9 7.0 %copy-start.62 = (f32[384]{0:T(512)S(1)}, f32[384]{0:T(512)}, u32[]{:S(2)}) copy-start(f32[384]{0:T(512)} %copy-done.61) | copy-start | bytes 4612
  304.9 7.0 %copy-start.66 = (f32[1,2,4,128]{3,1,2,0:T(2,128)S(1)}, f32[1,2,4,128]{3,1,2,0:T(2,128)}, u32[]{:S(2)}) copy-start(f32[1,2,4,128]{3,1,2,0:T(2,128)} %copy-done.65) | copy-start | bytes 12292
  328.5 24.3 %collective-permute-start.20 = (bf16[2560,1024]{1,0:T(8,128)(2,1)}, bf16[2560,1024]{1,0:T(8,128)(2,1)}, u32[]{:S(2)}, u32[]{:S(2)}) collective-permute-start(bf16[2560,1024]{1,0:T(8,128)(2,1)} %pad_maximum_fusion), channel_id=1, source_target_pairs={{0,1},{1,0},{2,3},{3,2},{4,5},{5,4},{6,7},{7,6},{8,9},{9,8},{10,11... | collective-permute-start | bytes 15728648 | tf_op jit(solution)/shard_map/ppermute | solution.py:155
  332.9 48.8 %collective-permute-start.19 = (bf16[1024,1024]{1,0:T(8,128)(2,1)}, bf16[1024,1024]{1,0:T(8,128)(2,1)}, u32[]{:S(2)}, u32[]{:S(2)}) collective-permute-start(bf16[1024,1024]{1,0:T(8,128)(2,1)} %fusion.48), channel_id=1, source_target_pairs={{0,2},{1,3},{2,0},{3,1},{4,6},{5,7},{6,4},{7,5},{8,10},{9,11},{10,... | collective-permute-start | bytes 6291464 | tf_op jit(solution)/shard_map/ppermute | solution.py:155
  333.2 8.6 %slice-start.2 = ((s8[6291456]{0:T(1024)(128)(4,1)}), s8[4194304]{0:T(1024)(128)(4,1)S(1)}, s32[]{:S(2)}) async-start(s8[6291456]{0:T(1024)(128)(4,1)} %bitcast.419), calls=%async_computation.8 | async-start | bytes 8388608
  333.6 8.2 %copy-start.27 = (bf16[384,3072]{0,1:T(8,128)(2,1)S(1)}, bf16[384,3072]{0,1:T(8,128)(2,1)}, u32[]{:S(2)}) copy-start(bf16[384,3072]{0,1:T(8,128)(2,1)} %get-tuple-element.294) | copy-start | bytes 7077892
  333.6 8.2 %slice-start.3 = ((s8[6291456]{0:T(1024)(128)(4,1)}), s8[2097152]{0:T(1024)(128)(4,1)S(1)}, s32[]{:S(2)}) async-start(s8[6291456]{0:T(1024)(128)(4,1)} %bitcast.419), calls=%async_computation.9 | async-start | bytes 4194304
  347.1 5.2 collective-permute-start.3
  350.7 65.0 %collective-permute-start.2 = (bf16[768,1024]{1,0:T(8,128)(2,1)}, bf16[768,1024]{1,0:T(8,128)(2,1)}, u32[]{:S(2)}, u32[]{:S(2)}) collective-permute-start(bf16[768,1024]{1,0:T(8,128)(2,1)} %fusion.68), channel_id=1, source_target_pairs={{0,2},{1,3},{2,0},{3,1},{4,6},{5,7},{6,4},{7,5},{8,10},{9,11},{10,... | collective-permute-start | bytes 4718600 | tf_op jit(solution)/shard_map/ppermute | solution.py:155
  352.4 63.3 %collective-permute-start.4 = (bf16[8,1024]{1,0:T(8,128)(2,1)S(1)}, bf16[8,1024]{1,0:T(8,128)(2,1)S(1)}, u32[]{:S(2)}, u32[]{:S(2)}) collective-permute-start(bf16[8,1024]{1,0:T(8,128)(2,1)S(1)} %fusion.117), channel_id=1, source_target_pairs={{0,2},{1,3},{2,0},{3,1},{4,6},{5,7},{6,4},{7,5},{8,10},{9,11},{10,... | collective-permute-start | bytes 49160 | tf_op jit(solution)/shard_map/ppermute | solution.py:155
  352.8 28.9 %slice-start = ((s8[8388608]{0:T(1024)(128)(4,1)}), s8[4194304]{0:T(1024)(128)(4,1)S(1)}, s32[]{:S(2)}) async-start(s8[8388608]{0:T(1024)(128)(4,1)} %bitcast.364), calls=%async_computation.6 | async-start | bytes 8388608
  355.9 25.8 %slice-start.1 = ((s8[8388608]{0:T(1024)(128)(4,1)}), s8[4194304]{0:T(1024)(128)(4,1)S(1)}, s32[]{:S(2)}) async-start(s8[8388608]{0:T(1024)(128)(4,1)} %bitcast.364), calls=%async_computation.7 | async-start | bytes 8388608
  370.4 145.7 %collective-permute-start.21 = (bf16[1280,1024]{1,0:T(8,128)(2,1)}, bf16[1280,1024]{1,0:T(8,128)(2,1)}, u32[]{:S(2)}, u32[]{:S(2)}) collective-permute-start(bf16[1280,1024]{1,0:T(8,128)(2,1)} %pad_maximum_fusion.2), channel_id=1, source_target_pairs={{0,2},{1,3},{2,0},{3,1},{4,6},{5,7},{6,4},{7,5},{8,10},{9,11},{10,... | collective-permute-start | bytes 7864328 | tf_op jit(solution)/shard_map/ppermute | solution.py:155
  385.4 289.3 %all-reduce.7.cloned.1.call-start = ((), (), s32[]{:S(2)}) async-start(), calls=%async_computation.5 | async-start | bytes 5242880 | tf_op jit(solution)/shard_map/psum | solution.py:284
  427.6 16.2 %collective-permute-start.11 = (bf16[97,1024]{1,0:T(8,128)(2,1)S(1)}, bf16[97,1024]{1,0:T(8,128)(2,1)S(1)}, u32[]{:S(2)}, u32[]{:S(2)}) collective-permute-start(bf16[97,1024]{1,0:T(8,128)(2,1)S(1)} %get-tuple-element.564), channel_id=1, source_target_pairs={{0,28},{4,0},{8,4},{12,8},{16,12},{20,16},{24,20},{28,24},{1,29},{... | collective-permute-start | bytes 595976 | tf_op jit(solution)/shard_map/ppermute | solution.py:169
  431.7 12.2 %collective-permute-start.10 = (bf16[97,1024]{1,0:T(8,128)(2,1)S(1)}, bf16[97,1024]{1,0:T(8,128)(2,1)S(1)}, u32[]{:S(2)}, u32[]{:S(2)}) collective-permute-start(bf16[97,1024]{1,0:T(8,128)(2,1)S(1)} %get-tuple-element.565), channel_id=1, source_target_pairs={{0,24},{4,28},{8,0},{12,4},{16,8},{20,12},{24,16},{28,20},{1,25},{... | collective-permute-start | bytes 595976 | tf_op jit(solution)/shard_map/ppermute | solution.py:169
  432.3 30.4 %collective-permute-start.9 = (bf16[97,1024]{1,0:T(8,128)(2,1)S(1)}, bf16[97,1024]{1,0:T(8,128)(2,1)S(1)}, u32[]{:S(2)}, u32[]{:S(2)}) collective-permute-start(bf16[97,1024]{1,0:T(8,128)(2,1)S(1)} %get-tuple-element.566), channel_id=1, source_target_pairs={{0,20},{4,24},{8,28},{12,0},{16,4},{20,8},{24,12},{28,16},{1,21},{... | collective-permute-start | bytes 595976 | tf_op jit(solution)/shard_map/ppermute | solution.py:169
  441.0 70.3 %collective-permute-start.8 = (bf16[97,1024]{1,0:T(8,128)(2,1)}, bf16[97,1024]{1,0:T(8,128)(2,1)S(1)}, u32[]{:S(2)}, u32[]{:S(2)}) collective-permute-start(bf16[97,1024]{1,0:T(8,128)(2,1)} %get-tuple-element.567), channel_id=1, source_target_pairs={{0,16},{4,20},{8,24},{12,28},{16,0},{20,4},{24,8},{28,12},{1,17},{... | collective-permute-start | bytes 595976 | tf_op jit(solution)/shard_map/ppermute | solution.py:169
  443.9 67.4 %collective-permute-start.7 = (bf16[97,1024]{1,0:T(8,128)(2,1)}, bf16[97,1024]{1,0:T(8,128)(2,1)S(1)}, u32[]{:S(2)}, u32[]{:S(2)}) collective-permute-start(bf16[97,1024]{1,0:T(8,128)(2,1)} %get-tuple-element.568), channel_id=1, source_target_pairs={{0,12},{4,16},{8,20},{12,24},{16,28},{20,0},{24,4},{28,8},{1,13},{... | collective-permute-start | bytes 595976 | tf_op jit(solution)/shard_map/ppermute | solution.py:169
  443.9 67.4 %collective-permute-start.6 = (bf16[97,1024]{1,0:T(8,128)(2,1)S(1)}, bf16[97,1024]{1,0:T(8,128)(2,1)S(1)}, u32[]{:S(2)}, u32[]{:S(2)}) collective-permute-start(bf16[97,1024]{1,0:T(8,128)(2,1)S(1)} %get-tuple-element.569), channel_id=1, source_target_pairs={{0,8},{4,12},{8,16},{12,20},{16,24},{20,28},{24,0},{28,4},{1,9},{5... | collective-permute-start | bytes 595976 | tf_op jit(solution)/shard_map/ppermute | solution.py:169
  462.7 48.6 %collective-permute-start.5 = (bf16[97,1024]{1,0:T(8,128)(2,1)S(1)}, bf16[97,1024]{1,0:T(8,128)(2,1)S(1)}, u32[]{:S(2)}, u32[]{:S(2)}) collective-permute-start(bf16[97,1024]{1,0:T(8,128)(2,1)S(1)} %get-tuple-element.563), channel_id=1, source_target_pairs={{0,4},{4,8},{8,12},{12,16},{16,20},{20,24},{24,28},{28,0},{1,5},{5... | collective-permute-start | bytes 595976 | tf_op jit(solution)/shard_map/ppermute | solution.py:169
  514.7 23.1 %collective-permute-start.12 = (bf16[97,1024]{1,0:T(8,128)(2,1)S(1)}, bf16[97,1024]{1,0:T(8,128)(2,1)}, u32[]{:S(2)}, u32[]{:S(2)}) collective-permute-start(bf16[97,1024]{1,0:T(8,128)(2,1)S(1)} %get-tuple-element.548), channel_id=1, source_target_pairs={{0,4},{4,8},{8,12},{12,16},{16,20},{20,24},{24,28},{28,0},{1,5},{5... | collective-permute-start | bytes 595976 | tf_op jit(solution)/shard_map/ppermute | solution.py:177
  531.8 14.2 %collective-permute-start.13 = (bf16[97,1024]{1,0:T(8,128)(2,1)S(1)}, bf16[97,1024]{1,0:T(8,128)(2,1)S(1)}, u32[]{:S(2)}, u32[]{:S(2)}) collective-permute-start(bf16[97,1024]{1,0:T(8,128)(2,1)S(1)} %get-tuple-element.548), channel_id=1, source_target_pairs={{0,8},{4,12},{8,16},{12,20},{16,24},{20,28},{24,0},{28,4},{1,9},{5... | collective-permute-start | bytes 595976 | tf_op jit(solution)/shard_map/ppermute | solution.py:177
  533.0 33.2 %collective-permute-start.14 = (bf16[97,1024]{1,0:T(8,128)(2,1)S(1)}, bf16[97,1024]{1,0:T(8,128)(2,1)S(1)}, u32[]{:S(2)}, u32[]{:S(2)}) collective-permute-start(bf16[97,1024]{1,0:T(8,128)(2,1)S(1)} %get-tuple-element.548), channel_id=1, source_target_pairs={{0,12},{4,16},{8,20},{12,24},{16,28},{20,0},{24,4},{28,8},{1,13},{... | collective-permute-start | bytes 595976 | tf_op jit(solution)/shard_map/ppermute | solution.py:177
  534.0 38.0 %collective-permute-start.15 = (bf16[97,1024]{1,0:T(8,128)(2,1)S(1)}, bf16[97,1024]{1,0:T(8,128)(2,1)S(1)}, u32[]{:S(2)}, u32[]{:S(2)}) collective-permute-start(bf16[97,1024]{1,0:T(8,128)(2,1)S(1)} %get-tuple-element.548), channel_id=1, source_target_pairs={{0,16},{4,20},{8,24},{12,28},{16,0},{20,4},{24,8},{28,12},{1,17},{... | collective-permute-start | bytes 595976 | tf_op jit(solution)/shard_map/ppermute | solution.py:177
  536.8 35.9 %collective-permute-start.16 = (bf16[97,1024]{1,0:T(8,128)(2,1)S(1)}, bf16[97,1024]{1,0:T(8,128)(2,1)S(1)}, u32[]{:S(2)}, u32[]{:S(2)}) collective-permute-start(bf16[97,1024]{1,0:T(8,128)(2,1)S(1)} %get-tuple-element.548), channel_id=1, source_target_pairs={{0,20},{4,24},{8,28},{12,0},{16,4},{20,8},{24,12},{28,16},{1,21},{... | collective-permute-start | bytes 595976 | tf_op jit(solution)/shard_map/ppermute | solution.py:177
  537.8 35.6 %collective-permute-start.17 = (bf16[97,1024]{1,0:T(8,128)(2,1)S(1)}, bf16[97,1024]{1,0:T(8,128)(2,1)S(1)}, u32[]{:S(2)}, u32[]{:S(2)}) collective-permute-start(bf16[97,1024]{1,0:T(8,128)(2,1)S(1)} %get-tuple-element.548), channel_id=1, source_target_pairs={{0,24},{4,28},{8,0},{12,4},{16,8},{20,12},{24,16},{28,20},{1,25},{... | collective-permute-start | bytes 595976 | tf_op jit(solution)/shard_map/ppermute | solution.py:177
  546.1 33.1 %collective-permute-start.18 = (bf16[97,1024]{1,0:T(8,128)(2,1)S(1)}, bf16[97,1024]{1,0:T(8,128)(2,1)S(1)}, u32[]{:S(2)}, u32[]{:S(2)}) collective-permute-start(bf16[97,1024]{1,0:T(8,128)(2,1)S(1)} %get-tuple-element.548), channel_id=1, source_target_pairs={{0,28},{4,0},{8,4},{12,8},{16,12},{20,16},{24,20},{28,24},{1,29},{... | collective-permute-start | bytes 595976 | tf_op jit(solution)/shard_map/ppermute | solution.py:177
  (65 other events, 169.6 us)
Sparse Core Ops, SparseCore 0:
  9.6 49.1 all-gather.5
  60.3 22.5 all-gather.7
  84.4 58.2 all-gather.9
  144.1 58.2 all-gather.11
  385.5 121.6 all-reduce.4
  527.4 147.2 all-reduce.6

commit v12 on v11

--- a/solution.py
+++ b/solution.py
@@ -179,6 +179,22 @@
     return result.reshape(buf.shape)
 
 
+def gather_pieces(piece, axis, size, steps, dim):
+    index = lax.axis_index(axis)
+    buf, first = piece, None
+    for step in steps:
+        low = (index // step) % 2 == 0
+        got = lax.ppermute(buf, axis, [(a, a ^ step) for a in range(size)])
+        first = got if first is None else first
+        buf = jnp.concatenate([jnp.where(low, buf, got), jnp.where(low, got, buf)], dim)
+    return buf, first
+
+
+def unpermute(full, order, dim):
+    pieces = jnp.split(full, len(order), dim)
+    return jnp.concatenate([pieces[order.index(k)] for k in range(len(order))], dim)
+
+
 def gather_small(pieces):
     packed = jnp.concatenate(pieces)
     shards = lax.all_gather(packed, "shard", axis=0, tiled=False)
@@ -212,10 +228,19 @@
     full_g1, full_s1, full_qb, full_vb, full_bo, full_g2, full_s2, full_bu, full_bd = gather_small(
         [ln1_gain, ln1_bias, q_bias, v_bias, b_out, ln2_gain, ln2_bias, b_up, b_down]
     )
-    full_qkv = lax.all_gather(w_qkv, "shard", axis=1, tiled=True)
-    full_out = lax.all_gather(w_out, "shard", axis=0, tiled=True)
-    full_up = lax.all_gather(w_up, "shard", axis=1, tiled=True)
-    full_down = lax.all_gather(w_down, "shard", axis=0, tiled=True)
+    gather_order = chunk_order(shard_count, bit_steps(shard_count))
+    gather_steps = bit_steps(shard_count)[::-1]
+    full_qkv, first = gather_pieces(w_qkv, "shard", shard_count, gather_steps, 1)
+    first, w_out = lax.optimization_barrier((first, w_out))
+    full_out, first = gather_pieces(w_out, "shard", shard_count, gather_steps, 0)
+    first, full_qkv, w_up = lax.optimization_barrier((first, full_qkv, w_up))
+    full_up, first = gather_pieces(w_up, "shard", shard_count, gather_steps, 1)
+    first, full_out, w_down = lax.optimization_barrier((first, full_out, w_down))
+    full_down, first = gather_pieces(w_down, "shard", shard_count, gather_steps, 0)
+    full_qkv = unpermute(full_qkv, gather_order, 1)
+    full_out = unpermute(full_out, gather_order, 0)
+    full_up = unpermute(full_up, gather_order, 1)
+    full_down = unpermute(full_down, gather_order, 0)
     inputs = tokens[0].astype(jnp.float32)
     _, model_width = inputs.shape
     distance, allowed = layout(cont_segment[0])

time: 693 us -> 718 us (1.036)
  other arithmetic: 88.2 us -> 120 us
  matrix products: 96.6 us -> 76.7 us
  local copies, waits for them, and re-layouts: 111 us -> 120 us
    ppermute x0 -> x8, waiting for transfers between devices: none -> 98.4 us  [gather_pieces(): got = lax.ppermute(buf, axis, [(a, a ^ step) for a in range(size)])]
    all_gather x4 -> x0, waiting for transfers between devices: 96 us -> none  [the longest x1 48.2 us: body_inner(): full_up = lax.all_gather(w_up, 'shard', axis=1, tiled=True)]
    select_n x0 -> x8, other arithmetic: none -> 22 us  [gather_pieces(): jnp.where(low, buf, got)]
    concatenate x0 -> x7, other arithmetic: none -> 13.6 us  [the longest x6 12.2 us: gather_pieces(): jnp.concatenate([jnp.where(low, buf, got), jnp.where(low, got, buf)], dim)]
    dot_general x1, matrix products: 16.5 us -> 5.89 us  [body_inner(): jnp.einsum('tf,if->ti', grad_pre, back_up, preferred_element_type=jnp.flo...]
    ppermute x0 -> x8, starting transfers between devices: none -> 7.88 us  [gather_pieces(): got = lax.ppermute(buf, axis, [(a, a ^ step) for a in range(size)])]
    dynamic_slice x28, local copies, waits for them, and re-layouts: 12.5 us -> 20.3 us  [head_slice(): part = lax.dynamic_slice_in_dim(matrix, block * block_width, block_width, 1)]
    unnamed x188 -> x210, local copies, waits for them, and re-layouts: 27.7 us -> 29.1 us
  transfers between devices with their start and end apart: 28 -> 32, of which waited for: 12 -> 13; matrix products, arithmetic and copies ran while one was open for 26% -> 28% of each run, Pallas kernels for 0% -> 0%
where the time goes in v12:
time: 718 us; the launch traced here: 713 us
  waiting for transfers between devices  291 us (41%)
  other arithmetic  120 us (17%)
  local copies, waits for them, and re-layouts  120 us (17%)
  matrix products  76.7 us (11%)
  starting transfers between devices  63.7 us (9%)
  loops' own time  19.2 us (3%)
  between operations  15.8 us (2%)
    ppermute x8, waiting for transfers between devices, gather_pieces(): got = lax.ppermute(buf, axis, [(a, a ^ step) for a in range(size)])  98.4 us
    psum x1, waiting for transfers between devices, body_inner(): total_a = lax.psum(joined_a, 'rep')  86.1 us
    ppermute x8, waiting for transfers between devices, halving(): lax.ppermute(jnp.concatenate(sends, 0), axis, [(a, a ^ step) for a in ran...  40.8 us
    add x6, other arithmetic, halving(): arrays.append(keep + got[offset:offset + keep.shape[0]].astype(jnp.float32))  36.2 us
    ppermute x7, starting transfers between devices, direct_reduce(): lax.ppermute(send.astype(jnp.bfloat16), axis, [(a, (a + shift) % size) fo...  36 us
    psum x1, waiting for transfers between devices, body_inner(): total_a1 = lax.psum(down_own.astype(jnp.bfloat16), 'rep')  34.9 us
    ppermute x7, waiting for transfers between devices, direct_reduce(): lax.ppermute(mine, axis, [(a, (a + shift) % size) for a in range(size)])  29.4 us
    unnamed x210, local copies, waits for them, and re-layouts  29.1 us
  transfers between devices with their start and end apart: 32, of which 13 were waited for; matrix products, arithmetic and copies ran while one was open for 28% of the time, Pallas kernels for 0%

profile of v12, /device:TPU:0, one launch (start us, length us, event | category | flops | bytes accessed | tf_op | source)
XLA Modules:
  0.0 712.6 jit_solution(8579115496671703224)
XLA Ops:
  7.2 3.1 collective-permute-start
  10.3 34.7 %collective-permute-done = bf16[1024,768]{1,0:T(8,128)(2,1)} collective-permute-done((bf16[1024,768]{1,0:T(8,128)(2,1)}, bf16[1024,768]{1,0:T(8,128)(2,1)}, u32[]{:S(2)}, u32[]{:S(2)}) %collective-permute-start) | collective-permute-done | bytes 1572896 | tf_op jit(solution)/shard_map/ppermute | solution.py:187
  51.3 5.4 all-gather
  60.1 11.9 %collective-permute-done.1 = bf16[256,1024]{1,0:T(8,128)(2,1)} collective-permute-done((bf16[256,1024]{1,0:T(8,128)(2,1)S(1)}, bf16[256,1024]{1,0:T(8,128)(2,1)}, u32[]{:S(2)}, u32[]{:S(2)}) %collective-permute-start.1) | collective-permute-done | bytes 524320 | tf_op jit(solution)/shard_map/ppermute | solution.py:187
  74.3 4.2 broadcast_select_fusion.5
  78.5 2.6 pad_maximum_fusion.2
  86.6 2.7 fusion.74
  93.4 36.1 %collective-permute-done.3 = bf16[1024,1024]{1,0:T(8,128)(2,1)} collective-permute-done((bf16[1024,1024]{1,0:T(8,128)(2,1)}, bf16[1024,1024]{1,0:T(8,128)(2,1)}, u32[]{:S(2)}, u32[]{:S(2)}) %collective-permute-start.3) | collective-permute-done | bytes 2097184 | tf_op jit(solution)/shard_map/ppermute | solution.py:187
  129.5 2.5 broadcast_select_fusion.9
  132.1 2.7 pad_maximum_fusion.5
  137.3 26.7 %while.32 = (s32[]{:T(128)}, bf16[4,384,256]{1,2,0:T(8,128)(2,1)}, f32[4,4,384]{2,1,0:T(4,128)S(1)}, s32[4]{0:T(128)S(1)}, bf16[384,1024]{0,1:T(8,128)(2,1)}, /*...) while((s32[]{:T(128)}, bf16[4,384,256]{1,2,0:T(8,128)(2,1)}, ...), condition=%wide.region_6.7_spmd.clone, body=%wide.region_3.6_spmd.clone.sunk | while | flops 157776416 | bytes 10964623 | solution.py:74
  167.5 15.6 %collective-permute-done.7 = bf16[1024,1024]{1,0:T(8,128)(2,1)} collective-permute-done((bf16[1024,1024]{1,0:T(8,128)(2,1)}, bf16[1024,1024]{1,0:T(8,128)(2,1)}, u32[]{:S(2)}, u32[]{:S(2)}) %collective-permute-start.7) | collective-permute-done | bytes 2097184 | tf_op jit(solution)/shard_map/ppermute | solution.py:187
  183.1 2.5 broadcast_select_fusion.7
  185.6 2.5 pad_maximum_fusion.6
  189.1 3.6 broadcast_select_fusion.3
  194.0 7.5 %multiply_convert_fusion.1 = (bf16[384,4096]{1,0:T(8,128)(2,1)S(1)}, f32[384,4096]{1,0:T(8,128)}) fusion(f32[4096]{0:T(1024)S(1)} %bitcast.401, bf16[1024,1024]{1,0:T(8,128)(2,1)S(1)} %get-tuple-element.655, bf16[1024,1024]{1,0:T(8,128)(2,1)S(1)} %get-tuple-element.590, bf16[1024,1024]{1,0:T(8,128)(2,1)S(1)} %get-tuple-element.656, ...), kind=kOutput, calls=%fused_computation.66 | convolution fusion | flops 3272474624 | bytes 19426304 | tf_op jit(solution)/shard_map/dot_general | solution.py:262
  204.9 3.4 copy.119
  208.4 5.7 fusion.91
  214.1 5.8 copy-done
  219.9 2.7 fusion.26
  224.0 4.1 broadcast_select_fusion.1
  230.4 13.2 %bitcast_add_fusion.1 = f32[2048,1024]{1,0:T(8,128)} fusion(bf16[2048,1024]{1,0:T(8,128)(2,1)} %collective-permute-done.6, f32[2,2048,1024]{2,1,0:T(8,128)} %copy-done, s32[]{:T(128)S(6)} %select_n.352), kind=kLoop, calls=%fused_computation.42 | loop fusion | flops 4194304 | bytes 20971524 | tf_op jit(solution)/shard_map/add | solution.py:158
  243.7 9.1 %convert_reduce_fusion = (f32[4096]{0:T(1024)S(1)}, bf16[384,4096]{1,0:T(8,128)(2,1)S(1)}) fusion(f32[384,4096]{1,0:T(8,128)} %get-tuple-element.650, bf16[4096,1024]{1,0:T(8,128)(2,1)S(1)} %pad_maximum_fusion.1, bf16[1,384,1024]{2,1,0:T(8,128)(2,1)S(1)} %copy-done.18), kind=kOutput, calls=%fused_computation.64 | convolution fusion | flops 3255824384 | bytes 18628608 | tf_op jit(solution)/shard_map/to,fo->tf/dot_general | solution.py:284
  252.8 5.9 multiply_reduce_fusion.1
  267.1 49.5 %while.33 = (s32[]{:T(128)}, bf16[4,384,256]{1,2,0:T(8,128)(2,1)}, bf16[4,384,256]{1,2,0:T(8,128)(2,1)}, bf16[4,384,256]{1,2,0:T(8,128)(2,1)}, s32[4]{0:T(128)S(...) while((s32[]{:T(128)}, bf16[4,384,256]{1,2,0:T(8,128)(2,1)}, ...), condition=%wide.region_13.14_spmd.clone, body=%wide.region_11.13_spmd.clone.sunk | while | flops 385251872 | bytes 30607116 | solution.py:113
  319.0 2.3 pad_maximum_fusion.11
  321.4 3.6 fusion.80
  325.1 2.2 fusion.34
  328.8 3.7 copy-done.1
  334.6 9.6 %fusion.35 = f32[4096,1024]{1,0:T(8,128)} fusion(bf16[384,1024]{1,0:T(8,128)(2,1)S(1)} %copy-done.51, bf16[384,1024]{1,0:T(8,128)(2,1)S(1)} %copy-done.52, bf16[384,1024]{1,0:T(8,128)(2,1)S(1)} %copy-done.53, bf16[384,1024]{1,0:T(8,128)(2,1)S(1)} %copy-done.50, f32[384,1024]{1,0:T(8,128)S(1)} %copy-done.24, f32[1024]{0:T(1024)S(1)} %bitcast.409, ...), kind=kOutput, calls=%fused_computation.93 | convolution fusion | flops 3235774464 | bytes 21507072 | tf_op jit(solution)/shard_map/tf,ti->fi/dot_general | solution.py:290
  344.3 4.0 fusion.27
  348.3 3.0 pad_maximum_fusion.4
  351.5 3.9 fusion.48
  357.4 8.1 %bitcast_add_fusion.2 = f32[1536,1024]{1,0:T(8,128)} fusion(bf16[1536,1024]{1,0:T(8,128)(2,1)} %collective-permute-done.9, f32[2,1536,1024]{2,1,0:T(8,128)} %copy-done.1, s32[]{:T(128)S(6)} %select_n.352), kind=kLoop, calls=%fused_computation.58 | loop fusion | flops 3145728 | bytes 15728644 | tf_op jit(solution)/shard_map/add | solution.py:158
  365.6 2.9 fusion.131
  371.0 3.5 fusion.68
  379.8 10.3 %bitcast_add_fusion = f32[2048,1024]{1,0:T(8,128)} fusion(f32[2,2048,1024]{2,1,0:T(8,128)} %bitcast.374, s32[]{:T(128)S(6)} %select_n.352, bf16[2560,1024]{1,0:T(8,128)(2,1)} %collective-permute-done.28), kind=kLoop, calls=%fused_computation.41 | loop fusion | flops 4194304 | bytes 20971524 | tf_op jit(solution)/shard_map/add | solution.py:158
  390.1 2.5 fusion.49
  393.3 10.8 %collective-permute-done.27 = bf16[1024,1024]{1,0:T(8,128)(2,1)} collective-permute-done((bf16[1024,1024]{1,0:T(8,128)(2,1)}, bf16[1024,1024]{1,0:T(8,128)(2,1)}, u32[]{:S(2)}, u32[]{:S(2)}) %collective-permute-start.27) | collective-permute-done | bytes 2097184 | tf_op jit(solution)/shard_map/ppermute | solution.py:155
  404.2 3.7 fusion.29
  408.1 30.0 %collective-permute-done.12 = bf16[8,1024]{1,0:T(8,128)(2,1)S(1)} collective-permute-done((bf16[8,1024]{1,0:T(8,128)(2,1)S(1)}, bf16[8,1024]{1,0:T(8,128)(2,1)S(1)}, u32[]{:S(2)}, u32[]{:S(2)}) %collective-permute-start.12) | collective-permute-done | bytes 16416 | tf_op jit(solution)/shard_map/ppermute | solution.py:155
  438.1 2.9 bitcast_add_fusion.5
  443.1 4.0 reshape.437
  447.1 2.9 fusion.110
  450.1 4.6 collective-permute-start.19
  455.1 8.7 %fusion.72 = bf16[1,384,1024]{2,1,0:T(8,128)(2,1)} fusion(f32[384,1024]{1,0:T(8,128)S(1)} %copy-done.25, bf16[384,4096]{1,0:T(8,128)(2,1)} %copy-done.27, bf16[4096,1024]{1,0:T(8,128)(2,1)} %copy-done.17, f32[1024]{0:T(1024)S(1)} %bitcast.410), kind=kOutput, calls=%fused_computation.169 | convolution fusion | flops 3222405120 | bytes 13897728 | tf_op jit(solution)/shard_map/dot_general | solution.py:275
  463.8 3.0 collective-permute-start.16
  470.3 26.1 %collective-permute-start.13 = (bf16[97,1024]{1,0:T(8,128)(2,1)}, bf16[97,1024]{1,0:T(8,128)(2,1)}, u32[]{:S(2)}, u32[]{:S(2)}) collective-permute-start(bf16[97,1024]{1,0:T(8,128)(2,1)} %get-tuple-element.595), channel_id=1, source_target_pairs={{0,4},{4,8},{8,12},{12,16},{16,20},{20,24},{24,28},{28,0},{1,5},{5... | collective-permute-start | bytes 595976 | tf_op jit(solution)/shard_map/ppermute | solution.py:169
  496.4 34.9 %all-reduce.5.cloned.1.call-done = bf16[1024,1024]{1,0:T(8,128)(2,1)} async-done(((bf16[1024,1024]{1,0:T(8,128)(2,1)}), bf16[1024,1024]{1,0:T(8,128)(2,1)}) %all-reduce.5.cloned.1.call-update) | async-done | bytes 2097168 | tf_op jit(solution)/shard_map/psum | solution.py:289
  531.3 4.1 convert_element_type.511
  536.8 2.6 bitcast_dynamic-update-slice_fusion.8
  540.9 5.0 fusion.50
  545.9 2.9 copy.112
  553.6 3.0 fusion.78
  558.7 2.8 collective-permute-start.23
  562.6 2.5 collective-permute-start.25
  566.7 4.4 collective-permute-done.21
  571.1 4.5 collective-permute-start.26
  576.3 15.1 %collective-permute-done.22 = bf16[97,1024]{1,0:T(8,128)(2,1)S(1)} collective-permute-done((bf16[97,1024]{1,0:T(8,128)(2,1)}, bf16[97,1024]{1,0:T(8,128)(2,1)S(1)}, u32[]{:S(2)}, u32[]{:S(2)}) %collective-permute-start.22) | collective-permute-done | bytes 198688 | tf_op jit(solution)/shard_map/ppermute | solution.py:177
  592.1 4.8 collective-permute-done.23
  599.0 5.1 collective-permute-done.26
  609.8 2.4 copy.113
  613.3 86.1 %all-reduce.7.cloned.1.call-done = bf16[1280,1024]{1,0:T(8,128)(2,1)} async-done(((bf16[1280,1024]{1,0:T(8,128)(2,1)}), bf16[1280,1024]{1,0:T(8,128)(2,1)}) %all-reduce.7.cloned.1.call-update) | async-done | bytes 2621456 | tf_op jit(solution)/shard_map/psum | solution.py:309
  701.5 4.1 slice_convert_fusion
  (485 shorter events, 149.9 us)
Async XLA Ops:
  7.2 524.2 %all-reduce.5.cloned.1.call-start = ((), (), s32[]{:S(2)}) async-start(), calls=%async_computation | async-start | bytes 4194304 | tf_op jit(solution)/shard_map/psum | solution.py:289
  7.2 37.8 %collective-permute-start = (bf16[1024,768]{1,0:T(8,128)(2,1)}, bf16[1024,768]{1,0:T(8,128)(2,1)}, u32[]{:S(2)}, u32[]{:S(2)}) collective-permute-start(bf16[1024,768]{1,0:T(8,128)(2,1)} %param.25), channel_id=1, source_target_pairs={{0,2},{1,3},{2,0},{3,1},{4,6},{5,7},{6,4},{7,5},{8,10},{9,11},{10,... | collective-permute-start | bytes 4718600 | tf_op jit(solution)/shard_map/ppermute | solution.py:187
  47.2 9.5 %copy-start.78 = (s32[1,2,64]{2,1,0:T(2,128)S(1)}, s32[1,2,64]{2,1,0:T(2,128)}, u32[]{:S(2)}) copy-start(s32[1,2,64]{2,1,0:T(2,128)} %param.21) | copy-start | bytes 1540
  47.2 9.7 %copy-start.4 = (bf16[1,384,1024]{2,1,0:T(8,128)(2,1)S(1)}, bf16[1,384,1024]{2,1,0:T(8,128)(2,1)}, u32[]{:S(2)}) copy-start(bf16[1,384,1024]{2,1,0:T(8,128)(2,1)} %param.20) | copy-start | bytes 2359300
  47.2 10.5 %copy-start.58 = (bf16[256,1024]{1,0:T(8,128)(2,1)S(1)}, bf16[256,1024]{1,0:T(8,128)(2,1)}, u32[]{:S(2)}) copy-start(bf16[256,1024]{1,0:T(8,128)(2,1)} %param.28) | copy-start | bytes 1572868
  49.3 25.0 %collective-permute-start.2 = (bf16[1024,1536]{1,0:T(8,128)(2,1)}, bf16[1024,1536]{1,0:T(8,128)(2,1)}, u32[]{:S(2)}, u32[]{:S(2)}) collective-permute-start(bf16[1024,1536]{1,0:T(8,128)(2,1)} %pad_maximum_fusion.8), channel_id=1, source_target_pairs={{0,1},{1,0},{2,3},{3,2},{4,5},{5,4},{6,7},{7,6},{8,9},{9,8},{10,11... | collective-permute-start | bytes 9437192 | tf_op jit(solution)/shard_map/ppermute | solution.py:187
  57.1 29.4 %copy-start.69 = (f32[384]{0:T(512)}, f32[384]{0:T(512)S(1)}, u32[]{:S(2)}) copy-start(f32[384]{0:T(512)S(1)} %broadcast_multiply_fusion.1) | copy-start | bytes 4612
  57.7 14.3 %collective-permute-start.1 = (bf16[256,1024]{1,0:T(8,128)(2,1)S(1)}, bf16[256,1024]{1,0:T(8,128)(2,1)}, u32[]{:S(2)}, u32[]{:S(2)}) collective-permute-start(bf16[256,1024]{1,0:T(8,128)(2,1)S(1)} %copy-done.58), channel_id=1, source_target_pairs={{0,2},{1,3},{2,0},{3,1},{4,6},{5,7},{6,4},{7,5},{8,10},{9,11},{10,... | collective-permute-start | bytes 1572872 | tf_op jit(solution)/shard_map/ppermute | solution.py:187
  59.4 27.1 %copy-start.76 = (f32[1,2,4,128]{3,1,2,0:T(2,128)}, f32[1,2,4,128]{3,1,2,0:T(2,128)S(1)}, u32[]{:S(2)}) copy-start(f32[1,2,4,128]{3,1,2,0:T(2,128)S(1)} %copy.126) | copy-start | bytes 12292
  59.4 27.1 %copy-start.67 = (f32[1,2,4,128]{3,1,2,0:T(2,128)}, f32[1,2,4,128]{3,1,2,0:T(2,128)S(1)}, u32[]{:S(2)}) copy-start(f32[1,2,4,128]{3,1,2,0:T(2,128)S(1)} %copy.125) | copy-start | bytes 12292
  59.7 14.6 %copy-start.12 = (bf16[1024,768]{1,0:T(8,128)(2,1)S(1)}, bf16[1024,768]{1,0:T(8,128)(2,1)}, u32[]{:S(2)}) copy-start(bf16[1024,768]{1,0:T(8,128)(2,1)} %copy-done.11) | copy-start | bytes 4718596
  60.1 18.4 %copy-start.73 = (f32[384]{0:T(512)}, f32[384]{0:T(512)S(1)}, u32[]{:S(2)}) copy-start(f32[384]{0:T(512)S(1)} %fusion.62) | copy-start | bytes 4612
  60.1 26.4 %copy-start.71 = (f32[384]{0:T(512)}, f32[384]{0:T(512)S(1)}, u32[]{:S(2)}) copy-start(f32[384]{0:T(512)S(1)} %fusion.120) | copy-start | bytes 4612
  74.3 8.5 %collective-permute-start.4 = (bf16[512,1024]{1,0:T(8,128)(2,1)}, bf16[512,1024]{1,0:T(8,128)(2,1)}, u32[]{:S(2)}, u32[]{:S(2)}) collective-permute-start(bf16[512,1024]{1,0:T(8,128)(2,1)} %pad_maximum_fusion.18), channel_id=1, source_target_pairs={{0,1},{1,0},{2,3},{3,2},{4,5},{5,4},{6,7},{7,6},{8,9},{9,8},{10,11... | collective-permute-start | bytes 3145736 | tf_op jit(solution)/shard_map/ppermute | solution.py:187
  81.1 48.4 %collective-permute-start.3 = (bf16[1024,1024]{1,0:T(8,128)(2,1)}, bf16[1024,1024]{1,0:T(8,128)(2,1)}, u32[]{:S(2)}, u32[]{:S(2)}) collective-permute-start(bf16[1024,1024]{1,0:T(8,128)(2,1)} %param.32), channel_id=1, source_target_pairs={{0,2},{1,3},{2,0},{3,1},{4,6},{5,7},{6,4},{7,5},{8,10},{9,11},{10,... | collective-permute-start | bytes 6291464 | tf_op jit(solution)/shard_map/ppermute | solution.py:187
  134.7 54.3 %collective-permute-start.5 = (bf16[1024,2048]{1,0:T(8,128)(2,1)}, bf16[1024,2048]{1,0:T(8,128)(2,1)}, u32[]{:S(2)}, u32[]{:S(2)}) collective-permute-start(bf16[1024,2048]{1,0:T(8,128)(2,1)} %pad_maximum_fusion.5), channel_id=1, source_target_pairs={{0,1},{1,0},{2,3},{3,2},{4,5},{5,4},{6,7},{7,6},{8,9},{9,8},{10,11... | collective-permute-start | bytes 12582920 | tf_op jit(solution)/shard_map/ppermute | solution.py:187
  134.8 48.4 %collective-permute-start.7 = (bf16[1024,1024]{1,0:T(8,128)(2,1)}, bf16[1024,1024]{1,0:T(8,128)(2,1)}, u32[]{:S(2)}, u32[]{:S(2)}) collective-permute-start(bf16[1024,1024]{1,0:T(8,128)(2,1)} %param.34), channel_id=1, source_target_pairs={{0,2},{1,3},{2,0},{3,1},{4,6},{5,7},{6,4},{7,5},{8,10},{9,11},{10,... | collective-permute-start | bytes 6291464 | tf_op jit(solution)/shard_map/ppermute | solution.py:187
  167.1 26.8 %copy-start.22 = (f32[384,1024]{1,0:T(8,128)}, f32[384,1024]{1,0:T(8,128)S(1)}, u32[]{:S(2)}) copy-start(f32[384,1024]{1,0:T(8,128)S(1)} %get-tuple-element.648) | copy-start | bytes 4718596
  189.0 34.9 %collective-permute-start.8 = (bf16[2048,1024]{1,0:T(8,128)(2,1)}, bf16[2048,1024]{1,0:T(8,128)(2,1)}, u32[]{:S(2)}, u32[]{:S(2)}) collective-permute-start(bf16[2048,1024]{1,0:T(8,128)(2,1)} %pad_maximum_fusion.6), channel_id=1, source_target_pairs={{0,1},{1,0},{2,3},{3,2},{4,5},{5,4},{6,7},{7,6},{8,9},{9,8},{10,11... | collective-permute-start | bytes 12582920 | tf_op jit(solution)/shard_map/ppermute | solution.py:187
  193.9 7.5 %copy-start.34 = (bf16[1024,1024]{1,0:T(8,128)(2,1)}, bf16[1024,1024]{1,0:T(8,128)(2,1)S(1)}, u32[]{:S(2)}) copy-start(bf16[1024,1024]{1,0:T(8,128)(2,1)S(1)} %get-tuple-element.589) | copy-start | bytes 6291460
  194.0 7.5 %copy-start.36 = (bf16[1024,1024]{1,0:T(8,128)(2,1)}, bf16[1024,1024]{1,0:T(8,128)(2,1)S(1)}, u32[]{:S(2)}) copy-start(bf16[1024,1024]{1,0:T(8,128)(2,1)S(1)} %get-tuple-element.590) | copy-start | bytes 6291460
  194.0 7.5 %copy-start.38 = (bf16[1024,1024]{1,0:T(8,128)(2,1)}, bf16[1024,1024]{1,0:T(8,128)(2,1)S(1)}, u32[]{:S(2)}) copy-start(bf16[1024,1024]{1,0:T(8,128)(2,1)S(1)} %get-tuple-element.655) | copy-start | bytes 6291460
  194.0 7.5 %copy-start.39 = (bf16[1024,1024]{1,0:T(8,128)(2,1)}, bf16[1024,1024]{1,0:T(8,128)(2,1)S(1)}, u32[]{:S(2)}) copy-start(bf16[1024,1024]{1,0:T(8,128)(2,1)S(1)} %get-tuple-element.656) | copy-start | bytes 6291460
  222.6 7.9 %collective-permute-start.6 = (bf16[2048,1024]{1,0:T(8,128)(2,1)}, bf16[2048,1024]{1,0:T(8,128)(2,1)}, u32[]{:S(2)}, u32[]{:S(2)}) collective-permute-start(bf16[2048,1024]{1,0:T(8,128)(2,1)} %fusion.26), channel_id=1, source_target_pairs={{0,1},{1,0},{2,3},{3,2},{4,5},{5,4},{6,7},{7,6},{8,9},{9,8},{10,11... | collective-permute-start | bytes 12582920 | tf_op jit(solution)/shard_map/ppermute | solution.py:155
  230.4 13.2 %copy-start.17 = (bf16[4096,1024]{1,0:T(8,128)(2,1)}, bf16[4096,1024]{1,0:T(8,128)(2,1)S(1)}, u32[]{:S(2)}) copy-start(bf16[4096,1024]{1,0:T(8,128)(2,1)S(1)} %pad_maximum_fusion.1) | copy-start | bytes 25165828
  230.4 13.2 %copy-start.18 = (bf16[1,384,1024]{2,1,0:T(8,128)(2,1)S(1)}, bf16[1,384,1024]{2,1,0:T(8,128)(2,1)}, u32[]{:S(2)}) copy-start(bf16[1,384,1024]{2,1,0:T(8,128)(2,1)} %param.22) | copy-start | bytes 2359300
  243.6 9.1 %copy-start.23 = (f32[384,1024]{1,0:T(8,128)S(1)}, f32[384,1024]{1,0:T(8,128)}, u32[]{:S(2)}) copy-start(f32[384,1024]{1,0:T(8,128)} %copy-done.22) | copy-start | bytes 4718596
  243.7 9.1 %copy-start.35 = (bf16[1024,1024]{1,0:T(8,128)(2,1)S(1)}, bf16[1024,1024]{1,0:T(8,128)(2,1)}, u32[]{:S(2)}) copy-start(bf16[1024,1024]{1,0:T(8,128)(2,1)} %copy-done.34) | copy-start | bytes 6291460
  243.7 9.1 %copy-start.37 = (bf16[1024,1024]{1,0:T(8,128)(2,1)S(1)}, bf16[1024,1024]{1,0:T(8,128)(2,1)}, u32[]{:S(2)}) copy-start(bf16[1024,1024]{1,0:T(8,128)(2,1)} %copy-done.36) | copy-start | bytes 6291460
  325.0 7.4 %copy-start.1 = (f32[2,1536,1024]{2,1,0:T(8,128)}, f32[2,1536,1024]{2,1,0:T(8,128)S(1)}, u32[]{:S(2)}) copy-start(f32[2,1536,1024]{2,1,0:T(8,128)S(1)} %fusion.80) | copy-start | bytes 37748740
  327.2 30.1 %collective-permute-start.9 = (bf16[1536,1024]{1,0:T(8,128)(2,1)}, bf16[1536,1024]{1,0:T(8,128)(2,1)}, u32[]{:S(2)}, u32[]{:S(2)}) collective-permute-start(bf16[1536,1024]{1,0:T(8,128)(2,1)} %fusion.34), channel_id=1, source_target_pairs={{0,1},{1,0},{2,3},{3,2},{4,5},{5,4},{6,7},{7,6},{8,9},{9,8},{10,11... | collective-permute-start | bytes 9437192 | tf_op jit(solution)/shard_map/ppermute | solution.py:155
  327.5 7.1 copy-start.50
  327.5 7.1 %copy-start.51 = (bf16[384,1024]{1,0:T(8,128)(2,1)S(1)}, bf16[384,1024]{1,0:T(8,128)(2,1)}, u32[]{:S(2)}) copy-start(bf16[384,1024]{1,0:T(8,128)(2,1)} %get-tuple-element.603) | copy-start | bytes 2359300
  327.5 7.1 %copy-start.52 = (bf16[384,1024]{1,0:T(8,128)(2,1)S(1)}, bf16[384,1024]{1,0:T(8,128)(2,1)}, u32[]{:S(2)}) copy-start(bf16[384,1024]{1,0:T(8,128)(2,1)} %get-tuple-element.604) | copy-start | bytes 2359300
  327.5 7.1 %copy-start.53 = (bf16[384,1024]{1,0:T(8,128)(2,1)S(1)}, bf16[384,1024]{1,0:T(8,128)(2,1)}, u32[]{:S(2)}) copy-start(bf16[384,1024]{1,0:T(8,128)(2,1)} %get-tuple-element.605) | copy-start | bytes 2359300
  351.3 25.3 %collective-permute-start.28 = (bf16[2560,1024]{1,0:T(8,128)(2,1)}, bf16[2560,1024]{1,0:T(8,128)(2,1)}, u32[]{:S(2)}, u32[]{:S(2)}) collective-permute-start(bf16[2560,1024]{1,0:T(8,128)(2,1)} %pad_maximum_fusion.4), channel_id=1, source_target_pairs={{0,1},{1,0},{2,3},{3,2},{4,5},{5,4},{6,7},{7,6},{8,9},{9,8},{10,11... | collective-permute-start | bytes 15728648 | tf_op jit(solution)/shard_map/ppermute | solution.py:155
  355.3 48.8 %collective-permute-start.27 = (bf16[1024,1024]{1,0:T(8,128)(2,1)}, bf16[1024,1024]{1,0:T(8,128)(2,1)}, u32[]{:S(2)}, u32[]{:S(2)}) collective-permute-start(bf16[1024,1024]{1,0:T(8,128)(2,1)} %fusion.48), channel_id=1, source_target_pairs={{0,2},{1,3},{2,0},{3,1},{4,6},{5,7},{6,4},{7,5},{8,10},{9,11},{10,... | collective-permute-start | bytes 6291464 | tf_op jit(solution)/shard_map/ppermute | solution.py:155
  357.3 8.2 %copy-start.33 = (bf16[384,3072]{0,1:T(8,128)(2,1)S(1)}, bf16[384,3072]{0,1:T(8,128)(2,1)}, u32[]{:S(2)}) copy-start(bf16[384,3072]{0,1:T(8,128)(2,1)} %get-tuple-element.304) | copy-start | bytes 7077892
  357.4 8.2 %copy-start.41 = (bf16[1024,768]{1,0:T(8,128)(2,1)S(1)}, bf16[1024,768]{1,0:T(8,128)(2,1)}, u32[]{:S(2)}) copy-start(bf16[1024,768]{1,0:T(8,128)(2,1)} %copy-done.40) | copy-start | bytes 4718596
  357.4 8.2 %copy-start.43 = (bf16[1024,768]{1,0:T(8,128)(2,1)S(1)}, bf16[1024,768]{1,0:T(8,128)(2,1)}, u32[]{:S(2)}) copy-start(bf16[1024,768]{1,0:T(8,128)(2,1)} %copy-done.42) | copy-start | bytes 4718596
  357.4 8.2 %copy-start.45 = (bf16[1024,768]{1,0:T(8,128)(2,1)S(1)}, bf16[1024,768]{1,0:T(8,128)(2,1)}, u32[]{:S(2)}) copy-start(bf16[1024,768]{1,0:T(8,128)(2,1)} %copy-done.44) | copy-start | bytes 4718596
  357.4 8.2 %copy-start.47 = (bf16[1024,768]{1,0:T(8,128)(2,1)S(1)}, bf16[1024,768]{1,0:T(8,128)(2,1)}, u32[]{:S(2)}) copy-start(bf16[1024,768]{1,0:T(8,128)(2,1)} %copy-done.46) | copy-start | bytes 4718596
  370.8 4.2 collective-permute-start.11
  374.5 63.6 %collective-permute-start.10 = (bf16[768,1024]{1,0:T(8,128)(2,1)}, bf16[768,1024]{1,0:T(8,128)(2,1)}, u32[]{:S(2)}, u32[]{:S(2)}) collective-permute-start(bf16[768,1024]{1,0:T(8,128)(2,1)} %fusion.68), channel_id=1, source_target_pairs={{0,2},{1,3},{2,0},{3,1},{4,6},{5,7},{6,4},{7,5},{8,10},{9,11},{10,... | collective-permute-start | bytes 4718600 | tf_op jit(solution)/shard_map/ppermute | solution.py:155
  375.0 63.1 %collective-permute-start.12 = (bf16[8,1024]{1,0:T(8,128)(2,1)S(1)}, bf16[8,1024]{1,0:T(8,128)(2,1)S(1)}, u32[]{:S(2)}, u32[]{:S(2)}) collective-permute-start(bf16[8,1024]{1,0:T(8,128)(2,1)S(1)} %fusion.119), channel_id=1, source_target_pairs={{0,2},{1,3},{2,0},{3,1},{4,6},{5,7},{6,4},{7,5},{8,10},{9,11},{10,... | collective-permute-start | bytes 49160 | tf_op jit(solution)/shard_map/ppermute | solution.py:155
  376.6 27.5 %slice-start = ((s8[8388608]{0:T(1024)(128)(4,1)}), s8[4194304]{0:T(1024)(128)(4,1)S(1)}, s32[]{:S(2)}) async-start(s8[8388608]{0:T(1024)(128)(4,1)} %bitcast.358), calls=%async_computation.2 | async-start | bytes 8388608
  379.8 24.4 %slice-start.1 = ((s8[8388608]{0:T(1024)(128)(4,1)}), s8[4194304]{0:T(1024)(128)(4,1)S(1)}, s32[]{:S(2)}) async-start(s8[8388608]{0:T(1024)(128)(4,1)} %bitcast.358), calls=%async_computation.3 | async-start | bytes 8388608
  392.8 148.1 %collective-permute-start.29 = (bf16[1280,1024]{1,0:T(8,128)(2,1)S(1)}, bf16[1280,1024]{1,0:T(8,128)(2,1)}, u32[]{:S(2)}, u32[]{:S(2)}) collective-permute-start(bf16[1280,1024]{1,0:T(8,128)(2,1)S(1)} %pad_maximum_fusion.9), channel_id=1, source_target_pairs={{0,2},{1,3},{2,0},{3,1},{4,6},{5,7},{6,4},{7,5},{8,10},{9,11},{10,... | collective-permute-start | bytes 7864328 | tf_op jit(solution)/shard_map/ppermute | solution.py:155
  407.8 291.5 %all-reduce.7.cloned.1.call-start = ((), (), s32[]{:S(2)}) async-start(), calls=%async_computation.1 | async-start | bytes 5242880 | tf_op jit(solution)/shard_map/psum | solution.py:309
  447.1 8.0 %copy-start.25 = (f32[384,1024]{1,0:T(8,128)S(1)}, f32[384,1024]{1,0:T(8,128)}, u32[]{:S(2)}) copy-start(f32[384,1024]{1,0:T(8,128)} %copy-done.22) | copy-start | bytes 4718596
  450.1 16.8 %collective-permute-start.19 = (bf16[97,1024]{1,0:T(8,128)(2,1)S(1)}, bf16[97,1024]{1,0:T(8,128)(2,1)}, u32[]{:S(2)}, u32[]{:S(2)}) collective-permute-start(bf16[97,1024]{1,0:T(8,128)(2,1)S(1)} %get-tuple-element.596), channel_id=1, source_target_pairs={{0,28},{4,0},{8,4},{12,8},{16,12},{20,16},{24,20},{28,24},{1,29},{... | collective-permute-start | bytes 595976 | tf_op jit(solution)/shard_map/ppermute | solution.py:169
  454.7 12.1 %collective-permute-start.18 = (bf16[97,1024]{1,0:T(8,128)(2,1)S(1)}, bf16[97,1024]{1,0:T(8,128)(2,1)}, u32[]{:S(2)}, u32[]{:S(2)}) collective-permute-start(bf16[97,1024]{1,0:T(8,128)(2,1)S(1)} %get-tuple-element.597), channel_id=1, source_target_pairs={{0,24},{4,28},{8,0},{12,4},{16,8},{20,12},{24,16},{28,20},{1,25},{... | collective-permute-start | bytes 595976 | tf_op jit(solution)/shard_map/ppermute | solution.py:169
  455.1 15.2 %collective-permute-start.17 = (bf16[97,1024]{1,0:T(8,128)(2,1)S(1)}, bf16[97,1024]{1,0:T(8,128)(2,1)}, u32[]{:S(2)}, u32[]{:S(2)}) collective-permute-start(bf16[97,1024]{1,0:T(8,128)(2,1)S(1)} %get-tuple-element.598), channel_id=1, source_target_pairs={{0,20},{4,24},{8,28},{12,0},{16,4},{20,8},{24,12},{28,16},{1,21},{... | collective-permute-start | bytes 595976 | tf_op jit(solution)/shard_map/ppermute | solution.py:169
  463.8 71.6 %collective-permute-start.16 = (bf16[97,1024]{1,0:T(8,128)(2,1)}, bf16[97,1024]{1,0:T(8,128)(2,1)}, u32[]{:S(2)}, u32[]{:S(2)}) collective-permute-start(bf16[97,1024]{1,0:T(8,128)(2,1)} %get-tuple-element.599), channel_id=1, source_target_pairs={{0,16},{4,20},{8,24},{12,28},{16,0},{20,4},{24,8},{28,12},{1,17},{... | collective-permute-start | bytes 595976 | tf_op jit(solution)/shard_map/ppermute | solution.py:169
  466.8 68.6 %collective-permute-start.15 = (bf16[97,1024]{1,0:T(8,128)(2,1)}, bf16[97,1024]{1,0:T(8,128)(2,1)}, u32[]{:S(2)}, u32[]{:S(2)}) collective-permute-start(bf16[97,1024]{1,0:T(8,128)(2,1)} %get-tuple-element.600), channel_id=1, source_target_pairs={{0,12},{4,16},{8,20},{12,24},{16,28},{20,0},{24,4},{28,8},{1,13},{... | collective-permute-start | bytes 595976 | tf_op jit(solution)/shard_map/ppermute | solution.py:169
  466.8 68.6 %collective-permute-start.14 = (bf16[97,1024]{1,0:T(8,128)(2,1)}, bf16[97,1024]{1,0:T(8,128)(2,1)}, u32[]{:S(2)}, u32[]{:S(2)}) collective-permute-start(bf16[97,1024]{1,0:T(8,128)(2,1)} %get-tuple-element.601), channel_id=1, source_target_pairs={{0,8},{4,12},{8,16},{12,20},{16,24},{20,28},{24,0},{28,4},{1,9},{5... | collective-permute-start | bytes 595976 | tf_op jit(solution)/shard_map/ppermute | solution.py:169
  470.3 65.1 %collective-permute-start.13 = (bf16[97,1024]{1,0:T(8,128)(2,1)}, bf16[97,1024]{1,0:T(8,128)(2,1)}, u32[]{:S(2)}, u32[]{:S(2)}) collective-permute-start(bf16[97,1024]{1,0:T(8,128)(2,1)} %get-tuple-element.595), channel_id=1, source_target_pairs={{0,4},{4,8},{8,12},{12,16},{16,20},{20,24},{24,28},{28,0},{1,5},{5... | collective-permute-start | bytes 595976 | tf_op jit(solution)/shard_map/ppermute | solution.py:169
  539.4 23.1 %collective-permute-start.20 = (bf16[97,1024]{1,0:T(8,128)(2,1)}, bf16[97,1024]{1,0:T(8,128)(2,1)}, u32[]{:S(2)}, u32[]{:S(2)}) collective-permute-start(bf16[97,1024]{1,0:T(8,128)(2,1)} %get-tuple-element.558), channel_id=1, source_target_pairs={{0,4},{4,8},{8,12},{12,16},{16,20},{20,24},{24,28},{28,0},{1,5},{5... | collective-permute-start | bytes 595976 | tf_op jit(solution)/shard_map/ppermute | solution.py:177
  556.6 14.5 %collective-permute-start.21 = (bf16[97,1024]{1,0:T(8,128)(2,1)}, bf16[97,1024]{1,0:T(8,128)(2,1)S(1)}, u32[]{:S(2)}, u32[]{:S(2)}) collective-permute-start(bf16[97,1024]{1,0:T(8,128)(2,1)} %get-tuple-element.558), channel_id=1, source_target_pairs={{0,8},{4,12},{8,16},{12,20},{16,24},{20,28},{24,0},{28,4},{1,9},{5... | collective-permute-start | bytes 595976 | tf_op jit(solution)/shard_map/ppermute | solution.py:177
  557.7 33.7 %collective-permute-start.22 = (bf16[97,1024]{1,0:T(8,128)(2,1)}, bf16[97,1024]{1,0:T(8,128)(2,1)S(1)}, u32[]{:S(2)}, u32[]{:S(2)}) collective-permute-start(bf16[97,1024]{1,0:T(8,128)(2,1)} %get-tuple-element.558), channel_id=1, source_target_pairs={{0,12},{4,16},{8,20},{12,24},{16,28},{20,0},{24,4},{28,8},{1,13},{... | collective-permute-start | bytes 595976 | tf_op jit(solution)/shard_map/ppermute | solution.py:177
  558.7 38.2 %collective-permute-start.23 = (bf16[97,1024]{1,0:T(8,128)(2,1)}, bf16[97,1024]{1,0:T(8,128)(2,1)S(1)}, u32[]{:S(2)}, u32[]{:S(2)}) collective-permute-start(bf16[97,1024]{1,0:T(8,128)(2,1)} %get-tuple-element.558), channel_id=1, source_target_pairs={{0,16},{4,20},{8,24},{12,28},{16,0},{20,4},{24,8},{28,12},{1,17},{... | collective-permute-start | bytes 595976 | tf_op jit(solution)/shard_map/ppermute | solution.py:177
  561.5 36.1 %collective-permute-start.24 = (bf16[97,1024]{1,0:T(8,128)(2,1)}, bf16[97,1024]{1,0:T(8,128)(2,1)S(1)}, u32[]{:S(2)}, u32[]{:S(2)}) collective-permute-start(bf16[97,1024]{1,0:T(8,128)(2,1)} %get-tuple-element.558), channel_id=1, source_target_pairs={{0,20},{4,24},{8,28},{12,0},{16,4},{20,8},{24,12},{28,16},{1,21},{... | collective-permute-start | bytes 595976 | tf_op jit(solution)/shard_map/ppermute | solution.py:177
  562.6 35.8 %collective-permute-start.25 = (bf16[97,1024]{1,0:T(8,128)(2,1)}, bf16[97,1024]{1,0:T(8,128)(2,1)S(1)}, u32[]{:S(2)}, u32[]{:S(2)}) collective-permute-start(bf16[97,1024]{1,0:T(8,128)(2,1)} %get-tuple-element.558), channel_id=1, source_target_pairs={{0,24},{4,28},{8,0},{12,4},{16,8},{20,12},{24,16},{28,20},{1,25},{... | collective-permute-start | bytes 595976 | tf_op jit(solution)/shard_map/ppermute | solution.py:177
  571.1 33.1 %collective-permute-start.26 = (bf16[97,1024]{1,0:T(8,128)(2,1)}, bf16[97,1024]{1,0:T(8,128)(2,1)S(1)}, u32[]{:S(2)}, u32[]{:S(2)}) collective-permute-start(bf16[97,1024]{1,0:T(8,128)(2,1)} %get-tuple-element.558), channel_id=1, source_target_pairs={{0,28},{4,0},{8,4},{12,8},{16,12},{20,16},{24,20},{28,24},{1,29},{... | collective-permute-start | bytes 595976 | tf_op jit(solution)/shard_map/ppermute | solution.py:177
  (64 other events, 165.3 us)
Sparse Core Ops, SparseCore 0:
  408.0 123.3 all-reduce.4
  552.1 147.2 all-reduce.6

commit v13 on v11

--- a/solution.py
+++ b/solution.py
@@ -164,18 +164,18 @@
     index = lax.axis_index(axis)
     chunks = buf.reshape(size, buf.shape[0] // size, *buf.shape[1:])
     total = lax.dynamic_index_in_dim(chunks, index, 0, keepdims=False)
+    low_chunks = chunks.astype(jnp.bfloat16)
     for shift in range(1, size):
-        send = lax.dynamic_index_in_dim(chunks, (index + shift) % size, 0, keepdims=False)
-        got = lax.ppermute(
-            send.astype(jnp.bfloat16), axis, [(a, (a + shift) % size) for a in range(size)]
-        )
+        partner = lax.bitwise_xor(index, shift)
+        send = lax.dynamic_index_in_dim(low_chunks, partner, 0, keepdims=False)
+        got = lax.ppermute(send, axis, [(a, a ^ shift) for a in range(size)])
         total = total + got.astype(jnp.float32)
     mine = total.astype(jnp.bfloat16)
     result = jnp.zeros((size, *mine.shape), jnp.bfloat16)
     result = lax.dynamic_update_index_in_dim(result, mine, index, 0)
     for shift in range(1, size):
-        got = lax.ppermute(mine, axis, [(a, (a + shift) % size) for a in range(size)])
-        result = lax.dynamic_update_index_in_dim(result, got, (index - shift) % size, 0)
+        got = lax.ppermute(mine, axis, [(a, a ^ shift) for a in range(size)])
+        result = lax.dynamic_update_index_in_dim(result, got, lax.bitwise_xor(index, shift), 0)
     return result.reshape(buf.shape)
 
 

time: 693 us -> 696 us (level)
  waiting for transfers between devices: 294 us -> 310 us
  starting transfers between devices: 56.7 us -> 44.7 us
    ppermute x14, waiting for transfers between devices: 29.6 us -> 50.4 us  [the longest x7 43.9 us: direct_reduce(): got = lax.ppermute(mine, axis, [(a, a ^ shift) for a in range(size)])]
    psum x1, waiting for transfers between devices: 86.3 us -> 73.2 us  [body_inner(): total_a = lax.psum(joined_a, 'rep')]
    ppermute x14, starting transfers between devices: 51.3 us -> 39.3 us  [the longest x7 28.8 us: direct_reduce(): got = lax.ppermute(send, axis, [(a, a ^ shift) for a in range(size)])]
    psum x1, waiting for transfers between devices: 33.7 us -> 41.6 us  [body_inner(): total_a1 = lax.psum(down_own.astype(jnp.bfloat16), 'rep')]
    unnamed x188 -> x190, local copies, waits for them, and re-layouts: 27.7 us -> 27.8 us
  transfers between devices with their start and end apart: 28 -> 28, of which waited for: 12 -> 13; matrix products, arithmetic and copies ran while one was open for 26% -> 26% of each run, Pallas kernels for 0% -> 0%
where the time goes in v13:
time: 696 us; the launch traced here: 691 us
  waiting for transfers between devices  310 us (45%)
  local copies, waits for them, and re-layouts  109 us (16%)
  matrix products  95.6 us (14%)
  other arithmetic  90.5 us (13%)
  starting transfers between devices  44.7 us (6%)
  loops' own time  18.9 us (3%)
  between operations  15.9 us (2%)
    psum x1, waiting for transfers between devices, body_inner(): total_a = lax.psum(joined_a, 'rep')  73.2 us
    all_gather x1, waiting for transfers between devices, body_inner(): full_up = lax.all_gather(w_up, 'shard', axis=1, tiled=True)  48.2 us
    ppermute x8, waiting for transfers between devices, halving(): lax.ppermute(jnp.concatenate(sends, 0), axis, [(a, a ^ step) for a in ran...  46.3 us
    ppermute x7, waiting for transfers between devices, direct_reduce(): got = lax.ppermute(mine, axis, [(a, a ^ shift) for a in range(size)])  43.9 us
    psum x1, waiting for transfers between devices, body_inner(): total_a1 = lax.psum(down_own.astype(jnp.bfloat16), 'rep')  41.6 us
    all_gather x1, waiting for transfers between devices, body_inner(): full_qkv = lax.all_gather(w_qkv, 'shard', axis=1, tiled=True)  38.1 us
    add x6, other arithmetic, halving(): arrays.append(keep + got[offset:offset + keep.shape[0]].astype(jnp.float32))  33.4 us
    ppermute x7, starting transfers between devices, direct_reduce(): got = lax.ppermute(send, axis, [(a, a ^ shift) for a in range(size)])  28.8 us
  transfers between devices with their start and end apart: 28, of which 13 were waited for; matrix products, arithmetic and copies ran while one was open for 26% of the time, Pallas kernels for 0%

profile of v13, /device:TPU:0, one launch (start us, length us, event | category | flops | bytes accessed | tf_op | source)
XLA Modules:
  0.0 691.3 jit_solution(3144196169438329892)
XLA Ops:
  12.2 6.5 all-gather
  20.6 38.1 %all-gather.6.cloned.1.call-done = bf16[1024,3072]{1,0:T(8,128)(2,1)} async-done(((bf16[1024,768]{1,0:T(8,128)(2,1)}), bf16[1024,3072]{1,0:T(8,128)(2,1)}) %all-gather.6.cloned.1.call-update) | async-done | bytes 6291472 | tf_op jit(solution)/shard_map/all_gather | solution.py:215
  58.7 4.9 fusion.79
  68.3 21.3 %while.32 = (s32[]{:T(128)}, bf16[4,384,256]{1,2,0:T(8,128)(2,1)}, f32[4,4,384]{2,1,0:T(4,128)}, s32[4]{0:T(128)S(1)}, bf16[384,1024]{0,1:T(8,128)(2,1)S(1)}, /*...) while((s32[]{:T(128)}, bf16[4,384,256]{1,2,0:T(8,128)(2,1)}, ...), condition=%wide.region_6.7_spmd.clone, body=%wide.region_3.6_spmd.clone.sunk | while | flops 157776416 | bytes 10964623 | solution.py:74
  90.8 3.3 fusion.125
  94.5 48.2 %all-gather.10.cloned.1.call-done = bf16[1024,4096]{1,0:T(8,128)(2,1)} async-done(((bf16[1024,1024]{1,0:T(8,128)(2,1)}), bf16[1024,4096]{1,0:T(8,128)(2,1)}) %all-gather.10.cloned.1.call-update) | async-done | bytes 8388624 | tf_op jit(solution)/shard_map/all_gather | solution.py:217
  142.7 10.6 %multiply_convert_fusion.1 = (bf16[384,4096]{1,0:T(8,128)(2,1)S(1)}, f32[384,4096]{1,0:T(8,128)}) fusion(f32[4096]{0:T(1024)S(1)} %bitcast.408, bf16[1024,4096]{1,0:T(8,128)(2,1)} %all-gather.10.cloned.1.call-done, f32[384,1024]{1,0:T(8,128)S(1)} %get-tuple-element.606, f32[1024]{0:T(1024)S(1)} %bitcast.415, f32[1024]{0:T(1024)S(1)} %bitcast.409, ...), kind=kOutput, calls=%fused_computation.62 | convolution fusion | flops 3238920192 | bytes 19426304 | tf_op jit(solution)/shard_map/dot_general | solution.py:237
  154.9 1.8 maximum_bitcast_fusion
  156.7 3.8 copy.119
  160.5 5.7 fusion.89
  166.2 5.8 copy-done
  172.0 2.7 fusion.26
  175.8 6.7 collective-permute-done
  182.6 10.3 %bitcast_add_fusion.1 = f32[2048,1024]{1,0:T(8,128)} fusion(bf16[2048,1024]{1,0:T(8,128)(2,1)} %collective-permute-done, f32[2,2048,1024]{2,1,0:T(8,128)} %copy-done, s32[]{:T(128)S(6)} %select_n.147), kind=kLoop, calls=%fused_computation.40 | loop fusion | flops 4194304 | bytes 20971524 | tf_op jit(solution)/shard_map/add | solution.py:158
  192.8 9.6 %all-gather.12.cloned.1.call-done = bf16[4096,1024]{1,0:T(8,128)(2,1)} async-done(((bf16[1024,1024]{1,0:T(8,128)(2,1)}), bf16[4096,1024]{1,0:T(8,128)(2,1)}) %all-gather.12.cloned.1.call-update) | async-done | bytes 8388624 | tf_op jit(solution)/shard_map/all_gather | solution.py:218
  202.4 10.8 %convert_reduce_fusion = (f32[4096]{0:T(1024)}, bf16[384,4096]{1,0:T(8,128)(2,1)S(1)}) fusion(f32[384,4096]{1,0:T(8,128)} %get-tuple-element.608, bf16[4096,1024]{1,0:T(8,128)(2,1)} %all-gather.12.cloned.1.call-done, bf16[1,384,1024]{2,1,0:T(8,128)(2,1)S(1)} %copy-done.18), kind=kOutput, calls=%fused_computation.60 | convolution fusion | flops 3255824384 | bytes 18628608 | tf_op jit(solution)/shard_map/to,fo->tf/dot_general | solution.py:259
  213.2 1.7 fusion.121
  215.6 16.5 %multiply_reduce_fusion.1 = (f32[1024]{0:T(1024)}, f32[384]{0:T(512)S(1)}, f32[1024]{0:T(1024)}, f32[384,1024]{1,0:T(8,128)S(1)}) fusion(f32[384,1024]{1,0:T(8,128)S(1)} %copy-done.7, f32[384]{0:T(512)S(1)} %fusion.112, f32[384]{0:T(512)S(1)} %broadcast_multiply_fusion, f32[1024]{0:T(1024)S(1)} %bitcast.410, bf16[384,4096]{1,0:T(8,128)(2,1)S(1)} %get-tuple-element.612, ...), kind=kOutput, calls=%fused_computation.137 | convolution fusion | flops 3224368640 | bytes 14696960 | tf_op jit(solution)/shard_map/tf,if->ti/dot_general | solution.py:268
  239.1 54.7 %while.33 = (s32[]{:T(128)}, bf16[4,384,256]{1,2,0:T(8,128)(2,1)}, bf16[4,384,256]{1,2,0:T(8,128)(2,1)}, bf16[4,384,256]{1,2,0:T(8,128)(2,1)}, s32[4]{0:T(128)S(...) while((s32[]{:T(128)}, bf16[4,384,256]{1,2,0:T(8,128)(2,1)}, ...), condition=%wide.region_13.14_spmd.clone, body=%wide.region_11.13_spmd.clone.sunk | while | flops 385251872 | bytes 30610428 | solution.py:113
  296.3 2.4 pad_maximum_fusion.4
  298.7 3.6 fusion.77
  302.4 2.2 fusion.34
  306.2 3.5 copy-done.1
  309.7 2.0 copy-done.4
  311.9 9.7 %fusion.35 = f32[4096,1024]{1,0:T(8,128)} fusion(bf16[384,1024]{1,0:T(8,128)(2,1)S(1)} %copy-done.33, bf16[384,1024]{1,0:T(8,128)(2,1)S(1)} %copy-done.34, bf16[384,1024]{1,0:T(8,128)(2,1)S(1)} %copy-done.35, bf16[384,1024]{1,0:T(8,128)(2,1)S(1)} %copy-done.32, f32[384,1024]{1,0:T(8,128)S(1)} %copy-done.8, f32[1024]{0:T(1024)S(1)} %bitcast.416, ...), kind=kOutput, calls=%fused_computation.82 | convolution fusion | flops 3235774464 | bytes 21507072 | tf_op jit(solution)/shard_map/tf,ti->fi/dot_general | solution.py:265
  321.6 4.0 fusion.27
  325.7 2.9 pad_maximum_fusion
  328.9 4.0 fusion.48
  333.7 8.2 %bitcast_add_fusion.2 = f32[1536,1024]{1,0:T(8,128)} fusion(bf16[1536,1024]{1,0:T(8,128)(2,1)} %collective-permute-done.1, f32[2,1536,1024]{2,1,0:T(8,128)} %copy-done.1, s32[]{:T(128)S(6)} %select_n.147), kind=kLoop, calls=%fused_computation.54 | loop fusion | flops 3145728 | bytes 15728644 | tf_op jit(solution)/shard_map/add | solution.py:158
  341.9 2.9 fusion.116
  347.3 3.5 fusion.68
  356.0 10.3 %bitcast_add_fusion = f32[2048,1024]{1,0:T(8,128)} fusion(f32[2,2048,1024]{2,1,0:T(8,128)} %bitcast.380, s32[]{:T(128)S(6)} %select_n.147, bf16[2560,1024]{1,0:T(8,128)(2,1)} %collective-permute-done.20), kind=kLoop, calls=%fused_computation.39 | loop fusion | flops 4194304 | bytes 20971524 | tf_op jit(solution)/shard_map/add | solution.py:158
  366.3 2.5 fusion.49
  372.2 9.6 %collective-permute-done.19 = bf16[1024,1024]{1,0:T(8,128)(2,1)} collective-permute-done((bf16[1024,1024]{1,0:T(8,128)(2,1)}, bf16[1024,1024]{1,0:T(8,128)(2,1)}, u32[]{:S(2)}, u32[]{:S(2)}) %collective-permute-start.19) | collective-permute-done | bytes 2097184 | tf_op jit(solution)/shard_map/ppermute | solution.py:155
  381.8 3.7 fusion.29
  385.8 30.0 %collective-permute-done.4 = bf16[8,1024]{1,0:T(8,128)(2,1)S(1)} collective-permute-done((bf16[8,1024]{1,0:T(8,128)(2,1)S(1)}, bf16[8,1024]{1,0:T(8,128)(2,1)S(1)}, u32[]{:S(2)}, u32[]{:S(2)}) %collective-permute-start.4) | collective-permute-done | bytes 16416 | tf_op jit(solution)/shard_map/ppermute | solution.py:155
  415.7 2.9 bitcast_add_fusion.5
  418.7 2.0 pad_maximum_fusion.1
  420.7 4.2 reshape.430
  424.9 2.4 convert_element_type.444
  428.2 4.1 collective-permute-start.11
  433.4 7.7 %fusion.71 = bf16[1,384,1024]{2,1,0:T(8,128)(2,1)} fusion(f32[384,1024]{1,0:T(8,128)S(1)} %copy-done.8, bf16[384,4096]{1,0:T(8,128)(2,1)S(1)} %copy-done.24, bf16[4096,1024]{1,0:T(8,128)(2,1)} %all-gather.12.cloned.1.call-done, f32[1024]{0:T(1024)S(1)} %bitcast.417), kind=kOutput, calls=%fused_computation.147 | convolution fusion | flops 3222405120 | bytes 13897728 | tf_op jit(solution)/shard_map/dot_general | solution.py:250
  441.1 2.4 collective-permute-start.8
  443.6 15.2 %collective-permute-start.7 = (bf16[97,1024]{1,0:T(8,128)(2,1)}, bf16[97,1024]{1,0:T(8,128)(2,1)S(1)}, u32[]{:S(2)}, u32[]{:S(2)}) collective-permute-start(bf16[97,1024]{1,0:T(8,128)(2,1)} %get-tuple-element.578), channel_id=1, source_target_pairs={{0,12},{4,8},{8,4},{12,0},{16,28},{20,24},{24,20},{28,16},{1,13},{... | collective-permute-start | bytes 595976 | tf_op jit(solution)/shard_map/ppermute | solution.py:171
  458.8 3.7 collective-permute-start.6
  462.5 6.5 collective-permute-done.9
  469.0 2.3 collective-permute-start.5
  471.2 41.6 %all-reduce.5.cloned.1.call-done = bf16[1024,1024]{1,0:T(8,128)(2,1)} async-done(((bf16[1024,1024]{1,0:T(8,128)(2,1)}), bf16[1024,1024]{1,0:T(8,128)(2,1)}) %all-reduce.5.cloned.1.call-update) | async-done | bytes 2097168 | tf_op jit(solution)/shard_map/psum | solution.py:264
  512.8 4.1 convert_element_type.459
  518.3 2.0 bitcast_dynamic-update-slice_fusion.8
  521.7 5.0 fusion.50
  526.7 2.9 copy.112
  534.4 3.0 fusion.75
  541.2 2.1 collective-permute-start.16
  546.5 18.2 %collective-permute-done.13 = bf16[97,1024]{1,0:T(8,128)(2,1)S(1)} collective-permute-done((bf16[97,1024]{1,0:T(8,128)(2,1)S(1)}, bf16[97,1024]{1,0:T(8,128)(2,1)S(1)}, u32[]{:S(2)}, u32[]{:S(2)}) %collective-permute-start.13) | collective-permute-done | bytes 198688 | tf_op jit(solution)/shard_map/ppermute | solution.py:177
  567.0 8.6 %collective-permute-done.14 = bf16[97,1024]{1,0:T(8,128)(2,1)S(1)} collective-permute-done((bf16[97,1024]{1,0:T(8,128)(2,1)S(1)}, bf16[97,1024]{1,0:T(8,128)(2,1)S(1)}, u32[]{:S(2)}, u32[]{:S(2)}) %collective-permute-start.14) | collective-permute-done | bytes 198688 | tf_op jit(solution)/shard_map/ppermute | solution.py:177
  577.0 14.8 %collective-permute-done.16 = bf16[97,1024]{1,0:T(8,128)(2,1)S(1)} collective-permute-done((bf16[97,1024]{1,0:T(8,128)(2,1)S(1)}, bf16[97,1024]{1,0:T(8,128)(2,1)S(1)}, u32[]{:S(2)}, u32[]{:S(2)}) %collective-permute-start.16) | collective-permute-done | bytes 198688 | tf_op jit(solution)/shard_map/ppermute | solution.py:177
  593.1 2.3 collective-permute-done.18
  596.2 1.9 reshape.431
  599.3 1.8 convert_bitcast_fusion
  601.1 2.4 copy.113
  604.6 73.2 %all-reduce.7.cloned.1.call-done = bf16[1280,1024]{1,0:T(8,128)(2,1)} async-done(((bf16[1280,1024]{1,0:T(8,128)(2,1)}), bf16[1280,1024]{1,0:T(8,128)(2,1)}) %all-reduce.7.cloned.1.call-update) | async-done | bytes 2621456 | tf_op jit(solution)/shard_map/psum | solution.py:284
  677.8 2.1 slice_convert_fusion.2
  679.9 4.1 slice_convert_fusion
  (475 shorter events, 121.4 us)
Async XLA Ops:
  7.2 51.5 %all-gather.6.cloned.1.call-start = ((), (), s32[]{:S(2)}) async-start(), calls=%async_computation | async-start | bytes 7864320 | tf_op jit(solution)/shard_map/all_gather | solution.py:215
  8.0 81.7 %all-gather.8.cloned.1.call-start = ((), (), s32[]{:S(2)}) async-start(), calls=%async_computation.1 | async-start | bytes 2621440 | tf_op jit(solution)/shard_map/all_gather | solution.py:216
  8.8 10.6 %copy-start.2 = (bf16[1,384,1024]{2,1,0:T(8,128)(2,1)S(1)}, bf16[1,384,1024]{2,1,0:T(8,128)(2,1)}, u32[]{:S(2)}) copy-start(bf16[1,384,1024]{2,1,0:T(8,128)(2,1)} %param.20) | copy-start | bytes 2359300
  8.8 133.9 %all-gather.10.cloned.1.call-start = ((), (), s32[]{:S(2)}) async-start(), calls=%async_computation.2 | async-start | bytes 10485760 | tf_op jit(solution)/shard_map/all_gather | solution.py:217
  9.5 10.6 %copy-start.68 = (s32[1,2,64]{2,1,0:T(2,128)S(1)}, s32[1,2,64]{2,1,0:T(2,128)}, u32[]{:S(2)}) copy-start(s32[1,2,64]{2,1,0:T(2,128)} %param.21) | copy-start | bytes 1540
  9.5 192.9 %all-gather.12.cloned.1.call-start = ((), (), s32[]{:S(2)}) async-start(), calls=%async_computation.3 | async-start | bytes 10485760 | tf_op jit(solution)/shard_map/all_gather | solution.py:218
  10.1 502.7 %all-reduce.5.cloned.1.call-start = ((), (), s32[]{:S(2)}) async-start(), calls=%async_computation.4 | async-start | bytes 4194304 | tf_op jit(solution)/shard_map/psum | solution.py:264
  19.3 44.3 %copy-start.60 = (f32[1,2,4,128]{3,1,2,0:T(2,128)}, f32[1,2,4,128]{3,1,2,0:T(2,128)S(1)}, u32[]{:S(2)}) copy-start(f32[1,2,4,128]{3,1,2,0:T(2,128)S(1)} %copy.126) | copy-start | bytes 12292
  19.3 44.3 %copy-start.39 = (f32[1,2,4,128]{3,1,2,0:T(2,128)}, f32[1,2,4,128]{3,1,2,0:T(2,128)S(1)}, u32[]{:S(2)}) copy-start(f32[1,2,4,128]{3,1,2,0:T(2,128)S(1)} %copy.125) | copy-start | bytes 12292
  19.5 44.1 %copy-start.43 = (f32[384]{0:T(512)}, f32[384]{0:T(512)S(1)}, u32[]{:S(2)}) copy-start(f32[384]{0:T(512)S(1)} %broadcast_multiply_fusion.1) | copy-start | bytes 4612
  19.9 43.8 %copy-start.50 = (f32[384]{0:T(512)}, f32[384]{0:T(512)S(1)}, u32[]{:S(2)}) copy-start(f32[384]{0:T(512)S(1)} %fusion.62) | copy-start | bytes 4612
  19.9 43.8 %copy-start.45 = (f32[384]{0:T(512)}, f32[384]{0:T(512)S(1)}, u32[]{:S(2)}) copy-start(f32[384]{0:T(512)S(1)} %fusion.111) | copy-start | bytes 4612
  20.5 122.2 %copy-start.64 = (f32[1,2,4,128]{3,1,2,0:T(2,128)}, f32[1,2,4,128]{3,1,2,0:T(2,128)S(1)}, u32[]{:S(2)}) copy-start(f32[1,2,4,128]{3,1,2,0:T(2,128)S(1)} %copy.131) | copy-start | bytes 12292
  20.5 211.7 %copy-start.58 = (f32[1,2,4,128]{3,1,2,0:T(2,128)}, f32[1,2,4,128]{3,1,2,0:T(2,128)S(1)}, u32[]{:S(2)}) copy-start(f32[1,2,4,128]{3,1,2,0:T(2,128)S(1)} %copy.130) | copy-start | bytes 12292
  94.1 59.1 %copy-start.6 = (f32[384,1024]{1,0:T(8,128)}, f32[384,1024]{1,0:T(8,128)S(1)}, u32[]{:S(2)}) copy-start(f32[384,1024]{1,0:T(8,128)S(1)} %get-tuple-element.606) | copy-start | bytes 4718596
  94.1 138.0 %copy-start.48 = (f32[384]{0:T(512)}, f32[384]{0:T(512)S(1)}, u32[]{:S(2)}) copy-start(f32[384]{0:T(512)S(1)} %broadcast_multiply_fusion) | copy-start | bytes 4612
  94.5 137.7 %copy-start.62 = (f32[384]{0:T(512)}, f32[384]{0:T(512)S(1)}, u32[]{:S(2)}) copy-start(f32[384]{0:T(512)S(1)} %fusion.112) | copy-start | bytes 4612
  174.7 7.9 %collective-permute-start = (bf16[2048,1024]{1,0:T(8,128)(2,1)}, bf16[2048,1024]{1,0:T(8,128)(2,1)}, u32[]{:S(2)}, u32[]{:S(2)}) collective-permute-start(bf16[2048,1024]{1,0:T(8,128)(2,1)} %fusion.26), channel_id=1, source_target_pairs={{0,1},{1,0},{2,3},{3,2},{4,5},{5,4},{6,7},{7,6},{8,9},{9,8},{10,11... | collective-permute-start | bytes 12582920 | tf_op jit(solution)/shard_map/ppermute | solution.py:155
  175.8 26.6 %copy-start.18 = (bf16[1,384,1024]{2,1,0:T(8,128)(2,1)S(1)}, bf16[1,384,1024]{2,1,0:T(8,128)(2,1)}, u32[]{:S(2)}) copy-start(bf16[1,384,1024]{2,1,0:T(8,128)(2,1)} %param.22) | copy-start | bytes 2359300
  239.1 6.6 copy-start.78
  252.7 6.7 copy-start.41
  252.7 6.7 copy-start.78
  266.4 6.7 copy-start.41
  266.4 6.7 copy-start.78
  280.1 6.7 copy-start.41
  280.1 6.7 copy-start.78
  302.4 7.3 %copy-start.1 = (f32[2,1536,1024]{2,1,0:T(8,128)}, f32[2,1536,1024]{2,1,0:T(8,128)S(1)}, u32[]{:S(2)}) copy-start(f32[2,1536,1024]{2,1,0:T(8,128)S(1)} %fusion.77) | copy-start | bytes 37748740
  304.6 29.1 %collective-permute-start.1 = (bf16[1536,1024]{1,0:T(8,128)(2,1)}, bf16[1536,1024]{1,0:T(8,128)(2,1)}, u32[]{:S(2)}, u32[]{:S(2)}) collective-permute-start(bf16[1536,1024]{1,0:T(8,128)(2,1)} %fusion.34), channel_id=1, source_target_pairs={{0,1},{1,0},{2,3},{3,2},{4,5},{5,4},{6,7},{7,6},{8,9},{9,8},{10,11... | collective-permute-start | bytes 9437192 | tf_op jit(solution)/shard_map/ppermute | solution.py:155
  304.8 7.0 %copy-start.8 = (f32[384,1024]{1,0:T(8,128)S(1)}, f32[384,1024]{1,0:T(8,128)}, u32[]{:S(2)}) copy-start(f32[384,1024]{1,0:T(8,128)} %copy-done.6) | copy-start | bytes 4718596
  304.9 7.0 %copy-start.32 = (bf16[384,1024]{1,0:T(8,128)(2,1)S(1)}, bf16[384,1024]{1,0:T(8,128)(2,1)}, u32[]{:S(2)}) copy-start(bf16[384,1024]{1,0:T(8,128)(2,1)} %get-tuple-element.563) | copy-start | bytes 2359300
  304.9 7.0 %copy-start.33 = (bf16[384,1024]{1,0:T(8,128)(2,1)S(1)}, bf16[384,1024]{1,0:T(8,128)(2,1)}, u32[]{:S(2)}) copy-start(bf16[384,1024]{1,0:T(8,128)(2,1)} %get-tuple-element.564) | copy-start | bytes 2359300
  304.9 7.0 %copy-start.34 = (bf16[384,1024]{1,0:T(8,128)(2,1)S(1)}, bf16[384,1024]{1,0:T(8,128)(2,1)}, u32[]{:S(2)}) copy-start(bf16[384,1024]{1,0:T(8,128)(2,1)} %get-tuple-element.565) | copy-start | bytes 2359300
  304.9 7.0 %copy-start.35 = (bf16[384,1024]{1,0:T(8,128)(2,1)S(1)}, bf16[384,1024]{1,0:T(8,128)(2,1)}, u32[]{:S(2)}) copy-start(bf16[384,1024]{1,0:T(8,128)(2,1)} %get-tuple-element.566) | copy-start | bytes 2359300
  304.9 7.0 %copy-start.49 = (f32[384]{0:T(512)S(1)}, f32[384]{0:T(512)}, u32[]{:S(2)}) copy-start(f32[384]{0:T(512)} %copy-done.48) | copy-start | bytes 4612
  304.9 7.0 %copy-start.59 = (f32[1,2,4,128]{3,1,2,0:T(2,128)S(1)}, f32[1,2,4,128]{3,1,2,0:T(2,128)}, u32[]{:S(2)}) copy-start(f32[1,2,4,128]{3,1,2,0:T(2,128)} %copy-done.58) | copy-start | bytes 12292
  304.9 7.0 %copy-start.63 = (f32[384]{0:T(512)S(1)}, f32[384]{0:T(512)}, u32[]{:S(2)}) copy-start(f32[384]{0:T(512)} %copy-done.62) | copy-start | bytes 4612
  304.9 7.0 %copy-start.65 = (f32[1,2,4,128]{3,1,2,0:T(2,128)S(1)}, f32[1,2,4,128]{3,1,2,0:T(2,128)}, u32[]{:S(2)}) copy-start(f32[1,2,4,128]{3,1,2,0:T(2,128)} %copy-done.64) | copy-start | bytes 12292
  328.6 24.3 %collective-permute-start.20 = (bf16[2560,1024]{1,0:T(8,128)(2,1)}, bf16[2560,1024]{1,0:T(8,128)(2,1)}, u32[]{:S(2)}, u32[]{:S(2)}) collective-permute-start(bf16[2560,1024]{1,0:T(8,128)(2,1)} %pad_maximum_fusion), channel_id=1, source_target_pairs={{0,1},{1,0},{2,3},{3,2},{4,5},{5,4},{6,7},{7,6},{8,9},{9,8},{10,11... | collective-permute-start | bytes 15728648 | tf_op jit(solution)/shard_map/ppermute | solution.py:155
  332.9 48.8 %collective-permute-start.19 = (bf16[1024,1024]{1,0:T(8,128)(2,1)}, bf16[1024,1024]{1,0:T(8,128)(2,1)}, u32[]{:S(2)}, u32[]{:S(2)}) collective-permute-start(bf16[1024,1024]{1,0:T(8,128)(2,1)} %fusion.48), channel_id=1, source_target_pairs={{0,2},{1,3},{2,0},{3,1},{4,6},{5,7},{6,4},{7,5},{8,10},{9,11},{10,... | collective-permute-start | bytes 6291464 | tf_op jit(solution)/shard_map/ppermute | solution.py:155
  333.3 8.6 %slice-start.2 = ((s8[6291456]{0:T(1024)(128)(4,1)}), s8[4194304]{0:T(1024)(128)(4,1)S(1)}, s32[]{:S(2)}) async-start(s8[6291456]{0:T(1024)(128)(4,1)} %bitcast.419), calls=%async_computation.8 | async-start | bytes 8388608
  333.7 8.2 %copy-start.28 = (bf16[384,3072]{0,1:T(8,128)(2,1)S(1)}, bf16[384,3072]{0,1:T(8,128)(2,1)}, u32[]{:S(2)}) copy-start(bf16[384,3072]{0,1:T(8,128)(2,1)} %get-tuple-element.294) | copy-start | bytes 7077892
  333.7 8.2 %slice-start.3 = ((s8[6291456]{0:T(1024)(128)(4,1)}), s8[2097152]{0:T(1024)(128)(4,1)S(1)}, s32[]{:S(2)}) async-start(s8[6291456]{0:T(1024)(128)(4,1)} %bitcast.419), calls=%async_computation.9 | async-start | bytes 4194304
  347.2 5.2 collective-permute-start.3
  350.8 65.0 %collective-permute-start.2 = (bf16[768,1024]{1,0:T(8,128)(2,1)}, bf16[768,1024]{1,0:T(8,128)(2,1)}, u32[]{:S(2)}, u32[]{:S(2)}) collective-permute-start(bf16[768,1024]{1,0:T(8,128)(2,1)} %fusion.68), channel_id=1, source_target_pairs={{0,2},{1,3},{2,0},{3,1},{4,6},{5,7},{6,4},{7,5},{8,10},{9,11},{10,... | collective-permute-start | bytes 4718600 | tf_op jit(solution)/shard_map/ppermute | solution.py:155
  352.5 63.2 %collective-permute-start.4 = (bf16[8,1024]{1,0:T(8,128)(2,1)S(1)}, bf16[8,1024]{1,0:T(8,128)(2,1)S(1)}, u32[]{:S(2)}, u32[]{:S(2)}) collective-permute-start(bf16[8,1024]{1,0:T(8,128)(2,1)S(1)} %fusion.110), channel_id=1, source_target_pairs={{0,2},{1,3},{2,0},{3,1},{4,6},{5,7},{6,4},{7,5},{8,10},{9,11},{10,... | collective-permute-start | bytes 49160 | tf_op jit(solution)/shard_map/ppermute | solution.py:155
  352.9 28.9 %slice-start = ((s8[8388608]{0:T(1024)(128)(4,1)}), s8[4194304]{0:T(1024)(128)(4,1)S(1)}, s32[]{:S(2)}) async-start(s8[8388608]{0:T(1024)(128)(4,1)} %bitcast.364), calls=%async_computation.6 | async-start | bytes 8388608
  356.0 25.8 %slice-start.1 = ((s8[8388608]{0:T(1024)(128)(4,1)}), s8[4194304]{0:T(1024)(128)(4,1)S(1)}, s32[]{:S(2)}) async-start(s8[8388608]{0:T(1024)(128)(4,1)} %bitcast.364), calls=%async_computation.7 | async-start | bytes 8388608
  370.5 151.2 %collective-permute-start.21 = (bf16[1280,1024]{1,0:T(8,128)(2,1)}, bf16[1280,1024]{1,0:T(8,128)(2,1)}, u32[]{:S(2)}, u32[]{:S(2)}) collective-permute-start(bf16[1280,1024]{1,0:T(8,128)(2,1)} %pad_maximum_fusion.2), channel_id=1, source_target_pairs={{0,2},{1,3},{2,0},{3,1},{4,6},{5,7},{6,4},{7,5},{8,10},{9,11},{10,... | collective-permute-start | bytes 7864328 | tf_op jit(solution)/shard_map/ppermute | solution.py:155
  385.5 292.4 %all-reduce.7.cloned.1.call-start = ((), (), s32[]{:S(2)}) async-start(), calls=%async_computation.5 | async-start | bytes 5242880 | tf_op jit(solution)/shard_map/psum | solution.py:284
  424.9 8.5 %copy-start.24 = (bf16[384,4096]{1,0:T(8,128)(2,1)S(1)}, bf16[384,4096]{1,0:T(8,128)(2,1)}, u32[]{:S(2)}) copy-start(bf16[384,4096]{1,0:T(8,128)(2,1)} %copy-done.23) | copy-start | bytes 9437188
  428.2 15.3 %collective-permute-start.11 = (bf16[97,1024]{1,0:T(8,128)(2,1)S(1)}, bf16[97,1024]{1,0:T(8,128)(2,1)S(1)}, u32[]{:S(2)}, u32[]{:S(2)}) collective-permute-start(bf16[97,1024]{1,0:T(8,128)(2,1)S(1)} %get-tuple-element.574), channel_id=1, source_target_pairs={{0,28},{4,24},{8,20},{12,16},{16,12},{20,8},{24,4},{28,0},{1,29},{... | collective-permute-start | bytes 595976 | tf_op jit(solution)/shard_map/ppermute | solution.py:171
  432.3 26.5 %collective-permute-start.10 = (bf16[97,1024]{1,0:T(8,128)(2,1)S(1)}, bf16[97,1024]{1,0:T(8,128)(2,1)S(1)}, u32[]{:S(2)}, u32[]{:S(2)}) collective-permute-start(bf16[97,1024]{1,0:T(8,128)(2,1)S(1)} %get-tuple-element.575), channel_id=1, source_target_pairs={{0,24},{4,28},{8,16},{12,20},{16,8},{20,12},{24,0},{28,4},{1,25},{... | collective-permute-start | bytes 595976 | tf_op jit(solution)/shard_map/ppermute | solution.py:171
  432.8 36.1 %collective-permute-start.9 = (bf16[97,1024]{1,0:T(8,128)(2,1)S(1)}, bf16[97,1024]{1,0:T(8,128)(2,1)S(1)}, u32[]{:S(2)}, u32[]{:S(2)}) collective-permute-start(bf16[97,1024]{1,0:T(8,128)(2,1)S(1)} %get-tuple-element.576), channel_id=1, source_target_pairs={{0,20},{4,16},{8,28},{12,24},{16,4},{20,0},{24,12},{28,8},{1,21},{... | collective-permute-start | bytes 595976 | tf_op jit(solution)/shard_map/ppermute | solution.py:171
  441.1 75.7 %collective-permute-start.8 = (bf16[97,1024]{1,0:T(8,128)(2,1)}, bf16[97,1024]{1,0:T(8,128)(2,1)S(1)}, u32[]{:S(2)}, u32[]{:S(2)}) collective-permute-start(bf16[97,1024]{1,0:T(8,128)(2,1)} %get-tuple-element.577), channel_id=1, source_target_pairs={{0,16},{4,20},{8,24},{12,28},{16,0},{20,4},{24,8},{28,12},{1,17},{... | collective-permute-start | bytes 595976 | tf_op jit(solution)/shard_map/ppermute | solution.py:171
  443.6 73.3 %collective-permute-start.7 = (bf16[97,1024]{1,0:T(8,128)(2,1)}, bf16[97,1024]{1,0:T(8,128)(2,1)S(1)}, u32[]{:S(2)}, u32[]{:S(2)}) collective-permute-start(bf16[97,1024]{1,0:T(8,128)(2,1)} %get-tuple-element.578), channel_id=1, source_target_pairs={{0,12},{4,8},{8,4},{12,0},{16,28},{20,24},{24,20},{28,16},{1,13},{... | collective-permute-start | bytes 595976 | tf_op jit(solution)/shard_map/ppermute | solution.py:171
  458.8 58.1 %collective-permute-start.6 = (bf16[97,1024]{1,0:T(8,128)(2,1)S(1)}, bf16[97,1024]{1,0:T(8,128)(2,1)S(1)}, u32[]{:S(2)}, u32[]{:S(2)}) collective-permute-start(bf16[97,1024]{1,0:T(8,128)(2,1)S(1)} %get-tuple-element.579), channel_id=1, source_target_pairs={{0,8},{4,12},{8,0},{12,4},{16,24},{20,28},{24,16},{28,20},{1,9},{5... | collective-permute-start | bytes 595976 | tf_op jit(solution)/shard_map/ppermute | solution.py:171
  469.0 47.9 %collective-permute-start.5 = (bf16[97,1024]{1,0:T(8,128)(2,1)S(1)}, bf16[97,1024]{1,0:T(8,128)(2,1)S(1)}, u32[]{:S(2)}, u32[]{:S(2)}) collective-permute-start(bf16[97,1024]{1,0:T(8,128)(2,1)S(1)} %get-tuple-element.573), channel_id=1, source_target_pairs={{0,4},{4,0},{8,12},{12,8},{16,20},{20,16},{24,28},{28,24},{1,5},{5... | collective-permute-start | bytes 595976 | tf_op jit(solution)/shard_map/ppermute | solution.py:171
  520.3 23.0 %collective-permute-start.12 = (bf16[97,1024]{1,0:T(8,128)(2,1)S(1)}, bf16[97,1024]{1,0:T(8,128)(2,1)}, u32[]{:S(2)}, u32[]{:S(2)}) collective-permute-start(bf16[97,1024]{1,0:T(8,128)(2,1)S(1)} %get-tuple-element.548), channel_id=1, source_target_pairs={{0,4},{4,0},{8,12},{12,8},{16,20},{20,16},{24,28},{28,24},{1,5},{5... | collective-permute-start | bytes 595976 | tf_op jit(solution)/shard_map/ppermute | solution.py:177
  537.4 27.2 %collective-permute-start.13 = (bf16[97,1024]{1,0:T(8,128)(2,1)S(1)}, bf16[97,1024]{1,0:T(8,128)(2,1)S(1)}, u32[]{:S(2)}, u32[]{:S(2)}) collective-permute-start(bf16[97,1024]{1,0:T(8,128)(2,1)S(1)} %get-tuple-element.548), channel_id=1, source_target_pairs={{0,8},{4,12},{8,0},{12,4},{16,24},{20,28},{24,16},{28,20},{1,9},{5... | collective-permute-start | bytes 595976 | tf_op jit(solution)/shard_map/ppermute | solution.py:177
  538.6 37.0 %collective-permute-start.14 = (bf16[97,1024]{1,0:T(8,128)(2,1)S(1)}, bf16[97,1024]{1,0:T(8,128)(2,1)S(1)}, u32[]{:S(2)}, u32[]{:S(2)}) collective-permute-start(bf16[97,1024]{1,0:T(8,128)(2,1)S(1)} %get-tuple-element.548), channel_id=1, source_target_pairs={{0,12},{4,8},{8,4},{12,0},{16,28},{20,24},{24,20},{28,16},{1,13},{... | collective-permute-start | bytes 595976 | tf_op jit(solution)/shard_map/ppermute | solution.py:177
  539.5 36.8 %collective-permute-start.15 = (bf16[97,1024]{1,0:T(8,128)(2,1)S(1)}, bf16[97,1024]{1,0:T(8,128)(2,1)S(1)}, u32[]{:S(2)}, u32[]{:S(2)}) collective-permute-start(bf16[97,1024]{1,0:T(8,128)(2,1)S(1)} %get-tuple-element.548), channel_id=1, source_target_pairs={{0,16},{4,20},{8,24},{12,28},{16,0},{20,4},{24,8},{28,12},{1,17},{... | collective-permute-start | bytes 595976 | tf_op jit(solution)/shard_map/ppermute | solution.py:177
  541.2 50.6 %collective-permute-start.16 = (bf16[97,1024]{1,0:T(8,128)(2,1)S(1)}, bf16[97,1024]{1,0:T(8,128)(2,1)S(1)}, u32[]{:S(2)}, u32[]{:S(2)}) collective-permute-start(bf16[97,1024]{1,0:T(8,128)(2,1)S(1)} %get-tuple-element.548), channel_id=1, source_target_pairs={{0,20},{4,16},{8,28},{12,24},{16,4},{20,0},{24,12},{28,8},{1,21},{... | collective-permute-start | bytes 595976 | tf_op jit(solution)/shard_map/ppermute | solution.py:177
  543.3 49.2 %collective-permute-start.17 = (bf16[97,1024]{1,0:T(8,128)(2,1)S(1)}, bf16[97,1024]{1,0:T(8,128)(2,1)S(1)}, u32[]{:S(2)}, u32[]{:S(2)}) collective-permute-start(bf16[97,1024]{1,0:T(8,128)(2,1)S(1)} %get-tuple-element.548), channel_id=1, source_target_pairs={{0,24},{4,28},{8,16},{12,20},{16,8},{20,12},{24,0},{28,4},{1,25},{... | collective-permute-start | bytes 595976 | tf_op jit(solution)/shard_map/ppermute | solution.py:177
  564.7 30.8 %collective-permute-start.18 = (bf16[97,1024]{1,0:T(8,128)(2,1)S(1)}, bf16[97,1024]{1,0:T(8,128)(2,1)S(1)}, u32[]{:S(2)}, u32[]{:S(2)}) collective-permute-start(bf16[97,1024]{1,0:T(8,128)(2,1)S(1)} %get-tuple-element.548), channel_id=1, source_target_pairs={{0,28},{4,24},{8,20},{12,16},{16,12},{20,8},{24,4},{28,0},{1,29},{... | collective-permute-start | bytes 595976 | tf_op jit(solution)/shard_map/ppermute | solution.py:177
  (66 other events, 176.4 us)
Sparse Core Ops, SparseCore 0:
  9.6 49.1 all-gather.5
  60.3 22.5 all-gather.7
  84.4 58.2 all-gather.9
  144.1 58.2 all-gather.11
  385.6 127.1 all-reduce.4
  533.0 144.8 all-reduce.6

commit v14 on v13

--- a/solution.py
+++ b/solution.py
@@ -164,11 +164,10 @@
     index = lax.axis_index(axis)
     chunks = buf.reshape(size, buf.shape[0] // size, *buf.shape[1:])
     total = lax.dynamic_index_in_dim(chunks, index, 0, keepdims=False)
-    low_chunks = chunks.astype(jnp.bfloat16)
     for shift in range(1, size):
         partner = lax.bitwise_xor(index, shift)
-        send = lax.dynamic_index_in_dim(low_chunks, partner, 0, keepdims=False)
-        got = lax.ppermute(send, axis, [(a, a ^ shift) for a in range(size)])
+        send = lax.dynamic_index_in_dim(chunks, partner, 0, keepdims=False)
+        got = lax.ppermute(send.astype(jnp.bfloat16), axis, [(a, a ^ shift) for a in range(size)])
         total = total + got.astype(jnp.float32)
     mine = total.astype(jnp.bfloat16)
     result = jnp.zeros((size, *mine.shape), jnp.bfloat16)
@@ -293,7 +292,6 @@
     qkv_rows = grad_qkv_t.shape[0] // shard_count
     qkv_half = halving([grad_qkv_t], "shard", shard_count, shard_steps[:1])
     qkv_half, grad_proj = lax.optimization_barrier((qkv_half, grad_proj))
-    (qkv_own,) = halving(qkv_half, "shard", shard_count, shard_steps[1:])
     grad_qb = jnp.sum(grad_q.astype(jnp.float32), 0)
     grad_vb = jnp.sum(grad_v.astype(jnp.float32), 0)
     grad_normed = jnp.einsum("tc,ic->ti", grad_proj, back_qkv, preferred_element_type=jnp.float32)
@@ -306,7 +304,8 @@
     pad_to = small_rows.shape[1] + (-small_rows.shape[1] % reps)
     small_rows = jnp.pad(small_rows, ((0, 0), (0, pad_to - small_rows.shape[1]), (0, 0)))
     small_rows = jnp.concatenate([small_rows[k] for k in order], 0)
-    (small_own,) = halving([small_rows], "shard", shard_count, shard_steps)
+    small_half = halving([small_rows], "shard", shard_count, shard_steps[:1])
+    qkv_own, small_own = halving(qkv_half + small_half, "shard", shard_count, shard_steps[1:])
     total_b = direct_reduce(jnp.concatenate([qkv_own, small_own], 0), "rep", reps)
     total_s = total_b[qkv_rows:]
     total_b = total_b[:qkv_rows]

time: 696 us -> 696 us (level)
    ppermute x8 -> x7, waiting for transfers between devices: 46.3 us -> 48.6 us  [halving(): lax.ppermute(jnp.concatenate(sends, 0), axis, [(a, a ^ step) for a in ran...]
    unnamed x190 -> x188, local copies, waits for them, and re-layouts: 27.8 us -> 26.4 us
  transfers between devices with their start and end apart: 28 -> 27, of which waited for: 13 -> 13; matrix products, arithmetic and copies ran while one was open for 26% -> 27% of each run, Pallas kernels for 0% -> 0%
where the time goes in v14:
time: 696 us; the launch traced here: 691 us
  waiting for transfers between devices  312 us (45%)
  local copies, waits for them, and re-layouts  108 us (16%)
  matrix products  96.6 us (14%)
  other arithmetic  90.8 us (13%)
  starting transfers between devices  41.7 us (6%)
  loops' own time  18.9 us (3%)
  between operations  15.9 us (2%)
    psum x1, waiting for transfers between devices, body_inner(): total_a = lax.psum(joined_a, 'rep')  73.1 us
    ppermute x7, waiting for transfers between devices, halving(): lax.ppermute(jnp.concatenate(sends, 0), axis, [(a, a ^ step) for a in ran...  48.6 us
    all_gather x1, waiting for transfers between devices, body_inner(): full_up = lax.all_gather(w_up, 'shard', axis=1, tiled=True)  48.2 us
    ppermute x7, waiting for transfers between devices, direct_reduce(): got = lax.ppermute(mine, axis, [(a, a ^ shift) for a in range(size)])  43.9 us
    psum x1, waiting for transfers between devices, body_inner(): total_a1 = lax.psum(down_own.astype(jnp.bfloat16), 'rep')  41.8 us
    all_gather x1, waiting for transfers between devices, body_inner(): full_qkv = lax.all_gather(w_qkv, 'shard', axis=1, tiled=True)  38.1 us
    add x6, other arithmetic, halving(): arrays.append(keep + got[offset:offset + keep.shape[0]].astype(jnp.float32))  34.8 us
    ppermute x7, starting transfers between devices, direct_reduce(): lax.ppermute(send.astype(jnp.bfloat16), axis, [(a, a ^ shift) for a in ra...  27.5 us
  transfers between devices with their start and end apart: 27, of which 13 were waited for; matrix products, arithmetic and copies ran while one was open for 27% of the time, Pallas kernels for 0%

profile of v14, /device:TPU:0, one launch (start us, length us, event | category | flops | bytes accessed | tf_op | source)
XLA Modules:
  0.0 691.2 jit_solution(11439496532126303739)
XLA Ops:
  12.2 6.5 all-gather
  20.6 38.1 %all-gather.6.cloned.1.call-done = bf16[1024,3072]{1,0:T(8,128)(2,1)} async-done(((bf16[1024,768]{1,0:T(8,128)(2,1)}), bf16[1024,3072]{1,0:T(8,128)(2,1)}) %all-gather.6.cloned.1.call-update) | async-done | bytes 6291472 | tf_op jit(solution)/shard_map/all_gather | solution.py:214
  58.7 4.9 fusion.79
  68.3 21.3 %while.32 = (s32[]{:T(128)}, bf16[4,384,256]{1,2,0:T(8,128)(2,1)}, f32[4,4,384]{2,1,0:T(4,128)}, s32[4]{0:T(128)S(1)}, bf16[384,1024]{0,1:T(8,128)(2,1)S(1)}, /*...) while((s32[]{:T(128)}, bf16[4,384,256]{1,2,0:T(8,128)(2,1)}, ...), condition=%wide.region_6.7_spmd.clone, body=%wide.region_3.6_spmd.clone.sunk | while | flops 157776416 | bytes 10964623 | solution.py:74
  90.8 3.3 fusion.132
  94.4 48.2 %all-gather.10.cloned.1.call-done = bf16[1024,4096]{1,0:T(8,128)(2,1)} async-done(((bf16[1024,1024]{1,0:T(8,128)(2,1)}), bf16[1024,4096]{1,0:T(8,128)(2,1)}) %all-gather.10.cloned.1.call-update) | async-done | bytes 8388624 | tf_op jit(solution)/shard_map/all_gather | solution.py:216
  142.7 10.6 %multiply_convert_fusion.1 = (bf16[384,4096]{1,0:T(8,128)(2,1)S(1)}, f32[384,4096]{1,0:T(8,128)}) fusion(f32[4096]{0:T(1024)S(1)} %bitcast.408, bf16[1024,4096]{1,0:T(8,128)(2,1)} %all-gather.10.cloned.1.call-done, f32[384,1024]{1,0:T(8,128)S(1)} %get-tuple-element.606, f32[1024]{0:T(1024)S(1)} %bitcast.415, f32[1024]{0:T(1024)S(1)} %bitcast.409, ...), kind=kOutput, calls=%fused_computation.62 | convolution fusion | flops 3238920192 | bytes 19426304 | tf_op jit(solution)/shard_map/dot_general | solution.py:236
  156.7 3.8 copy.119
  160.5 5.7 fusion.89
  166.2 5.8 copy-done
  172.0 2.7 fusion.26
  175.8 6.7 collective-permute-done
  182.6 10.3 %bitcast_add_fusion.1 = f32[2048,1024]{1,0:T(8,128)} fusion(bf16[2048,1024]{1,0:T(8,128)(2,1)} %collective-permute-done, f32[2,2048,1024]{2,1,0:T(8,128)} %copy-done, s32[]{:T(128)S(6)} %select_n.143), kind=kLoop, calls=%fused_computation.40 | loop fusion | flops 4194304 | bytes 20971524 | tf_op jit(solution)/shard_map/add | solution.py:158
  192.8 9.6 %all-gather.12.cloned.1.call-done = bf16[4096,1024]{1,0:T(8,128)(2,1)} async-done(((bf16[1024,1024]{1,0:T(8,128)(2,1)}), bf16[4096,1024]{1,0:T(8,128)(2,1)}) %all-gather.12.cloned.1.call-update) | async-done | bytes 8388624 | tf_op jit(solution)/shard_map/all_gather | solution.py:217
  202.4 10.8 %convert_reduce_fusion = (f32[4096]{0:T(1024)}, bf16[384,4096]{1,0:T(8,128)(2,1)S(1)}) fusion(f32[384,4096]{1,0:T(8,128)} %get-tuple-element.608, bf16[4096,1024]{1,0:T(8,128)(2,1)} %all-gather.12.cloned.1.call-done, bf16[1,384,1024]{2,1,0:T(8,128)(2,1)S(1)} %copy-done.18), kind=kOutput, calls=%fused_computation.60 | convolution fusion | flops 3255824384 | bytes 18628608 | tf_op jit(solution)/shard_map/to,fo->tf/dot_general | solution.py:258
  213.2 1.8 fusion.128
  215.6 16.5 %multiply_reduce_fusion.1 = (f32[1024]{0:T(1024)}, f32[384]{0:T(512)S(1)}, f32[1024]{0:T(1024)}, f32[384,1024]{1,0:T(8,128)S(1)}) fusion(f32[384,1024]{1,0:T(8,128)S(1)} %copy-done.7, f32[384]{0:T(512)S(1)} %fusion.119, f32[384]{0:T(512)S(1)} %broadcast_multiply_fusion, f32[1024]{0:T(1024)S(1)} %bitcast.410, bf16[384,4096]{1,0:T(8,128)(2,1)S(1)} %get-tuple-element.612, ...), kind=kOutput, calls=%fused_computation.138 | convolution fusion | flops 3224368640 | bytes 14696960 | tf_op jit(solution)/shard_map/tf,if->ti/dot_general | solution.py:267
  239.1 54.7 %while.33 = (s32[]{:T(128)}, bf16[4,384,256]{1,2,0:T(8,128)(2,1)}, bf16[4,384,256]{1,2,0:T(8,128)(2,1)}, bf16[4,384,256]{1,2,0:T(8,128)(2,1)}, s32[4]{0:T(128)S(...) while((s32[]{:T(128)}, bf16[4,384,256]{1,2,0:T(8,128)(2,1)}, ...), condition=%wide.region_13.14_spmd.clone, body=%wide.region_11.13_spmd.clone.sunk | while | flops 385251872 | bytes 30610428 | solution.py:113
  296.3 2.4 pad_maximum_fusion.4
  298.7 3.6 fusion.77
  302.4 2.2 fusion.34
  306.2 3.5 copy-done.1
  309.6 2.0 copy-done.4
  311.9 9.6 %fusion.35 = f32[4096,1024]{1,0:T(8,128)} fusion(bf16[384,1024]{1,0:T(8,128)(2,1)S(1)} %copy-done.32, bf16[384,1024]{1,0:T(8,128)(2,1)S(1)} %copy-done.33, bf16[384,1024]{1,0:T(8,128)(2,1)S(1)} %copy-done.34, bf16[384,1024]{1,0:T(8,128)(2,1)S(1)} %copy-done.31, f32[384,1024]{1,0:T(8,128)S(1)} %copy-done.8, f32[1024]{0:T(1024)S(1)} %bitcast.416, ...), kind=kOutput, calls=%fused_computation.82 | convolution fusion | flops 3235774464 | bytes 21507072 | tf_op jit(solution)/shard_map/tf,ti->fi/dot_general | solution.py:264
  321.5 4.0 fusion.27
  325.7 2.9 pad_maximum_fusion
  328.9 4.0 fusion.48
  333.6 8.2 %bitcast_add_fusion.2 = f32[1536,1024]{1,0:T(8,128)} fusion(bf16[1536,1024]{1,0:T(8,128)(2,1)} %collective-permute-done.1, f32[2,1536,1024]{2,1,0:T(8,128)} %copy-done.1, s32[]{:T(128)S(6)} %select_n.143), kind=kLoop, calls=%fused_computation.54 | loop fusion | flops 3145728 | bytes 15728644 | tf_op jit(solution)/shard_map/add | solution.py:158
  341.9 2.9 fusion.123
  347.2 2.3 fusion.68
  352.6 1.8 bitcast_add_fusion.6
  354.5 10.8 %bitcast_add_fusion = f32[2048,1024]{1,0:T(8,128)} fusion(f32[2,2048,1024]{2,1,0:T(8,128)} %bitcast.380, s32[]{:T(128)S(6)} %select_n.143, bf16[2560,1024]{1,0:T(8,128)(2,1)} %collective-permute-done.19), kind=kLoop, calls=%fused_computation.39 | loop fusion | flops 4194304 | bytes 20971524 | tf_op jit(solution)/shard_map/add | solution.py:158
  365.3 2.5 fusion.49
  369.9 11.8 %collective-permute-done.18 = bf16[1024,1024]{1,0:T(8,128)(2,1)} collective-permute-done((bf16[1024,1024]{1,0:T(8,128)(2,1)}, bf16[1024,1024]{1,0:T(8,128)(2,1)}, u32[]{:S(2)}, u32[]{:S(2)}) %collective-permute-start.18) | collective-permute-done | bytes 2097184 | tf_op jit(solution)/shard_map/ppermute | solution.py:155
  381.7 3.7 fusion.29
  385.7 30.0 %collective-permute-done.3 = bf16[776,1024]{1,0:T(8,128)(2,1)} collective-permute-done((bf16[776,1024]{1,0:T(8,128)(2,1)}, bf16[776,1024]{1,0:T(8,128)(2,1)}, u32[]{:S(2)}, u32[]{:S(2)}) %collective-permute-start.3) | collective-permute-done | bytes 1589280 | tf_op jit(solution)/shard_map/ppermute | solution.py:155
  416.5 2.9 bitcast_add_fusion.5
  419.4 2.0 pad_maximum_fusion.1
  421.5 4.1 reshape.437
  425.6 2.8 fusion.108
  428.4 4.3 collective-permute-start.10
  433.8 8.7 %fusion.71 = bf16[1,384,1024]{2,1,0:T(8,128)(2,1)} fusion(f32[384,1024]{1,0:T(8,128)S(1)} %copy-done.8, bf16[384,4096]{1,0:T(8,128)(2,1)} %copy-done.23, bf16[4096,1024]{1,0:T(8,128)(2,1)} %all-gather.12.cloned.1.call-done, f32[1024]{0:T(1024)S(1)} %bitcast.417), kind=kOutput, calls=%fused_computation.148 | convolution fusion | flops 3222405120 | bytes 13897728 | tf_op jit(solution)/shard_map/dot_general | solution.py:249
  442.5 2.2 collective-permute-start.7
  444.7 14.2 %collective-permute-start.6 = (bf16[97,1024]{1,0:T(8,128)(2,1)}, bf16[97,1024]{1,0:T(8,128)(2,1)S(1)}, u32[]{:S(2)}, u32[]{:S(2)}) collective-permute-start(bf16[97,1024]{1,0:T(8,128)(2,1)} %get-tuple-element.568), channel_id=1, source_target_pairs={{0,12},{4,8},{8,4},{12,0},{16,28},{20,24},{24,20},{28,16},{1,13},{... | collective-permute-start | bytes 595976 | tf_op jit(solution)/shard_map/ppermute | solution.py:170
  458.9 3.7 collective-permute-start.5
  462.6 6.4 collective-permute-done.8
  469.0 2.0 collective-permute-start.4
  470.9 41.8 %all-reduce.5.cloned.1.call-done = bf16[1024,1024]{1,0:T(8,128)(2,1)} async-done(((bf16[1024,1024]{1,0:T(8,128)(2,1)}), bf16[1024,1024]{1,0:T(8,128)(2,1)}) %all-reduce.5.cloned.1.call-update) | async-done | bytes 2097168 | tf_op jit(solution)/shard_map/psum | solution.py:263
  512.7 4.1 convert_element_type.511
  518.3 2.0 bitcast_dynamic-update-slice_fusion.8
  521.7 5.0 fusion.50
  526.6 2.9 copy.112
  534.3 3.0 fusion.75
  541.1 2.1 collective-permute-start.15
  546.4 18.2 %collective-permute-done.12 = bf16[97,1024]{1,0:T(8,128)(2,1)S(1)} collective-permute-done((bf16[97,1024]{1,0:T(8,128)(2,1)S(1)}, bf16[97,1024]{1,0:T(8,128)(2,1)S(1)}, u32[]{:S(2)}, u32[]{:S(2)}) %collective-permute-start.12) | collective-permute-done | bytes 198688 | tf_op jit(solution)/shard_map/ppermute | solution.py:176
  566.8 8.6 %collective-permute-done.13 = bf16[97,1024]{1,0:T(8,128)(2,1)S(1)} collective-permute-done((bf16[97,1024]{1,0:T(8,128)(2,1)S(1)}, bf16[97,1024]{1,0:T(8,128)(2,1)S(1)}, u32[]{:S(2)}, u32[]{:S(2)}) %collective-permute-start.13) | collective-permute-done | bytes 198688 | tf_op jit(solution)/shard_map/ppermute | solution.py:176
  576.9 14.8 %collective-permute-done.15 = bf16[97,1024]{1,0:T(8,128)(2,1)S(1)} collective-permute-done((bf16[97,1024]{1,0:T(8,128)(2,1)S(1)}, bf16[97,1024]{1,0:T(8,128)(2,1)S(1)}, u32[]{:S(2)}, u32[]{:S(2)}) %collective-permute-start.15) | collective-permute-done | bytes 198688 | tf_op jit(solution)/shard_map/ppermute | solution.py:176
  593.1 2.3 collective-permute-done.17
  596.1 1.9 reshape.438
  599.2 1.8 convert_bitcast_fusion
  601.0 2.4 copy.113
  604.6 73.1 %all-reduce.7.cloned.1.call-done = bf16[1280,1024]{1,0:T(8,128)(2,1)} async-done(((bf16[1280,1024]{1,0:T(8,128)(2,1)}), bf16[1280,1024]{1,0:T(8,128)(2,1)}) %all-reduce.7.cloned.1.call-update) | async-done | bytes 2621456 | tf_op jit(solution)/shard_map/psum | solution.py:283
  677.7 2.1 slice_convert_fusion.2
  679.8 4.1 slice_convert_fusion
  (471 shorter events, 119.3 us)
Async XLA Ops:
  7.2 51.5 %all-gather.6.cloned.1.call-start = ((), (), s32[]{:S(2)}) async-start(), calls=%async_computation | async-start | bytes 7864320 | tf_op jit(solution)/shard_map/all_gather | solution.py:214
  8.0 81.6 %all-gather.8.cloned.1.call-start = ((), (), s32[]{:S(2)}) async-start(), calls=%async_computation.1 | async-start | bytes 2621440 | tf_op jit(solution)/shard_map/all_gather | solution.py:215
  8.8 10.6 %copy-start.2 = (bf16[1,384,1024]{2,1,0:T(8,128)(2,1)S(1)}, bf16[1,384,1024]{2,1,0:T(8,128)(2,1)}, u32[]{:S(2)}) copy-start(bf16[1,384,1024]{2,1,0:T(8,128)(2,1)} %param.20) | copy-start | bytes 2359300
  8.8 133.9 %all-gather.10.cloned.1.call-start = ((), (), s32[]{:S(2)}) async-start(), calls=%async_computation.2 | async-start | bytes 10485760 | tf_op jit(solution)/shard_map/all_gather | solution.py:216
  9.5 10.6 %copy-start.67 = (s32[1,2,64]{2,1,0:T(2,128)S(1)}, s32[1,2,64]{2,1,0:T(2,128)}, u32[]{:S(2)}) copy-start(s32[1,2,64]{2,1,0:T(2,128)} %param.21) | copy-start | bytes 1540
  9.5 192.9 %all-gather.12.cloned.1.call-start = ((), (), s32[]{:S(2)}) async-start(), calls=%async_computation.3 | async-start | bytes 10485760 | tf_op jit(solution)/shard_map/all_gather | solution.py:217
  10.1 502.6 %all-reduce.5.cloned.1.call-start = ((), (), s32[]{:S(2)}) async-start(), calls=%async_computation.4 | async-start | bytes 4194304 | tf_op jit(solution)/shard_map/psum | solution.py:263
  19.3 44.3 %copy-start.59 = (f32[1,2,4,128]{3,1,2,0:T(2,128)}, f32[1,2,4,128]{3,1,2,0:T(2,128)S(1)}, u32[]{:S(2)}) copy-start(f32[1,2,4,128]{3,1,2,0:T(2,128)S(1)} %copy.126) | copy-start | bytes 12292
  19.3 44.3 %copy-start.38 = (f32[1,2,4,128]{3,1,2,0:T(2,128)}, f32[1,2,4,128]{3,1,2,0:T(2,128)S(1)}, u32[]{:S(2)}) copy-start(f32[1,2,4,128]{3,1,2,0:T(2,128)S(1)} %copy.125) | copy-start | bytes 12292
  19.5 44.1 %copy-start.42 = (f32[384]{0:T(512)}, f32[384]{0:T(512)S(1)}, u32[]{:S(2)}) copy-start(f32[384]{0:T(512)S(1)} %broadcast_multiply_fusion.1) | copy-start | bytes 4612
  19.9 43.8 %copy-start.49 = (f32[384]{0:T(512)}, f32[384]{0:T(512)S(1)}, u32[]{:S(2)}) copy-start(f32[384]{0:T(512)S(1)} %fusion.62) | copy-start | bytes 4612
  19.9 43.8 %copy-start.44 = (f32[384]{0:T(512)}, f32[384]{0:T(512)S(1)}, u32[]{:S(2)}) copy-start(f32[384]{0:T(512)S(1)} %fusion.118) | copy-start | bytes 4612
  20.5 122.2 %copy-start.63 = (f32[1,2,4,128]{3,1,2,0:T(2,128)}, f32[1,2,4,128]{3,1,2,0:T(2,128)S(1)}, u32[]{:S(2)}) copy-start(f32[1,2,4,128]{3,1,2,0:T(2,128)S(1)} %copy.131) | copy-start | bytes 12292
  20.5 211.7 %copy-start.57 = (f32[1,2,4,128]{3,1,2,0:T(2,128)}, f32[1,2,4,128]{3,1,2,0:T(2,128)S(1)}, u32[]{:S(2)}) copy-start(f32[1,2,4,128]{3,1,2,0:T(2,128)S(1)} %copy.130) | copy-start | bytes 12292
  94.1 59.2 %copy-start.6 = (f32[384,1024]{1,0:T(8,128)}, f32[384,1024]{1,0:T(8,128)S(1)}, u32[]{:S(2)}) copy-start(f32[384,1024]{1,0:T(8,128)S(1)} %get-tuple-element.606) | copy-start | bytes 4718596
  94.1 138.0 %copy-start.47 = (f32[384]{0:T(512)}, f32[384]{0:T(512)S(1)}, u32[]{:S(2)}) copy-start(f32[384]{0:T(512)S(1)} %broadcast_multiply_fusion) | copy-start | bytes 4612
  94.4 137.7 %copy-start.61 = (f32[384]{0:T(512)}, f32[384]{0:T(512)S(1)}, u32[]{:S(2)}) copy-start(f32[384]{0:T(512)S(1)} %fusion.119) | copy-start | bytes 4612
  174.7 7.9 %collective-permute-start = (bf16[2048,1024]{1,0:T(8,128)(2,1)}, bf16[2048,1024]{1,0:T(8,128)(2,1)}, u32[]{:S(2)}, u32[]{:S(2)}) collective-permute-start(bf16[2048,1024]{1,0:T(8,128)(2,1)} %fusion.26), channel_id=1, source_target_pairs={{0,1},{1,0},{2,3},{3,2},{4,5},{5,4},{6,7},{7,6},{8,9},{9,8},{10,11... | collective-permute-start | bytes 12582920 | tf_op jit(solution)/shard_map/ppermute | solution.py:155
  175.8 26.6 %copy-start.18 = (bf16[1,384,1024]{2,1,0:T(8,128)(2,1)S(1)}, bf16[1,384,1024]{2,1,0:T(8,128)(2,1)}, u32[]{:S(2)}) copy-start(bf16[1,384,1024]{2,1,0:T(8,128)(2,1)} %param.22) | copy-start | bytes 2359300
  239.1 6.6 copy-start.40
  239.1 6.6 copy-start.77
  252.7 6.7 copy-start.40
  252.7 6.7 copy-start.77
  266.4 6.7 copy-start.40
  266.4 6.7 copy-start.77
  280.1 6.7 copy-start.40
  280.1 6.7 copy-start.77
  302.4 7.3 %copy-start.1 = (f32[2,1536,1024]{2,1,0:T(8,128)}, f32[2,1536,1024]{2,1,0:T(8,128)S(1)}, u32[]{:S(2)}) copy-start(f32[2,1536,1024]{2,1,0:T(8,128)S(1)} %fusion.77) | copy-start | bytes 37748740
  304.6 29.0 %collective-permute-start.1 = (bf16[1536,1024]{1,0:T(8,128)(2,1)}, bf16[1536,1024]{1,0:T(8,128)(2,1)}, u32[]{:S(2)}, u32[]{:S(2)}) collective-permute-start(bf16[1536,1024]{1,0:T(8,128)(2,1)} %fusion.34), channel_id=1, source_target_pairs={{0,1},{1,0},{2,3},{3,2},{4,5},{5,4},{6,7},{7,6},{8,9},{9,8},{10,11... | collective-permute-start | bytes 9437192 | tf_op jit(solution)/shard_map/ppermute | solution.py:155
  304.8 7.0 %copy-start.8 = (f32[384,1024]{1,0:T(8,128)S(1)}, f32[384,1024]{1,0:T(8,128)}, u32[]{:S(2)}) copy-start(f32[384,1024]{1,0:T(8,128)} %copy-done.6) | copy-start | bytes 4718596
  304.8 7.0 %copy-start.31 = (bf16[384,1024]{1,0:T(8,128)(2,1)S(1)}, bf16[384,1024]{1,0:T(8,128)(2,1)}, u32[]{:S(2)}) copy-start(bf16[384,1024]{1,0:T(8,128)(2,1)} %get-tuple-element.570) | copy-start | bytes 2359300
  304.9 7.0 %copy-start.32 = (bf16[384,1024]{1,0:T(8,128)(2,1)S(1)}, bf16[384,1024]{1,0:T(8,128)(2,1)}, u32[]{:S(2)}) copy-start(bf16[384,1024]{1,0:T(8,128)(2,1)} %get-tuple-element.571) | copy-start | bytes 2359300
  304.9 7.0 %copy-start.33 = (bf16[384,1024]{1,0:T(8,128)(2,1)S(1)}, bf16[384,1024]{1,0:T(8,128)(2,1)}, u32[]{:S(2)}) copy-start(bf16[384,1024]{1,0:T(8,128)(2,1)} %get-tuple-element.572) | copy-start | bytes 2359300
  304.9 7.0 %copy-start.34 = (bf16[384,1024]{1,0:T(8,128)(2,1)S(1)}, bf16[384,1024]{1,0:T(8,128)(2,1)}, u32[]{:S(2)}) copy-start(bf16[384,1024]{1,0:T(8,128)(2,1)} %get-tuple-element.573) | copy-start | bytes 2359300
  304.9 7.0 %copy-start.48 = (f32[384]{0:T(512)S(1)}, f32[384]{0:T(512)}, u32[]{:S(2)}) copy-start(f32[384]{0:T(512)} %copy-done.47) | copy-start | bytes 4612
  304.9 7.0 %copy-start.58 = (f32[1,2,4,128]{3,1,2,0:T(2,128)S(1)}, f32[1,2,4,128]{3,1,2,0:T(2,128)}, u32[]{:S(2)}) copy-start(f32[1,2,4,128]{3,1,2,0:T(2,128)} %copy-done.57) | copy-start | bytes 12292
  304.9 7.0 %copy-start.62 = (f32[384]{0:T(512)S(1)}, f32[384]{0:T(512)}, u32[]{:S(2)}) copy-start(f32[384]{0:T(512)} %copy-done.61) | copy-start | bytes 4612
  304.9 7.0 %copy-start.64 = (f32[1,2,4,128]{3,1,2,0:T(2,128)S(1)}, f32[1,2,4,128]{3,1,2,0:T(2,128)}, u32[]{:S(2)}) copy-start(f32[1,2,4,128]{3,1,2,0:T(2,128)} %copy-done.63) | copy-start | bytes 12292
  328.6 24.0 %collective-permute-start.19 = (bf16[2560,1024]{1,0:T(8,128)(2,1)}, bf16[2560,1024]{1,0:T(8,128)(2,1)}, u32[]{:S(2)}, u32[]{:S(2)}) collective-permute-start(bf16[2560,1024]{1,0:T(8,128)(2,1)} %pad_maximum_fusion), channel_id=1, source_target_pairs={{0,1},{1,0},{2,3},{3,2},{4,5},{5,4},{6,7},{7,6},{8,9},{9,8},{10,11... | collective-permute-start | bytes 15728648 | tf_op jit(solution)/shard_map/ppermute | solution.py:155
  332.9 48.8 %collective-permute-start.18 = (bf16[1024,1024]{1,0:T(8,128)(2,1)}, bf16[1024,1024]{1,0:T(8,128)(2,1)}, u32[]{:S(2)}, u32[]{:S(2)}) collective-permute-start(bf16[1024,1024]{1,0:T(8,128)(2,1)} %fusion.48), channel_id=1, source_target_pairs={{0,2},{1,3},{2,0},{3,1},{4,6},{5,7},{6,4},{7,5},{8,10},{9,11},{10,... | collective-permute-start | bytes 6291464 | tf_op jit(solution)/shard_map/ppermute | solution.py:155
  333.2 8.6 %slice-start.2 = ((s8[6291456]{0:T(1024)(128)(4,1)}), s8[4194304]{0:T(1024)(128)(4,1)S(1)}, s32[]{:S(2)}) async-start(s8[6291456]{0:T(1024)(128)(4,1)} %bitcast.419), calls=%async_computation.8 | async-start | bytes 8388608
  333.6 8.3 %copy-start.27 = (bf16[384,3072]{0,1:T(8,128)(2,1)S(1)}, bf16[384,3072]{0,1:T(8,128)(2,1)}, u32[]{:S(2)}) copy-start(bf16[384,3072]{0,1:T(8,128)(2,1)} %get-tuple-element.294) | copy-start | bytes 7077892
  333.6 8.2 %slice-start.3 = ((s8[6291456]{0:T(1024)(128)(4,1)}), s8[2097152]{0:T(1024)(128)(4,1)S(1)}, s32[]{:S(2)}) async-start(s8[6291456]{0:T(1024)(128)(4,1)} %bitcast.419), calls=%async_computation.9 | async-start | bytes 4194304
  347.1 2.4 collective-permute-start.2
  350.9 64.9 %collective-permute-start.3 = (bf16[776,1024]{1,0:T(8,128)(2,1)}, bf16[776,1024]{1,0:T(8,128)(2,1)}, u32[]{:S(2)}, u32[]{:S(2)}) collective-permute-start(bf16[776,1024]{1,0:T(8,128)(2,1)} %pad_maximum_fusion.5), channel_id=1, source_target_pairs={{0,2},{1,3},{2,0},{3,1},{4,6},{5,7},{6,4},{7,5},{8,10},{9,11},{10,... | collective-permute-start | bytes 4767752 | tf_op jit(solution)/shard_map/ppermute | solution.py:155
  352.6 29.2 %slice-start = ((s8[8388608]{0:T(1024)(128)(4,1)}), s8[4194304]{0:T(1024)(128)(4,1)S(1)}, s32[]{:S(2)}) async-start(s8[8388608]{0:T(1024)(128)(4,1)} %bitcast.364), calls=%async_computation.6 | async-start | bytes 8388608
  354.4 10.9 %copy-start.20 = (f32[512,1024]{1,0:T(8,128)}, f32[512,1024]{1,0:T(8,128)S(1)}, u32[]{:S(2)}) copy-start(f32[512,1024]{1,0:T(8,128)S(1)} %bitcast_add_fusion.6) | copy-start | bytes 6291460
  354.5 27.2 %slice-start.1 = ((s8[8388608]{0:T(1024)(128)(4,1)}), s8[4194304]{0:T(1024)(128)(4,1)S(1)}, s32[]{:S(2)}) async-start(s8[8388608]{0:T(1024)(128)(4,1)} %bitcast.364), calls=%async_computation.7 | async-start | bytes 8388608
  369.6 152.1 %collective-permute-start.20 = (bf16[1280,1024]{1,0:T(8,128)(2,1)}, bf16[1280,1024]{1,0:T(8,128)(2,1)}, u32[]{:S(2)}, u32[]{:S(2)}) collective-permute-start(bf16[1280,1024]{1,0:T(8,128)(2,1)} %pad_maximum_fusion.2), channel_id=1, source_target_pairs={{0,2},{1,3},{2,0},{3,1},{4,6},{5,7},{6,4},{7,5},{8,10},{9,11},{10,... | collective-permute-start | bytes 7864328 | tf_op jit(solution)/shard_map/ppermute | solution.py:155
  385.4 292.2 %all-reduce.7.cloned.1.call-start = ((), (), s32[]{:S(2)}) async-start(), calls=%async_computation.5 | async-start | bytes 5242880 | tf_op jit(solution)/shard_map/psum | solution.py:283
  428.4 16.3 %collective-permute-start.10 = (bf16[97,1024]{1,0:T(8,128)(2,1)S(1)}, bf16[97,1024]{1,0:T(8,128)(2,1)S(1)}, u32[]{:S(2)}, u32[]{:S(2)}) collective-permute-start(bf16[97,1024]{1,0:T(8,128)(2,1)S(1)} %get-tuple-element.564), channel_id=1, source_target_pairs={{0,28},{4,24},{8,20},{12,16},{16,12},{20,8},{24,4},{28,0},{1,29},{... | collective-permute-start | bytes 595976 | tf_op jit(solution)/shard_map/ppermute | solution.py:170
  432.7 26.2 %collective-permute-start.9 = (bf16[97,1024]{1,0:T(8,128)(2,1)S(1)}, bf16[97,1024]{1,0:T(8,128)(2,1)S(1)}, u32[]{:S(2)}, u32[]{:S(2)}) collective-permute-start(bf16[97,1024]{1,0:T(8,128)(2,1)S(1)} %get-tuple-element.565), channel_id=1, source_target_pairs={{0,24},{4,28},{8,16},{12,20},{16,8},{20,12},{24,0},{28,4},{1,25},{... | collective-permute-start | bytes 595976 | tf_op jit(solution)/shard_map/ppermute | solution.py:170
  433.2 35.8 %collective-permute-start.8 = (bf16[97,1024]{1,0:T(8,128)(2,1)S(1)}, bf16[97,1024]{1,0:T(8,128)(2,1)S(1)}, u32[]{:S(2)}, u32[]{:S(2)}) collective-permute-start(bf16[97,1024]{1,0:T(8,128)(2,1)S(1)} %get-tuple-element.566), channel_id=1, source_target_pairs={{0,20},{4,16},{8,28},{12,24},{16,4},{20,0},{24,12},{28,8},{1,21},{... | collective-permute-start | bytes 595976 | tf_op jit(solution)/shard_map/ppermute | solution.py:170
  442.5 74.3 %collective-permute-start.7 = (bf16[97,1024]{1,0:T(8,128)(2,1)}, bf16[97,1024]{1,0:T(8,128)(2,1)S(1)}, u32[]{:S(2)}, u32[]{:S(2)}) collective-permute-start(bf16[97,1024]{1,0:T(8,128)(2,1)} %get-tuple-element.567), channel_id=1, source_target_pairs={{0,16},{4,20},{8,24},{12,28},{16,0},{20,4},{24,8},{28,12},{1,17},{... | collective-permute-start | bytes 595976 | tf_op jit(solution)/shard_map/ppermute | solution.py:170
  444.7 72.1 %collective-permute-start.6 = (bf16[97,1024]{1,0:T(8,128)(2,1)}, bf16[97,1024]{1,0:T(8,128)(2,1)S(1)}, u32[]{:S(2)}, u32[]{:S(2)}) collective-permute-start(bf16[97,1024]{1,0:T(8,128)(2,1)} %get-tuple-element.568), channel_id=1, source_target_pairs={{0,12},{4,8},{8,4},{12,0},{16,28},{20,24},{24,20},{28,16},{1,13},{... | collective-permute-start | bytes 595976 | tf_op jit(solution)/shard_map/ppermute | solution.py:170
  458.9 57.9 %collective-permute-start.5 = (bf16[97,1024]{1,0:T(8,128)(2,1)S(1)}, bf16[97,1024]{1,0:T(8,128)(2,1)S(1)}, u32[]{:S(2)}, u32[]{:S(2)}) collective-permute-start(bf16[97,1024]{1,0:T(8,128)(2,1)S(1)} %get-tuple-element.569), channel_id=1, source_target_pairs={{0,8},{4,12},{8,0},{12,4},{16,24},{20,28},{24,16},{28,20},{1,9},{5... | collective-permute-start | bytes 595976 | tf_op jit(solution)/shard_map/ppermute | solution.py:170
  469.0 47.8 %collective-permute-start.4 = (bf16[97,1024]{1,0:T(8,128)(2,1)S(1)}, bf16[97,1024]{1,0:T(8,128)(2,1)S(1)}, u32[]{:S(2)}, u32[]{:S(2)}) collective-permute-start(bf16[97,1024]{1,0:T(8,128)(2,1)S(1)} %get-tuple-element.563), channel_id=1, source_target_pairs={{0,4},{4,0},{8,12},{12,8},{16,20},{20,16},{24,28},{28,24},{1,5},{5... | collective-permute-start | bytes 595976 | tf_op jit(solution)/shard_map/ppermute | solution.py:170
  520.2 23.0 %collective-permute-start.11 = (bf16[97,1024]{1,0:T(8,128)(2,1)S(1)}, bf16[97,1024]{1,0:T(8,128)(2,1)}, u32[]{:S(2)}, u32[]{:S(2)}) collective-permute-start(bf16[97,1024]{1,0:T(8,128)(2,1)S(1)} %get-tuple-element.548), channel_id=1, source_target_pairs={{0,4},{4,0},{8,12},{12,8},{16,20},{20,16},{24,28},{28,24},{1,5},{5... | collective-permute-start | bytes 595976 | tf_op jit(solution)/shard_map/ppermute | solution.py:176
  537.3 27.2 %collective-permute-start.12 = (bf16[97,1024]{1,0:T(8,128)(2,1)S(1)}, bf16[97,1024]{1,0:T(8,128)(2,1)S(1)}, u32[]{:S(2)}, u32[]{:S(2)}) collective-permute-start(bf16[97,1024]{1,0:T(8,128)(2,1)S(1)} %get-tuple-element.548), channel_id=1, source_target_pairs={{0,8},{4,12},{8,0},{12,4},{16,24},{20,28},{24,16},{28,20},{1,9},{5... | collective-permute-start | bytes 595976 | tf_op jit(solution)/shard_map/ppermute | solution.py:176
  538.5 37.0 %collective-permute-start.13 = (bf16[97,1024]{1,0:T(8,128)(2,1)S(1)}, bf16[97,1024]{1,0:T(8,128)(2,1)S(1)}, u32[]{:S(2)}, u32[]{:S(2)}) collective-permute-start(bf16[97,1024]{1,0:T(8,128)(2,1)S(1)} %get-tuple-element.548), channel_id=1, source_target_pairs={{0,12},{4,8},{8,4},{12,0},{16,28},{20,24},{24,20},{28,16},{1,13},{... | collective-permute-start | bytes 595976 | tf_op jit(solution)/shard_map/ppermute | solution.py:176
  539.4 36.8 %collective-permute-start.14 = (bf16[97,1024]{1,0:T(8,128)(2,1)S(1)}, bf16[97,1024]{1,0:T(8,128)(2,1)S(1)}, u32[]{:S(2)}, u32[]{:S(2)}) collective-permute-start(bf16[97,1024]{1,0:T(8,128)(2,1)S(1)} %get-tuple-element.548), channel_id=1, source_target_pairs={{0,16},{4,20},{8,24},{12,28},{16,0},{20,4},{24,8},{28,12},{1,17},{... | collective-permute-start | bytes 595976 | tf_op jit(solution)/shard_map/ppermute | solution.py:176
  541.1 50.6 %collective-permute-start.15 = (bf16[97,1024]{1,0:T(8,128)(2,1)S(1)}, bf16[97,1024]{1,0:T(8,128)(2,1)S(1)}, u32[]{:S(2)}, u32[]{:S(2)}) collective-permute-start(bf16[97,1024]{1,0:T(8,128)(2,1)S(1)} %get-tuple-element.548), channel_id=1, source_target_pairs={{0,20},{4,16},{8,28},{12,24},{16,4},{20,0},{24,12},{28,8},{1,21},{... | collective-permute-start | bytes 595976 | tf_op jit(solution)/shard_map/ppermute | solution.py:176
  543.2 49.2 %collective-permute-start.16 = (bf16[97,1024]{1,0:T(8,128)(2,1)S(1)}, bf16[97,1024]{1,0:T(8,128)(2,1)S(1)}, u32[]{:S(2)}, u32[]{:S(2)}) collective-permute-start(bf16[97,1024]{1,0:T(8,128)(2,1)S(1)} %get-tuple-element.548), channel_id=1, source_target_pairs={{0,24},{4,28},{8,16},{12,20},{16,8},{20,12},{24,0},{28,4},{1,25},{... | collective-permute-start | bytes 595976 | tf_op jit(solution)/shard_map/ppermute | solution.py:176
  564.6 30.8 %collective-permute-start.17 = (bf16[97,1024]{1,0:T(8,128)(2,1)S(1)}, bf16[97,1024]{1,0:T(8,128)(2,1)S(1)}, u32[]{:S(2)}, u32[]{:S(2)}) collective-permute-start(bf16[97,1024]{1,0:T(8,128)(2,1)S(1)} %get-tuple-element.548), channel_id=1, source_target_pairs={{0,28},{4,24},{8,20},{12,16},{16,12},{20,8},{24,4},{28,0},{1,29},{... | collective-permute-start | bytes 595976 | tf_op jit(solution)/shard_map/ppermute | solution.py:176
  (64 other events, 167.7 us)
Sparse Core Ops, SparseCore 0:
  9.6 49.1 all-gather.5
  60.3 22.5 all-gather.7
  84.4 58.2 all-gather.9
  144.1 58.2 all-gather.11
  385.5 127.1 all-reduce.4
  532.9 144.7 all-reduce.6
